TPU v7x, 512 devices: a whole 4x8x8 slice. The times are simulated.
512 devices in a mesh: band: 32 (over z, x), lev: 16 (over y, core).
Axes of the slice: x: 4, y: 8, z: 8, core: 2. Of those that a mesh axis runs over, the one named last changes fastest.
Arguments:
- spectral: bfloat16 [4, 128, 640, 640], P(None, 'lev', 'band'), may hold values from -6 to 6
- legendre_value: bfloat16 [640, 32, 640], P('band'), may hold values from -0.009765625 to 0.009765625
- legendre_slope: bfloat16 [640, 32, 640], P('band'), may hold values from -0.009765625 to 0.009765625
- wave_numbers: int32 [640], replicated, may hold values from 0 to 639, each once
- aerosol_old: bfloat16 [40, 128, 32, 2688], P(None, 'lev', 'band'), may hold values from 0 to 2
- vertical_weight: bfloat16 [3, 128, 32, 2688], P(None, 'lev', 'band'), may hold values from 0 to 0.59765625
- send_blocks: int32 [32, 5, 4], P('band'), may hold values from -1 to 20, as said below
- depart_slot: int32 [672, 4], P('band'), may hold values from 0 to 19, as said below
- depart_offset: int32 [672, 4, 128], P('band'), may hold values from 0 to 124
- depart_weight: bfloat16 [672, 4, 4, 128], P('band'), may hold values from 0 to 0.5
Outputs:
- wind_grid: bfloat16 [2, 128, 32, 2688], P(None, 'lev', 'band')
- aerosol_new: bfloat16 [40, 128, 32, 2688], P(None, 'lev', 'band')
- aerosol_flux: bfloat16 [2, 128, 32, 2688], P(None, 'lev', 'band')
Inputs may be any that keep to these rules, and one draw needn't show every extreme that they name: `send_blocks`: row b, offset o lists up to 4 of band b's own blocks (block l * 21 + c is the band's latitude l, longitudes c * 128 onward) that band b + o - 2 reads; -1 marks an empty slot; offsets toward bands that do not exist are empty; some rows are full. `depart_slot`: slot o * 4 + e of band r's pool is what band r - o + 2 lists at offset o, slot e; arrival block g belongs to band g // 21 and every slot it names is filled.
All inputs are finite; a program needn't handle non-finite values.
Results may differ from a plain program's by a relative error of at most 0.0062.
Values may be sent and summed in bfloat16 or wider, within the bound.
No kernel may reach another device: no remote copies, remote signals or barrier semaphores. Data moves between devices by JAX's collectives and lax.ppermute only.
A program may use at most 128 MiB of HBM per device.

v0:
```python
import math

import jax
import jax.numpy as jnp
from jax import lax
from jax.sharding import PartitionSpec as P

WAVES = 640
NLON = 2688
BLK = 128


def extended(cells, sides, width):
    for axis, dim in sides:
        count = lax.axis_size(axis)
        ends = count - 1
        head = lax.slice_in_dim(cells, 0, width, axis=dim)
        tail = lax.slice_in_dim(cells, cells.shape[dim] - width, cells.shape[dim], axis=dim)
        cells = jnp.concatenate(
            [
                lax.ppermute(tail, axis, [(i, (i + 1) % count) for i in range(ends)]),
                cells,
                lax.ppermute(head, axis, [((i + 1) % count, i) for i in range(ends)]),
            ],
            axis=dim,
        )
    return cells


def shifted(value, axis, steps):
    count = lax.axis_size(axis)
    leading, last = (max(0, -steps), min(count, count - steps))
    return lax.ppermute(value, axis, [(source, source + steps) for source in range(leading, last)])


def fourier_table(wave_numbers, lon_count):
    longitudes = jnp.arange(lon_count, dtype=jnp.int32)
    phases = wave_numbers[:, None] * longitudes[None, :] % lon_count
    angles = phases.astype(jnp.float32) * (2.0 * math.pi / lon_count)
    doubled = jnp.where(wave_numbers == 0, 1.0, 2.0).astype(jnp.float32)[:, None]
    return jnp.stack([doubled * jnp.cos(angles), -doubled * jnp.sin(angles)]).astype(jnp.bfloat16)


def stencil_matrix(depart_offset, depart_weight):
    width = depart_offset.shape[-1]
    columns = jnp.arange(width, dtype=jnp.int32)
    summed = jnp.zeros(depart_offset.shape[:2] + (width, width), jnp.float32)
    for term_index in range(depart_weight.shape[2]):
        matches = columns[None, None, :, None] == depart_offset[:, :, None, :] + term_index
        summed = summed + jnp.where(
            matches, depart_weight[:, :, term_index, None, :].astype(jnp.float32), 0.0
        )
    return summed


def shards(
    spectral,
    legendre_value,
    legendre_slope,
    wave_numbers,
    aerosol_old,
    vertical_weight,
    send_blocks,
    depart_slot,
    depart_offset,
    depart_weight,
):
    band_here = lax.axis_index("band")
    wave_local = spectral.shape[2]
    own_waves = lax.dynamic_slice_in_dim(wave_numbers, band_here * wave_local, wave_local, 0)
    value_terms = jnp.einsum(
        "slj,xksj->xkls", legendre_value, spectral, preferred_element_type=jnp.float32
    )
    slope_terms = jnp.einsum(
        "slj,xksj->xkls", legendre_slope, spectral, preferred_element_type=jnp.float32
    )
    factor = own_waves.astype(jnp.float32) / WAVES
    coefficients = jnp.stack(
        [
            -slope_terms[0] - factor * value_terms[3],
            -slope_terms[1] + factor * value_terms[2],
            slope_terms[2] - factor * value_terms[1],
            slope_terms[3] + factor * value_terms[0],
        ]
    ).astype(jnp.bfloat16)
    fourier = fourier_table(wave_numbers, NLON)
    received = lax.all_to_all(coefficients, "band", split_axis=2, concat_axis=3, tiled=True)
    paired = received.reshape(2, 2, received.shape[1], received.shape[2], received.shape[3])
    wind_grid = jnp.einsum(
        "wxklm,xmi->wkli", paired, fourier, preferred_element_type=jnp.float32
    ).astype(jnp.bfloat16)
    padded = extended(aerosol_old, (("lev", 1),), 1)
    weights = vertical_weight.astype(jnp.float32)
    vertical_sum = (
        weights[0] * padded[:, :-2] + weights[1] * padded[:, 1:-1] + weights[2] * padded[:, 2:]
    )
    remapped = vertical_sum.astype(jnp.bfloat16)
    bin_count, level_count, lat_count, lon_count = remapped.shape
    block_count = lon_count // BLK
    blocks = remapped.reshape(bin_count, level_count, lat_count, block_count, BLK).transpose(
        2, 3, 0, 1, 4
    )
    blocks = blocks.reshape(lat_count * block_count, bin_count * level_count, BLK)
    listed = send_blocks[0]
    outgoing = jnp.take(blocks, jnp.clip(listed, 0, blocks.shape[0] - 1), axis=0)
    stencil = stencil_matrix(depart_offset, depart_weight).astype(jnp.bfloat16)
    offsets = listed.shape[0]
    reach_bands = offsets // 2
    pieces = []
    for offset_index in range(offsets):
        shift_by = offset_index - reach_bands
        if shift_by == 0:
            pieces.append(outgoing[offset_index])
        else:
            pieces.append(shifted(outgoing[offset_index], "band", shift_by))
    pooled = jnp.stack(pieces)
    flattened = pooled.reshape(pooled.shape[0] * pooled.shape[1], pooled.shape[2], pooled.shape[3])
    chosen = jnp.take(flattened, depart_slot, axis=0)
    block_rows = jnp.einsum("jifq,jiqp->jfp", chosen, stencil, preferred_element_type=jnp.float32)
    aerosol_new = block_rows.reshape(lat_count, block_count, bin_count, level_count, BLK).transpose(
        2, 3, 0, 1, 4
    )
    aerosol_new = aerosol_new.reshape(bin_count, level_count, lat_count, lon_count).astype(
        jnp.bfloat16
    )
    average = jnp.mean(aerosol_new.astype(jnp.float32), axis=0)
    aerosol_flux = (wind_grid.astype(jnp.float32) * average[None]).astype(jnp.bfloat16)
    return (wind_grid, aerosol_new, aerosol_flux)


def solution(mesh):
    return jax.shard_map(
        shards,
        mesh=mesh,
        in_specs=(
            P(None, "lev", "band", None),
            P("band", None, None),
            P("band", None, None),
            P(),
            P(None, "lev", "band", None),
            P(None, "lev", "band", None),
            P("band", None, None),
            P("band", None),
            P("band", None, None),
            P("band", None, None, None),
        ),
        out_specs=(
            P(None, "lev", "band", None),
            P(None, "lev", "band", None),
            P(None, "lev", "band", None),
        ),
        check_vma=False,
    )
```

profile of v0, /device:TPU:90, one launch (start us, length us, event | category | flops | bytes accessed | tf_op | source)
XLA Modules:
  0.0 130.1 jit_solution(15123765636053419091)
XLA Ops:
  0.7 3.6 %fusion.41 = (bf16[40,1,1,2688]{3,1,0,2:T(2,128)(2,1)}, bf16[40,1,1,2688]{3,1,0,2:T(2,128)(2,1)S(1)}) fusion(bf16[40,8,1,2688]{3,1,0,2:T(8,128)(2,1)} %bitcast.107), kind=kLoop, calls=%fused_computation.98 | loop fusion | bytes 860160 | tf_op jit(solution)/shard_map/slice | solution.py:18
  4.3 1.9 %collective-permute-start = (bf16[40,1,1,2688]{3,1,0,2:T(2,128)(2,1)}, bf16[40,1,1,2688]{3,1,0,2:T(2,128)(2,1)}, u32[]{:S(2)}, u32[]{:S(2)}) collective-permute-start(bf16[40,1,1,2688]{3,1,0,2:T(2,128)(2,1)} %get-tuple-element.18), channel_id=1, source_target_pairs={{0,1},{1,2},{2,3},{3,4},{4,5},{5,6},{6,7},{7,8},{8,9},{9,10},{10,1... | collective-permute-start | bytes 645128 | tf_op jit(solution)/shard_map/ppermute | solution.py:21
  6.2 3.6 %collective-permute-start.1 = (bf16[40,1,1,2688]{3,1,0,2:T(2,128)(2,1)S(1)}, bf16[40,1,1,2688]{3,1,0,2:T(2,128)(2,1)}, u32[]{:S(2)}, u32[]{:S(2)}) collective-permute-start(bf16[40,1,1,2688]{3,1,0,2:T(2,128)(2,1)S(1)} %get-tuple-element.19), channel_id=1, source_target_pairs={{1,0},{2,1},{3,2},{4,3},{5,4},{6,5},{7,6},{8,7},{9,8},{10,9},{11,1... | collective-permute-start | bytes 645128 | tf_op jit(solution)/shard_map/ppermute | solution.py:23
  9.8 1.5 %convolution_bitcast_fusion = f32[4,8,32,20]{2,1,0,3:T(8,128)S(1)} fusion(bf16[20,32,640]{2,1,0:T(8,128)(2,1)S(1)} %copy-done, bf16[4,8,20,640]{3,1,2,0:T(8,128)(2,1)} %param.10), kind=kOutput, calls=%fused_computation.42 | convolution fusion | flops 26214400 | bytes 1720320 | tf_op jit(solution)/shard_map/slj,xksj->xkls/dot_general | solution.py:71
  11.4 0.4 convolution_bitcast_fusion.1
  12.0 0.6 copy.67
  12.6 1.0 reshape.270
  13.6 12.6 %all-to-all-start = ((bf16[32,2,320]{2,1,0:T(2,128)(2,1)}), bf16[32,2,320]{2,1,0:T(2,128)(2,1)}, u32[]{:S(2)}, u32[]{:S(2)}) async-start(bf16[32,2,320]{2,1,0:T(2,128)(2,1)} %reshape.270), calls=%async_computation | async-start | bytes 98304 | tf_op jit(solution)/shard_map/all_to_all | solution.py:87
  26.3 0.9 convert_element_type.95
  27.7 0.1 copy.69
  27.8 32.0 %multiply_convert_fusion.1 = (bf16[1,640,2688]{2,1,0:T(8,128)(2,1)}, bf16[1,640,2688]{2,1,0:T(8,128)(2,1)}) fusion(s32[640]{0:T(1024)S(1)} %copy-done.14, f32[640]{0:T(1024)S(1)} %get-tuple-element.41, f32[640]{0:T(1024)S(1)} %get-tuple-element.42), kind=kLoop, calls=%fused_computation.9 | loop fusion | flops 22364160 | bytes 6888960 | tf_op jit(solution)/shard_map/convert.5
  59.8 0.8 slice_convert_fusion.3
  60.6 3.3 %copy_bitcast_fusion.1 = bf16[21,320,128]{2,1,0:T(8,128)(2,1)S(1)} fusion(bf16[40,8,1,2688]{3,1,0,2:T(8,128)(2,1)S(1)} %bitcast.108, bf16[40,1,1,2688]{3,1,0,2:T(2,128)(2,1)} %collective-permute-done.1, bf16[40,1,1,2688]{3,1,0,2:T(2,128)(2,1)} %collective-permute-done, f32[8,2688]{1,0:T(8,128)S(1)} %get-tuple-element.30, ...), kind=kLoop, calls=%fused_computation.40 | loop fusion | flops 12902400 | bytes 4128768 | tf_op jit(solution)/shard_map/reshape | solution.py:103
  64.0 2.0 %gather_fusion = bf16[20,320,128]{2,1,0:T(8,128)(2,1)} fusion(bf16[21,320,128]{2,1,0:T(8,128)(2,1)S(1)} %copy_bitcast_fusion.1, s32[1024]{0:T(1024)S(1)} %pad_clamp_fusion.1), kind=kCustom, calls=%fused_computation | custom fusion | bytes 3276880 | tf_op jit(solution)/shard_map/jit(_take)/gather | solution.py:105
  66.0 1.6 %broadcast_select_fusion = bf16[5,4,320,128]{3,2,1,0:T(8,128)(2,1)S(1)} fusion(bf16[5,4,320,128]{3,2,1,0:T(8,128)(2,1)} %bitcast.106, pred[5,4]{1,0:T(8,128)(4,1)S(1)} %copy.70), kind=kLoop, calls=%fused_computation.41 | loop fusion | flops 819200 | bytes 3276820 | tf_op jit(solution)/shard_map/jit(_take)/select_n | solution.py:105
  67.6 1.2 copy-done.1
  68.8 4.0 %collective-permute-start.2 = (bf16[4,320,128]{2,1,0:T(8,128)(2,1)S(1)}, bf16[4,320,128]{2,1,0:T(8,128)(2,1)S(1)}, u32[]{:S(2)}, u32[]{:S(2)}) collective-permute-start(bf16[4,320,128]{2,1,0:T(8,128)(2,1)S(1)} %get-tuple-element.24), channel_id=1, source_target_pairs={{32,0},{48,16},{64,32},{80,48},{96,64},{112,80},{128,96},{144,112}... | collective-permute-start | bytes 983048 | tf_op jit(solution)/shard_map/ppermute | solution.py:33
  72.8 0.7 broadcast_add_fusion.2
  73.5 3.4 %collective-permute-start.3 = (bf16[4,320,128]{2,1,0:T(8,128)(2,1)S(1)}, bf16[4,320,128]{2,1,0:T(8,128)(2,1)S(1)}, u32[]{:S(2)}, u32[]{:S(2)}) collective-permute-start(bf16[4,320,128]{2,1,0:T(8,128)(2,1)S(1)} %get-tuple-element.23), channel_id=1, source_target_pairs={{16,0},{32,16},{48,32},{64,48},{80,64},{96,80},{112,96},{128,112},... | collective-permute-start | bytes 983048 | tf_op jit(solution)/shard_map/ppermute | solution.py:33
  76.9 1.2 reshape.271
  78.2 1.0 reshape.237
  79.1 3.7 %collective-permute-done.2 = bf16[4,320,128]{2,1,0:T(8,128)(2,1)S(1)} collective-permute-done((bf16[4,320,128]{2,1,0:T(8,128)(2,1)S(1)}, bf16[4,320,128]{2,1,0:T(8,128)(2,1)S(1)}, u32[]{:S(2)}, u32[]{:S(2)}) %collective-permute-start.2) | collective-permute-done | bytes 327712 | tf_op jit(solution)/shard_map/ppermute | solution.py:33
  82.8 6.7 %collective-permute-done.3 = bf16[4,320,128]{2,1,0:T(8,128)(2,1)S(1)} collective-permute-done((bf16[4,320,128]{2,1,0:T(8,128)(2,1)S(1)}, bf16[4,320,128]{2,1,0:T(8,128)(2,1)S(1)}, u32[]{:S(2)}, u32[]{:S(2)}) %collective-permute-start.3) | collective-permute-done | bytes 327712 | tf_op jit(solution)/shard_map/ppermute | solution.py:33
  89.5 1.3 slice_bitcast_fusion
  90.8 2.5 %collective-permute-start.4 = (bf16[4,320,128]{2,1,0:T(8,128)(2,1)S(1)}, bf16[4,320,128]{2,1,0:T(8,128)(2,1)S(1)}, u32[]{:S(2)}, u32[]{:S(2)}) collective-permute-start(bf16[4,320,128]{2,1,0:T(8,128)(2,1)S(1)} %get-tuple-element.21), channel_id=1, source_target_pairs={{0,16},{16,32},{32,48},{48,64},{64,80},{80,96},{96,112},{112,128},... | collective-permute-start | bytes 983048 | tf_op jit(solution)/shard_map/ppermute | solution.py:33
  93.3 5.9 %collective-permute-start.5 = (bf16[4,320,128]{2,1,0:T(8,128)(2,1)S(1)}, bf16[4,320,128]{2,1,0:T(8,128)(2,1)S(1)}, u32[]{:S(2)}, u32[]{:S(2)}) collective-permute-start(bf16[4,320,128]{2,1,0:T(8,128)(2,1)S(1)} %get-tuple-element.20), channel_id=1, source_target_pairs={{0,32},{16,48},{32,64},{48,80},{64,96},{80,112},{96,128},{112,144}... | collective-permute-start | bytes 983048 | tf_op jit(solution)/shard_map/ppermute | solution.py:33
  99.2 4.1 %fusion.11 = bf16[2,8,2688]{2,1,0:T(8,128)(2,1)S(1)} fusion(bf16[2,2,8,640]{3,2,1,0:T(8,128)(2,1)} %reshape.237, bf16[1,640,2688]{2,1,0:T(8,128)(2,1)} %get-tuple-element.40, bf16[1,640,2688]{2,1,0:T(8,128)(2,1)} %get-tuple-element.39), kind=kOutput, calls=%fused_computation.26 | convolution fusion | flops 113584128 | bytes 7008256 | tf_op jit(solution)/shard_map/wxklm,xmi->wkli/dot_general | solution.py:89
  103.5 11.5 %collective-permute-done.5 = bf16[4,320,128]{2,1,0:T(8,128)(2,1)S(1)} collective-permute-done((bf16[4,320,128]{2,1,0:T(8,128)(2,1)S(1)}, bf16[4,320,128]{2,1,0:T(8,128)(2,1)S(1)}, u32[]{:S(2)}, u32[]{:S(2)}) %collective-permute-start.5) | collective-permute-done | bytes 327712 | tf_op jit(solution)/shard_map/ppermute | solution.py:33
  115.1 6.4 %gather_fusion.1 = bf16[84,320,128]{2,1,0:T(8,128)(2,1)} fusion(bf16[20,320,128]{2,1,0:T(8,128)(2,1)S(1)} %bitcast.104, s32[1024]{0:T(1024)S(1)} %pad_clamp_fusion), kind=kCustom, calls=%fused_computation.1 | custom fusion | bytes 13762896 | tf_op jit(solution)/shard_map/jit(_take)/gather | solution.py:118
  121.6 6.4 %convert_reduce_fusion = (f32[21,8,128]{2,1,0:T(8,128)S(1)}, bf16[21,320,128]{2,1,0:T(8,128)(2,1)S(1)}) fusion(f32[21,4,128]{2,1,0:T(4,128)S(1)} %bitcast.114, s32[21,4,128]{2,1,0:T(4,128)S(1)} %copy-done.8, f32[21,4,128]{2,1,0:T(4,128)S(1)} %bitcast.115, s32[21,4,128]{2,1,0:T(4,128)S(1)} %copy-done.9, f32[21,4,128]{2,1,0:T(4,128)S(1)} %bitcast.113, ...), kind=kOutput, calls=%fused_computation.21 | convolution fusion | flops 903318528 | bytes 9031764 | tf_op jit(solution)/shard_map/jifq,jiqp->jfp/dot_general | solution.py:119
  128.0 1.4 %copy_bitcast_fusion = bf16[40,8,1,2688]{3,1,2,0:T(8,128)(2,1)} fusion(bf16[21,320,128]{2,1,0:T(8,128)(2,1)S(1)} %get-tuple-element.44), kind=kLoop, calls=%fused_computation.39 | loop fusion | bytes 3440640 | tf_op jit(solution)/shard_map/convert_element_type | solution.py:123
  129.4 0.7 fusion.28
  (60 shorter events, 1.2 us)
Async XLA Ops:
  0.6 9.2 %copy-start = (bf16[20,32,640]{2,1,0:T(8,128)(2,1)S(1)}, bf16[20,32,640]{2,1,0:T(8,128)(2,1)}, u32[]{:S(2)}) copy-start(bf16[20,32,640]{2,1,0:T(8,128)(2,1)} %param.11) | copy-start | bytes 2457604
  0.6 10.7 %copy-start.3 = (bf16[4,8,20,640]{3,1,2,0:T(8,128)(2,1)S(1)}, bf16[4,8,20,640]{3,1,2,0:T(8,128)(2,1)}, u32[]{:S(2)}) copy-start(bf16[4,8,20,640]{3,1,2,0:T(8,128)(2,1)} %param.10) | copy-start | bytes 2457604
  0.7 10.7 %copy-start.4 = (bf16[20,32,640]{2,1,0:T(8,128)(2,1)S(1)}, bf16[20,32,640]{2,1,0:T(8,128)(2,1)}, u32[]{:S(2)}) copy-start(bf16[20,32,640]{2,1,0:T(8,128)(2,1)} %param.12) | copy-start | bytes 2457604
  0.7 11.1 %copy-start.14 = (s32[640]{0:T(1024)S(1)}, s32[640]{0:T(1024)}, u32[]{:S(2)}) copy-start(s32[640]{0:T(1024)} %param.13) | copy-start | bytes 7684
  0.7 25.5 %copy-start.15 = (s32[1,5,4]{1,2,0:T(4,128)S(1)}, s32[1,5,4]{1,2,0:T(4,128)}, u32[]{:S(2)}) copy-start(s32[1,5,4]{1,2,0:T(4,128)} %param.16) | copy-start | bytes 244
  0.7 25.5 %copy-start.16 = (s32[21,4]{0,1:T(4,128)S(1)}, s32[21,4]{0,1:T(4,128)}, u32[]{:S(2)}) copy-start(s32[21,4]{0,1:T(4,128)} %param.17) | copy-start | bytes 1012
  4.3 56.4 %collective-permute-start = (bf16[40,1,1,2688]{3,1,0,2:T(2,128)(2,1)}, bf16[40,1,1,2688]{3,1,0,2:T(2,128)(2,1)}, u32[]{:S(2)}, u32[]{:S(2)}) collective-permute-start(bf16[40,1,1,2688]{3,1,0,2:T(2,128)(2,1)} %get-tuple-element.18), channel_id=1, source_target_pairs={{0,1},{1,2},{2,3},{3,4},{4,5},{5,6},{6,7},{7,8},{8,9},{9,10},{10,1... | collective-permute-start | bytes 645128 | tf_op jit(solution)/shard_map/ppermute | solution.py:21
  6.2 54.5 %collective-permute-start.1 = (bf16[40,1,1,2688]{3,1,0,2:T(2,128)(2,1)S(1)}, bf16[40,1,1,2688]{3,1,0,2:T(2,128)(2,1)}, u32[]{:S(2)}, u32[]{:S(2)}) collective-permute-start(bf16[40,1,1,2688]{3,1,0,2:T(2,128)(2,1)S(1)} %get-tuple-element.19), channel_id=1, source_target_pairs={{1,0},{2,1},{3,2},{4,3},{5,4},{6,5},{7,6},{8,7},{9,8},{10,9},{11,1... | collective-permute-start | bytes 645128 | tf_op jit(solution)/shard_map/ppermute | solution.py:23
  13.6 63.3 %all-to-all-start = ((bf16[32,2,320]{2,1,0:T(2,128)(2,1)}), bf16[32,2,320]{2,1,0:T(2,128)(2,1)}, u32[]{:S(2)}, u32[]{:S(2)}) async-start(bf16[32,2,320]{2,1,0:T(2,128)(2,1)} %reshape.270), calls=%async_computation | async-start | bytes 98304 | tf_op jit(solution)/shard_map/all_to_all | solution.py:87
  27.8 32.0 %copy-start.5 = (bf16[21,4,4,128]{3,2,1,0:T(4,128)(2,1)S(1)}, bf16[21,4,4,128]{3,2,1,0:T(4,128)(2,1)}, u32[]{:S(2)}) copy-start(bf16[21,4,4,128]{3,2,1,0:T(4,128)(2,1)} %param.19) | copy-start | bytes 258052
  27.8 32.8 %copy-start.2 = (bf16[40,8,1,2688]{3,1,2,0:T(8,128)(2,1)S(1)}, bf16[40,8,1,2688]{3,1,2,0:T(8,128)(2,1)}, u32[]{:S(2)}) copy-start(bf16[40,8,1,2688]{3,1,2,0:T(8,128)(2,1)} %param.14) | copy-start | bytes 5160964
  64.0 8.9 %copy-start.7 = (s32[21,4,128]{2,1,0:T(4,128)S(1)}, s32[21,4,128]{2,1,0:T(4,128)}, u32[]{:S(2)}) copy-start(s32[21,4,128]{2,1,0:T(4,128)} %param.18) | copy-start | bytes 129028
  67.6 1.2 copy-start.1
  68.8 13.9 %collective-permute-start.2 = (bf16[4,320,128]{2,1,0:T(8,128)(2,1)S(1)}, bf16[4,320,128]{2,1,0:T(8,128)(2,1)S(1)}, u32[]{:S(2)}, u32[]{:S(2)}) collective-permute-start(bf16[4,320,128]{2,1,0:T(8,128)(2,1)S(1)} %get-tuple-element.24), channel_id=1, source_target_pairs={{32,0},{48,16},{64,32},{80,48},{96,64},{112,80},{128,96},{144,112}... | collective-permute-start | bytes 983048 | tf_op jit(solution)/shard_map/ppermute | solution.py:33
  73.5 16.0 %collective-permute-start.3 = (bf16[4,320,128]{2,1,0:T(8,128)(2,1)S(1)}, bf16[4,320,128]{2,1,0:T(8,128)(2,1)S(1)}, u32[]{:S(2)}, u32[]{:S(2)}) collective-permute-start(bf16[4,320,128]{2,1,0:T(8,128)(2,1)S(1)} %get-tuple-element.23), channel_id=1, source_target_pairs={{16,0},{32,16},{48,32},{64,48},{80,64},{96,80},{112,96},{128,112},... | collective-permute-start | bytes 983048 | tf_op jit(solution)/shard_map/ppermute | solution.py:33
  90.8 12.6 %collective-permute-start.4 = (bf16[4,320,128]{2,1,0:T(8,128)(2,1)S(1)}, bf16[4,320,128]{2,1,0:T(8,128)(2,1)S(1)}, u32[]{:S(2)}, u32[]{:S(2)}) collective-permute-start(bf16[4,320,128]{2,1,0:T(8,128)(2,1)S(1)} %get-tuple-element.21), channel_id=1, source_target_pairs={{0,16},{16,32},{32,48},{48,64},{64,80},{80,96},{96,112},{112,128},... | collective-permute-start | bytes 983048 | tf_op jit(solution)/shard_map/ppermute | solution.py:33
  93.3 21.7 %collective-permute-start.5 = (bf16[4,320,128]{2,1,0:T(8,128)(2,1)S(1)}, bf16[4,320,128]{2,1,0:T(8,128)(2,1)S(1)}, u32[]{:S(2)}, u32[]{:S(2)}) collective-permute-start(bf16[4,320,128]{2,1,0:T(8,128)(2,1)S(1)} %get-tuple-element.20), channel_id=1, source_target_pairs={{0,32},{16,48},{32,64},{48,80},{64,96},{80,112},{96,128},{112,144}... | collective-permute-start | bytes 983048 | tf_op jit(solution)/shard_map/ppermute | solution.py:33
  103.4 26.0 %copy-start.6 = (bf16[2,8,2688]{2,1,0:T(8,128)(2,1)}, bf16[2,8,2688]{2,1,0:T(8,128)(2,1)S(1)}, u32[]{:S(2)}) copy-start(bf16[2,8,2688]{2,1,0:T(8,128)(2,1)S(1)} %fusion.11) | copy-start | bytes 258052
  115.1 6.5 %copy-start.8 = (s32[21,4,128]{2,1,0:T(4,128)S(1)}, s32[21,4,128]{2,1,0:T(4,128)}, u32[]{:S(2)}) copy-start(s32[21,4,128]{2,1,0:T(4,128)} %get-tuple-element.37) | copy-start | bytes 129028
  115.1 6.5 %copy-start.9 = (s32[21,4,128]{2,1,0:T(4,128)S(1)}, s32[21,4,128]{2,1,0:T(4,128)}, u32[]{:S(2)}) copy-start(s32[21,4,128]{2,1,0:T(4,128)} %get-tuple-element.38) | copy-start | bytes 129028
  115.1 6.5 %copy-start.10 = (f32[21,4,1,128]{3,2,1,0:T(1,128)S(1)}, f32[21,4,1,128]{3,2,1,0:T(1,128)}, u32[]{:S(2)}) copy-start(f32[21,4,1,128]{3,2,1,0:T(1,128)} %get-tuple-element.32) | copy-start | bytes 129028
  115.1 6.5 %copy-start.11 = (f32[21,4,1,128]{3,2,1,0:T(1,128)S(1)}, f32[21,4,1,128]{3,2,1,0:T(1,128)}, u32[]{:S(2)}) copy-start(f32[21,4,1,128]{3,2,1,0:T(1,128)} %get-tuple-element.33) | copy-start | bytes 129028
  115.1 6.5 %copy-start.12 = (f32[21,4,1,128]{3,2,1,0:T(1,128)S(1)}, f32[21,4,1,128]{3,2,1,0:T(1,128)}, u32[]{:S(2)}) copy-start(f32[21,4,1,128]{3,2,1,0:T(1,128)} %get-tuple-element.34) | copy-start | bytes 129028
  115.1 6.5 %copy-start.13 = (f32[21,4,1,128]{3,2,1,0:T(1,128)S(1)}, f32[21,4,1,128]{3,2,1,0:T(1,128)}, u32[]{:S(2)}) copy-start(f32[21,4,1,128]{3,2,1,0:T(1,128)} %get-tuple-element.35) | copy-start | bytes 129028
where the time goes:
time: 131 us; the launch traced here: 130 us
  other arithmetic  40.3 us (31%)
  starting transfers between devices  33.9 us (26%)
  waiting for transfers between devices  21.9 us (17%)
  local copies, waits for them, and re-layouts  20.4 us (16%)
  matrix products  12.5 us (10%)
    another operation x2, other arithmetic  32.1 us
    ppermute x4, waiting for transfers between devices, shifted(): lax.ppermute(value, axis, [(source, source + steps) for source in range(l...  21.9 us
    ppermute x4, starting transfers between devices, shifted(): lax.ppermute(value, axis, [(source, source + steps) for source in range(l...  15.8 us
    all_to_all x1, starting transfers between devices, shards(): lax.all_to_all(coefficients, 'band', split_axis=2, concat_axis=3, tiled=T...  12.6 us
    gather x1, local copies, waits for them, and re-layouts, shards(): chosen = jnp.take(flattened, depart_slot, axis=0)  6.44 us
    dot_general x1, matrix products, shards(): jnp.einsum('jifq,jiqp->jfp', chosen, stencil, preferred_element_type=jnp....  6.41 us
    dot_general x1, matrix products, shards(): jnp.einsum('wxklm,xmi->wkli', paired, fourier, preferred_element_type=jnp...  4.14 us
    ppermute x1, starting transfers between devices, extended(): lax.ppermute(head, axis, [((i + 1) % count, i) for i in range(ends)])  3.64 us
  transfers between devices with their start and end apart: 7, of which 3 were waited for; matrix products, arithmetic and copies ran while one was open for 40% of the time, Pallas kernels for 0%

commit v1 on v0

--- a/solution.py
+++ b/solution.py
@@ -34,11 +34,22 @@
 
 
 def fourier_table(wave_numbers, lon_count):
-    longitudes = jnp.arange(lon_count, dtype=jnp.int32)
-    phases = wave_numbers[:, None] * longitudes[None, :] % lon_count
-    angles = phases.astype(jnp.float32) * (2.0 * math.pi / lon_count)
+    inner = BLK
+    outer = lon_count // inner
+    waves = wave_numbers[:, None]
+    near = (waves * jnp.arange(inner, dtype=jnp.int32)[None, :]) % lon_count
+    far = (waves * (jnp.arange(outer, dtype=jnp.int32) * inner)[None, :]) % lon_count
+    scale = 2.0 * math.pi / lon_count
+    near_angle = near.astype(jnp.float32) * scale
+    far_angle = far.astype(jnp.float32) * scale
+    near_cos = jnp.cos(near_angle)[:, None, :]
+    near_sin = jnp.sin(near_angle)[:, None, :]
+    far_cos = jnp.cos(far_angle)[:, :, None]
+    far_sin = jnp.sin(far_angle)[:, :, None]
+    cosine = (near_cos * far_cos - near_sin * far_sin).reshape(-1, lon_count)
+    sine = (near_sin * far_cos + near_cos * far_sin).reshape(-1, lon_count)
     doubled = jnp.where(wave_numbers == 0, 1.0, 2.0).astype(jnp.float32)[:, None]
-    return jnp.stack([doubled * jnp.cos(angles), -doubled * jnp.sin(angles)]).astype(jnp.bfloat16)
+    return jnp.stack([doubled * cosine, -doubled * sine]).astype(jnp.bfloat16)
 
 
 def stencil_matrix(depart_offset, depart_weight):

time: 131 us -> 132 us (level)
  the two profiles are of different devices: /device:TPU:90 before, /device:TPU:66 now
where the time goes in v1:
time: 132 us; the launch traced here: 131 us
  local copies, waits for them, and re-layouts  35.6 us (27%)
  starting transfers between devices  32.7 us (25%)
  other arithmetic  24.3 us (18%)
  waiting for transfers between devices  23.8 us (18%)
  matrix products  13.8 us (10%)
    ppermute x4, waiting for transfers between devices, shifted(): lax.ppermute(value, axis, [(source, source + steps) for source in range(l...  23.8 us
    ppermute x4, starting transfers between devices, shifted(): lax.ppermute(value, axis, [(source, source + steps) for source in range(l...  15.8 us
    all_to_all x1, starting transfers between devices, shards(): lax.all_to_all(coefficients, 'band', split_axis=2, concat_axis=3, tiled=T...  12.6 us
    another operation x2, other arithmetic  8.57 us
    sub x1, local copies, waits for them, and re-layouts, fourier_table(): cosine = (near_cos * far_cos - near_sin * far_sin).reshape(-1, lon_count)  8.48 us
    add x1, local copies, waits for them, and re-layouts, fourier_table(): sine = (near_sin * far_cos + near_cos * far_sin).reshape(-1, lon_count)  8.42 us
    sub x1, other arithmetic, fourier_table(): cosine = (near_cos * far_cos - near_sin * far_sin).reshape(-1, lon_count)  6.84 us
    gather x1, local copies, waits for them, and re-layouts, shards(): chosen = jnp.take(flattened, depart_slot, axis=0)  6.43 us
  transfers between devices with their start and end apart: 7, of which 3 were waited for; matrix products, arithmetic and copies ran while one was open for 37% of the time, Pallas kernels for 0%

profile of v1, /device:TPU:66, one launch (start us, length us, event | category | flops | bytes accessed | tf_op | source)
XLA Modules:
  0.0 131.4 jit_solution(8513237777807747096)
XLA Ops:
  0.7 1.1 copy-done
  1.8 1.5 %convolution_bitcast_fusion = f32[4,8,32,20]{2,1,0,3:T(8,128)S(1)} fusion(bf16[20,32,640]{2,1,0:T(8,128)(2,1)S(1)} %copy-done, bf16[4,8,20,640]{3,1,2,0:T(8,128)(2,1)} %param.10), kind=kOutput, calls=%fused_computation.37 | convolution fusion | flops 26214400 | bytes 1720320 | tf_op jit(solution)/shard_map/slj,xksj->xkls/dot_general | solution.py:82
  3.3 1.8 %convolution_bitcast_fusion.1 = f32[4,8,32,20]{2,1,0,3:T(8,128)S(1)} fusion(bf16[20,32,640]{2,1,0:T(8,128)(2,1)} %param.12, bf16[4,8,20,640]{3,1,2,0:T(8,128)(2,1)} %param.10), kind=kOutput, calls=%fused_computation.38 | convolution fusion | flops 26214400 | bytes 1720320 | tf_op jit(solution)/shard_map/slj,xksj->xkls/dot_general | solution.py:85
  6.0 1.0 reshape.387
  6.9 12.6 %all-to-all-start = ((bf16[32,2,320]{2,1,0:T(2,128)(2,1)}), bf16[32,2,320]{2,1,0:T(2,128)(2,1)S(1)}, u32[]{:S(2)}, u32[]{:S(2)}) async-start(bf16[32,2,320]{2,1,0:T(2,128)(2,1)} %reshape.387), calls=%async_computation | async-start | bytes 98304 | tf_op jit(solution)/shard_map/all_to_all | solution.py:98
  20.0 1.3 collective-permute-start.1
  21.3 3.1 %collective-permute-start = (bf16[40,1,1,2688]{3,1,0,2:T(2,128)(2,1)S(1)}, bf16[40,1,1,2688]{3,1,0,2:T(2,128)(2,1)S(1)}, u32[]{:S(2)}, u32[]{:S(2)}) collective-permute-start(bf16[40,1,1,2688]{3,1,0,2:T(2,128)(2,1)S(1)} %get-tuple-element.18), channel_id=1, source_target_pairs={{0,1},{1,2},{2,3},{3,4},{4,5},{5,6},{6,7},{7,8},{8,9},{9,10},{10,1... | collective-permute-start | bytes 645128 | tf_op jit(solution)/shard_map/ppermute | solution.py:21
  24.4 1.4 %fusion.28 = (f32[640,128]{0,1:T(8,128)S(1)}, f32[640,128]{0,1:T(8,128)S(1)}) fusion(s32[640]{0:T(1024)S(1)} %copy-done.20), kind=kLoop, calls=%fused_computation.59 | loop fusion | flops 737280 | bytes 657920 | tf_op jit(solution)/shard_map/cos | solution.py:45
  26.2 6.8 %multiply_subtract_fusion = (f32[640,21,128]{0,2,1:T(8,128)}, f32[640,21,128]{0,2,1:T(8,128)}) fusion(f32[640,21]{0,1:T(8,128)S(1)} %get-tuple-element.42, f32[640,128]{0,1:T(8,128)S(1)} %get-tuple-element.46, f32[640,21]{0,1:T(8,128)S(1)} %get-tuple-element.41, f32[640,128]{0,1:T(8,128)S(1)} %get-tuple-element.45), kind=kLoop, calls=%fused_computation.8 | loop fusion | flops 10321920 | bytes 14525440 | tf_op jit(solution)/shard_map/sub | solution.py:49
  33.1 8.4 %copy.76 = f32[1,640,2688]{2,1,0:T(8,128)} copy(f32[1,640,2688]{1,2,0:T(8,128)} %bitcast.108) | data formatting | bytes 13762560 | tf_op jit(solution)/shard_map/add | solution.py:50
  41.5 8.5 %copy.75 = f32[1,640,2688]{2,1,0:T(8,128)} copy(f32[1,640,2688]{1,2,0:T(8,128)} %bitcast.107) | data formatting | bytes 13762560 | tf_op jit(solution)/shard_map/sub | solution.py:49
  50.0 0.7 slice_bitcast_fusion.6
  51.3 8.5 %multiply_convert_fusion = (bf16[1,640,2688]{2,1,0:T(8,128)(2,1)}, bf16[1,640,2688]{2,1,0:T(8,128)(2,1)}) fusion(f32[1,640,2688]{2,1,0:T(8,128)} %copy.76, f32[640]{0:T(1024)S(1)} %get-tuple-element.44, f32[1,640,2688]{2,1,0:T(8,128)} %copy.75, f32[640]{0:T(1024)S(1)} %get-tuple-element.43), kind=kLoop, calls=%fused_computation.5 | loop fusion | flops 6881280 | bytes 20648960 | tf_op jit(solution)/shard_map/convert.6
  59.8 0.8 slice_convert_fusion.3
  60.6 0.7 copy-done.4
  61.4 3.3 %copy_bitcast_fusion.1 = bf16[21,320,128]{2,1,0:T(8,128)(2,1)S(1)} fusion(bf16[40,8,1,2688]{3,1,0,2:T(8,128)(2,1)S(1)} %bitcast.112, bf16[40,1,1,2688]{3,1,0,2:T(2,128)(2,1)} %copy-done.4, bf16[40,1,1,2688]{3,1,0,2:T(2,128)(2,1)} %copy-done.5, f32[8,2688]{1,0:T(8,128)S(1)} %copy-done.7, f32[8,2688]{1,0:T(8,128)S(1)} %copy-done.8, ...), kind=kLoop, calls=%fused_computation.35 | loop fusion | flops 12902400 | bytes 4128768 | tf_op jit(solution)/shard_map/reshape | solution.py:114
  64.8 2.0 %gather_fusion = bf16[20,320,128]{2,1,0:T(8,128)(2,1)} fusion(bf16[21,320,128]{2,1,0:T(8,128)(2,1)S(1)} %copy_bitcast_fusion.1, s32[1024]{0:T(1024)S(1)} %pad_clamp_fusion.1), kind=kCustom, calls=%fused_computation | custom fusion | bytes 3276880 | tf_op jit(solution)/shard_map/jit(_take)/gather | solution.py:116
  66.8 1.6 %broadcast_select_fusion = bf16[5,4,320,128]{3,2,1,0:T(8,128)(2,1)S(1)} fusion(bf16[5,4,320,128]{3,2,1,0:T(8,128)(2,1)} %bitcast.110, pred[5,4]{1,0:T(8,128)(4,1)S(1)} %copy.78), kind=kLoop, calls=%fused_computation.36 | loop fusion | flops 819200 | bytes 3276820 | tf_op jit(solution)/shard_map/jit(_take)/select_n | solution.py:116
  68.4 1.2 copy-done.1
  69.6 4.0 %collective-permute-start.2 = (bf16[4,320,128]{2,1,0:T(8,128)(2,1)S(1)}, bf16[4,320,128]{2,1,0:T(8,128)(2,1)S(1)}, u32[]{:S(2)}, u32[]{:S(2)}) collective-permute-start(bf16[4,320,128]{2,1,0:T(8,128)(2,1)S(1)} %get-tuple-element.24), channel_id=1, source_target_pairs={{32,0},{48,16},{64,32},{80,48},{96,64},{112,80},{128,96},{144,112}... | collective-permute-start | bytes 983048 | tf_op jit(solution)/shard_map/ppermute | solution.py:33
  73.6 0.7 broadcast_add_fusion.2
  74.3 3.4 %collective-permute-start.3 = (bf16[4,320,128]{2,1,0:T(8,128)(2,1)S(1)}, bf16[4,320,128]{2,1,0:T(8,128)(2,1)S(1)}, u32[]{:S(2)}, u32[]{:S(2)}) collective-permute-start(bf16[4,320,128]{2,1,0:T(8,128)(2,1)S(1)} %get-tuple-element.23), channel_id=1, source_target_pairs={{16,0},{32,16},{48,32},{64,48},{80,64},{96,80},{112,96},{128,112},... | collective-permute-start | bytes 983048 | tf_op jit(solution)/shard_map/ppermute | solution.py:33
  78.5 5.0 %collective-permute-done.2 = bf16[4,320,128]{2,1,0:T(8,128)(2,1)S(1)} collective-permute-done((bf16[4,320,128]{2,1,0:T(8,128)(2,1)S(1)}, bf16[4,320,128]{2,1,0:T(8,128)(2,1)S(1)}, u32[]{:S(2)}, u32[]{:S(2)}) %collective-permute-start.2) | collective-permute-done | bytes 327712 | tf_op jit(solution)/shard_map/ppermute | solution.py:33
  83.5 7.1 %collective-permute-done.3 = bf16[4,320,128]{2,1,0:T(8,128)(2,1)S(1)} collective-permute-done((bf16[4,320,128]{2,1,0:T(8,128)(2,1)S(1)}, bf16[4,320,128]{2,1,0:T(8,128)(2,1)S(1)}, u32[]{:S(2)}, u32[]{:S(2)}) %collective-permute-start.3) | collective-permute-done | bytes 327712 | tf_op jit(solution)/shard_map/ppermute | solution.py:33
  90.7 1.3 slice_bitcast_fusion
  91.9 2.3 %collective-permute-start.4 = (bf16[4,320,128]{2,1,0:T(8,128)(2,1)S(1)}, bf16[4,320,128]{2,1,0:T(8,128)(2,1)S(1)}, u32[]{:S(2)}, u32[]{:S(2)}) collective-permute-start(bf16[4,320,128]{2,1,0:T(8,128)(2,1)S(1)} %get-tuple-element.21), channel_id=1, source_target_pairs={{0,16},{16,32},{32,48},{48,64},{64,80},{80,96},{96,112},{112,128},... | collective-permute-start | bytes 983048 | tf_op jit(solution)/shard_map/ppermute | solution.py:33
  94.3 6.1 %collective-permute-start.5 = (bf16[4,320,128]{2,1,0:T(8,128)(2,1)S(1)}, bf16[4,320,128]{2,1,0:T(8,128)(2,1)S(1)}, u32[]{:S(2)}, u32[]{:S(2)}) collective-permute-start(bf16[4,320,128]{2,1,0:T(8,128)(2,1)S(1)} %get-tuple-element.20), channel_id=1, source_target_pairs={{0,32},{16,48},{32,64},{48,80},{64,96},{80,112},{96,128},{112,144}... | collective-permute-start | bytes 983048 | tf_op jit(solution)/shard_map/ppermute | solution.py:33
  100.4 4.1 %fusion.6 = bf16[2,8,2688]{2,1,0:T(8,128)(2,1)S(1)} fusion(bf16[2,2,8,640]{3,2,1,0:T(8,128)(2,1)S(1)} %reshape.354, bf16[1,640,2688]{2,1,0:T(8,128)(2,1)} %get-tuple-element.49, bf16[1,640,2688]{2,1,0:T(8,128)(2,1)} %get-tuple-element.50), kind=kOutput, calls=%fused_computation.21 | convolution fusion | flops 113584128 | bytes 7008256 | tf_op jit(solution)/shard_map/wxklm,xmi->wkli/dot_general | solution.py:100
  104.6 11.7 %collective-permute-done.5 = bf16[4,320,128]{2,1,0:T(8,128)(2,1)S(1)} collective-permute-done((bf16[4,320,128]{2,1,0:T(8,128)(2,1)S(1)}, bf16[4,320,128]{2,1,0:T(8,128)(2,1)S(1)}, u32[]{:S(2)}, u32[]{:S(2)}) %collective-permute-start.5) | collective-permute-done | bytes 327712 | tf_op jit(solution)/shard_map/ppermute | solution.py:33
  116.4 6.4 %gather_fusion.1 = bf16[84,320,128]{2,1,0:T(8,128)(2,1)} fusion(bf16[20,320,128]{2,1,0:T(8,128)(2,1)S(1)} %bitcast.106, s32[1024]{0:T(1024)S(1)} %pad_clamp_fusion), kind=kCustom, calls=%fused_computation.1 | custom fusion | bytes 13762896 | tf_op jit(solution)/shard_map/jit(_take)/gather | solution.py:129
  122.9 6.4 %convert_reduce_fusion = (f32[21,8,128]{2,1,0:T(8,128)S(1)}, bf16[21,320,128]{2,1,0:T(8,128)(2,1)S(1)}) fusion(f32[21,4,128]{2,1,0:T(4,128)S(1)} %bitcast.118, s32[21,4,128]{2,1,0:T(4,128)S(1)} %copy-done.14, f32[21,4,128]{2,1,0:T(4,128)S(1)} %bitcast.119, s32[21,4,128]{2,1,0:T(4,128)S(1)} %copy-done.15, f32[21,4,128]{2,1,0:T(4,128)S(1)} %bitcast.117, ...), kind=kOutput, calls=%fused_computation.16 | convolution fusion | flops 903318528 | bytes 9031764 | tf_op jit(solution)/shard_map/jifq,jiqp->jfp/dot_general | solution.py:130
  129.3 1.4 %copy_bitcast_fusion = bf16[40,8,1,2688]{3,1,2,0:T(8,128)(2,1)} fusion(bf16[21,320,128]{2,1,0:T(8,128)(2,1)S(1)} %get-tuple-element.48), kind=kLoop, calls=%fused_computation.34 | loop fusion | bytes 3440640 | tf_op jit(solution)/shard_map/convert_element_type | solution.py:134
  (78 shorter events, 4.3 us)
Async XLA Ops:
  0.6 1.2 copy-start
  0.6 4.5 %copy-start.20 = (s32[640]{0:T(1024)S(1)}, s32[640]{0:T(1024)}, u32[]{:S(2)}) copy-start(s32[640]{0:T(1024)} %param.13) | copy-start | bytes 7684
  0.7 18.8 %copy-start.2 = (bf16[40,8,1,2688]{3,1,2,0:T(8,128)(2,1)S(1)}, bf16[40,8,1,2688]{3,1,2,0:T(8,128)(2,1)}, u32[]{:S(2)}) copy-start(bf16[40,8,1,2688]{3,1,2,0:T(8,128)(2,1)} %param.14) | copy-start | bytes 5160964
  3.3 22.5 %copy-start.21 = (s32[1,5,4]{1,2,0:T(4,128)S(1)}, s32[1,5,4]{1,2,0:T(4,128)}, u32[]{:S(2)}) copy-start(s32[1,5,4]{1,2,0:T(4,128)} %param.16) | copy-start | bytes 244
  3.3 22.5 %copy-start.22 = (s32[21,4]{0,1:T(4,128)S(1)}, s32[21,4]{0,1:T(4,128)}, u32[]{:S(2)}) copy-start(s32[21,4]{0,1:T(4,128)} %param.17) | copy-start | bytes 1012
  6.9 70.8 %all-to-all-start = ((bf16[32,2,320]{2,1,0:T(2,128)(2,1)}), bf16[32,2,320]{2,1,0:T(2,128)(2,1)S(1)}, u32[]{:S(2)}, u32[]{:S(2)}) async-start(bf16[32,2,320]{2,1,0:T(2,128)(2,1)} %reshape.387), calls=%async_computation | async-start | bytes 98304 | tf_op jit(solution)/shard_map/all_to_all | solution.py:98
  20.0 40.5 %collective-permute-start.1 = (bf16[40,1,1,2688]{3,1,0,2:T(2,128)(2,1)S(1)}, bf16[40,1,1,2688]{3,1,0,2:T(2,128)(2,1)S(1)}, u32[]{:S(2)}, u32[]{:S(2)}) collective-permute-start(bf16[40,1,1,2688]{3,1,0,2:T(2,128)(2,1)S(1)} %get-tuple-element.19), channel_id=1, source_target_pairs={{1,0},{2,1},{3,2},{4,3},{5,4},{6,5},{7,6},{8,7},{9,8},{10,9},{11,1... | collective-permute-start | bytes 645128 | tf_op jit(solution)/shard_map/ppermute | solution.py:23
  21.3 39.2 %collective-permute-start = (bf16[40,1,1,2688]{3,1,0,2:T(2,128)(2,1)S(1)}, bf16[40,1,1,2688]{3,1,0,2:T(2,128)(2,1)S(1)}, u32[]{:S(2)}, u32[]{:S(2)}) collective-permute-start(bf16[40,1,1,2688]{3,1,0,2:T(2,128)(2,1)S(1)} %get-tuple-element.18), channel_id=1, source_target_pairs={{0,1},{1,2},{2,3},{3,4},{4,5},{5,6},{6,7},{7,8},{8,9},{9,10},{10,1... | collective-permute-start | bytes 645128 | tf_op jit(solution)/shard_map/ppermute | solution.py:21
  41.5 8.5 %copy-start.9 = (bf16[3,8,1,2688]{3,1,2,0:T(8,128)(2,1)S(1)}, bf16[3,8,1,2688]{3,1,2,0:T(8,128)(2,1)}, u32[]{:S(2)}) copy-start(bf16[3,8,1,2688]{3,1,2,0:T(8,128)(2,1)} %param.15) | copy-start | bytes 387076
  51.3 8.5 %copy-start.6 = (bf16[21,4,4,128]{3,2,1,0:T(4,128)(2,1)S(1)}, bf16[21,4,4,128]{3,2,1,0:T(4,128)(2,1)}, u32[]{:S(2)}) copy-start(bf16[21,4,4,128]{3,2,1,0:T(4,128)(2,1)} %param.19) | copy-start | bytes 258052
  51.3 10.2 %copy-start.3 = (bf16[40,8,1,2688]{3,1,2,0:T(8,128)(2,1)S(1)}, bf16[40,8,1,2688]{3,1,2,0:T(8,128)(2,1)}, u32[]{:S(2)}) copy-start(bf16[40,8,1,2688]{3,1,2,0:T(8,128)(2,1)} %param.14) | copy-start | bytes 5160964
  51.3 10.2 %copy-start.7 = (f32[8,2688]{1,0:T(8,128)S(1)}, f32[8,2688]{1,0:T(8,128)}, u32[]{:S(2)}) copy-start(f32[8,2688]{1,0:T(8,128)} %get-tuple-element.32) | copy-start | bytes 258052
  51.3 10.2 %copy-start.8 = (f32[8,2688]{1,0:T(8,128)S(1)}, f32[8,2688]{1,0:T(8,128)}, u32[]{:S(2)}) copy-start(f32[8,2688]{1,0:T(8,128)} %get-tuple-element.33) | copy-start | bytes 258052
  60.5 0.8 copy-start.4
  60.5 0.9 copy-start.5
  64.7 8.9 %copy-start.11 = (s32[21,4,128]{2,1,0:T(4,128)S(1)}, s32[21,4,128]{2,1,0:T(4,128)}, u32[]{:S(2)}) copy-start(s32[21,4,128]{2,1,0:T(4,128)} %param.18) | copy-start | bytes 129028
  68.4 1.2 copy-start.1
  69.6 13.9 %collective-permute-start.2 = (bf16[4,320,128]{2,1,0:T(8,128)(2,1)S(1)}, bf16[4,320,128]{2,1,0:T(8,128)(2,1)S(1)}, u32[]{:S(2)}, u32[]{:S(2)}) collective-permute-start(bf16[4,320,128]{2,1,0:T(8,128)(2,1)S(1)} %get-tuple-element.24), channel_id=1, source_target_pairs={{32,0},{48,16},{64,32},{80,48},{96,64},{112,80},{128,96},{144,112}... | collective-permute-start | bytes 983048 | tf_op jit(solution)/shard_map/ppermute | solution.py:33
  74.3 16.4 %collective-permute-start.3 = (bf16[4,320,128]{2,1,0:T(8,128)(2,1)S(1)}, bf16[4,320,128]{2,1,0:T(8,128)(2,1)S(1)}, u32[]{:S(2)}, u32[]{:S(2)}) collective-permute-start(bf16[4,320,128]{2,1,0:T(8,128)(2,1)S(1)} %get-tuple-element.23), channel_id=1, source_target_pairs={{16,0},{32,16},{48,32},{64,48},{80,64},{96,80},{112,96},{128,112},... | collective-permute-start | bytes 983048 | tf_op jit(solution)/shard_map/ppermute | solution.py:33
  91.9 12.6 %collective-permute-start.4 = (bf16[4,320,128]{2,1,0:T(8,128)(2,1)S(1)}, bf16[4,320,128]{2,1,0:T(8,128)(2,1)S(1)}, u32[]{:S(2)}, u32[]{:S(2)}) collective-permute-start(bf16[4,320,128]{2,1,0:T(8,128)(2,1)S(1)} %get-tuple-element.21), channel_id=1, source_target_pairs={{0,16},{16,32},{32,48},{48,64},{64,80},{80,96},{96,112},{112,128},... | collective-permute-start | bytes 983048 | tf_op jit(solution)/shard_map/ppermute | solution.py:33
  94.3 22.0 %collective-permute-start.5 = (bf16[4,320,128]{2,1,0:T(8,128)(2,1)S(1)}, bf16[4,320,128]{2,1,0:T(8,128)(2,1)S(1)}, u32[]{:S(2)}, u32[]{:S(2)}) collective-permute-start(bf16[4,320,128]{2,1,0:T(8,128)(2,1)S(1)} %get-tuple-element.20), channel_id=1, source_target_pairs={{0,32},{16,48},{32,64},{48,80},{64,96},{80,112},{96,128},{112,144}... | collective-permute-start | bytes 983048 | tf_op jit(solution)/shard_map/ppermute | solution.py:33
  104.5 26.2 %copy-start.10 = (bf16[2,8,2688]{2,1,0:T(8,128)(2,1)}, bf16[2,8,2688]{2,1,0:T(8,128)(2,1)S(1)}, u32[]{:S(2)}) copy-start(bf16[2,8,2688]{2,1,0:T(8,128)(2,1)S(1)} %fusion.6) | copy-start | bytes 258052
  116.3 6.5 %copy-start.12 = (s32[21,4,128]{2,1,0:T(4,128)S(1)}, s32[21,4,128]{2,1,0:T(4,128)}, u32[]{:S(2)}) copy-start(s32[21,4,128]{2,1,0:T(4,128)} %param.18) | copy-start | bytes 129028
  116.3 6.5 %copy-start.13 = (s32[21,4,128]{2,1,0:T(4,128)S(1)}, s32[21,4,128]{2,1,0:T(4,128)}, u32[]{:S(2)}) copy-start(s32[21,4,128]{2,1,0:T(4,128)} %get-tuple-element.38) | copy-start | bytes 129028
  116.3 6.5 %copy-start.14 = (s32[21,4,128]{2,1,0:T(4,128)S(1)}, s32[21,4,128]{2,1,0:T(4,128)}, u32[]{:S(2)}) copy-start(s32[21,4,128]{2,1,0:T(4,128)} %get-tuple-element.39) | copy-start | bytes 129028
  116.4 6.5 %copy-start.15 = (s32[21,4,128]{2,1,0:T(4,128)S(1)}, s32[21,4,128]{2,1,0:T(4,128)}, u32[]{:S(2)}) copy-start(s32[21,4,128]{2,1,0:T(4,128)} %get-tuple-element.40) | copy-start | bytes 129028
  116.4 6.5 %copy-start.16 = (f32[21,4,1,128]{3,2,1,0:T(1,128)S(1)}, f32[21,4,1,128]{3,2,1,0:T(1,128)}, u32[]{:S(2)}) copy-start(f32[21,4,1,128]{3,2,1,0:T(1,128)} %get-tuple-element.34) | copy-start | bytes 129028
  116.4 6.5 %copy-start.17 = (f32[21,4,1,128]{3,2,1,0:T(1,128)S(1)}, f32[21,4,1,128]{3,2,1,0:T(1,128)}, u32[]{:S(2)}) copy-start(f32[21,4,1,128]{3,2,1,0:T(1,128)} %get-tuple-element.35) | copy-start | bytes 129028
  116.4 6.5 %copy-start.18 = (f32[21,4,1,128]{3,2,1,0:T(1,128)S(1)}, f32[21,4,1,128]{3,2,1,0:T(1,128)}, u32[]{:S(2)}) copy-start(f32[21,4,1,128]{3,2,1,0:T(1,128)} %get-tuple-element.36) | copy-start | bytes 129028
  116.4 6.5 %copy-start.19 = (f32[21,4,1,128]{3,2,1,0:T(1,128)S(1)}, f32[21,4,1,128]{3,2,1,0:T(1,128)}, u32[]{:S(2)}) copy-start(f32[21,4,1,128]{3,2,1,0:T(1,128)} %get-tuple-element.37) | copy-start | bytes 129028

commit v2 on v1

--- a/solution.py
+++ b/solution.py
@@ -33,23 +33,28 @@
     return lax.ppermute(value, axis, [(source, source + steps) for source in range(leading, last)])
 
 
-def fourier_table(wave_numbers, lon_count):
+def synthesis(coefficients, wave_numbers, lon_count):
     inner = BLK
     outer = lon_count // inner
     waves = wave_numbers[:, None]
+    scale = 2.0 * math.pi / lon_count
     near = (waves * jnp.arange(inner, dtype=jnp.int32)[None, :]) % lon_count
     far = (waves * (jnp.arange(outer, dtype=jnp.int32) * inner)[None, :]) % lon_count
-    scale = 2.0 * math.pi / lon_count
     near_angle = near.astype(jnp.float32) * scale
     far_angle = far.astype(jnp.float32) * scale
-    near_cos = jnp.cos(near_angle)[:, None, :]
-    near_sin = jnp.sin(near_angle)[:, None, :]
-    far_cos = jnp.cos(far_angle)[:, :, None]
-    far_sin = jnp.sin(far_angle)[:, :, None]
-    cosine = (near_cos * far_cos - near_sin * far_sin).reshape(-1, lon_count)
-    sine = (near_sin * far_cos + near_cos * far_sin).reshape(-1, lon_count)
-    doubled = jnp.where(wave_numbers == 0, 1.0, 2.0).astype(jnp.float32)[:, None]
-    return jnp.stack([doubled * cosine, -doubled * sine]).astype(jnp.bfloat16)
+    doubled = jnp.where(wave_numbers == 0, 1.0, 2.0).astype(jnp.float32)
+    far_cos = (doubled[:, None] * jnp.cos(far_angle)).T
+    far_sin = (doubled[:, None] * jnp.sin(far_angle)).T
+    wide = coefficients.astype(jnp.float32)
+    real = wide[0::2][..., None, :]
+    imag = wide[1::2][..., None, :]
+    first = real * far_cos - imag * far_sin
+    second = -(real * far_sin + imag * far_cos)
+    lhs = jnp.concatenate([first, second], axis=-1)
+    rhs = jnp.concatenate([jnp.cos(near_angle), jnp.sin(near_angle)], axis=0)
+    out = jnp.einsum("wklom,mi->wkloi", lhs, rhs, precision=lax.Precision.HIGHEST,
+                     preferred_element_type=jnp.float32)
+    return out.reshape(out.shape[:3] + (lon_count,))
 
 
 def stencil_matrix(depart_offset, depart_weight):
@@ -94,12 +99,8 @@
             slope_terms[3] + factor * value_terms[0],
         ]
     ).astype(jnp.bfloat16)
-    fourier = fourier_table(wave_numbers, NLON)
     received = lax.all_to_all(coefficients, "band", split_axis=2, concat_axis=3, tiled=True)
-    paired = received.reshape(2, 2, received.shape[1], received.shape[2], received.shape[3])
-    wind_grid = jnp.einsum(
-        "wxklm,xmi->wkli", paired, fourier, preferred_element_type=jnp.float32
-    ).astype(jnp.bfloat16)
+    wind_grid = synthesis(received, wave_numbers, NLON).astype(jnp.bfloat16)
     padded = extended(aerosol_old, (("lev", 1),), 1)
     weights = vertical_weight.astype(jnp.float32)
     vertical_sum = (

time: 132 us -> 105 us (0.80)
  the two profiles are of different devices: /device:TPU:66 before, /device:TPU:90 now
where the time goes in v2:
time: 105 us; the launch traced here: 104 us
  starting transfers between devices  34.1 us (32%)
  local copies, waits for them, and re-layouts  24.4 us (23%)
  waiting for transfers between devices  22.6 us (22%)
  other arithmetic  12.1 us (12%)
  matrix products  10 us (10%)
  between operations  1.19 us (1%)
    ppermute x4, waiting for transfers between devices, shifted(): lax.ppermute(value, axis, [(source, source + steps) for source in range(l...  22.6 us
    ppermute x4, starting transfers between devices, shifted(): lax.ppermute(value, axis, [(source, source + steps) for source in range(l...  15.9 us
    all_to_all x1, starting transfers between devices, shards(): lax.all_to_all(coefficients, 'band', split_axis=2, concat_axis=3, tiled=T...  12.6 us
    gather x1, local copies, waits for them, and re-layouts, shards(): chosen = jnp.take(flattened, depart_slot, axis=0)  6.45 us
    dot_general x1, matrix products, shards(): jnp.einsum('jifq,jiqp->jfp', chosen, stencil, preferred_element_type=jnp....  6.41 us
    unnamed x47, local copies, waits for them, and re-layouts  5.44 us
    reshape x1, other arithmetic, shards(): blocks.reshape(lat_count * block_count, bin_count * level_count, BLK)  5.39 us
    slice x1, local copies, waits for them, and re-layouts, extended(): lax.slice_in_dim(cells, cells.shape[dim] - width, cells.shape[dim], axis=...  3.69 us
  transfers between devices with their start and end apart: 7, of which 4 were waited for; matrix products, arithmetic and copies ran while one was open for 22% of the time, Pallas kernels for 0%

profile of v2, /device:TPU:90, one launch (start us, length us, event | category | flops | bytes accessed | tf_op | source)
XLA Modules:
  0.0 104.3 jit_solution(3614210575544386369)
XLA Ops:
  0.7 3.7 %fusion.50 = (bf16[40,1,1,2688]{3,1,0,2:T(2,128)(2,1)}, bf16[40,1,1,2688]{3,1,0,2:T(2,128)(2,1)}) fusion(bf16[40,8,1,2688]{3,1,0,2:T(8,128)(2,1)} %bitcast.104), kind=kLoop, calls=%fused_computation.115 | loop fusion | bytes 860160 | tf_op jit(solution)/shard_map/slice | solution.py:18
  4.4 1.9 %collective-permute-start = (bf16[40,1,1,2688]{3,1,0,2:T(2,128)(2,1)}, bf16[40,1,1,2688]{3,1,0,2:T(2,128)(2,1)}, u32[]{:S(2)}, u32[]{:S(2)}) collective-permute-start(bf16[40,1,1,2688]{3,1,0,2:T(2,128)(2,1)} %get-tuple-element.21), channel_id=1, source_target_pairs={{0,1},{1,2},{2,3},{3,4},{4,5},{5,6},{6,7},{7,8},{8,9},{9,10},{10,1... | collective-permute-start | bytes 645128 | tf_op jit(solution)/shard_map/ppermute | solution.py:21
  6.3 3.6 %collective-permute-start.1 = (bf16[40,1,1,2688]{3,1,0,2:T(2,128)(2,1)}, bf16[40,1,1,2688]{3,1,0,2:T(2,128)(2,1)}, u32[]{:S(2)}, u32[]{:S(2)}) collective-permute-start(bf16[40,1,1,2688]{3,1,0,2:T(2,128)(2,1)} %get-tuple-element.22), channel_id=1, source_target_pairs={{1,0},{2,1},{3,2},{4,3},{5,4},{6,5},{7,6},{8,7},{9,8},{10,9},{11,1... | collective-permute-start | bytes 645128 | tf_op jit(solution)/shard_map/ppermute | solution.py:23
  10.0 1.5 %convolution_bitcast_fusion = f32[4,8,32,20]{2,1,0,3:T(8,128)S(1)} fusion(bf16[20,32,640]{2,1,0:T(8,128)(2,1)S(1)} %copy-done, bf16[4,8,20,640]{3,1,2,0:T(8,128)(2,1)} %param.10), kind=kOutput, calls=%fused_computation.33 | convolution fusion | flops 26214400 | bytes 1720320 | tf_op jit(solution)/shard_map/slj,xksj->xkls/dot_general | solution.py:87
  12.8 1.0 reshape.320
  13.7 12.6 %all-to-all-start = ((bf16[32,2,320]{2,1,0:T(2,128)(2,1)}), bf16[32,2,320]{2,1,0:T(2,128)(2,1)}, u32[]{:S(2)}, u32[]{:S(2)}) async-start(bf16[32,2,320]{2,1,0:T(2,128)(2,1)} %reshape.320), calls=%async_computation | async-start | bytes 98304 | tf_op jit(solution)/shard_map/all_to_all | solution.py:102
  26.4 1.4 %fusion.31 = (f32[640,128]{1,0:T(8,128)S(1)}, f32[640,128]{1,0:T(8,128)S(1)}) fusion(s32[640]{0:T(1024)S(1)} %copy-done.18), kind=kLoop, calls=%fused_computation.61 | loop fusion | flops 737280 | bytes 657920 | tf_op jit(solution)/shard_map/cos | solution.py:54
  28.4 0.8 slice_convert_fusion.3
  29.2 0.7 broadcast_add_fusion.2
  30.0 1.0 cosine_multiply_fusion
  31.0 5.4 %copy_bitcast_fusion.1 = bf16[21,320,128]{2,1,0:T(8,128)(2,1)S(1)} fusion(bf16[40,8,1,2688]{3,1,0,2:T(8,128)(2,1)} %bitcast.105, bf16[40,1,1,2688]{3,1,0,2:T(2,128)(2,1)} %collective-permute-done.1, bf16[40,1,1,2688]{3,1,0,2:T(2,128)(2,1)} %collective-permute-done, f32[8,2688]{1,0:T(8,128)S(1)} %get-tuple-element.33, f32[8,2688]{1,0:T(8,128)S(1)} %get-tuple-element.34, ...), kind=kLoop, calls=%fused_computation.31 | loop fusion | flops 12902400 | bytes 4128768 | tf_op jit(solution)/shard_map/reshape | solution.py:115
  36.4 2.0 %gather_fusion = bf16[20,320,128]{2,1,0:T(8,128)(2,1)} fusion(bf16[21,320,128]{2,1,0:T(8,128)(2,1)S(1)} %copy_bitcast_fusion.1, s32[1024]{0:T(1024)S(1)} %pad_clamp_fusion.1), kind=kCustom, calls=%fused_computation | custom fusion | bytes 3276880 | tf_op jit(solution)/shard_map/jit(_take)/gather | solution.py:117
  38.4 1.6 %broadcast_select_fusion = bf16[5,4,320,128]{3,2,1,0:T(8,128)(2,1)S(1)} fusion(bf16[5,4,320,128]{3,2,1,0:T(8,128)(2,1)} %bitcast.103, pred[5,4]{1,0:T(8,128)(4,1)S(1)} %copy.88), kind=kLoop, calls=%fused_computation.32 | loop fusion | flops 819200 | bytes 3276820 | tf_op jit(solution)/shard_map/jit(_take)/select_n | solution.py:117
  40.1 1.2 %copy-done.1 = bf16[5,4,320,128]{3,2,1,0:T(8,128)(2,1)} copy-done((bf16[5,4,320,128]{3,2,1,0:T(8,128)(2,1)}, bf16[5,4,320,128]{3,2,1,0:T(8,128)(2,1)S(1)}, u32[]{:S(2)}) %copy-start.1) | copy-done | bytes 1638424
  41.3 4.0 %collective-permute-start.2 = (bf16[4,320,128]{2,1,0:T(8,128)(2,1)S(1)}, bf16[4,320,128]{2,1,0:T(8,128)(2,1)}, u32[]{:S(2)}, u32[]{:S(2)}) collective-permute-start(bf16[4,320,128]{2,1,0:T(8,128)(2,1)S(1)} %get-tuple-element.27), channel_id=1, source_target_pairs={{32,0},{48,16},{64,32},{80,48},{96,64},{112,80},{128,96},{144,112}... | collective-permute-start | bytes 983048 | tf_op jit(solution)/shard_map/ppermute | solution.py:33
  45.3 1.2 %reshape.321 = bf16[32,4,8,20]{3,2,1,0:T(8,128)(2,1)S(1)} reshape(bf16[32,2,320]{2,1,0:T(2,128)(2,1)} %all-to-all-done) | data formatting | bytes 81920
  47.5 3.5 %collective-permute-start.3 = (bf16[4,320,128]{2,1,0:T(8,128)(2,1)S(1)}, bf16[4,320,128]{2,1,0:T(8,128)(2,1)S(1)}, u32[]{:S(2)}, u32[]{:S(2)}) collective-permute-start(bf16[4,320,128]{2,1,0:T(8,128)(2,1)S(1)} %get-tuple-element.26), channel_id=1, source_target_pairs={{16,0},{32,16},{48,32},{64,48},{80,64},{96,80},{112,96},{128,112},... | collective-permute-start | bytes 983048 | tf_op jit(solution)/shard_map/ppermute | solution.py:33
  51.0 4.3 %collective-permute-done.2 = bf16[4,320,128]{2,1,0:T(8,128)(2,1)} collective-permute-done((bf16[4,320,128]{2,1,0:T(8,128)(2,1)S(1)}, bf16[4,320,128]{2,1,0:T(8,128)(2,1)}, u32[]{:S(2)}, u32[]{:S(2)}) %collective-permute-start.2) | collective-permute-done | bytes 327712 | tf_op jit(solution)/shard_map/ppermute | solution.py:33
  55.3 1.0 bitcast_dynamic-update-slice_fusion.3
  56.3 5.6 %collective-permute-done.3 = bf16[4,320,128]{2,1,0:T(8,128)(2,1)S(1)} collective-permute-done((bf16[4,320,128]{2,1,0:T(8,128)(2,1)S(1)}, bf16[4,320,128]{2,1,0:T(8,128)(2,1)S(1)}, u32[]{:S(2)}, u32[]{:S(2)}) %collective-permute-start.3) | collective-permute-done | bytes 327712 | tf_op jit(solution)/shard_map/ppermute | solution.py:33
  62.0 2.1 %slice_bitcast_fusion = (bf16[4,320,128]{2,1,0:T(8,128)(2,1)}, bf16[4,320,128]{2,1,0:T(8,128)(2,1)}, bf16[5,4,320,128]{3,2,1,0:T(8,128)(2,1)S(1)}) fusion(bf16[5,4,320,128]{3,2,1,0:T(8,128)(2,1)} %copy-done.1, bf16[5,4,320,128]{3,2,1,0:T(8,128)(2,1)S(1)} %bitcast_dynamic-update-slice_fusion.2), kind=kLoop, calls=%fused_computation.48 | loop fusion | bytes 1966080 | tf_op jit(solution)/shard_map/squeeze | solution.py:127
  64.1 2.5 %collective-permute-start.4 = (bf16[4,320,128]{2,1,0:T(8,128)(2,1)}, bf16[4,320,128]{2,1,0:T(8,128)(2,1)}, u32[]{:S(2)}, u32[]{:S(2)}) collective-permute-start(bf16[4,320,128]{2,1,0:T(8,128)(2,1)} %get-tuple-element.24), channel_id=1, source_target_pairs={{0,16},{16,32},{32,48},{48,64},{64,80},{80,96},{96,112},{112,128},... | collective-permute-start | bytes 983048 | tf_op jit(solution)/shard_map/ppermute | solution.py:33
  66.8 5.9 %collective-permute-start.5 = (bf16[4,320,128]{2,1,0:T(8,128)(2,1)}, bf16[4,320,128]{2,1,0:T(8,128)(2,1)}, u32[]{:S(2)}, u32[]{:S(2)}) collective-permute-start(bf16[4,320,128]{2,1,0:T(8,128)(2,1)} %get-tuple-element.23), channel_id=1, source_target_pairs={{0,32},{16,48},{32,64},{48,80},{64,96},{80,112},{96,128},{112,144}... | collective-permute-start | bytes 983048 | tf_op jit(solution)/shard_map/ppermute | solution.py:33
  72.8 1.7 %fusion.19 = bf16[2,8,21,128]{3,2,1,0:T(8,128)(2,1)S(1)} fusion(f32[2,8,1,21,640]{4,3,1,0,2:T(8,128)S(1)} %get-tuple-element.36, f32[2,8,1,21,640]{4,3,1,0,2:T(8,128)S(1)} %get-tuple-element.35, f32[640,128]{1,0:T(8,128)S(1)} %get-tuple-element.49, f32[640,128]{1,0:T(8,128)S(1)} %get-tuple-element.48), kind=kOutput, calls=%fused_computation.35 | convolution fusion | flops 661239808 | bytes 2461696 | tf_op jit(solution)/shard_map/wklom,mi->wkloi/dot_general | solution.py:55
  74.6 2.3 %collective-permute-done.4 = bf16[4,320,128]{2,1,0:T(8,128)(2,1)} collective-permute-done((bf16[4,320,128]{2,1,0:T(8,128)(2,1)}, bf16[4,320,128]{2,1,0:T(8,128)(2,1)}, u32[]{:S(2)}, u32[]{:S(2)}) %collective-permute-start.4) | collective-permute-done | bytes 327712 | tf_op jit(solution)/shard_map/ppermute | solution.py:33
  76.8 1.0 bitcast_dynamic-update-slice_fusion.1
  77.8 10.4 %collective-permute-done.5 = bf16[4,320,128]{2,1,0:T(8,128)(2,1)} collective-permute-done((bf16[4,320,128]{2,1,0:T(8,128)(2,1)}, bf16[4,320,128]{2,1,0:T(8,128)(2,1)}, u32[]{:S(2)}, u32[]{:S(2)}) %collective-permute-start.5) | collective-permute-done | bytes 327712 | tf_op jit(solution)/shard_map/ppermute | solution.py:33
  88.2 1.0 bitcast_dynamic-update-slice_fusion
  89.3 6.5 %gather_fusion.1 = bf16[84,320,128]{2,1,0:T(8,128)(2,1)} fusion(bf16[20,320,128]{2,1,0:T(8,128)(2,1)S(1)} %bitcast.101, s32[1024]{0:T(1024)S(1)} %pad_clamp_fusion), kind=kCustom, calls=%fused_computation.1 | custom fusion | bytes 13762896 | tf_op jit(solution)/shard_map/jit(_take)/gather | solution.py:130
  95.9 6.4 %convert_reduce_fusion = (f32[21,8,128]{2,1,0:T(8,128)S(1)}, bf16[21,320,128]{2,1,0:T(8,128)(2,1)S(1)}) fusion(f32[21,4,128]{2,1,0:T(4,128)S(1)} %bitcast.111, s32[21,4,128]{2,1,0:T(4,128)S(1)} %copy-done.12, f32[21,4,128]{2,1,0:T(4,128)S(1)} %bitcast.112, s32[21,4,128]{2,1,0:T(4,128)S(1)} %copy-done.13, f32[21,4,128]{2,1,0:T(4,128)S(1)} %bitcast.110, ...), kind=kOutput, calls=%fused_computation.10 | convolution fusion | flops 903318528 | bytes 9031764 | tf_op jit(solution)/shard_map/jifq,jiqp->jfp/dot_general | solution.py:131
  102.3 1.4 %copy_bitcast_fusion = bf16[40,8,1,2688]{3,1,2,0:T(8,128)(2,1)} fusion(bf16[21,320,128]{2,1,0:T(8,128)(2,1)S(1)} %get-tuple-element.51), kind=kLoop, calls=%fused_computation.30 | loop fusion | bytes 3440640 | tf_op jit(solution)/shard_map/convert_element_type | solution.py:135
  103.7 0.7 fusion.33
  (74 shorter events, 3.4 us)
Async XLA Ops:
  0.6 9.3 %copy-start = (bf16[20,32,640]{2,1,0:T(8,128)(2,1)S(1)}, bf16[20,32,640]{2,1,0:T(8,128)(2,1)}, u32[]{:S(2)}) copy-start(bf16[20,32,640]{2,1,0:T(8,128)(2,1)} %param.11) | copy-start | bytes 2457604
  0.6 10.9 %copy-start.2 = (bf16[4,8,20,640]{3,1,2,0:T(8,128)(2,1)S(1)}, bf16[4,8,20,640]{3,1,2,0:T(8,128)(2,1)}, u32[]{:S(2)}) copy-start(bf16[4,8,20,640]{3,1,2,0:T(8,128)(2,1)} %param.10) | copy-start | bytes 2457604
  0.7 10.9 %copy-start.3 = (bf16[20,32,640]{2,1,0:T(8,128)(2,1)S(1)}, bf16[20,32,640]{2,1,0:T(8,128)(2,1)}, u32[]{:S(2)}) copy-start(bf16[20,32,640]{2,1,0:T(8,128)(2,1)} %param.12) | copy-start | bytes 2457604
  4.4 26.6 %collective-permute-start = (bf16[40,1,1,2688]{3,1,0,2:T(2,128)(2,1)}, bf16[40,1,1,2688]{3,1,0,2:T(2,128)(2,1)}, u32[]{:S(2)}, u32[]{:S(2)}) collective-permute-start(bf16[40,1,1,2688]{3,1,0,2:T(2,128)(2,1)} %get-tuple-element.21), channel_id=1, source_target_pairs={{0,1},{1,2},{2,3},{3,4},{4,5},{5,6},{6,7},{7,8},{8,9},{9,10},{10,1... | collective-permute-start | bytes 645128 | tf_op jit(solution)/shard_map/ppermute | solution.py:21
  6.3 24.7 %collective-permute-start.1 = (bf16[40,1,1,2688]{3,1,0,2:T(2,128)(2,1)}, bf16[40,1,1,2688]{3,1,0,2:T(2,128)(2,1)}, u32[]{:S(2)}, u32[]{:S(2)}) collective-permute-start(bf16[40,1,1,2688]{3,1,0,2:T(2,128)(2,1)} %get-tuple-element.22), channel_id=1, source_target_pairs={{1,0},{2,1},{3,2},{4,3},{5,4},{6,5},{7,6},{8,7},{9,8},{10,9},{11,1... | collective-permute-start | bytes 645128 | tf_op jit(solution)/shard_map/ppermute | solution.py:23
  9.9 2.0 %copy-start.18 = (s32[640]{0:T(1024)S(1)}, s32[640]{0:T(1024)}, u32[]{:S(2)}) copy-start(s32[640]{0:T(1024)} %param.13) | copy-start | bytes 7684
  11.5 14.8 %copy-start.19 = (s32[1,5,4]{1,2,0:T(4,128)S(1)}, s32[1,5,4]{1,2,0:T(4,128)}, u32[]{:S(2)}) copy-start(s32[1,5,4]{1,2,0:T(4,128)} %param.16) | copy-start | bytes 244
  11.5 14.9 %copy-start.20 = (s32[21,4]{0,1:T(4,128)S(1)}, s32[21,4]{0,1:T(4,128)}, u32[]{:S(2)}) copy-start(s32[21,4]{0,1:T(4,128)} %param.17) | copy-start | bytes 1012
  11.5 16.3 %copy-start.8 = (bf16[3,8,1,2688]{3,1,2,0:T(8,128)(2,1)S(1)}, bf16[3,8,1,2688]{3,1,2,0:T(8,128)(2,1)}, u32[]{:S(2)}) copy-start(bf16[3,8,1,2688]{3,1,2,0:T(8,128)(2,1)} %param.15) | copy-start | bytes 387076
  11.9 16.5 %copy-start.4 = (bf16[21,4,4,128]{3,2,1,0:T(4,128)(2,1)S(1)}, bf16[21,4,4,128]{3,2,1,0:T(4,128)(2,1)}, u32[]{:S(2)}) copy-start(bf16[21,4,4,128]{3,2,1,0:T(4,128)(2,1)} %param.19) | copy-start | bytes 258052
  12.0 17.2 %copy-start.9 = (s32[21,4,128]{2,1,0:T(4,128)S(1)}, s32[21,4,128]{2,1,0:T(4,128)}, u32[]{:S(2)}) copy-start(s32[21,4,128]{2,1,0:T(4,128)} %param.18) | copy-start | bytes 129028
  13.7 31.5 %all-to-all-start = ((bf16[32,2,320]{2,1,0:T(2,128)(2,1)}), bf16[32,2,320]{2,1,0:T(2,128)(2,1)}, u32[]{:S(2)}, u32[]{:S(2)}) async-start(bf16[32,2,320]{2,1,0:T(2,128)(2,1)} %reshape.320), calls=%async_computation | async-start | bytes 98304 | tf_op jit(solution)/shard_map/all_to_all | solution.py:102
  40.0 1.2 %copy-start.1 = (bf16[5,4,320,128]{3,2,1,0:T(8,128)(2,1)}, bf16[5,4,320,128]{3,2,1,0:T(8,128)(2,1)S(1)}, u32[]{:S(2)}) copy-start(bf16[5,4,320,128]{3,2,1,0:T(8,128)(2,1)S(1)} %broadcast_select_fusion) | copy-start | bytes 4915204
  41.3 14.0 %collective-permute-start.2 = (bf16[4,320,128]{2,1,0:T(8,128)(2,1)S(1)}, bf16[4,320,128]{2,1,0:T(8,128)(2,1)}, u32[]{:S(2)}, u32[]{:S(2)}) collective-permute-start(bf16[4,320,128]{2,1,0:T(8,128)(2,1)S(1)} %get-tuple-element.27), channel_id=1, source_target_pairs={{32,0},{48,16},{64,32},{80,48},{96,64},{112,80},{128,96},{144,112}... | collective-permute-start | bytes 983048 | tf_op jit(solution)/shard_map/ppermute | solution.py:33
  47.2 19.4 %copy-start.6 = (f32[21,640]{1,0:T(8,128)S(1)}, f32[21,640]{1,0:T(8,128)}, u32[]{:S(2)}) copy-start(f32[21,640]{1,0:T(8,128)} %get-tuple-element.46) | copy-start | bytes 161284
  47.4 19.1 %copy-start.7 = (f32[21,640]{1,0:T(8,128)S(1)}, f32[21,640]{1,0:T(8,128)}, u32[]{:S(2)}) copy-start(f32[21,640]{1,0:T(8,128)} %get-tuple-element.47) | copy-start | bytes 161284
  47.5 14.5 %collective-permute-start.3 = (bf16[4,320,128]{2,1,0:T(8,128)(2,1)S(1)}, bf16[4,320,128]{2,1,0:T(8,128)(2,1)S(1)}, u32[]{:S(2)}, u32[]{:S(2)}) collective-permute-start(bf16[4,320,128]{2,1,0:T(8,128)(2,1)S(1)} %get-tuple-element.26), channel_id=1, source_target_pairs={{16,0},{32,16},{48,32},{64,48},{80,64},{96,80},{112,96},{128,112},... | collective-permute-start | bytes 983048 | tf_op jit(solution)/shard_map/ppermute | solution.py:33
  64.1 12.8 %collective-permute-start.4 = (bf16[4,320,128]{2,1,0:T(8,128)(2,1)}, bf16[4,320,128]{2,1,0:T(8,128)(2,1)}, u32[]{:S(2)}, u32[]{:S(2)}) collective-permute-start(bf16[4,320,128]{2,1,0:T(8,128)(2,1)} %get-tuple-element.24), channel_id=1, source_target_pairs={{0,16},{16,32},{32,48},{48,64},{64,80},{80,96},{96,112},{112,128},... | collective-permute-start | bytes 983048 | tf_op jit(solution)/shard_map/ppermute | solution.py:33
  66.8 21.4 %collective-permute-start.5 = (bf16[4,320,128]{2,1,0:T(8,128)(2,1)}, bf16[4,320,128]{2,1,0:T(8,128)(2,1)}, u32[]{:S(2)}, u32[]{:S(2)}) collective-permute-start(bf16[4,320,128]{2,1,0:T(8,128)(2,1)} %get-tuple-element.23), channel_id=1, source_target_pairs={{0,32},{16,48},{32,64},{48,80},{64,96},{80,112},{96,128},{112,144}... | collective-permute-start | bytes 983048 | tf_op jit(solution)/shard_map/ppermute | solution.py:33
  74.6 29.1 %copy-start.5 = (bf16[2,8,1,2688]{3,1,0,2:T(8,128)(2,1)}, bf16[2,8,1,2688]{3,1,0,2:T(8,128)(2,1)S(1)}, u32[]{:S(2)}) copy-start(bf16[2,8,1,2688]{3,1,0,2:T(8,128)(2,1)S(1)} %convert_element_type.135) | copy-start | bytes 258052
  89.3 6.5 %copy-start.10 = (s32[21,4,128]{2,1,0:T(4,128)S(1)}, s32[21,4,128]{2,1,0:T(4,128)}, u32[]{:S(2)}) copy-start(s32[21,4,128]{2,1,0:T(4,128)} %param.18) | copy-start | bytes 129028
  89.3 6.5 %copy-start.11 = (s32[21,4,128]{2,1,0:T(4,128)S(1)}, s32[21,4,128]{2,1,0:T(4,128)}, u32[]{:S(2)}) copy-start(s32[21,4,128]{2,1,0:T(4,128)} %get-tuple-element.43) | copy-start | bytes 129028
  89.3 6.5 %copy-start.12 = (s32[21,4,128]{2,1,0:T(4,128)S(1)}, s32[21,4,128]{2,1,0:T(4,128)}, u32[]{:S(2)}) copy-start(s32[21,4,128]{2,1,0:T(4,128)} %get-tuple-element.44) | copy-start | bytes 129028
  89.3 6.5 %copy-start.13 = (s32[21,4,128]{2,1,0:T(4,128)S(1)}, s32[21,4,128]{2,1,0:T(4,128)}, u32[]{:S(2)}) copy-start(s32[21,4,128]{2,1,0:T(4,128)} %get-tuple-element.45) | copy-start | bytes 129028
  89.3 6.5 %copy-start.14 = (f32[21,4,1,128]{3,2,1,0:T(1,128)S(1)}, f32[21,4,1,128]{3,2,1,0:T(1,128)}, u32[]{:S(2)}) copy-start(f32[21,4,1,128]{3,2,1,0:T(1,128)} %get-tuple-element.37) | copy-start | bytes 129028
  89.3 6.5 %copy-start.15 = (f32[21,4,1,128]{3,2,1,0:T(1,128)S(1)}, f32[21,4,1,128]{3,2,1,0:T(1,128)}, u32[]{:S(2)}) copy-start(f32[21,4,1,128]{3,2,1,0:T(1,128)} %get-tuple-element.38) | copy-start | bytes 129028
  89.3 6.5 %copy-start.16 = (f32[21,4,1,128]{3,2,1,0:T(1,128)S(1)}, f32[21,4,1,128]{3,2,1,0:T(1,128)}, u32[]{:S(2)}) copy-start(f32[21,4,1,128]{3,2,1,0:T(1,128)} %get-tuple-element.39) | copy-start | bytes 129028
  89.3 6.5 %copy-start.17 = (f32[21,4,1,128]{3,2,1,0:T(1,128)S(1)}, f32[21,4,1,128]{3,2,1,0:T(1,128)}, u32[]{:S(2)}) copy-start(f32[21,4,1,128]{3,2,1,0:T(1,128)} %get-tuple-element.40) | copy-start | bytes 129028

commit v3 on v2

--- a/solution.py
+++ b/solution.py
@@ -3,6 +3,8 @@
 import jax
 import jax.numpy as jnp
 from jax import lax
+from jax.experimental import pallas as pl
+from jax.experimental.pallas import tpu as pltpu
 from jax.sharding import PartitionSpec as P
 
 WAVES = 640
@@ -69,6 +71,67 @@
     return summed
 
 
+def pack_blocks(listed, remapped, offsets, cap):
+    rows = remapped.shape[0]
+
+    def body(listed_ref, *refs):
+        for index in range(offsets):
+            refs[offsets + index][...] = refs[index][...][None]
+
+    def source_map(index):
+        return lambda entry, table: (0, table[index * cap + entry])
+
+    out_shape = [jax.ShapeDtypeStruct((cap, rows, BLK), remapped.dtype) for _ in range(offsets)]
+    grid_spec = pltpu.PrefetchScalarGridSpec(
+        num_scalar_prefetch=1,
+        grid=(cap,),
+        in_specs=[pl.BlockSpec((rows, BLK), source_map(index)) for index in range(offsets)],
+        out_specs=[pl.BlockSpec((1, rows, BLK), lambda entry, table: (entry, 0, 0))
+                   for _ in range(offsets)],
+    )
+    return pl.pallas_call(body, grid_spec=grid_spec, out_shape=out_shape)(
+        listed, *([remapped] * offsets))
+
+
+def apply_stencil(slots, stencil, pieces, bin_count, level_count):
+    block_count, rows_per_block = stencil.shape[0], stencil.shape[1]
+    count = len(pieces)
+    cap, rows, _ = pieces[0].shape
+
+    def body(slot_ref, stencil_ref, *refs):
+        piece_refs = refs[:count]
+        out_ref, mean_ref, acc_ref = refs[count:]
+        block = pl.program_id(0)
+        acc_ref[...] = jnp.zeros_like(acc_ref)
+        for row in range(rows_per_block):
+            slot = slot_ref[block * rows_per_block + row]
+            piece = slot // cap
+            entry = slot % cap
+            weights = stencil_ref[0, row]
+            for index in range(count):
+                @pl.when(piece == index)
+                def _(index=index):
+                    acc_ref[...] += jnp.dot(piece_refs[index][entry], weights,
+                                            preferred_element_type=jnp.float32)
+        result = acc_ref[...].astype(out_ref.dtype)
+        out_ref[...] = result
+        summed = result.astype(jnp.float32).reshape(bin_count, level_count, BLK).sum(axis=0)
+        mean_ref[...] = summed / bin_count
+
+    grid_spec = pltpu.PrefetchScalarGridSpec(
+        num_scalar_prefetch=1,
+        grid=(block_count,),
+        in_specs=[pl.BlockSpec((1, rows_per_block, BLK, BLK), lambda b, table: (b, 0, 0, 0))]
+        + [pl.BlockSpec((cap, rows, BLK), lambda b, table: (0, 0, 0)) for _ in range(count)],
+        out_specs=[pl.BlockSpec((rows, BLK), lambda b, table: (0, b)),
+                   pl.BlockSpec((level_count, BLK), lambda b, table: (0, b))],
+        scratch_shapes=[pltpu.VMEM((rows, BLK), jnp.float32)],
+    )
+    out_shape = [jax.ShapeDtypeStruct((rows, block_count * BLK), pieces[0].dtype),
+                 jax.ShapeDtypeStruct((level_count, block_count * BLK), jnp.float32)]
+    return pl.pallas_call(body, grid_spec=grid_spec, out_shape=out_shape)(slots, stencil, *pieces)
+
+
 def shards(
     spectral,
     legendre_value,
@@ -106,17 +169,14 @@
     vertical_sum = (
         weights[0] * padded[:, :-2] + weights[1] * padded[:, 1:-1] + weights[2] * padded[:, 2:]
     )
-    remapped = vertical_sum.astype(jnp.bfloat16)
-    bin_count, level_count, lat_count, lon_count = remapped.shape
-    block_count = lon_count // BLK
-    blocks = remapped.reshape(bin_count, level_count, lat_count, block_count, BLK).transpose(
-        2, 3, 0, 1, 4
-    )
-    blocks = blocks.reshape(lat_count * block_count, bin_count * level_count, BLK)
-    listed = send_blocks[0]
-    outgoing = jnp.take(blocks, jnp.clip(listed, 0, blocks.shape[0] - 1), axis=0)
+    bin_count, level_count, lat_count, lon_count = aerosol_old.shape
+    rows = bin_count * level_count
+    remapped = vertical_sum.astype(jnp.bfloat16).reshape(rows, lat_count * lon_count)
+    block_total = lat_count * lon_count // BLK
+    listed = jnp.clip(send_blocks[0], 0, block_total - 1)
+    offsets, cap = listed.shape
+    outgoing = pack_blocks(listed.reshape(-1), remapped, offsets, cap)
     stencil = stencil_matrix(depart_offset, depart_weight).astype(jnp.bfloat16)
-    offsets = listed.shape[0]
     reach_bands = offsets // 2
     pieces = []
     for offset_index in range(offsets):
@@ -125,17 +185,9 @@
             pieces.append(outgoing[offset_index])
         else:
             pieces.append(shifted(outgoing[offset_index], "band", shift_by))
-    pooled = jnp.stack(pieces)
-    flattened = pooled.reshape(pooled.shape[0] * pooled.shape[1], pooled.shape[2], pooled.shape[3])
-    chosen = jnp.take(flattened, depart_slot, axis=0)
-    block_rows = jnp.einsum("jifq,jiqp->jfp", chosen, stencil, preferred_element_type=jnp.float32)
-    aerosol_new = block_rows.reshape(lat_count, block_count, bin_count, level_count, BLK).transpose(
-        2, 3, 0, 1, 4
-    )
-    aerosol_new = aerosol_new.reshape(bin_count, level_count, lat_count, lon_count).astype(
-        jnp.bfloat16
-    )
-    average = jnp.mean(aerosol_new.astype(jnp.float32), axis=0)
+    flat_new, average = apply_stencil(depart_slot.reshape(-1), stencil, pieces, bin_count, level_count)
+    aerosol_new = flat_new.reshape(bin_count, level_count, lat_count, lon_count)
+    average = average.reshape(level_count, lat_count, lon_count)
     aerosol_flux = (wind_grid.astype(jnp.float32) * average[None]).astype(jnp.bfloat16)
     return (wind_grid, aerosol_new, aerosol_flux)
 

time: 105 us -> 104 us (level)
  the two profiles are of different devices: /device:TPU:90 before, /device:TPU:74 now
where the time goes in v3:
time: 104 us; the launch traced here: 103 us
  starting transfers between devices  32.5 us (31%)
  Pallas kernels  24.9 us (24%)
  waiting for transfers between devices  14.8 us (14%)
  other arithmetic  13.5 us (13%)
  local copies, waits for them, and re-layouts  11.4 us (11%)
  matrix products  5.13 us (5%)
    pallas_call x1, Pallas kernels, apply_stencil(): pl.pallas_call(body, grid_spec=grid_spec, out_shape=out_shape)  20.4 us
    ppermute x4, starting transfers between devices, shifted(): lax.ppermute(value, axis, [(source, source + steps) for source in range(l...  15.5 us
    ppermute x4, waiting for transfers between devices, shifted(): lax.ppermute(value, axis, [(source, source + steps) for source in range(l...  14.8 us
    all_to_all x1, starting transfers between devices, shards(): lax.all_to_all(coefficients, 'band', split_axis=2, concat_axis=3, tiled=T...  12.6 us
    pallas_call x1, Pallas kernels, pack_blocks(): pl.pallas_call(body, grid_spec=grid_spec, out_shape=out_shape)  4.5 us
    convert_element_type x1, other arithmetic, shards(): stencil = stencil_matrix(depart_offset, depart_weight).astype(jnp.bfloat16)  4.03 us
    unnamed x37, local copies, waits for them, and re-layouts  4.02 us
    reshape x1, other arithmetic, shards(): vertical_sum.astype(jnp.bfloat16).reshape(rows, lat_count * lon_count)  3.99 us
  transfers between devices with their start and end apart: 7, of which 3 were waited for; matrix products, arithmetic and copies ran while one was open for 16% of the time, Pallas kernels for 0%

profile of v3, /device:TPU:74, one launch (start us, length us, event | category | flops | bytes accessed | tf_op | source)
XLA Modules:
  0.0 103.1 jit_solution(4886213760165517554)
XLA Ops:
  0.7 1.1 %copy-done = bf16[20,32,640]{2,1,0:T(8,128)(2,1)S(1)} copy-done((bf16[20,32,640]{2,1,0:T(8,128)(2,1)S(1)}, bf16[20,32,640]{2,1,0:T(8,128)(2,1)}, u32[]{:S(2)}) %copy-start) | copy-done | bytes 819224
  1.8 1.7 %convolution_bitcast_fusion = f32[4,8,32,20]{2,1,0,3:T(8,128)S(1)} fusion(bf16[20,32,640]{2,1,0:T(8,128)(2,1)S(1)} %copy-done, bf16[4,8,20,640]{3,1,2,0:T(8,128)(2,1)} %param.10), kind=kOutput, calls=%fused_computation.13 | convolution fusion | flops 26214400 | bytes 1720320 | tf_op jit(solution)/shard_map/slj,xksj->xkls/dot_general | solution.py:150
  3.4 1.8 %convolution_bitcast_fusion.1 = f32[4,8,32,20]{2,1,0,3:T(8,128)S(1)} fusion(bf16[20,32,640]{2,1,0:T(8,128)(2,1)} %param.12, bf16[4,8,20,640]{3,1,2,0:T(8,128)(2,1)} %param.10), kind=kOutput, calls=%fused_computation.14 | convolution fusion | flops 26214400 | bytes 1720320 | tf_op jit(solution)/shard_map/slj,xksj->xkls/dot_general | solution.py:153
  5.5 0.6 copy.56
  6.1 0.9 reshape.234
  7.0 12.6 %all-to-all-start = ((bf16[32,2,320]{2,1,0:T(2,128)(2,1)}), bf16[32,2,320]{2,1,0:T(2,128)(2,1)S(1)}, u32[]{:S(2)}, u32[]{:S(2)}) async-start(bf16[32,2,320]{2,1,0:T(2,128)(2,1)} %reshape.234), calls=%async_computation | async-start | bytes 98304 | tf_op jit(solution)/shard_map/all_to_all | solution.py:165
  19.6 0.6 fusion.33
  20.2 0.7 copy.72
  20.9 1.9 %collective-permute-start.1 = (bf16[40,1,1,2688]{3,0,2,1:T(8,128)(2,1)}, bf16[40,1,1,2688]{3,0,2,1:T(8,128)(2,1)}, u32[]{:S(2)}, u32[]{:S(2)}) collective-permute-start(bf16[40,1,1,2688]{3,0,2,1:T(8,128)(2,1)} %copy.72), channel_id=1, source_target_pairs={{1,0},{2,1},{3,2},{4,3},{5,4},{6,5},{7,6},{8,7},{9,8},{10,9},{11,1... | collective-permute-start | bytes 645128 | tf_op jit(solution)/shard_map/ppermute | solution.py:25
  22.8 0.7 copy.71
  23.5 2.5 %collective-permute-start = (bf16[40,1,1,2688]{3,0,2,1:T(8,128)(2,1)}, bf16[40,1,1,2688]{3,0,2,1:T(8,128)(2,1)}, u32[]{:S(2)}, u32[]{:S(2)}) collective-permute-start(bf16[40,1,1,2688]{3,0,2,1:T(8,128)(2,1)} %copy.71), channel_id=1, source_target_pairs={{0,1},{1,2},{2,3},{3,4},{4,5},{5,6},{6,7},{7,8},{8,9},{9,10},{10,1... | collective-permute-start | bytes 645128 | tf_op jit(solution)/shard_map/ppermute | solution.py:23
  26.1 2.2 %fusion.16 = (f32[640,128]{1,0:T(8,128)S(1)}, f32[640,128]{1,0:T(8,128)}) fusion(s32[640]{0:T(1024)S(1)} %copy-done.13), kind=kLoop, calls=%fused_computation.32 | loop fusion | flops 737280 | bytes 657920 | tf_op jit(solution)/shard_map/cos | solution.py:56
  28.5 0.7 slice_bitcast_fusion.2
  29.2 1.0 cosine_multiply_fusion
  30.2 4.0 %add_convert_fusion.stencil_ref = bf16[21,4,128,128]{3,2,1,0:T(8,128)(2,1)} fusion(f32[21,4,128]{2,1,0:T(4,128)S(1)} %bitcast.55, s32[21,4,128]{2,1,0:T(4,128)S(1)} %get-tuple-element.50, f32[21,4,128]{2,1,0:T(4,128)S(1)} %bitcast.56, s32[21,4,128]{2,1,0:T(4,128)S(1)} %get-tuple-element.51, f32[21,4,128]{2,1,0:T(4,128)S(1)} %bitcast.54, ...), kind=kLoop, calls=%fused_computation | loop fusion | flops 16515072 | bytes 3096576 | tf_op jit(solution)/shard_map/convert_element_type | solution.py:179
  34.3 0.6 min.12.listed_ref
  35.1 0.6 reshape.223.slot_ref
  37.0 0.7 slice_bitcast_fusion.4
  37.7 1.3 %copy.64 = bf16[40,1,1,2688]{3,1,2,0:T(2,128)(2,1)S(1)} copy(bf16[40,1,1,2688]{3,0,2,1:T(8,128)(2,1)} %collective-permute-done.1) | data formatting | bytes 430080 | tf_op jit(solution)/shard_map/ppermute | solution.py:25
  39.0 1.3 %copy.62 = bf16[40,1,1,2688]{3,1,2,0:T(2,128)(2,1)S(1)} copy(bf16[40,1,1,2688]{3,0,2,1:T(8,128)(2,1)} %collective-permute-done) | data formatting | bytes 430080 | tf_op jit(solution)/shard_map/ppermute | solution.py:23
  40.2 4.0 %fusion.3.refs_0_.refs_1_.refs_2_.refs_3_.refs_4_ = bf16[320,2688]{1,0:T(8,128)(2,1)} fusion(bf16[40,8,1,2688]{3,1,2,0:T(8,128)(2,1)S(1)} %copy-done.1, bf16[40,1,1,2688]{3,1,2,0:T(2,128)(2,1)S(1)} %copy.64, bf16[40,1,1,2688]{3,1,2,0:T(2,128)(2,1)S(1)} %copy.62, f32[8,2688]{1,0:T(8,128)} %get-tuple-element.39, f32[8,2688]{1,0:T(8,128)} %get-tuple-element.40, ...), kind=kLoop, calls=%fused_computation.10 | loop fusion | flops 12902400 | bytes 4128768 | tf_op jit(solution)/shard_map/reshape | solution.py:174
  44.3 4.5 %shard_map.121 = (bf16[4,320,128]{2,1,0:T(8,128)(2,1)}, bf16[4,320,128]{2,1,0:T(8,128)(2,1)}, bf16[4,320,128]{2,1,0:T(8,128)(2,1)}, bf16[4,320,128]{2,1,0:T(8,128)(2,1)}, bf16[4,320,128]{2,1,0:T(8,128)(2,1)}) custom-call(s32[20]{0:T(128)} %min.12.listed_ref, bf16[320,2688]{1,0:T(8,128)(2,1)} %fusion.3.refs_0_.refs_1_.refs_2_.refs_3_.refs_4_, ...), custom_call_target="tpu_custom_call" | custom-call | tf_op jit(solution)/shard_map/pallas_call | solution.py:92
  48.8 4.0 %collective-permute-start.2 = (bf16[4,320,128]{2,1,0:T(8,128)(2,1)}, bf16[4,320,128]{2,1,0:T(8,128)(2,1)S(1)}, u32[]{:S(2)}, u32[]{:S(2)}) collective-permute-start(bf16[4,320,128]{2,1,0:T(8,128)(2,1)} %get-tuple-element.10), channel_id=1, source_target_pairs={{32,0},{48,16},{64,32},{80,48},{96,64},{112,80},{128,96},{144,112}... | collective-permute-start | bytes 983048 | tf_op jit(solution)/shard_map/ppermute | solution.py:35
  52.8 3.4 %collective-permute-start.3 = (bf16[4,320,128]{2,1,0:T(8,128)(2,1)}, bf16[4,320,128]{2,1,0:T(8,128)(2,1)S(1)}, u32[]{:S(2)}, u32[]{:S(2)}) collective-permute-start(bf16[4,320,128]{2,1,0:T(8,128)(2,1)} %get-tuple-element.11), channel_id=1, source_target_pairs={{16,0},{32,16},{48,32},{64,48},{80,64},{96,80},{112,96},{128,112},... | collective-permute-start | bytes 983048 | tf_op jit(solution)/shard_map/ppermute | solution.py:35
  56.2 2.5 %collective-permute-start.4 = (bf16[4,320,128]{2,1,0:T(8,128)(2,1)}, bf16[4,320,128]{2,1,0:T(8,128)(2,1)}, u32[]{:S(2)}, u32[]{:S(2)}) collective-permute-start(bf16[4,320,128]{2,1,0:T(8,128)(2,1)} %get-tuple-element.13), channel_id=1, source_target_pairs={{0,16},{16,32},{32,48},{48,64},{64,80},{80,96},{96,112},{112,128},... | collective-permute-start | bytes 983048 | tf_op jit(solution)/shard_map/ppermute | solution.py:35
  58.7 5.6 %collective-permute-start.5 = (bf16[4,320,128]{2,1,0:T(8,128)(2,1)}, bf16[4,320,128]{2,1,0:T(8,128)(2,1)}, u32[]{:S(2)}, u32[]{:S(2)}) collective-permute-start(bf16[4,320,128]{2,1,0:T(8,128)(2,1)} %get-tuple-element.14), channel_id=1, source_target_pairs={{0,32},{16,48},{32,64},{48,80},{64,96},{80,112},{96,128},{112,144}... | collective-permute-start | bytes 983048 | tf_op jit(solution)/shard_map/ppermute | solution.py:35
  64.5 1.7 %fusion.4 = bf16[2,8,21,128]{3,2,1,0:T(8,128)(2,1)S(1)} fusion(f32[2,8,1,21,640]{4,3,1,0,2:T(8,128)S(1)} %get-tuple-element.42, f32[2,8,1,21,640]{4,3,1,0,2:T(8,128)S(1)} %get-tuple-element.41, f32[640,128]{1,0:T(8,128)S(1)} %copy-done.2, f32[640,128]{1,0:T(8,128)S(1)} %get-tuple-element.54), kind=kOutput, calls=%fused_computation.15 | convolution fusion | flops 661239808 | bytes 2461696 | tf_op jit(solution)/shard_map/wklom,mi->wkloi/dot_general | solution.py:57
  66.4 3.6 %collective-permute-done.3.refs_1_ = bf16[4,320,128]{2,1,0:T(8,128)(2,1)S(1)} collective-permute-done((bf16[4,320,128]{2,1,0:T(8,128)(2,1)}, bf16[4,320,128]{2,1,0:T(8,128)(2,1)S(1)}, u32[]{:S(2)}, u32[]{:S(2)}) %collective-permute-start.3) | collective-permute-done | bytes 327712 | tf_op jit(solution)/shard_map/ppermute | solution.py:35
  70.0 1.0 collective-permute-done.4.refs_3_
  71.0 10.1 %collective-permute-done.5.refs_4_ = bf16[4,320,128]{2,1,0:T(8,128)(2,1)} collective-permute-done((bf16[4,320,128]{2,1,0:T(8,128)(2,1)}, bf16[4,320,128]{2,1,0:T(8,128)(2,1)}, u32[]{:S(2)}, u32[]{:S(2)}) %collective-permute-start.5) | collective-permute-done | bytes 327712 | tf_op jit(solution)/shard_map/ppermute | solution.py:35
  81.1 20.4 %shard_map.122 = (bf16[320,2688]{1,0:T(8,128)(2,1)}, f32[8,2688]{1,0:T(8,128)}) custom-call(s32[84]{0:T(128)} %reshape.223.slot_ref, bf16[21,4,128,128]{3,2,1,0:T(8,128)(2,1)} %add_convert_fusion.stencil_ref, bf16[4,320,128]{2,1,0:T(8,128)(2,1)} %copy-done.5, bf16[4,320,128]{2,1,0:T(8,128)(2,1)} %copy-done.6, ...), custom_call_target="tpu_custom_call" | custom-call | tf_op jit(solution)/shard_map/pallas_call | solution.py:132
  101.5 1.5 %fusion.18 = bf16[2,8,1,2688]{3,1,2,0:T(8,128)(2,1)} fusion(bf16[2,8,1,2688]{3,1,0,2:T(8,128)(2,1)S(1)} %convert_element_type.101, f32[8,2688]{1,0:T(8,128)} %get-tuple-element.16), kind=kLoop, calls=%fused_computation.37 | loop fusion | flops 129024 | bytes 258048
  (52 shorter events, 2.3 us)
Async XLA Ops:
  0.6 1.2 %copy-start = (bf16[20,32,640]{2,1,0:T(8,128)(2,1)S(1)}, bf16[20,32,640]{2,1,0:T(8,128)(2,1)}, u32[]{:S(2)}) copy-start(bf16[20,32,640]{2,1,0:T(8,128)(2,1)} %param.11) | copy-start | bytes 2457604
  0.6 4.6 %copy-start.13 = (s32[640]{0:T(1024)S(1)}, s32[640]{0:T(1024)}, u32[]{:S(2)}) copy-start(s32[640]{0:T(1024)} %param.13) | copy-start | bytes 7684
  1.8 17.8 %copy-start.1 = (bf16[40,8,1,2688]{3,1,2,0:T(8,128)(2,1)S(1)}, bf16[40,8,1,2688]{3,1,2,0:T(8,128)(2,1)}, u32[]{:S(2)}) copy-start(bf16[40,8,1,2688]{3,1,2,0:T(8,128)(2,1)} %param.14) | copy-start | bytes 5160964
  5.3 23.0 %copy-start.9 = (s32[21,4,128]{2,1,0:T(4,128)S(1)}, s32[21,4,128]{2,1,0:T(4,128)}, u32[]{:S(2)}) copy-start(s32[21,4,128]{2,1,0:T(4,128)} %param.18) | copy-start | bytes 129028
  5.3 23.0 %copy-start.3 = (bf16[21,4,4,128]{3,2,1,0:T(4,128)(2,1)S(1)}, bf16[21,4,4,128]{3,2,1,0:T(4,128)(2,1)}, u32[]{:S(2)}) copy-start(bf16[21,4,4,128]{3,2,1,0:T(4,128)(2,1)} %param.19) | copy-start | bytes 258052
  5.4 23.0 %copy-start.12 = (bf16[3,8,1,2688]{3,1,2,0:T(8,128)(2,1)S(1)}, bf16[3,8,1,2688]{3,1,2,0:T(8,128)(2,1)}, u32[]{:S(2)}) copy-start(bf16[3,8,1,2688]{3,1,2,0:T(8,128)(2,1)} %param.15) | copy-start | bytes 387076
  7.0 28.7 %all-to-all-start = ((bf16[32,2,320]{2,1,0:T(2,128)(2,1)}), bf16[32,2,320]{2,1,0:T(2,128)(2,1)S(1)}, u32[]{:S(2)}, u32[]{:S(2)}) async-start(bf16[32,2,320]{2,1,0:T(2,128)(2,1)} %reshape.234), calls=%async_computation | async-start | bytes 98304 | tf_op jit(solution)/shard_map/all_to_all | solution.py:165
  20.9 16.8 %collective-permute-start.1 = (bf16[40,1,1,2688]{3,0,2,1:T(8,128)(2,1)}, bf16[40,1,1,2688]{3,0,2,1:T(8,128)(2,1)}, u32[]{:S(2)}, u32[]{:S(2)}) collective-permute-start(bf16[40,1,1,2688]{3,0,2,1:T(8,128)(2,1)} %copy.72), channel_id=1, source_target_pairs={{1,0},{2,1},{3,2},{4,3},{5,4},{6,5},{7,6},{8,7},{9,8},{10,9},{11,1... | collective-permute-start | bytes 645128 | tf_op jit(solution)/shard_map/ppermute | solution.py:25
  23.5 10.7 %copy-start.15 = (s32[1,5,4]{1,2,0:T(4,128)S(1)}, s32[1,5,4]{1,2,0:T(4,128)}, u32[]{:S(2)}) copy-start(s32[1,5,4]{1,2,0:T(4,128)} %param.16) | copy-start | bytes 244
  23.5 11.5 %copy-start.14 = (s32[21,4]{0,1:T(4,128)S(1)}, s32[21,4]{0,1:T(4,128)}, u32[]{:S(2)}) copy-start(s32[21,4]{0,1:T(4,128)} %param.17) | copy-start | bytes 1012
  23.5 15.5 %collective-permute-start = (bf16[40,1,1,2688]{3,0,2,1:T(8,128)(2,1)}, bf16[40,1,1,2688]{3,0,2,1:T(8,128)(2,1)}, u32[]{:S(2)}, u32[]{:S(2)}) collective-permute-start(bf16[40,1,1,2688]{3,0,2,1:T(8,128)(2,1)} %copy.71), channel_id=1, source_target_pairs={{0,1},{1,2},{2,3},{3,4},{4,5},{5,6},{6,7},{7,8},{8,9},{9,10},{10,1... | collective-permute-start | bytes 645128 | tf_op jit(solution)/shard_map/ppermute | solution.py:23
  44.2 20.0 %copy-start.7 = (f32[21,640]{1,0:T(8,128)S(1)}, f32[21,640]{1,0:T(8,128)}, u32[]{:S(2)}) copy-start(f32[21,640]{1,0:T(8,128)} %get-tuple-element.52) | copy-start | bytes 161284
  44.2 20.0 %copy-start.8 = (f32[21,640]{1,0:T(8,128)S(1)}, f32[21,640]{1,0:T(8,128)}, u32[]{:S(2)}) copy-start(f32[21,640]{1,0:T(8,128)} %get-tuple-element.53) | copy-start | bytes 161284
  44.2 20.0 %copy-start.10 = (f32[2,8,640]{2,1,0:T(8,128)S(1)}, f32[2,8,640]{2,1,0:T(8,128)}, u32[]{:S(2)}) copy-start(f32[2,8,640]{2,1,0:T(8,128)} %get-tuple-element.47) | copy-start | bytes 122884
  44.2 20.0 %copy-start.11 = (f32[2,8,640]{2,1,0:T(8,128)S(1)}, f32[2,8,640]{2,1,0:T(8,128)}, u32[]{:S(2)}) copy-start(f32[2,8,640]{2,1,0:T(8,128)} %get-tuple-element.48) | copy-start | bytes 122884
  44.3 20.3 %copy-start.2 = (f32[640,128]{1,0:T(8,128)S(1)}, f32[640,128]{1,0:T(8,128)}, u32[]{:S(2)}) copy-start(f32[640,128]{1,0:T(8,128)} %get-tuple-element.55) | copy-start | bytes 983044
  48.8 17.6 %collective-permute-start.2 = (bf16[4,320,128]{2,1,0:T(8,128)(2,1)}, bf16[4,320,128]{2,1,0:T(8,128)(2,1)S(1)}, u32[]{:S(2)}, u32[]{:S(2)}) collective-permute-start(bf16[4,320,128]{2,1,0:T(8,128)(2,1)} %get-tuple-element.10), channel_id=1, source_target_pairs={{32,0},{48,16},{64,32},{80,48},{96,64},{112,80},{128,96},{144,112}... | collective-permute-start | bytes 983048 | tf_op jit(solution)/shard_map/ppermute | solution.py:35
  52.8 17.2 %collective-permute-start.3 = (bf16[4,320,128]{2,1,0:T(8,128)(2,1)}, bf16[4,320,128]{2,1,0:T(8,128)(2,1)S(1)}, u32[]{:S(2)}, u32[]{:S(2)}) collective-permute-start(bf16[4,320,128]{2,1,0:T(8,128)(2,1)} %get-tuple-element.11), channel_id=1, source_target_pairs={{16,0},{32,16},{48,32},{64,48},{80,64},{96,80},{112,96},{128,112},... | collective-permute-start | bytes 983048 | tf_op jit(solution)/shard_map/ppermute | solution.py:35
  56.2 14.8 %collective-permute-start.4 = (bf16[4,320,128]{2,1,0:T(8,128)(2,1)}, bf16[4,320,128]{2,1,0:T(8,128)(2,1)}, u32[]{:S(2)}, u32[]{:S(2)}) collective-permute-start(bf16[4,320,128]{2,1,0:T(8,128)(2,1)} %get-tuple-element.13), channel_id=1, source_target_pairs={{0,16},{16,32},{32,48},{48,64},{64,80},{80,96},{96,112},{112,128},... | collective-permute-start | bytes 983048 | tf_op jit(solution)/shard_map/ppermute | solution.py:35
  58.7 22.5 %collective-permute-start.5 = (bf16[4,320,128]{2,1,0:T(8,128)(2,1)}, bf16[4,320,128]{2,1,0:T(8,128)(2,1)}, u32[]{:S(2)}, u32[]{:S(2)}) collective-permute-start(bf16[4,320,128]{2,1,0:T(8,128)(2,1)} %get-tuple-element.14), channel_id=1, source_target_pairs={{0,32},{16,48},{32,64},{48,80},{64,96},{80,112},{96,128},{112,144}... | collective-permute-start | bytes 983048 | tf_op jit(solution)/shard_map/ppermute | solution.py:35
  66.3 36.8 %copy-start.4 = (bf16[2,8,1,2688]{3,1,0,2:T(8,128)(2,1)}, bf16[2,8,1,2688]{3,1,0,2:T(8,128)(2,1)S(1)}, u32[]{:S(2)}) copy-start(bf16[2,8,1,2688]{3,1,0,2:T(8,128)(2,1)S(1)} %convert_element_type.101) | copy-start | bytes 258052
  66.4 14.8 %copy-start.5 = (bf16[4,320,128]{2,1,0:T(8,128)(2,1)}, bf16[4,320,128]{2,1,0:T(8,128)(2,1)S(1)}, u32[]{:S(2)}) copy-start(bf16[4,320,128]{2,1,0:T(8,128)(2,1)S(1)} %collective-permute-done.2.refs_0_) | copy-start | bytes 983044
  70.0 11.2 %copy-start.6 = (bf16[4,320,128]{2,1,0:T(8,128)(2,1)}, bf16[4,320,128]{2,1,0:T(8,128)(2,1)S(1)}, u32[]{:S(2)}) copy-start(bf16[4,320,128]{2,1,0:T(8,128)(2,1)S(1)} %collective-permute-done.3.refs_1_) | copy-start | bytes 983044

commit v4 on v3

--- a/solution.py
+++ b/solution.py
@@ -74,23 +74,32 @@
 def pack_blocks(listed, remapped, offsets, cap):
     rows = remapped.shape[0]
 
-    def body(listed_ref, *refs):
+    def body(listed_ref, source_ref, *refs):
+        out_refs = refs[:offsets]
+        sems = refs[offsets]
+        copies = []
         for index in range(offsets):
-            refs[offsets + index][...] = refs[index][...][None]
-
-    def source_map(index):
-        return lambda entry, table: (0, table[index * cap + entry])
+            for entry in range(cap):
+                column = pl.multiple_of(listed_ref[index * cap + entry] * BLK, BLK)
+                copy = pltpu.make_async_copy(
+                    source_ref.at[:, pl.ds(column, BLK)],
+                    out_refs[index].at[entry],
+                    sems.at[index * cap + entry],
+                )
+                copy.start()
+                copies.append(copy)
+        for copy in copies:
+            copy.wait()
 
     out_shape = [jax.ShapeDtypeStruct((cap, rows, BLK), remapped.dtype) for _ in range(offsets)]
     grid_spec = pltpu.PrefetchScalarGridSpec(
         num_scalar_prefetch=1,
-        grid=(cap,),
-        in_specs=[pl.BlockSpec((rows, BLK), source_map(index)) for index in range(offsets)],
-        out_specs=[pl.BlockSpec((1, rows, BLK), lambda entry, table: (entry, 0, 0))
-                   for _ in range(offsets)],
-    )
-    return pl.pallas_call(body, grid_spec=grid_spec, out_shape=out_shape)(
-        listed, *([remapped] * offsets))
+        grid=(1,),
+        in_specs=[pl.BlockSpec(memory_space=pl.ANY)],
+        out_specs=[pl.BlockSpec(memory_space=pl.ANY) for _ in range(offsets)],
+        scratch_shapes=[pltpu.SemaphoreType.DMA((offsets * cap,))],
+    )
+    return pl.pallas_call(body, grid_spec=grid_spec, out_shape=out_shape)(listed, remapped)
 
 
 def apply_stencil(slots, stencil, pieces, bin_count, level_count):
@@ -100,20 +109,24 @@
 
     def body(slot_ref, stencil_ref, *refs):
         piece_refs = refs[:count]
-        out_ref, mean_ref, acc_ref = refs[count:]
+        out_ref, mean_ref, pool_ref, sems = refs[count:]
         block = pl.program_id(0)
-        acc_ref[...] = jnp.zeros_like(acc_ref)
+
+        @pl.when(block == 0)
+        def _():
+            copies = [pltpu.make_async_copy(piece_refs[index], pool_ref.at[pl.ds(index * cap, cap)],
+                                            sems.at[index]) for index in range(count)]
+            for copy in copies:
+                copy.start()
+            for copy in copies:
+                copy.wait()
+
+        total = None
         for row in range(rows_per_block):
-            slot = slot_ref[block * rows_per_block + row]
-            piece = slot // cap
-            entry = slot % cap
-            weights = stencil_ref[0, row]
-            for index in range(count):
-                @pl.when(piece == index)
-                def _(index=index):
-                    acc_ref[...] += jnp.dot(piece_refs[index][entry], weights,
-                                            preferred_element_type=jnp.float32)
-        result = acc_ref[...].astype(out_ref.dtype)
+            slot = jnp.clip(slot_ref[block * rows_per_block + row], 0, count * cap - 1)
+            term = jnp.dot(pool_ref[slot], stencil_ref[0, row], preferred_element_type=jnp.float32)
+            total = term if total is None else total + term
+        result = total.astype(out_ref.dtype)
         out_ref[...] = result
         summed = result.astype(jnp.float32).reshape(bin_count, level_count, BLK).sum(axis=0)
         mean_ref[...] = summed / bin_count
@@ -122,14 +135,18 @@
         num_scalar_prefetch=1,
         grid=(block_count,),
         in_specs=[pl.BlockSpec((1, rows_per_block, BLK, BLK), lambda b, table: (b, 0, 0, 0))]
-        + [pl.BlockSpec((cap, rows, BLK), lambda b, table: (0, 0, 0)) for _ in range(count)],
+        + [pl.BlockSpec(memory_space=pl.ANY) for _ in range(count)],
         out_specs=[pl.BlockSpec((rows, BLK), lambda b, table: (0, b)),
                    pl.BlockSpec((level_count, BLK), lambda b, table: (0, b))],
-        scratch_shapes=[pltpu.VMEM((rows, BLK), jnp.float32)],
+        scratch_shapes=[pltpu.VMEM((count * cap, rows, BLK), pieces[0].dtype),
+                        pltpu.SemaphoreType.DMA((count,))],
     )
     out_shape = [jax.ShapeDtypeStruct((rows, block_count * BLK), pieces[0].dtype),
                  jax.ShapeDtypeStruct((level_count, block_count * BLK), jnp.float32)]
-    return pl.pallas_call(body, grid_spec=grid_spec, out_shape=out_shape)(slots, stencil, *pieces)
+    return pl.pallas_call(
+        body, grid_spec=grid_spec, out_shape=out_shape,
+        compiler_params=pltpu.CompilerParams(dimension_semantics=("arbitrary",)),
+    )(slots, stencil, *pieces)
 
 
 def shards(

time: 104 us -> 147 us (1.41)
  the two profiles are of different devices: /device:TPU:74 before, /device:TPU:82 now
where the time goes in v4:
time: 147 us; the launch traced here: 146 us
  Pallas kernels  67.6 us (46%)
  starting transfers between devices  32.3 us (22%)
  other arithmetic  14.3 us (10%)
  waiting for transfers between devices  14.1 us (10%)
  local copies, waits for them, and re-layouts  11.4 us (8%)
  matrix products  5.13 us (3%)
    pallas_call x1, Pallas kernels, pack_blocks(): pl.pallas_call(body, grid_spec=grid_spec, out_shape=out_shape)  51.7 us
    pallas_call x1, Pallas kernels, apply_stencil(): pl.pallas_call(body, grid_spec=grid_spec, out_shape=out_shape, compiler_p...  15.9 us
    ppermute x4, starting transfers between devices, shifted(): lax.ppermute(value, axis, [(source, source + steps) for source in range(l...  15.3 us
    ppermute x4, waiting for transfers between devices, shifted(): lax.ppermute(value, axis, [(source, source + steps) for source in range(l...  14.1 us
    all_to_all x1, starting transfers between devices, shards(): lax.all_to_all(coefficients, 'band', split_axis=2, concat_axis=3, tiled=T...  12.6 us
    convert_element_type x1, other arithmetic, shards(): stencil = stencil_matrix(depart_offset, depart_weight).astype(jnp.bfloat16)  4.02 us
    reshape x1, other arithmetic, shards(): vertical_sum.astype(jnp.bfloat16).reshape(rows, lat_count * lon_count)  3.99 us
    unnamed x29, local copies, waits for them, and re-layouts  3.99 us
  transfers between devices with their start and end apart: 7, of which 3 were waited for; matrix products, arithmetic and copies ran while one was open for 12% of the time, Pallas kernels for 0%

profile of v4, /device:TPU:82, one launch (start us, length us, event | category | flops | bytes accessed | tf_op | source)
XLA Modules:
  0.0 145.8 jit_solution(13197697940234526889)
XLA Ops:
  0.7 1.1 copy-done
  1.8 1.7 %convolution_bitcast_fusion = f32[4,8,32,20]{2,1,0,3:T(8,128)S(1)} fusion(bf16[20,32,640]{2,1,0:T(8,128)(2,1)S(1)} %copy-done, bf16[4,8,20,640]{3,1,2,0:T(8,128)(2,1)} %param.10), kind=kOutput, calls=%fused_computation.13 | convolution fusion | flops 26214400 | bytes 1720320 | tf_op jit(solution)/shard_map/slj,xksj->xkls/dot_general | solution.py:167
  3.4 1.8 %convolution_bitcast_fusion.1 = f32[4,8,32,20]{2,1,0,3:T(8,128)S(1)} fusion(bf16[20,32,640]{2,1,0:T(8,128)(2,1)} %param.12, bf16[4,8,20,640]{3,1,2,0:T(8,128)(2,1)} %param.10), kind=kOutput, calls=%fused_computation.14 | convolution fusion | flops 26214400 | bytes 1720320 | tf_op jit(solution)/shard_map/slj,xksj->xkls/dot_general | solution.py:170
  6.1 0.9 reshape.234
  7.0 12.6 %all-to-all-start = ((bf16[32,2,320]{2,1,0:T(2,128)(2,1)}), bf16[32,2,320]{2,1,0:T(2,128)(2,1)S(1)}, u32[]{:S(2)}, u32[]{:S(2)}) async-start(bf16[32,2,320]{2,1,0:T(2,128)(2,1)} %reshape.234), calls=%async_computation | async-start | bytes 98304 | tf_op jit(solution)/shard_map/all_to_all | solution.py:182
  19.6 0.6 fusion.33
  20.2 0.7 copy.72
  20.9 1.9 %collective-permute-start.1 = (bf16[40,1,1,2688]{3,0,2,1:T(8,128)(2,1)}, bf16[40,1,1,2688]{3,0,2,1:T(8,128)(2,1)}, u32[]{:S(2)}, u32[]{:S(2)}) collective-permute-start(bf16[40,1,1,2688]{3,0,2,1:T(8,128)(2,1)} %copy.72), channel_id=1, source_target_pairs={{1,0},{2,1},{3,2},{4,3},{5,4},{6,5},{7,6},{8,7},{9,8},{10,9},{11,1... | collective-permute-start | bytes 645128 | tf_op jit(solution)/shard_map/ppermute | solution.py:25
  22.8 0.7 copy.71
  23.5 2.5 %collective-permute-start = (bf16[40,1,1,2688]{3,0,2,1:T(8,128)(2,1)}, bf16[40,1,1,2688]{3,0,2,1:T(8,128)(2,1)}, u32[]{:S(2)}, u32[]{:S(2)}) collective-permute-start(bf16[40,1,1,2688]{3,0,2,1:T(8,128)(2,1)} %copy.71), channel_id=1, source_target_pairs={{0,1},{1,2},{2,3},{3,4},{4,5},{5,6},{6,7},{7,8},{8,9},{9,10},{10,1... | collective-permute-start | bytes 645128 | tf_op jit(solution)/shard_map/ppermute | solution.py:23
  26.0 2.2 %fusion.16 = (f32[640,128]{1,0:T(8,128)S(1)}, f32[640,128]{1,0:T(8,128)}) fusion(s32[640]{0:T(1024)S(1)} %copy-done.9), kind=kLoop, calls=%fused_computation.32 | loop fusion | flops 737280 | bytes 657920 | tf_op jit(solution)/shard_map/cos | solution.py:56
  28.5 0.7 slice_bitcast_fusion.2
  29.2 1.0 cosine_multiply_fusion
  30.2 4.0 %add_convert_fusion.stencil_ref = bf16[21,4,128,128]{3,2,1,0:T(8,128)(2,1)} fusion(f32[21,4,128]{2,1,0:T(4,128)S(1)} %bitcast.55, s32[21,4,128]{2,1,0:T(4,128)S(1)} %get-tuple-element.50, f32[21,4,128]{2,1,0:T(4,128)S(1)} %bitcast.56, s32[21,4,128]{2,1,0:T(4,128)S(1)} %get-tuple-element.51, f32[21,4,128]{2,1,0:T(4,128)S(1)} %bitcast.54, ...), kind=kLoop, calls=%fused_computation | loop fusion | flops 16515072 | bytes 3096576 | tf_op jit(solution)/shard_map/convert_element_type | solution.py:196
  34.3 0.7 min.12.listed_ref
  35.1 0.6 reshape.223.slot_ref
  37.1 0.6 slice_bitcast_fusion.4
  37.7 1.3 copy.64
  39.0 1.3 copy.62
  40.3 4.0 %fusion.3.source_ref = bf16[320,2688]{1,0:T(8,128)(2,1)} fusion(bf16[40,8,1,2688]{3,1,2,0:T(8,128)(2,1)S(1)} %copy-done.1, bf16[40,1,1,2688]{3,1,2,0:T(2,128)(2,1)S(1)} %copy.64, bf16[40,1,1,2688]{3,1,2,0:T(2,128)(2,1)S(1)} %copy.62, f32[8,2688]{1,0:T(8,128)} %get-tuple-element.39, f32[8,2688]{1,0:T(8,128)} %get-tuple-element.40, f32[8,2688]{1,0:T(8,128)} %get-tuple-element.38), kind=kLoop, calls=%fused_computation.10 | loop fusion | flops 12902400 | bytes 4128768 | tf_op jit(solution)/shard_map/reshape | solution.py:191
  44.3 51.7 %shard_map.121 = (bf16[4,320,128]{2,1,0:T(8,128)(2,1)}, bf16[4,320,128]{2,1,0:T(8,128)(2,1)}, bf16[4,320,128]{2,1,0:T(8,128)(2,1)}, bf16[4,320,128]{2,1,0:T(8,128)(2,1)}, bf16[4,320,128]{2,1,0:T(8,128)(2,1)}) custom-call(s32[20]{0:T(128)} %min.12.listed_ref, bf16[320,2688]{1,0:T(8,128)(2,1)} %fusion.3.source_ref), custom_call_target="tpu_custom_call" | custom-call | tf_op jit(solution)/shard_map/pallas_call | solution.py:102
  96.0 4.0 %collective-permute-start.2 = (bf16[4,320,128]{2,1,0:T(8,128)(2,1)}, bf16[4,320,128]{2,1,0:T(8,128)(2,1)S(1)}, u32[]{:S(2)}, u32[]{:S(2)}) collective-permute-start(bf16[4,320,128]{2,1,0:T(8,128)(2,1)} %get-tuple-element.10), channel_id=1, source_target_pairs={{32,0},{48,16},{64,32},{80,48},{96,64},{112,80},{128,96},{144,112}... | collective-permute-start | bytes 983048 | tf_op jit(solution)/shard_map/ppermute | solution.py:35
  100.0 3.4 %collective-permute-start.3 = (bf16[4,320,128]{2,1,0:T(8,128)(2,1)}, bf16[4,320,128]{2,1,0:T(8,128)(2,1)S(1)}, u32[]{:S(2)}, u32[]{:S(2)}) collective-permute-start(bf16[4,320,128]{2,1,0:T(8,128)(2,1)} %get-tuple-element.11), channel_id=1, source_target_pairs={{16,0},{32,16},{48,32},{64,48},{80,64},{96,80},{112,96},{128,112},... | collective-permute-start | bytes 983048 | tf_op jit(solution)/shard_map/ppermute | solution.py:35
  103.3 2.5 %collective-permute-start.4 = (bf16[4,320,128]{2,1,0:T(8,128)(2,1)}, bf16[4,320,128]{2,1,0:T(8,128)(2,1)}, u32[]{:S(2)}, u32[]{:S(2)}) collective-permute-start(bf16[4,320,128]{2,1,0:T(8,128)(2,1)} %get-tuple-element.13), channel_id=1, source_target_pairs={{0,16},{16,32},{32,48},{48,64},{64,80},{80,96},{96,112},{112,128},... | collective-permute-start | bytes 983048 | tf_op jit(solution)/shard_map/ppermute | solution.py:35
  105.8 5.5 %collective-permute-start.5 = (bf16[4,320,128]{2,1,0:T(8,128)(2,1)}, bf16[4,320,128]{2,1,0:T(8,128)(2,1)}, u32[]{:S(2)}, u32[]{:S(2)}) collective-permute-start(bf16[4,320,128]{2,1,0:T(8,128)(2,1)} %get-tuple-element.14), channel_id=1, source_target_pairs={{0,32},{16,48},{32,64},{48,80},{64,96},{80,112},{96,128},{112,144}... | collective-permute-start | bytes 983048 | tf_op jit(solution)/shard_map/ppermute | solution.py:35
  111.3 1.1 multiply_subtract_fusion
  112.4 1.7 %fusion.4 = bf16[2,8,21,128]{3,2,1,0:T(8,128)(2,1)S(1)} fusion(f32[2,8,1,21,640]{4,3,1,0,2:T(8,128)S(1)} %get-tuple-element.42, f32[2,8,1,21,640]{4,3,1,0,2:T(8,128)S(1)} %get-tuple-element.41, f32[640,128]{1,0:T(8,128)S(1)} %copy-done.2, f32[640,128]{1,0:T(8,128)S(1)} %get-tuple-element.54), kind=kOutput, calls=%fused_computation.15 | convolution fusion | flops 661239808 | bytes 2461696 | tf_op jit(solution)/shard_map/wklom,mi->wkloi/dot_general | solution.py:57
  114.3 2.9 %collective-permute-done.3.refs_1_ = bf16[4,320,128]{2,1,0:T(8,128)(2,1)S(1)} collective-permute-done((bf16[4,320,128]{2,1,0:T(8,128)(2,1)}, bf16[4,320,128]{2,1,0:T(8,128)(2,1)S(1)}, u32[]{:S(2)}, u32[]{:S(2)}) %collective-permute-start.3) | collective-permute-done | bytes 327712 | tf_op jit(solution)/shard_map/ppermute | solution.py:35
  117.2 1.0 collective-permute-done.4.refs_3_
  118.2 10.1 %collective-permute-done.5.refs_4_ = bf16[4,320,128]{2,1,0:T(8,128)(2,1)} collective-permute-done((bf16[4,320,128]{2,1,0:T(8,128)(2,1)}, bf16[4,320,128]{2,1,0:T(8,128)(2,1)}, u32[]{:S(2)}, u32[]{:S(2)}) %collective-permute-start.5) | collective-permute-done | bytes 327712 | tf_op jit(solution)/shard_map/ppermute | solution.py:35
  128.4 15.9 %shard_map.122 = (bf16[320,2688]{1,0:T(8,128)(2,1)}, f32[8,2688]{1,0:T(8,128)}) custom-call(s32[84]{0:T(128)} %reshape.223.slot_ref, bf16[21,4,128,128]{3,2,1,0:T(8,128)(2,1)} %add_convert_fusion.stencil_ref, bf16[4,320,128]{2,1,0:T(8,128)(2,1)} %copy-done.5, bf16[4,320,128]{2,1,0:T(8,128)(2,1)} %copy-done.6, ...), custom_call_target="tpu_custom_call" | custom-call | tf_op jit(solution)/shard_map/pallas_call | solution.py:146
  144.3 1.5 %fusion.18 = bf16[2,8,1,2688]{3,1,2,0:T(8,128)(2,1)} fusion(bf16[2,8,1,2688]{3,1,0,2:T(8,128)(2,1)S(1)} %convert_element_type.101, f32[8,2688]{1,0:T(8,128)} %get-tuple-element.16), kind=kLoop, calls=%fused_computation.37 | loop fusion | flops 129024 | bytes 258048
  (44 shorter events, 2.6 us)
Async XLA Ops:
  0.6 1.2 copy-start
  0.6 4.6 %copy-start.9 = (s32[640]{0:T(1024)S(1)}, s32[640]{0:T(1024)}, u32[]{:S(2)}) copy-start(s32[640]{0:T(1024)} %param.13) | copy-start | bytes 7684
  1.8 17.8 %copy-start.1 = (bf16[40,8,1,2688]{3,1,2,0:T(8,128)(2,1)S(1)}, bf16[40,8,1,2688]{3,1,2,0:T(8,128)(2,1)}, u32[]{:S(2)}) copy-start(bf16[40,8,1,2688]{3,1,2,0:T(8,128)(2,1)} %param.14) | copy-start | bytes 5160964
  5.3 23.0 %copy-start.7 = (s32[21,4,128]{2,1,0:T(4,128)S(1)}, s32[21,4,128]{2,1,0:T(4,128)}, u32[]{:S(2)}) copy-start(s32[21,4,128]{2,1,0:T(4,128)} %param.18) | copy-start | bytes 129028
  5.3 23.0 %copy-start.3 = (bf16[21,4,4,128]{3,2,1,0:T(4,128)(2,1)S(1)}, bf16[21,4,4,128]{3,2,1,0:T(4,128)(2,1)}, u32[]{:S(2)}) copy-start(bf16[21,4,4,128]{3,2,1,0:T(4,128)(2,1)} %param.19) | copy-start | bytes 258052
  5.4 23.0 %copy-start.8 = (bf16[3,8,1,2688]{3,1,2,0:T(8,128)(2,1)S(1)}, bf16[3,8,1,2688]{3,1,2,0:T(8,128)(2,1)}, u32[]{:S(2)}) copy-start(bf16[3,8,1,2688]{3,1,2,0:T(8,128)(2,1)} %param.15) | copy-start | bytes 387076
  7.0 28.7 %all-to-all-start = ((bf16[32,2,320]{2,1,0:T(2,128)(2,1)}), bf16[32,2,320]{2,1,0:T(2,128)(2,1)S(1)}, u32[]{:S(2)}, u32[]{:S(2)}) async-start(bf16[32,2,320]{2,1,0:T(2,128)(2,1)} %reshape.234), calls=%async_computation | async-start | bytes 98304 | tf_op jit(solution)/shard_map/all_to_all | solution.py:182
  20.9 16.9 %collective-permute-start.1 = (bf16[40,1,1,2688]{3,0,2,1:T(8,128)(2,1)}, bf16[40,1,1,2688]{3,0,2,1:T(8,128)(2,1)}, u32[]{:S(2)}, u32[]{:S(2)}) collective-permute-start(bf16[40,1,1,2688]{3,0,2,1:T(8,128)(2,1)} %copy.72), channel_id=1, source_target_pairs={{1,0},{2,1},{3,2},{4,3},{5,4},{6,5},{7,6},{8,7},{9,8},{10,9},{11,1... | collective-permute-start | bytes 645128 | tf_op jit(solution)/shard_map/ppermute | solution.py:25
  23.5 10.7 %copy-start.11 = (s32[1,5,4]{1,2,0:T(4,128)S(1)}, s32[1,5,4]{1,2,0:T(4,128)}, u32[]{:S(2)}) copy-start(s32[1,5,4]{1,2,0:T(4,128)} %param.16) | copy-start | bytes 244
  23.5 11.5 %copy-start.10 = (s32[21,4]{0,1:T(4,128)S(1)}, s32[21,4]{0,1:T(4,128)}, u32[]{:S(2)}) copy-start(s32[21,4]{0,1:T(4,128)} %param.17) | copy-start | bytes 1012
  23.5 15.5 %collective-permute-start = (bf16[40,1,1,2688]{3,0,2,1:T(8,128)(2,1)}, bf16[40,1,1,2688]{3,0,2,1:T(8,128)(2,1)}, u32[]{:S(2)}, u32[]{:S(2)}) collective-permute-start(bf16[40,1,1,2688]{3,0,2,1:T(8,128)(2,1)} %copy.71), channel_id=1, source_target_pairs={{0,1},{1,2},{2,3},{3,4},{4,5},{5,6},{6,7},{7,8},{8,9},{9,10},{10,1... | collective-permute-start | bytes 645128 | tf_op jit(solution)/shard_map/ppermute | solution.py:23
  44.3 68.2 %copy-start.2 = (f32[640,128]{1,0:T(8,128)S(1)}, f32[640,128]{1,0:T(8,128)}, u32[]{:S(2)}) copy-start(f32[640,128]{1,0:T(8,128)} %get-tuple-element.55) | copy-start | bytes 983044
  96.0 18.3 %collective-permute-start.2 = (bf16[4,320,128]{2,1,0:T(8,128)(2,1)}, bf16[4,320,128]{2,1,0:T(8,128)(2,1)S(1)}, u32[]{:S(2)}, u32[]{:S(2)}) collective-permute-start(bf16[4,320,128]{2,1,0:T(8,128)(2,1)} %get-tuple-element.10), channel_id=1, source_target_pairs={{32,0},{48,16},{64,32},{80,48},{96,64},{112,80},{128,96},{144,112}... | collective-permute-start | bytes 983048 | tf_op jit(solution)/shard_map/ppermute | solution.py:35
  100.0 17.2 %collective-permute-start.3 = (bf16[4,320,128]{2,1,0:T(8,128)(2,1)}, bf16[4,320,128]{2,1,0:T(8,128)(2,1)S(1)}, u32[]{:S(2)}, u32[]{:S(2)}) collective-permute-start(bf16[4,320,128]{2,1,0:T(8,128)(2,1)} %get-tuple-element.11), channel_id=1, source_target_pairs={{16,0},{32,16},{48,32},{64,48},{80,64},{96,80},{112,96},{128,112},... | collective-permute-start | bytes 983048 | tf_op jit(solution)/shard_map/ppermute | solution.py:35
  103.3 14.9 %collective-permute-start.4 = (bf16[4,320,128]{2,1,0:T(8,128)(2,1)}, bf16[4,320,128]{2,1,0:T(8,128)(2,1)}, u32[]{:S(2)}, u32[]{:S(2)}) collective-permute-start(bf16[4,320,128]{2,1,0:T(8,128)(2,1)} %get-tuple-element.13), channel_id=1, source_target_pairs={{0,16},{16,32},{32,48},{48,64},{64,80},{80,96},{96,112},{112,128},... | collective-permute-start | bytes 983048 | tf_op jit(solution)/shard_map/ppermute | solution.py:35
  105.8 22.5 %collective-permute-start.5 = (bf16[4,320,128]{2,1,0:T(8,128)(2,1)}, bf16[4,320,128]{2,1,0:T(8,128)(2,1)}, u32[]{:S(2)}, u32[]{:S(2)}) collective-permute-start(bf16[4,320,128]{2,1,0:T(8,128)(2,1)} %get-tuple-element.14), channel_id=1, source_target_pairs={{0,32},{16,48},{32,64},{48,80},{64,96},{80,112},{96,128},{112,144}... | collective-permute-start | bytes 983048 | tf_op jit(solution)/shard_map/ppermute | solution.py:35
  114.2 31.6 %copy-start.4 = (bf16[2,8,1,2688]{3,1,0,2:T(8,128)(2,1)}, bf16[2,8,1,2688]{3,1,0,2:T(8,128)(2,1)S(1)}, u32[]{:S(2)}) copy-start(bf16[2,8,1,2688]{3,1,0,2:T(8,128)(2,1)S(1)} %convert_element_type.101) | copy-start | bytes 258052
  114.3 14.1 %copy-start.5 = (bf16[4,320,128]{2,1,0:T(8,128)(2,1)}, bf16[4,320,128]{2,1,0:T(8,128)(2,1)S(1)}, u32[]{:S(2)}) copy-start(bf16[4,320,128]{2,1,0:T(8,128)(2,1)S(1)} %collective-permute-done.2.refs_0_) | copy-start | bytes 983044
  117.2 11.2 %copy-start.6 = (bf16[4,320,128]{2,1,0:T(8,128)(2,1)}, bf16[4,320,128]{2,1,0:T(8,128)(2,1)S(1)}, u32[]{:S(2)}) copy-start(bf16[4,320,128]{2,1,0:T(8,128)(2,1)S(1)} %collective-permute-done.3.refs_1_) | copy-start | bytes 983044

commit v5 on v4

--- a/solution.py
+++ b/solution.py
@@ -74,32 +74,23 @@
 def pack_blocks(listed, remapped, offsets, cap):
     rows = remapped.shape[0]
 
-    def body(listed_ref, source_ref, *refs):
-        out_refs = refs[:offsets]
-        sems = refs[offsets]
-        copies = []
+    def body(listed_ref, *refs):
         for index in range(offsets):
-            for entry in range(cap):
-                column = pl.multiple_of(listed_ref[index * cap + entry] * BLK, BLK)
-                copy = pltpu.make_async_copy(
-                    source_ref.at[:, pl.ds(column, BLK)],
-                    out_refs[index].at[entry],
-                    sems.at[index * cap + entry],
-                )
-                copy.start()
-                copies.append(copy)
-        for copy in copies:
-            copy.wait()
+            refs[offsets + index][...] = refs[index][...][None]
+
+    def source_map(index):
+        return lambda entry, table: (0, table[index * cap + entry])
 
     out_shape = [jax.ShapeDtypeStruct((cap, rows, BLK), remapped.dtype) for _ in range(offsets)]
     grid_spec = pltpu.PrefetchScalarGridSpec(
         num_scalar_prefetch=1,
-        grid=(1,),
-        in_specs=[pl.BlockSpec(memory_space=pl.ANY)],
-        out_specs=[pl.BlockSpec(memory_space=pl.ANY) for _ in range(offsets)],
-        scratch_shapes=[pltpu.SemaphoreType.DMA((offsets * cap,))],
-    )
-    return pl.pallas_call(body, grid_spec=grid_spec, out_shape=out_shape)(listed, remapped)
+        grid=(cap,),
+        in_specs=[pl.BlockSpec((rows, BLK), source_map(index)) for index in range(offsets)],
+        out_specs=[pl.BlockSpec((1, rows, BLK), lambda entry, table: (entry, 0, 0))
+                   for _ in range(offsets)],
+    )
+    return pl.pallas_call(body, grid_spec=grid_spec, out_shape=out_shape)(
+        listed, *([remapped] * offsets))
 
 
 def apply_stencil(slots, stencil, pieces, bin_count, level_count):
@@ -161,6 +152,32 @@
     depart_offset,
     depart_weight,
 ):
+    padded = extended(aerosol_old, (("lev", 1),), 1)
+    weights = vertical_weight.astype(jnp.float32)
+    vertical_sum = (
+        weights[0] * padded[:, :-2] + weights[1] * padded[:, 1:-1] + weights[2] * padded[:, 2:]
+    )
+    bin_count, level_count, lat_count, lon_count = aerosol_old.shape
+    rows = bin_count * level_count
+    remapped = vertical_sum.astype(jnp.bfloat16).reshape(rows, lat_count * lon_count)
+    block_total = lat_count * lon_count // BLK
+    listed = jnp.clip(send_blocks[0], 0, block_total - 1)
+    offsets, cap = listed.shape
+    outgoing = pack_blocks(listed.reshape(-1), remapped, offsets, cap)
+    outgoing, spectral, legendre_value, legendre_slope, depart_offset, depart_weight = (
+        lax.optimization_barrier(
+            (outgoing, spectral, legendre_value, legendre_slope, depart_offset, depart_weight)
+        )
+    )
+    stencil = stencil_matrix(depart_offset, depart_weight).astype(jnp.bfloat16)
+    reach_bands = offsets // 2
+    pieces = []
+    for offset_index in range(offsets):
+        shift_by = offset_index - reach_bands
+        if shift_by == 0:
+            pieces.append(outgoing[offset_index])
+        else:
+            pieces.append(shifted(outgoing[offset_index], "band", shift_by))
     band_here = lax.axis_index("band")
     wave_local = spectral.shape[2]
     own_waves = lax.dynamic_slice_in_dim(wave_numbers, band_here * wave_local, wave_local, 0)
@@ -181,30 +198,13 @@
     ).astype(jnp.bfloat16)
     received = lax.all_to_all(coefficients, "band", split_axis=2, concat_axis=3, tiled=True)
     wind_grid = synthesis(received, wave_numbers, NLON).astype(jnp.bfloat16)
-    padded = extended(aerosol_old, (("lev", 1),), 1)
-    weights = vertical_weight.astype(jnp.float32)
-    vertical_sum = (
-        weights[0] * padded[:, :-2] + weights[1] * padded[:, 1:-1] + weights[2] * padded[:, 2:]
-    )
-    bin_count, level_count, lat_count, lon_count = aerosol_old.shape
-    rows = bin_count * level_count
-    remapped = vertical_sum.astype(jnp.bfloat16).reshape(rows, lat_count * lon_count)
-    block_total = lat_count * lon_count // BLK
-    listed = jnp.clip(send_blocks[0], 0, block_total - 1)
-    offsets, cap = listed.shape
-    outgoing = pack_blocks(listed.reshape(-1), remapped, offsets, cap)
-    stencil = stencil_matrix(depart_offset, depart_weight).astype(jnp.bfloat16)
-    reach_bands = offsets // 2
-    pieces = []
-    for offset_index in range(offsets):
-        shift_by = offset_index - reach_bands
-        if shift_by == 0:
-            pieces.append(outgoing[offset_index])
-        else:
-            pieces.append(shifted(outgoing[offset_index], "band", shift_by))
-    flat_new, average = apply_stencil(depart_slot.reshape(-1), stencil, pieces, bin_count, level_count)
+    pooled = jnp.stack(pieces)
+    flattened = pooled.reshape(offsets * cap, rows, BLK)
+    chosen = jnp.take(flattened, depart_slot, axis=0)
+    block_rows = jnp.einsum("jifq,jiqp->jfp", chosen, stencil, preferred_element_type=jnp.float32)
+    flat_new = block_rows.astype(jnp.bfloat16).transpose(1, 0, 2).reshape(rows, block_total * BLK)
     aerosol_new = flat_new.reshape(bin_count, level_count, lat_count, lon_count)
-    average = average.reshape(level_count, lat_count, lon_count)
+    average = jnp.mean(aerosol_new.astype(jnp.float32), axis=0)
     aerosol_flux = (wind_grid.astype(jnp.float32) * average[None]).astype(jnp.bfloat16)
     return (wind_grid, aerosol_new, aerosol_flux)
 

time: 147 us -> 96.7 us (0.66)
  the two profiles are of different devices: /device:TPU:82 before, /device:TPU:25 now
where the time goes in v5:
time: 96.7 us; the launch traced here: 95.5 us
  starting transfers between devices  33 us (34%)
  local copies, waits for them, and re-layouts  24.5 us (25%)
  other arithmetic  12.5 us (13%)
  waiting for transfers between devices  11.1 us (11%)
  matrix products  8.8 us (9%)
  Pallas kernels  4.45 us (5%)
  between operations  1.13 us (1%)
    ppermute x4, starting transfers between devices, shifted(): lax.ppermute(value, axis, [(source, source + steps) for source in range(l...  13.3 us
    all_to_all x1, starting transfers between devices, shards(): lax.all_to_all(coefficients, 'band', split_axis=2, concat_axis=3, tiled=T...  12.8 us
    all_to_all x1, waiting for transfers between devices, shards(): lax.all_to_all(coefficients, 'band', split_axis=2, concat_axis=3, tiled=T...  11.1 us
    gather x1, local copies, waits for them, and re-layouts, shards(): chosen = jnp.take(flattened, depart_slot, axis=0)  6.47 us
    dot_general x1, matrix products, shards(): jnp.einsum('jifq,jiqp->jfp', chosen, stencil, preferred_element_type=jnp....  6.33 us
    unnamed x48, local copies, waits for them, and re-layouts  5.96 us
    ppermute x1, starting transfers between devices, extended(): lax.ppermute(tail, axis, [(i, (i + 1) % count) for i in range(ends)])  4.96 us
    pallas_call x1, Pallas kernels, pack_blocks(): pl.pallas_call(body, grid_spec=grid_spec, out_shape=out_shape)  4.45 us
  transfers between devices with their start and end apart: 7, of which 1 were waited for; matrix products, arithmetic and copies ran while one was open for 19% of the time, Pallas kernels for 0%

profile of v5, /device:TPU:25, one launch (start us, length us, event | category | flops | bytes accessed | tf_op | source)
XLA Modules:
  0.0 95.5 jit_solution(12373638113700476278)
XLA Ops:
  0.7 2.8 %fusion.53 = (bf16[40,1,1,2688]{3,1,2,0:T(2,128)(2,1)S(1)}, bf16[40,1,1,2688]{3,1,2,0:T(2,128)(2,1)S(1)}) fusion(bf16[40,8,1,2688]{3,1,2,0:T(8,128)(2,1)} %param.14), kind=kLoop, calls=%fused_computation.105 | loop fusion | bytes 860160 | tf_op jit(solution)/shard_map/slice | solution.py:20
  3.5 0.7 copy.80
  4.2 5.0 %collective-permute-start = (bf16[40,1,1,2688]{3,0,2,1:T(8,128)(2,1)}, bf16[40,1,1,2688]{3,0,2,1:T(8,128)(2,1)}, u32[]{:S(2)}, u32[]{:S(2)}) collective-permute-start(bf16[40,1,1,2688]{3,0,2,1:T(8,128)(2,1)} %copy.80), channel_id=1, source_target_pairs={{0,1},{1,2},{2,3},{3,4},{4,5},{5,6},{6,7},{7,8},{8,9},{9,10},{10,1... | collective-permute-start | bytes 645128 | tf_op jit(solution)/shard_map/ppermute | solution.py:23
  9.2 0.7 copy.81
  9.9 1.9 %collective-permute-start.1 = (bf16[40,1,1,2688]{3,0,2,1:T(8,128)(2,1)}, bf16[40,1,1,2688]{3,0,2,1:T(8,128)(2,1)}, u32[]{:S(2)}, u32[]{:S(2)}) collective-permute-start(bf16[40,1,1,2688]{3,0,2,1:T(8,128)(2,1)} %copy.81), channel_id=1, source_target_pairs={{1,0},{2,1},{3,2},{4,3},{5,4},{6,5},{7,6},{8,7},{9,8},{10,9},{11,1... | collective-permute-start | bytes 645128 | tf_op jit(solution)/shard_map/ppermute | solution.py:25
  11.8 0.7 compare_select_fusion
  12.5 0.7 compare_and_fusion
  13.2 0.7 compare_select_fusion.1
  13.9 2.1 %fusion.34 = (f32[640,128]{1,0:T(8,128)S(1)}, f32[640,128]{1,0:T(8,128)S(1)}) fusion(s32[640]{0:T(1024)} %param.13), kind=kLoop, calls=%fused_computation.54 | loop fusion | flops 737280 | bytes 657920 | tf_op jit(solution)/shard_map/cos | solution.py:56
  17.2 1.0 %cosine_multiply_fusion = (f32[21,640]{1,0:T(8,128)S(1)}, f32[21,640]{1,0:T(8,128)}) fusion(s32[21]{0:T(128)S(1)} %iota_multiply_fusion, s32[640]{0:T(1024)S(1)} %copy-done.18, f32[640]{0:T(1024)S(1)} %compare_select_fusion.1), kind=kLoop, calls=%fused_computation.80 | loop fusion | flops 147840 | bytes 112724 | tf_op jit(solution)/shard_map/mul | solution.py:48
  18.1 1.3 %copy.62 = bf16[40,1,1,2688]{3,1,2,0:T(2,128)(2,1)S(1)} copy(bf16[40,1,1,2688]{3,0,2,1:T(8,128)(2,1)} %collective-permute-done) | data formatting | bytes 430080 | tf_op jit(solution)/shard_map/ppermute | solution.py:23
  19.4 1.3 %copy.64 = bf16[40,1,1,2688]{3,1,2,0:T(2,128)(2,1)S(1)} copy(bf16[40,1,1,2688]{3,0,2,1:T(8,128)(2,1)} %collective-permute-done.1) | data formatting | bytes 430080 | tf_op jit(solution)/shard_map/ppermute | solution.py:25
  20.7 3.0 %fusion.18.refs_0_.refs_1_.refs_2_.refs_3_.refs_4_ = bf16[320,2688]{1,0:T(8,128)(2,1)} fusion(bf16[40,8,1,2688]{3,1,2,0:T(8,128)(2,1)S(1)} %copy-done.1, bf16[40,1,1,2688]{3,1,2,0:T(2,128)(2,1)S(1)} %copy.64, bf16[40,1,1,2688]{3,1,2,0:T(2,128)(2,1)S(1)} %copy.62, f32[8,2688]{1,0:T(8,128)S(1)} %get-tuple-element.55, f32[8,2688]{1,0:T(8,128)S(1)} %get-tuple-element.56, ...), kind=kLoop, calls=%fused_computation.26 | loop fusion | flops 12902400 | bytes 4128768 | tf_op jit(solution)/shard_map/reshape | solution.py:162
  23.7 4.5 %shard_map.121 = (bf16[4,320,128]{2,1,0:T(8,128)(2,1)}, bf16[4,320,128]{2,1,0:T(8,128)(2,1)}, bf16[4,320,128]{2,1,0:T(8,128)(2,1)}, bf16[4,320,128]{2,1,0:T(8,128)(2,1)}, bf16[4,320,128]{2,1,0:T(8,128)(2,1)}) custom-call(s32[20]{0:T(128)} %min.12.listed_ref, bf16[320,2688]{1,0:T(8,128)(2,1)} %fusion.18.refs_0_.refs_1_.refs_2_.refs_3_.refs_4_, ...), custom_call_target="tpu_custom_call" | custom-call | tf_op jit(solution)/shard_map/pallas_call | solution.py:92
  28.2 1.4 %collective-permute-start.2 = (bf16[4,320,128]{2,1,0:T(8,128)(2,1)}, bf16[4,320,128]{2,1,0:T(8,128)(2,1)}, u32[]{:S(2)}, u32[]{:S(2)}) collective-permute-start(bf16[4,320,128]{2,1,0:T(8,128)(2,1)} %get-tuple-element.26), channel_id=1, source_target_pairs={{32,0},{48,16},{64,32},{80,48},{96,64},{112,80},{128,96},{144,112}... | collective-permute-start | bytes 983048 | tf_op jit(solution)/shard_map/ppermute | solution.py:35
  29.6 1.3 %collective-permute-start.3 = (bf16[4,320,128]{2,1,0:T(8,128)(2,1)}, bf16[4,320,128]{2,1,0:T(8,128)(2,1)}, u32[]{:S(2)}, u32[]{:S(2)}) collective-permute-start(bf16[4,320,128]{2,1,0:T(8,128)(2,1)} %get-tuple-element.27), channel_id=1, source_target_pairs={{16,0},{32,16},{48,32},{64,48},{80,64},{96,80},{112,96},{128,112},... | collective-permute-start | bytes 983048 | tf_op jit(solution)/shard_map/ppermute | solution.py:35
  30.9 4.7 %collective-permute-start.4 = (bf16[4,320,128]{2,1,0:T(8,128)(2,1)}, bf16[4,320,128]{2,1,0:T(8,128)(2,1)}, u32[]{:S(2)}, u32[]{:S(2)}) collective-permute-start(bf16[4,320,128]{2,1,0:T(8,128)(2,1)} %get-tuple-element.29), channel_id=1, source_target_pairs={{0,16},{16,32},{32,48},{48,64},{64,80},{80,96},{96,112},{112,128},... | collective-permute-start | bytes 983048 | tf_op jit(solution)/shard_map/ppermute | solution.py:35
  35.6 5.9 %collective-permute-start.5 = (bf16[4,320,128]{2,1,0:T(8,128)(2,1)}, bf16[4,320,128]{2,1,0:T(8,128)(2,1)}, u32[]{:S(2)}, u32[]{:S(2)}) collective-permute-start(bf16[4,320,128]{2,1,0:T(8,128)(2,1)} %get-tuple-element.30), channel_id=1, source_target_pairs={{0,32},{16,48},{32,64},{48,80},{64,96},{80,112},{96,128},{112,144}... | collective-permute-start | bytes 983048 | tf_op jit(solution)/shard_map/ppermute | solution.py:35
  41.5 0.8 slice_convert_fusion.3
  43.8 1.0 %reshape.264 = bf16[32,2,320]{2,1,0:T(2,128)(2,1)} reshape(bf16[32,4,8,20]{3,2,1,0:T(8,128)(2,1)S(1)} %bitcast.70) | data formatting | bytes 81920
  44.8 12.8 %all-to-all-start = ((bf16[32,2,320]{2,1,0:T(2,128)(2,1)}), bf16[32,2,320]{2,1,0:T(2,128)(2,1)S(1)}, u32[]{:S(2)}, u32[]{:S(2)}) async-start(bf16[32,2,320]{2,1,0:T(2,128)(2,1)} %reshape.264), calls=%async_computation | async-start | bytes 98304 | tf_op jit(solution)/shard_map/all_to_all | solution.py:199
  58.3 11.1 %all-to-all-done = bf16[32,2,320]{2,1,0:T(2,128)(2,1)S(1)} async-done(((bf16[32,2,320]{2,1,0:T(2,128)(2,1)}), bf16[32,2,320]{2,1,0:T(2,128)(2,1)S(1)}, u32[]{:S(2)}, u32[]{:S(2)}) %all-to-all-start) | async-done | bytes 40992 | tf_op jit(solution)/shard_map/all_to_all | solution.py:199
  71.0 1.7 %fusion.22 = bf16[2,8,21,128]{3,2,1,0:T(8,128)(2,1)S(1)} fusion(f32[2,8,1,21,640]{4,3,1,0,2:T(8,128)S(1)} %get-tuple-element.58, f32[2,8,1,21,640]{4,3,1,0,2:T(8,128)S(1)} %get-tuple-element.57, f32[640,128]{1,0:T(8,128)S(1)} %get-tuple-element.71, f32[640,128]{1,0:T(8,128)S(1)} %get-tuple-element.70), kind=kOutput, calls=%fused_computation.32 | convolution fusion | flops 661239808 | bytes 2461696 | tf_op jit(solution)/shard_map/wklom,mi->wkloi/dot_general | solution.py:57
  72.8 1.0 %bitcast_dynamic-update-slice_fusion.4 = bf16[5,4,320,128]{3,2,1,0:T(8,128)(2,1)S(1)} fusion(bf16[4,320,128]{2,1,0:T(8,128)(2,1)} %collective-permute-done.2), kind=kLoop, calls=%fused_computation.49 | loop fusion | bytes 655360
  73.9 1.0 %bitcast_dynamic-update-slice_fusion.3 = bf16[5,4,320,128]{3,2,1,0:T(8,128)(2,1)S(1)} fusion(bf16[5,4,320,128]{3,2,1,0:T(8,128)(2,1)S(1)} %bitcast_dynamic-update-slice_fusion.4, bf16[4,320,128]{2,1,0:T(8,128)(2,1)} %collective-permute-done.3), kind=kLoop, calls=%fused_computation.48 | loop fusion | bytes 655360
  75.0 1.0 %bitcast_dynamic-update-slice_fusion.1 = bf16[5,4,320,128]{3,2,1,0:T(8,128)(2,1)S(1)} fusion(bf16[5,4,320,128]{3,2,1,0:T(8,128)(2,1)S(1)} %bitcast_dynamic-update-slice_fusion.2, bf16[4,320,128]{2,1,0:T(8,128)(2,1)} %collective-permute-done.4), kind=kLoop, calls=%fused_computation.46 | loop fusion | bytes 655360
  76.0 1.0 %bitcast_dynamic-update-slice_fusion = bf16[5,4,320,128]{3,2,1,0:T(8,128)(2,1)S(1)} fusion(bf16[5,4,320,128]{3,2,1,0:T(8,128)(2,1)S(1)} %bitcast_dynamic-update-slice_fusion.1, bf16[4,320,128]{2,1,0:T(8,128)(2,1)} %collective-permute-done.5), kind=kLoop, calls=%fused_computation.45 | loop fusion | bytes 655360 | tf_op jit(solution)/shard_map/stack | solution.py:201
  77.1 6.5 %gather_fusion = bf16[84,320,128]{2,1,0:T(8,128)(2,1)} fusion(bf16[20,320,128]{2,1,0:T(8,128)(2,1)S(1)} %bitcast.67, s32[1024]{0:T(1024)S(1)} %pad_clamp_fusion), kind=kCustom, calls=%fused_computation | custom fusion | bytes 13762896 | tf_op jit(solution)/shard_map/jit(_take)/gather | solution.py:203
  83.6 6.3 %fusion.19 = bf16[320,21,128]{2,0,1:T(8,128)(2,1)S(1)} fusion(f32[21,4,128]{2,1,0:T(4,128)S(1)} %bitcast.74, s32[21,4,128]{2,1,0:T(4,128)S(1)} %copy-done.12, f32[21,4,128]{2,1,0:T(4,128)S(1)} %bitcast.75, s32[21,4,128]{2,1,0:T(4,128)S(1)} %copy-done.13, f32[21,4,128]{2,1,0:T(4,128)S(1)} %bitcast.76, s32[21,4,128]{2,1,0:T(4,128)S(1)} %copy-done.11, ...), kind=kOutput, calls=%fused_computation.29 | convolution fusion | flops 901619712 | bytes 8945748 | tf_op jit(solution)/shard_map/jifq,jiqp->jfp/dot_general | solution.py:204
  90.0 1.1 %copy.72 = bf16[320,21,128]{2,1,0:T(8,128)(2,1)S(1)} copy(bf16[320,21,128]{2,0,1:T(8,128)(2,1)S(1)} %fusion.19) | data formatting | bytes 3440640 | tf_op jit(solution)/shard_map/convert_element_type | solution.py:205
  91.1 2.0 %reshape_reshape.3 = bf16[40,8,1,2688]{3,1,0,2:T(8,128)(2,1)} reshape(bf16[320,21,128]{2,1,0:T(8,128)(2,1)S(1)} %copy.72) | data formatting | bytes 3440640 | tf_op jit(solution)/shard_map/reshape;reshape | solution.py:206
  93.1 1.7 %convert_reduce_fusion = f32[8,2688]{1,0:T(8,128)S(1)} fusion(bf16[40,8,1,2688]{3,1,0,2:T(8,128)(2,1)} %reshape_reshape.3), kind=kLoop, calls=%fused_computation.10 | loop fusion | flops 1698816 | bytes 1806336 | tf_op jit(solution)/shard_map/reduce_sum | solution.py:207
  (73 shorter events, 5.7 us)
Async XLA Ops:
  0.6 41.7 %copy-start = (bf16[20,32,640]{2,1,0:T(8,128)(2,1)S(1)}, bf16[20,32,640]{2,1,0:T(8,128)(2,1)}, u32[]{:S(2)}) copy-start(bf16[20,32,640]{2,1,0:T(8,128)(2,1)} %param.12) | copy-start | bytes 2457604
  0.6 20.0 %copy-start.1 = (bf16[40,8,1,2688]{3,1,2,0:T(8,128)(2,1)S(1)}, bf16[40,8,1,2688]{3,1,2,0:T(8,128)(2,1)}, u32[]{:S(2)}) copy-start(bf16[40,8,1,2688]{3,1,2,0:T(8,128)(2,1)} %param.14) | copy-start | bytes 5160964
  0.7 16.4 %copy-start.18 = (s32[640]{0:T(1024)S(1)}, s32[640]{0:T(1024)}, u32[]{:S(2)}) copy-start(s32[640]{0:T(1024)} %param.13) | copy-start | bytes 7684
  0.7 15.3 %copy-start.8 = (bf16[3,8,1,2688]{3,1,2,0:T(8,128)(2,1)S(1)}, bf16[3,8,1,2688]{3,1,2,0:T(8,128)(2,1)}, u32[]{:S(2)}) copy-start(bf16[3,8,1,2688]{3,1,2,0:T(8,128)(2,1)} %param.15) | copy-start | bytes 387076
  0.7 15.4 %copy-start.19 = (s32[1,5,4]{1,2,0:T(4,128)S(1)}, s32[1,5,4]{1,2,0:T(4,128)}, u32[]{:S(2)}) copy-start(s32[1,5,4]{1,2,0:T(4,128)} %param.16) | copy-start | bytes 244
  4.2 13.9 %collective-permute-start = (bf16[40,1,1,2688]{3,0,2,1:T(8,128)(2,1)}, bf16[40,1,1,2688]{3,0,2,1:T(8,128)(2,1)}, u32[]{:S(2)}, u32[]{:S(2)}) collective-permute-start(bf16[40,1,1,2688]{3,0,2,1:T(8,128)(2,1)} %copy.80), channel_id=1, source_target_pairs={{0,1},{1,2},{2,3},{3,4},{4,5},{5,6},{6,7},{7,8},{8,9},{9,10},{10,1... | collective-permute-start | bytes 645128 | tf_op jit(solution)/shard_map/ppermute | solution.py:23
  9.9 9.5 %collective-permute-start.1 = (bf16[40,1,1,2688]{3,0,2,1:T(8,128)(2,1)}, bf16[40,1,1,2688]{3,0,2,1:T(8,128)(2,1)}, u32[]{:S(2)}, u32[]{:S(2)}) collective-permute-start(bf16[40,1,1,2688]{3,0,2,1:T(8,128)(2,1)} %copy.81), channel_id=1, source_target_pairs={{1,0},{2,1},{3,2},{4,3},{5,4},{6,5},{7,6},{8,7},{9,8},{10,9},{11,1... | collective-permute-start | bytes 645128 | tf_op jit(solution)/shard_map/ppermute | solution.py:25
  23.7 17.8 %copy-start.4 = (bf16[21,4,4,128]{3,2,1,0:T(4,128)(2,1)S(1)}, bf16[21,4,4,128]{3,2,1,0:T(4,128)(2,1)}, u32[]{:S(2)}) copy-start(bf16[21,4,4,128]{3,2,1,0:T(4,128)(2,1)} %param.19) | copy-start | bytes 258052
  23.7 18.6 %copy-start.2 = (bf16[4,8,20,640]{3,1,2,0:T(8,128)(2,1)S(1)}, bf16[4,8,20,640]{3,1,2,0:T(8,128)(2,1)}, u32[]{:S(2)}) copy-start(bf16[4,8,20,640]{3,1,2,0:T(8,128)(2,1)} %param.10) | copy-start | bytes 2457604
  23.7 19.0 %copy-start.3 = (bf16[20,32,640]{2,1,0:T(8,128)(2,1)S(1)}, bf16[20,32,640]{2,1,0:T(8,128)(2,1)}, u32[]{:S(2)}) copy-start(bf16[20,32,640]{2,1,0:T(8,128)(2,1)} %param.11) | copy-start | bytes 2457604
  28.2 29.4 %copy-start.9 = (s32[21,4,128]{2,1,0:T(4,128)S(1)}, s32[21,4,128]{2,1,0:T(4,128)}, u32[]{:S(2)}) copy-start(s32[21,4,128]{2,1,0:T(4,128)} %param.18) | copy-start | bytes 129028
  28.2 44.6 %collective-permute-start.2 = (bf16[4,320,128]{2,1,0:T(8,128)(2,1)}, bf16[4,320,128]{2,1,0:T(8,128)(2,1)}, u32[]{:S(2)}, u32[]{:S(2)}) collective-permute-start(bf16[4,320,128]{2,1,0:T(8,128)(2,1)} %get-tuple-element.26), channel_id=1, source_target_pairs={{32,0},{48,16},{64,32},{80,48},{96,64},{112,80},{128,96},{144,112}... | collective-permute-start | bytes 983048 | tf_op jit(solution)/shard_map/ppermute | solution.py:35
  29.6 44.3 %collective-permute-start.3 = (bf16[4,320,128]{2,1,0:T(8,128)(2,1)}, bf16[4,320,128]{2,1,0:T(8,128)(2,1)}, u32[]{:S(2)}, u32[]{:S(2)}) collective-permute-start(bf16[4,320,128]{2,1,0:T(8,128)(2,1)} %get-tuple-element.27), channel_id=1, source_target_pairs={{16,0},{32,16},{48,32},{64,48},{80,64},{96,80},{112,96},{128,112},... | collective-permute-start | bytes 983048 | tf_op jit(solution)/shard_map/ppermute | solution.py:35
  30.9 44.0 %collective-permute-start.4 = (bf16[4,320,128]{2,1,0:T(8,128)(2,1)}, bf16[4,320,128]{2,1,0:T(8,128)(2,1)}, u32[]{:S(2)}, u32[]{:S(2)}) collective-permute-start(bf16[4,320,128]{2,1,0:T(8,128)(2,1)} %get-tuple-element.29), channel_id=1, source_target_pairs={{0,16},{16,32},{32,48},{48,64},{64,80},{80,96},{96,112},{112,128},... | collective-permute-start | bytes 983048 | tf_op jit(solution)/shard_map/ppermute | solution.py:35
  35.6 40.4 %collective-permute-start.5 = (bf16[4,320,128]{2,1,0:T(8,128)(2,1)}, bf16[4,320,128]{2,1,0:T(8,128)(2,1)}, u32[]{:S(2)}, u32[]{:S(2)}) collective-permute-start(bf16[4,320,128]{2,1,0:T(8,128)(2,1)} %get-tuple-element.30), channel_id=1, source_target_pairs={{0,32},{16,48},{32,64},{48,80},{64,96},{80,112},{96,128},{112,144}... | collective-permute-start | bytes 983048 | tf_op jit(solution)/shard_map/ppermute | solution.py:35
  43.1 27.7 %copy-start.7 = (f32[21,640]{1,0:T(8,128)S(1)}, f32[21,640]{1,0:T(8,128)}, u32[]{:S(2)}) copy-start(f32[21,640]{1,0:T(8,128)} %get-tuple-element.69) | copy-start | bytes 161284
  44.8 24.6 %all-to-all-start = ((bf16[32,2,320]{2,1,0:T(2,128)(2,1)}), bf16[32,2,320]{2,1,0:T(2,128)(2,1)S(1)}, u32[]{:S(2)}, u32[]{:S(2)}) async-start(bf16[32,2,320]{2,1,0:T(2,128)(2,1)} %reshape.264), calls=%async_computation | async-start | bytes 98304 | tf_op jit(solution)/shard_map/all_to_all | solution.py:199
  70.5 4.4 %copy-start.6 = (bf16[4,320,128]{2,1,0:T(8,128)(2,1)S(1)}, bf16[4,320,128]{2,1,0:T(8,128)(2,1)}, u32[]{:S(2)}) copy-start(bf16[4,320,128]{2,1,0:T(8,128)(2,1)} %get-tuple-element.28) | copy-start | bytes 983044
  72.8 22.0 %copy-start.5 = (bf16[2,8,1,2688]{3,1,0,2:T(8,128)(2,1)}, bf16[2,8,1,2688]{3,1,0,2:T(8,128)(2,1)S(1)}, u32[]{:S(2)}) copy-start(bf16[2,8,1,2688]{3,1,0,2:T(8,128)(2,1)S(1)} %convert_element_type.124) | copy-start | bytes 258052
  77.0 6.6 %copy-start.10 = (s32[21,4,128]{2,1,0:T(4,128)S(1)}, s32[21,4,128]{2,1,0:T(4,128)}, u32[]{:S(2)}) copy-start(s32[21,4,128]{2,1,0:T(4,128)} %param.18) | copy-start | bytes 129028
  77.0 6.5 %copy-start.11 = (s32[21,4,128]{2,1,0:T(4,128)S(1)}, s32[21,4,128]{2,1,0:T(4,128)}, u32[]{:S(2)}) copy-start(s32[21,4,128]{2,1,0:T(4,128)} %get-tuple-element.65) | copy-start | bytes 129028
  77.0 6.5 %copy-start.12 = (s32[21,4,128]{2,1,0:T(4,128)S(1)}, s32[21,4,128]{2,1,0:T(4,128)}, u32[]{:S(2)}) copy-start(s32[21,4,128]{2,1,0:T(4,128)} %get-tuple-element.66) | copy-start | bytes 129028
  77.0 6.5 %copy-start.13 = (s32[21,4,128]{2,1,0:T(4,128)S(1)}, s32[21,4,128]{2,1,0:T(4,128)}, u32[]{:S(2)}) copy-start(s32[21,4,128]{2,1,0:T(4,128)} %get-tuple-element.67) | copy-start | bytes 129028
  77.1 6.5 %copy-start.14 = (f32[21,4,1,128]{3,2,1,0:T(1,128)S(1)}, f32[21,4,1,128]{3,2,1,0:T(1,128)}, u32[]{:S(2)}) copy-start(f32[21,4,1,128]{3,2,1,0:T(1,128)} %get-tuple-element.59) | copy-start | bytes 129028
  77.1 6.5 %copy-start.15 = (f32[21,4,1,128]{3,2,1,0:T(1,128)S(1)}, f32[21,4,1,128]{3,2,1,0:T(1,128)}, u32[]{:S(2)}) copy-start(f32[21,4,1,128]{3,2,1,0:T(1,128)} %get-tuple-element.60) | copy-start | bytes 129028
  77.1 6.5 %copy-start.16 = (f32[21,4,1,128]{3,2,1,0:T(1,128)S(1)}, f32[21,4,1,128]{3,2,1,0:T(1,128)}, u32[]{:S(2)}) copy-start(f32[21,4,1,128]{3,2,1,0:T(1,128)} %get-tuple-element.61) | copy-start | bytes 129028
  77.1 6.5 %copy-start.17 = (f32[21,4,1,128]{3,2,1,0:T(1,128)S(1)}, f32[21,4,1,128]{3,2,1,0:T(1,128)}, u32[]{:S(2)}) copy-start(f32[21,4,1,128]{3,2,1,0:T(1,128)} %get-tuple-element.62) | copy-start | bytes 129028

commit v6 on v5

--- a/solution.py
+++ b/solution.py
@@ -97,6 +97,7 @@
     block_count, rows_per_block = stencil.shape[0], stencil.shape[1]
     count = len(pieces)
     cap, rows, _ = pieces[0].shape
+    group = 3 if block_count % 3 == 0 else 1
 
     def body(slot_ref, stencil_ref, *refs):
         piece_refs = refs[:count]
@@ -112,23 +113,26 @@
             for copy in copies:
                 copy.wait()
 
-        total = None
-        for row in range(rows_per_block):
-            slot = jnp.clip(slot_ref[block * rows_per_block + row], 0, count * cap - 1)
-            term = jnp.dot(pool_ref[slot], stencil_ref[0, row], preferred_element_type=jnp.float32)
-            total = term if total is None else total + term
-        result = total.astype(out_ref.dtype)
-        out_ref[...] = result
-        summed = result.astype(jnp.float32).reshape(bin_count, level_count, BLK).sum(axis=0)
-        mean_ref[...] = summed / bin_count
+        for member in range(group):
+            total = None
+            for row in range(rows_per_block):
+                flat = (block * group + member) * rows_per_block + row
+                slot = jnp.clip(slot_ref[flat], 0, count * cap - 1)
+                term = jnp.dot(pool_ref[slot], stencil_ref[member, row],
+                               preferred_element_type=jnp.float32)
+                total = term if total is None else total + term
+            result = total.astype(out_ref.dtype)
+            out_ref[:, member * BLK:(member + 1) * BLK] = result
+            summed = result.astype(jnp.float32).reshape(bin_count, level_count, BLK).sum(axis=0)
+            mean_ref[:, member * BLK:(member + 1) * BLK] = summed / bin_count
 
     grid_spec = pltpu.PrefetchScalarGridSpec(
         num_scalar_prefetch=1,
-        grid=(block_count,),
-        in_specs=[pl.BlockSpec((1, rows_per_block, BLK, BLK), lambda b, table: (b, 0, 0, 0))]
+        grid=(block_count // group,),
+        in_specs=[pl.BlockSpec((group, rows_per_block, BLK, BLK), lambda b, table: (b, 0, 0, 0))]
         + [pl.BlockSpec(memory_space=pl.ANY) for _ in range(count)],
-        out_specs=[pl.BlockSpec((rows, BLK), lambda b, table: (0, b)),
-                   pl.BlockSpec((level_count, BLK), lambda b, table: (0, b))],
+        out_specs=[pl.BlockSpec((rows, group * BLK), lambda b, table: (0, b)),
+                   pl.BlockSpec((level_count, group * BLK), lambda b, table: (0, b))],
         scratch_shapes=[pltpu.VMEM((count * cap, rows, BLK), pieces[0].dtype),
                         pltpu.SemaphoreType.DMA((count,))],
     )
@@ -198,13 +202,9 @@
     ).astype(jnp.bfloat16)
     received = lax.all_to_all(coefficients, "band", split_axis=2, concat_axis=3, tiled=True)
     wind_grid = synthesis(received, wave_numbers, NLON).astype(jnp.bfloat16)
-    pooled = jnp.stack(pieces)
-    flattened = pooled.reshape(offsets * cap, rows, BLK)
-    chosen = jnp.take(flattened, depart_slot, axis=0)
-    block_rows = jnp.einsum("jifq,jiqp->jfp", chosen, stencil, preferred_element_type=jnp.float32)
-    flat_new = block_rows.astype(jnp.bfloat16).transpose(1, 0, 2).reshape(rows, block_total * BLK)
+    flat_new, average = apply_stencil(depart_slot.reshape(-1), stencil, pieces, bin_count, level_count)
     aerosol_new = flat_new.reshape(bin_count, level_count, lat_count, lon_count)
-    average = jnp.mean(aerosol_new.astype(jnp.float32), axis=0)
+    average = average.reshape(level_count, lat_count, lon_count)
     aerosol_flux = (wind_grid.astype(jnp.float32) * average[None]).astype(jnp.bfloat16)
     return (wind_grid, aerosol_new, aerosol_flux)
 

time: 96.7 us -> 83 us (0.86)
  local copies, waits for them, and re-layouts: 24.5 us -> 11.8 us
  Pallas kernels: 4.45 us -> 13.3 us
  matrix products: 8.8 us -> 2.47 us
  waiting for transfers between devices: 11.1 us -> 6.59 us
  other arithmetic: 12.5 us -> 14 us
    pallas_call x0 -> x1, Pallas kernels: none -> 8.8 us  [apply_stencil(): pl.pallas_call(body, grid_spec=grid_spec, out_shape=out_shape, compiler_p...]
    gather x1 -> x0, local copies, waits for them, and re-layouts: 6.47 us -> none  [shards(): chosen = jnp.take(flattened, depart_slot, axis=0)]
    dot_general x1 -> x0, matrix products: 6.33 us -> none  [shards(): jnp.einsum('jifq,jiqp->jfp', chosen, stencil, preferred_element_type=jnp....]
    all_to_all x1, waiting for transfers between devices: 11.1 us -> 5.02 us  [shards(): lax.all_to_all(coefficients, 'band', split_axis=2, concat_axis=3, tiled=T...]
    convert_element_type x0 -> x1, other arithmetic: none -> 5.09 us  [shards(): stencil = stencil_matrix(depart_offset, depart_weight).astype(jnp.bfloat16)]
    another operation x2 -> x0, local copies, waits for them, and re-layouts: 2.98 us -> none  [the longest x1 1.97 us: shards(): aerosol_new = flat_new.reshape(bin_count, level_count, lat_count, lon_count)]
    unnamed x48 -> x31, local copies, waits for them, and re-layouts: 5.96 us -> 3.58 us
    reduce_sum x1 -> x0, other arithmetic: 1.71 us -> none  [shards(): average = jnp.mean(aerosol_new.astype(jnp.float32), axis=0)]
  transfers between devices with their start and end apart: 7 -> 7, of which waited for: 1 -> 2; matrix products, arithmetic and copies ran while one was open for 19% -> 20% of each run, Pallas kernels for 0% -> 0%
where the time goes in v6:
time: 83 us; the launch traced here: 82.2 us
  starting transfers between devices  33.1 us (40%)
  other arithmetic  14 us (17%)
  Pallas kernels  13.3 us (16%)
  local copies, waits for them, and re-layouts  11.8 us (14%)
  waiting for transfers between devices  6.59 us (8%)
  matrix products  2.47 us (3%)
  between operations  0.98 us (1%)
    ppermute x4, starting transfers between devices, shifted(): lax.ppermute(value, axis, [(source, source + steps) for source in range(l...  13.2 us
    all_to_all x1, starting transfers between devices, shards(): lax.all_to_all(coefficients, 'band', split_axis=2, concat_axis=3, tiled=T...  13 us
    pallas_call x1, Pallas kernels, apply_stencil(): pl.pallas_call(body, grid_spec=grid_spec, out_shape=out_shape, compiler_p...  8.8 us
    convert_element_type x1, other arithmetic, shards(): stencil = stencil_matrix(depart_offset, depart_weight).astype(jnp.bfloat16)  5.09 us
    all_to_all x1, waiting for transfers between devices, shards(): lax.all_to_all(coefficients, 'band', split_axis=2, concat_axis=3, tiled=T...  5.02 us
    ppermute x1, starting transfers between devices, extended(): lax.ppermute(tail, axis, [(i, (i + 1) % count) for i in range(ends)])  4.96 us
    pallas_call x1, Pallas kernels, pack_blocks(): pl.pallas_call(body, grid_spec=grid_spec, out_shape=out_shape)  4.47 us
    unnamed x31, local copies, waits for them, and re-layouts  3.58 us
  transfers between devices with their start and end apart: 7, of which 2 were waited for; matrix products, arithmetic and copies ran while one was open for 20% of the time, Pallas kernels for 0%

profile of v6, /device:TPU:25, one launch (start us, length us, event | category | flops | bytes accessed | tf_op | source)
XLA Modules:
  0.0 82.2 jit_solution(15459299160020173100)
XLA Ops:
  0.7 2.8 %fusion.33 = (bf16[40,1,1,2688]{3,1,2,0:T(2,128)(2,1)S(1)}, bf16[40,1,1,2688]{3,1,2,0:T(2,128)(2,1)S(1)}) fusion(bf16[40,8,1,2688]{3,1,2,0:T(8,128)(2,1)} %param.14), kind=kLoop, calls=%fused_computation.77 | loop fusion | bytes 860160 | tf_op jit(solution)/shard_map/slice | solution.py:20
  3.5 0.7 copy.71
  4.2 5.0 %collective-permute-start = (bf16[40,1,1,2688]{3,0,2,1:T(8,128)(2,1)}, bf16[40,1,1,2688]{3,0,2,1:T(8,128)(2,1)}, u32[]{:S(2)}, u32[]{:S(2)}) collective-permute-start(bf16[40,1,1,2688]{3,0,2,1:T(8,128)(2,1)} %copy.71), channel_id=1, source_target_pairs={{0,1},{1,2},{2,3},{3,4},{4,5},{5,6},{6,7},{7,8},{8,9},{9,10},{10,1... | collective-permute-start | bytes 645128 | tf_op jit(solution)/shard_map/ppermute | solution.py:23
  9.2 0.7 copy.72
  9.9 1.9 %collective-permute-start.1 = (bf16[40,1,1,2688]{3,0,2,1:T(8,128)(2,1)}, bf16[40,1,1,2688]{3,0,2,1:T(8,128)(2,1)}, u32[]{:S(2)}, u32[]{:S(2)}) collective-permute-start(bf16[40,1,1,2688]{3,0,2,1:T(8,128)(2,1)} %copy.72), channel_id=1, source_target_pairs={{1,0},{2,1},{3,2},{4,3},{5,4},{6,5},{7,6},{8,7},{9,8},{10,9},{11,1... | collective-permute-start | bytes 645128 | tf_op jit(solution)/shard_map/ppermute | solution.py:25
  11.8 1.4 %fusion.16 = (f32[640,128]{1,0:T(8,128)S(1)}, f32[640,128]{1,0:T(8,128)S(1)}) fusion(s32[640]{0:T(1024)S(1)} %copy-done.10), kind=kLoop, calls=%fused_computation.32 | loop fusion | flops 737280 | bytes 657920 | tf_op jit(solution)/shard_map/cos | solution.py:56
  13.4 0.6 min.12.listed_ref
  14.1 0.6 reshape.224.slot_ref
  14.8 1.0 %cosine_multiply_fusion = (f32[21,640]{1,0:T(8,128)S(1)}, f32[21,640]{1,0:T(8,128)}) fusion(s32[21]{0:T(128)S(1)} %iota_multiply_fusion, s32[640]{0:T(1024)S(1)} %copy-done.10, f32[640]{0:T(1024)S(1)} %compare_select_fusion), kind=kLoop, calls=%fused_computation.58 | loop fusion | flops 147840 | bytes 112724 | tf_op jit(solution)/shard_map/mul | solution.py:48
  15.8 1.3 %copy.56 = bf16[40,1,1,2688]{3,1,2,0:T(2,128)(2,1)S(1)} copy(bf16[40,1,1,2688]{3,0,2,1:T(8,128)(2,1)} %collective-permute-done) | data formatting | bytes 430080 | tf_op jit(solution)/shard_map/ppermute | solution.py:23
  17.0 1.6 %collective-permute-done.1 = bf16[40,1,1,2688]{3,0,2,1:T(8,128)(2,1)} collective-permute-done((bf16[40,1,1,2688]{3,0,2,1:T(8,128)(2,1)}, bf16[40,1,1,2688]{3,0,2,1:T(8,128)(2,1)}, u32[]{:S(2)}, u32[]{:S(2)}) %collective-permute-start.1) | collective-permute-done | bytes 215072 | tf_op jit(solution)/shard_map/ppermute | solution.py:25
  18.6 1.3 %copy.58 = bf16[40,1,1,2688]{3,1,2,0:T(2,128)(2,1)S(1)} copy(bf16[40,1,1,2688]{3,0,2,1:T(8,128)(2,1)} %collective-permute-done.1) | data formatting | bytes 430080 | tf_op jit(solution)/shard_map/ppermute | solution.py:25
  19.9 3.0 %fusion.3.refs_0_.refs_1_.refs_2_.refs_3_.refs_4_ = bf16[320,2688]{1,0:T(8,128)(2,1)} fusion(bf16[40,8,1,2688]{3,1,2,0:T(8,128)(2,1)S(1)} %copy-done.1, bf16[40,1,1,2688]{3,1,2,0:T(2,128)(2,1)S(1)} %copy.58, bf16[40,1,1,2688]{3,1,2,0:T(2,128)(2,1)S(1)} %copy.56, f32[8,2688]{1,0:T(8,128)S(1)} %get-tuple-element.59, f32[8,2688]{1,0:T(8,128)S(1)} %get-tuple-element.60, ...), kind=kLoop, calls=%fused_computation.10 | loop fusion | flops 12902400 | bytes 4128768 | tf_op jit(solution)/shard_map/reshape | solution.py:166
  22.9 4.5 %shard_map.121 = (bf16[4,320,128]{2,1,0:T(8,128)(2,1)}, bf16[4,320,128]{2,1,0:T(8,128)(2,1)}, bf16[4,320,128]{2,1,0:T(8,128)(2,1)}, bf16[4,320,128]{2,1,0:T(8,128)(2,1)}, bf16[4,320,128]{2,1,0:T(8,128)(2,1)}) custom-call(s32[20]{0:T(128)} %min.12.listed_ref, bf16[320,2688]{1,0:T(8,128)(2,1)} %fusion.3.refs_0_.refs_1_.refs_2_.refs_3_.refs_4_, ...), custom_call_target="tpu_custom_call" | custom-call | tf_op jit(solution)/shard_map/pallas_call | solution.py:92
  27.4 0.8 slice_convert_fusion.3
  28.1 0.7 broadcast_add_fusion.2
  28.8 1.3 %collective-permute-start.2 = (bf16[4,320,128]{2,1,0:T(8,128)(2,1)}, bf16[4,320,128]{2,1,0:T(8,128)(2,1)S(1)}, u32[]{:S(2)}, u32[]{:S(2)}) collective-permute-start(bf16[4,320,128]{2,1,0:T(8,128)(2,1)} %get-tuple-element.30), channel_id=1, source_target_pairs={{32,0},{48,16},{64,32},{80,48},{96,64},{112,80},{128,96},{144,112}... | collective-permute-start | bytes 983048 | tf_op jit(solution)/shard_map/ppermute | solution.py:35
  30.1 1.3 %collective-permute-start.3 = (bf16[4,320,128]{2,1,0:T(8,128)(2,1)}, bf16[4,320,128]{2,1,0:T(8,128)(2,1)}, u32[]{:S(2)}, u32[]{:S(2)}) collective-permute-start(bf16[4,320,128]{2,1,0:T(8,128)(2,1)} %get-tuple-element.31), channel_id=1, source_target_pairs={{16,0},{32,16},{48,32},{64,48},{80,64},{96,80},{112,96},{128,112},... | collective-permute-start | bytes 983048 | tf_op jit(solution)/shard_map/ppermute | solution.py:35
  31.4 4.7 %collective-permute-start.4 = (bf16[4,320,128]{2,1,0:T(8,128)(2,1)}, bf16[4,320,128]{2,1,0:T(8,128)(2,1)}, u32[]{:S(2)}, u32[]{:S(2)}) collective-permute-start(bf16[4,320,128]{2,1,0:T(8,128)(2,1)} %get-tuple-element.33), channel_id=1, source_target_pairs={{0,16},{16,32},{32,48},{48,64},{64,80},{80,96},{96,112},{112,128},... | collective-permute-start | bytes 983048 | tf_op jit(solution)/shard_map/ppermute | solution.py:35
  36.1 5.9 %collective-permute-start.5 = (bf16[4,320,128]{2,1,0:T(8,128)(2,1)}, bf16[4,320,128]{2,1,0:T(8,128)(2,1)}, u32[]{:S(2)}, u32[]{:S(2)}) collective-permute-start(bf16[4,320,128]{2,1,0:T(8,128)(2,1)} %get-tuple-element.34), channel_id=1, source_target_pairs={{0,32},{16,48},{32,64},{48,80},{64,96},{80,112},{96,128},{112,144}... | collective-permute-start | bytes 983048 | tf_op jit(solution)/shard_map/ppermute | solution.py:35
  42.1 0.4 convolution_bitcast_fusion.1
  42.5 0.4 convolution_bitcast_fusion
  43.0 0.5 copy.61
  43.6 1.0 %reshape.234 = bf16[32,2,320]{2,1,0:T(2,128)(2,1)} reshape(bf16[32,4,8,20]{3,2,1,0:T(8,128)(2,1)S(1)} %bitcast.50) | data formatting | bytes 81920
  44.5 13.0 %all-to-all-start = ((bf16[32,2,320]{2,1,0:T(2,128)(2,1)}), bf16[32,2,320]{2,1,0:T(2,128)(2,1)S(1)}, u32[]{:S(2)}, u32[]{:S(2)}) async-start(bf16[32,2,320]{2,1,0:T(2,128)(2,1)} %reshape.234), calls=%async_computation | async-start | bytes 98304 | tf_op jit(solution)/shard_map/all_to_all | solution.py:203
  57.5 5.1 %add_convert_fusion.stencil_ref = bf16[21,4,128,128]{3,2,1,0:T(8,128)(2,1)} fusion(f32[21,4,128]{2,1,0:T(4,128)} %bitcast.54, s32[21,4,128]{2,1,0:T(4,128)} %get-tuple-element.70, f32[21,4,128]{2,1,0:T(4,128)} %bitcast.55, s32[21,4,128]{2,1,0:T(4,128)} %get-tuple-element.71, f32[21,4,128]{2,1,0:T(4,128)} %bitcast.56, s32[21,4,128]{2,1,0:T(4,128)} %get-tuple-element.69, ...), kind=kLoop, calls=%fused_computation | loop fusion | flops 16515072 | bytes 3096576 | tf_op jit(solution)/shard_map/convert_element_type | solution.py:176
  62.6 5.0 %all-to-all-done = bf16[32,2,320]{2,1,0:T(2,128)(2,1)S(1)} async-done(((bf16[32,2,320]{2,1,0:T(2,128)(2,1)}), bf16[32,2,320]{2,1,0:T(2,128)(2,1)S(1)}, u32[]{:S(2)}, u32[]{:S(2)}) %all-to-all-start) | async-done | bytes 40992 | tf_op jit(solution)/shard_map/all_to_all | solution.py:203
  68.0 0.4 copy.62
  69.3 1.7 %fusion.4 = bf16[2,8,21,128]{3,2,1,0:T(8,128)(2,1)S(1)} fusion(f32[2,8,1,21,640]{4,3,1,0,2:T(8,128)S(1)} %get-tuple-element.62, f32[2,8,1,21,640]{4,3,1,0,2:T(8,128)S(1)} %get-tuple-element.61, f32[640,128]{1,0:T(8,128)S(1)} %get-tuple-element.75, f32[640,128]{1,0:T(8,128)S(1)} %get-tuple-element.74), kind=kOutput, calls=%fused_computation.15 | convolution fusion | flops 661239808 | bytes 2461696 | tf_op jit(solution)/shard_map/wklom,mi->wkloi/dot_general | solution.py:57
  71.1 0.7 copy-done.6
  71.8 8.8 %shard_map.122 = (bf16[320,2688]{1,0:T(8,128)(2,1)}, f32[8,2688]{1,0:T(8,128)}) custom-call(s32[84]{0:T(128)} %reshape.224.slot_ref, bf16[21,4,128,128]{3,2,1,0:T(8,128)(2,1)} %add_convert_fusion.stencil_ref, bf16[4,320,128]{2,1,0:T(8,128)(2,1)} %copy-done.6, bf16[4,320,128]{2,1,0:T(8,128)(2,1)} %collective-permute-done.3.refs_1_, ...), custom_call_target="tpu_custom_call" | custom-call | tf_op jit(solution)/shard_map/pallas_call | solution.py:141
  80.6 1.5 %fusion.18 = bf16[2,8,1,2688]{3,1,2,0:T(8,128)(2,1)} fusion(bf16[2,8,1,2688]{3,1,0,2:T(8,128)(2,1)S(1)} %convert_element_type.106, f32[8,2688]{1,0:T(8,128)} %get-tuple-element.36), kind=kLoop, calls=%fused_computation.37 | loop fusion | flops 129024 | bytes 258048
  (46 shorter events, 1.8 us)
Async XLA Ops:
  0.6 41.4 %copy-start = (bf16[20,32,640]{2,1,0:T(8,128)(2,1)S(1)}, bf16[20,32,640]{2,1,0:T(8,128)(2,1)}, u32[]{:S(2)}) copy-start(bf16[20,32,640]{2,1,0:T(8,128)(2,1)} %param.12) | copy-start | bytes 2457604
  0.6 19.2 %copy-start.1 = (bf16[40,8,1,2688]{3,1,2,0:T(8,128)(2,1)S(1)}, bf16[40,8,1,2688]{3,1,2,0:T(8,128)(2,1)}, u32[]{:S(2)}) copy-start(bf16[40,8,1,2688]{3,1,2,0:T(8,128)(2,1)} %param.14) | copy-start | bytes 5160964
  0.7 11.2 %copy-start.10 = (s32[640]{0:T(1024)S(1)}, s32[640]{0:T(1024)}, u32[]{:S(2)}) copy-start(s32[640]{0:T(1024)} %param.13) | copy-start | bytes 7684
  0.7 12.6 %copy-start.9 = (bf16[3,8,1,2688]{3,1,2,0:T(8,128)(2,1)S(1)}, bf16[3,8,1,2688]{3,1,2,0:T(8,128)(2,1)}, u32[]{:S(2)}) copy-start(bf16[3,8,1,2688]{3,1,2,0:T(8,128)(2,1)} %param.15) | copy-start | bytes 387076
  0.7 12.7 %copy-start.12 = (s32[1,5,4]{1,2,0:T(4,128)S(1)}, s32[1,5,4]{1,2,0:T(4,128)}, u32[]{:S(2)}) copy-start(s32[1,5,4]{1,2,0:T(4,128)} %param.16) | copy-start | bytes 244
  0.7 13.4 %copy-start.11 = (s32[21,4]{0,1:T(4,128)S(1)}, s32[21,4]{0,1:T(4,128)}, u32[]{:S(2)}) copy-start(s32[21,4]{0,1:T(4,128)} %param.17) | copy-start | bytes 1012
  4.2 11.6 %collective-permute-start = (bf16[40,1,1,2688]{3,0,2,1:T(8,128)(2,1)}, bf16[40,1,1,2688]{3,0,2,1:T(8,128)(2,1)}, u32[]{:S(2)}, u32[]{:S(2)}) collective-permute-start(bf16[40,1,1,2688]{3,0,2,1:T(8,128)(2,1)} %copy.71), channel_id=1, source_target_pairs={{0,1},{1,2},{2,3},{3,4},{4,5},{5,6},{6,7},{7,8},{8,9},{9,10},{10,1... | collective-permute-start | bytes 645128 | tf_op jit(solution)/shard_map/ppermute | solution.py:23
  9.9 8.7 %collective-permute-start.1 = (bf16[40,1,1,2688]{3,0,2,1:T(8,128)(2,1)}, bf16[40,1,1,2688]{3,0,2,1:T(8,128)(2,1)}, u32[]{:S(2)}, u32[]{:S(2)}) collective-permute-start(bf16[40,1,1,2688]{3,0,2,1:T(8,128)(2,1)} %copy.72), channel_id=1, source_target_pairs={{1,0},{2,1},{3,2},{4,3},{5,4},{6,5},{7,6},{8,7},{9,8},{10,9},{11,1... | collective-permute-start | bytes 645128 | tf_op jit(solution)/shard_map/ppermute | solution.py:25
  22.9 4.5 %copy-start.4 = (bf16[21,4,4,128]{3,2,1,0:T(4,128)(2,1)S(1)}, bf16[21,4,4,128]{3,2,1,0:T(4,128)(2,1)}, u32[]{:S(2)}) copy-start(bf16[21,4,4,128]{3,2,1,0:T(4,128)(2,1)} %param.19) | copy-start | bytes 258052
  22.9 5.3 %copy-start.8 = (s32[21,4,128]{2,1,0:T(4,128)S(1)}, s32[21,4,128]{2,1,0:T(4,128)}, u32[]{:S(2)}) copy-start(s32[21,4,128]{2,1,0:T(4,128)} %param.18) | copy-start | bytes 129028
  22.9 19.2 %copy-start.2 = (bf16[4,8,20,640]{3,1,2,0:T(8,128)(2,1)S(1)}, bf16[4,8,20,640]{3,1,2,0:T(8,128)(2,1)}, u32[]{:S(2)}) copy-start(bf16[4,8,20,640]{3,1,2,0:T(8,128)(2,1)} %param.10) | copy-start | bytes 2457604
  22.9 19.6 %copy-start.3 = (bf16[20,32,640]{2,1,0:T(8,128)(2,1)S(1)}, bf16[20,32,640]{2,1,0:T(8,128)(2,1)}, u32[]{:S(2)}) copy-start(bf16[20,32,640]{2,1,0:T(8,128)(2,1)} %param.11) | copy-start | bytes 2457604
  28.8 42.3 %collective-permute-start.2 = (bf16[4,320,128]{2,1,0:T(8,128)(2,1)}, bf16[4,320,128]{2,1,0:T(8,128)(2,1)S(1)}, u32[]{:S(2)}, u32[]{:S(2)}) collective-permute-start(bf16[4,320,128]{2,1,0:T(8,128)(2,1)} %get-tuple-element.30), channel_id=1, source_target_pairs={{32,0},{48,16},{64,32},{80,48},{96,64},{112,80},{128,96},{144,112}... | collective-permute-start | bytes 983048 | tf_op jit(solution)/shard_map/ppermute | solution.py:35
  30.1 41.0 %collective-permute-start.3 = (bf16[4,320,128]{2,1,0:T(8,128)(2,1)}, bf16[4,320,128]{2,1,0:T(8,128)(2,1)}, u32[]{:S(2)}, u32[]{:S(2)}) collective-permute-start(bf16[4,320,128]{2,1,0:T(8,128)(2,1)} %get-tuple-element.31), channel_id=1, source_target_pairs={{16,0},{32,16},{48,32},{64,48},{80,64},{96,80},{112,96},{128,112},... | collective-permute-start | bytes 983048 | tf_op jit(solution)/shard_map/ppermute | solution.py:35
  31.4 39.7 %collective-permute-start.4 = (bf16[4,320,128]{2,1,0:T(8,128)(2,1)}, bf16[4,320,128]{2,1,0:T(8,128)(2,1)}, u32[]{:S(2)}, u32[]{:S(2)}) collective-permute-start(bf16[4,320,128]{2,1,0:T(8,128)(2,1)} %get-tuple-element.33), channel_id=1, source_target_pairs={{0,16},{16,32},{32,48},{48,64},{64,80},{80,96},{96,112},{112,128},... | collective-permute-start | bytes 983048 | tf_op jit(solution)/shard_map/ppermute | solution.py:35
  36.1 35.0 %collective-permute-start.5 = (bf16[4,320,128]{2,1,0:T(8,128)(2,1)}, bf16[4,320,128]{2,1,0:T(8,128)(2,1)}, u32[]{:S(2)}, u32[]{:S(2)}) collective-permute-start(bf16[4,320,128]{2,1,0:T(8,128)(2,1)} %get-tuple-element.34), channel_id=1, source_target_pairs={{0,32},{16,48},{32,64},{48,80},{64,96},{80,112},{96,128},{112,144}... | collective-permute-start | bytes 983048 | tf_op jit(solution)/shard_map/ppermute | solution.py:35
  44.5 24.5 %copy-start.7 = (f32[21,640]{1,0:T(8,128)S(1)}, f32[21,640]{1,0:T(8,128)}, u32[]{:S(2)}) copy-start(f32[21,640]{1,0:T(8,128)} %get-tuple-element.73) | copy-start | bytes 161284
  44.5 23.1 %all-to-all-start = ((bf16[32,2,320]{2,1,0:T(2,128)(2,1)}), bf16[32,2,320]{2,1,0:T(2,128)(2,1)S(1)}, u32[]{:S(2)}, u32[]{:S(2)}) async-start(bf16[32,2,320]{2,1,0:T(2,128)(2,1)} %reshape.234), calls=%async_computation | async-start | bytes 98304 | tf_op jit(solution)/shard_map/all_to_all | solution.py:203
  71.1 11.1 %copy-start.5 = (bf16[2,8,1,2688]{3,1,0,2:T(8,128)(2,1)}, bf16[2,8,1,2688]{3,1,0,2:T(8,128)(2,1)S(1)}, u32[]{:S(2)}) copy-start(bf16[2,8,1,2688]{3,1,0,2:T(8,128)(2,1)S(1)} %convert_element_type.106) | copy-start | bytes 258052
  71.1 0.7 copy-start.6

commit v7 on v6

--- a/solution.py
+++ b/solution.py
@@ -97,7 +97,7 @@
     block_count, rows_per_block = stencil.shape[0], stencil.shape[1]
     count = len(pieces)
     cap, rows, _ = pieces[0].shape
-    group = 3 if block_count % 3 == 0 else 1
+    group = 7 if block_count % 7 == 0 else 1
 
     def body(slot_ref, stencil_ref, *refs):
         piece_refs = refs[:count]
@@ -157,31 +157,6 @@
     depart_weight,
 ):
     padded = extended(aerosol_old, (("lev", 1),), 1)
-    weights = vertical_weight.astype(jnp.float32)
-    vertical_sum = (
-        weights[0] * padded[:, :-2] + weights[1] * padded[:, 1:-1] + weights[2] * padded[:, 2:]
-    )
-    bin_count, level_count, lat_count, lon_count = aerosol_old.shape
-    rows = bin_count * level_count
-    remapped = vertical_sum.astype(jnp.bfloat16).reshape(rows, lat_count * lon_count)
-    block_total = lat_count * lon_count // BLK
-    listed = jnp.clip(send_blocks[0], 0, block_total - 1)
-    offsets, cap = listed.shape
-    outgoing = pack_blocks(listed.reshape(-1), remapped, offsets, cap)
-    outgoing, spectral, legendre_value, legendre_slope, depart_offset, depart_weight = (
-        lax.optimization_barrier(
-            (outgoing, spectral, legendre_value, legendre_slope, depart_offset, depart_weight)
-        )
-    )
-    stencil = stencil_matrix(depart_offset, depart_weight).astype(jnp.bfloat16)
-    reach_bands = offsets // 2
-    pieces = []
-    for offset_index in range(offsets):
-        shift_by = offset_index - reach_bands
-        if shift_by == 0:
-            pieces.append(outgoing[offset_index])
-        else:
-            pieces.append(shifted(outgoing[offset_index], "band", shift_by))
     band_here = lax.axis_index("band")
     wave_local = spectral.shape[2]
     own_waves = lax.dynamic_slice_in_dim(wave_numbers, band_here * wave_local, wave_local, 0)
@@ -201,6 +176,30 @@
         ]
     ).astype(jnp.bfloat16)
     received = lax.all_to_all(coefficients, "band", split_axis=2, concat_axis=3, tiled=True)
+    received, padded = lax.optimization_barrier((received, padded))
+    weights = vertical_weight.astype(jnp.float32)
+    vertical_sum = (
+        weights[0] * padded[:, :-2] + weights[1] * padded[:, 1:-1] + weights[2] * padded[:, 2:]
+    )
+    bin_count, level_count, lat_count, lon_count = aerosol_old.shape
+    rows = bin_count * level_count
+    remapped = vertical_sum.astype(jnp.bfloat16).reshape(rows, lat_count * lon_count)
+    block_total = lat_count * lon_count // BLK
+    listed = jnp.clip(send_blocks[0], 0, block_total - 1)
+    offsets, cap = listed.shape
+    outgoing = pack_blocks(listed.reshape(-1), remapped, offsets, cap)
+    outgoing, received, depart_offset, depart_weight = lax.optimization_barrier(
+        (outgoing, received, depart_offset, depart_weight)
+    )
+    stencil = stencil_matrix(depart_offset, depart_weight).astype(jnp.bfloat16)
+    reach_bands = offsets // 2
+    pieces = []
+    for offset_index in range(offsets):
+        shift_by = offset_index - reach_bands
+        if shift_by == 0:
+            pieces.append(outgoing[offset_index])
+        else:
+            pieces.append(shifted(outgoing[offset_index], "band", shift_by))
     wind_grid = synthesis(received, wave_numbers, NLON).astype(jnp.bfloat16)
     flat_new, average = apply_stencil(depart_slot.reshape(-1), stencil, pieces, bin_count, level_count)
     aerosol_new = flat_new.reshape(bin_count, level_count, lat_count, lon_count)

time: 83 us -> 88.4 us (1.065)
  the two profiles are of different devices: /device:TPU:25 before, /device:TPU:91 now
where the time goes in v7:
time: 88.4 us; the launch traced here: 87.6 us
  starting transfers between devices  33.8 us (38%)
  other arithmetic  13 us (15%)
  local copies, waits for them, and re-layouts  12.7 us (14%)
  Pallas kernels  11.4 us (13%)
  waiting for transfers between devices  10.6 us (12%)
  matrix products  5.05 us (6%)
  between operations  1.04 us (1%)
    ppermute x4, starting transfers between devices, shifted(): lax.ppermute(value, axis, [(source, source + steps) for source in range(l...  14.4 us
    all_to_all x1, starting transfers between devices, shards(): lax.all_to_all(coefficients, 'band', split_axis=2, concat_axis=3, tiled=T...  12 us
    ppermute x4, waiting for transfers between devices, shifted(): lax.ppermute(value, axis, [(source, source + steps) for source in range(l...  10.6 us
    pallas_call x1, Pallas kernels, apply_stencil(): pl.pallas_call(body, grid_spec=grid_spec, out_shape=out_shape, compiler_p...  7.05 us
    ppermute x1, starting transfers between devices, extended(): lax.ppermute(tail, axis, [(i, (i + 1) % count) for i in range(ends)])  5.53 us
    unnamed x35, local copies, waits for them, and re-layouts  4.82 us
    pallas_call x1, Pallas kernels, pack_blocks(): pl.pallas_call(body, grid_spec=grid_spec, out_shape=out_shape)  4.38 us
    convert_element_type x1, other arithmetic, shards(): stencil = stencil_matrix(depart_offset, depart_weight).astype(jnp.bfloat16)  4.03 us
  transfers between devices with their start and end apart: 7, of which 2 were waited for; matrix products, arithmetic and copies ran while one was open for 18% of the time, Pallas kernels for 0%

profile of v7, /device:TPU:91, one launch (start us, length us, event | category | flops | bytes accessed | tf_op | source)
XLA Modules:
  0.0 87.6 jit_solution(9441597556872711159)
XLA Ops:
  0.7 1.1 %copy-done = bf16[20,32,640]{2,1,0:T(8,128)(2,1)S(1)} copy-done((bf16[20,32,640]{2,1,0:T(8,128)(2,1)S(1)}, bf16[20,32,640]{2,1,0:T(8,128)(2,1)}, u32[]{:S(2)}) %copy-start) | copy-done | bytes 819224
  1.8 1.5 %convolution_bitcast_fusion = f32[4,8,32,20]{2,1,0,3:T(8,128)S(1)} fusion(bf16[20,32,640]{2,1,0:T(8,128)(2,1)S(1)} %copy-done, bf16[4,8,20,640]{3,1,2,0:T(8,128)(2,1)} %param.10), kind=kOutput, calls=%fused_computation.12 | convolution fusion | flops 26214400 | bytes 1720320 | tf_op jit(solution)/shard_map/slj,xksj->xkls/dot_general | solution.py:163
  3.3 1.8 %convolution_bitcast_fusion.1 = f32[4,8,32,20]{2,1,0,3:T(8,128)S(1)} fusion(bf16[20,32,640]{2,1,0:T(8,128)(2,1)} %param.12, bf16[4,8,20,640]{3,1,2,0:T(8,128)(2,1)} %param.10), kind=kOutput, calls=%fused_computation.13 | convolution fusion | flops 26214400 | bytes 1720320 | tf_op jit(solution)/shard_map/slj,xksj->xkls/dot_general | solution.py:166
  6.0 1.0 %reshape.219 = bf16[32,2,320]{2,1,0:T(2,128)(2,1)} reshape(bf16[32,4,8,20]{3,2,1,0:T(8,128)(2,1)S(1)} %bitcast.50) | data formatting | bytes 81920
  6.9 12.0 %all-to-all-start = ((bf16[32,2,320]{2,1,0:T(2,128)(2,1)}), bf16[32,2,320]{2,1,0:T(2,128)(2,1)}, u32[]{:S(2)}, u32[]{:S(2)}) async-start(bf16[32,2,320]{2,1,0:T(2,128)(2,1)} %reshape.219), calls=%async_computation | async-start | bytes 98304 | tf_op jit(solution)/shard_map/all_to_all | solution.py:178
  19.6 0.7 copy.57
  20.3 5.5 %collective-permute-start = (bf16[40,1,1,2688]{3,0,2,1:T(8,128)(2,1)}, bf16[40,1,1,2688]{3,0,2,1:T(8,128)(2,1)}, u32[]{:S(2)}, u32[]{:S(2)}) collective-permute-start(bf16[40,1,1,2688]{3,0,2,1:T(8,128)(2,1)} %copy.57), channel_id=1, source_target_pairs={{0,1},{1,2},{2,3},{3,4},{4,5},{5,6},{6,7},{7,8},{8,9},{9,10},{10,1... | collective-permute-start | bytes 645128 | tf_op jit(solution)/shard_map/ppermute | solution.py:23
  25.8 0.7 copy.58
  26.5 1.9 %collective-permute-start.1 = (bf16[40,1,1,2688]{3,0,2,1:T(8,128)(2,1)}, bf16[40,1,1,2688]{3,0,2,1:T(8,128)(2,1)}, u32[]{:S(2)}, u32[]{:S(2)}) collective-permute-start(bf16[40,1,1,2688]{3,0,2,1:T(8,128)(2,1)} %copy.58), channel_id=1, source_target_pairs={{1,0},{2,1},{3,2},{4,3},{5,4},{6,5},{7,6},{8,7},{9,8},{10,9},{11,1... | collective-permute-start | bytes 645128 | tf_op jit(solution)/shard_map/ppermute | solution.py:25
  28.5 1.4 %fusion.16 = (f32[640,128]{1,0:T(8,128)S(1)}, f32[640,128]{1,0:T(8,128)S(1)}) fusion(s32[640]{0:T(1024)S(1)} %copy-done.12), kind=kLoop, calls=%fused_computation.31 | loop fusion | flops 737280 | bytes 657920 | tf_op jit(solution)/shard_map/cos | solution.py:56
  29.9 0.7 slice_bitcast_fusion.2
  30.6 1.0 %cosine_multiply_fusion = (f32[21,640]{1,0:T(8,128)}, f32[21,640]{1,0:T(8,128)}) fusion(s32[21]{0:T(128)S(1)} %iota_multiply_fusion, s32[640]{0:T(1024)S(1)} %copy-done.12, f32[640]{0:T(1024)S(1)} %compare_select_fusion), kind=kLoop, calls=%fused_computation.57 | loop fusion | flops 147840 | bytes 112724 | tf_op jit(solution)/shard_map/mul | solution.py:48
  31.7 0.6 min.12.listed_ref
  32.4 0.7 reshape.210.slot_ref
  33.1 1.2 %reshape.220 = bf16[32,4,8,20]{3,2,1,0:T(8,128)(2,1)S(1)} reshape(bf16[32,2,320]{2,1,0:T(2,128)(2,1)} %all-to-all-done) | data formatting | bytes 81920
  34.2 0.8 copy.45
  35.1 1.3 %all_to_all.10 = bf16[4,8,1,640]{3,1,0,2:T(8,128)(2,1)S(1)} reshape(bf16[4,8,32,20]{3,2,1,0:T(8,128)(2,1)} %copy.45) | data formatting | bytes 81920 | tf_op jit(solution)/shard_map/all_to_all | solution.py:178
  36.3 1.3 %copy.48 = bf16[40,1,1,2688]{3,1,2,0:T(2,128)(2,1)S(1)} copy(bf16[40,1,1,2688]{3,0,2,1:T(8,128)(2,1)} %collective-permute-done) | data formatting | bytes 430080 | tf_op jit(solution)/shard_map/ppermute | solution.py:23
  37.6 1.3 %copy.49 = bf16[40,1,1,2688]{3,1,2,0:T(2,128)(2,1)S(1)} copy(bf16[40,1,1,2688]{3,0,2,1:T(8,128)(2,1)} %collective-permute-done.1) | data formatting | bytes 430080 | tf_op jit(solution)/shard_map/ppermute | solution.py:25
  39.0 1.9 %pad_maximum_fusion = bf16[40,10,1,2688]{3,1,2,0:T(8,128)(2,1)S(1)} fusion(bf16[40,1,1,2688]{3,1,2,0:T(2,128)(2,1)S(1)} %copy.49, bf16[40,8,1,2688]{3,1,2,0:T(8,128)(2,1)S(1)} %copy-done.1, bf16[40,1,1,2688]{3,1,2,0:T(2,128)(2,1)S(1)} %copy.48), kind=kLoop, calls=%fused_computation.5 | loop fusion | flops 6451200 | bytes 4300800 | tf_op jit(solution)/shard_map/concatenate | solution.py:21
  40.8 2.5 %fusion.3.refs_0_.refs_1_.refs_2_.refs_3_.refs_4_ = bf16[320,2688]{1,0:T(8,128)(2,1)} fusion(bf16[40,10,1,2688]{3,1,2,0:T(8,128)(2,1)S(1)} %pad_maximum_fusion, f32[8,2688]{1,0:T(8,128)S(1)} %copy-done.4, f32[8,2688]{1,0:T(8,128)S(1)} %copy-done.5, f32[8,2688]{1,0:T(8,128)S(1)} %get-tuple-element.55), kind=kLoop, calls=%fused_computation.11 | loop fusion | flops 7741440 | bytes 7139328 | tf_op jit(solution)/shard_map/reshape | solution.py:186
  43.3 4.4 %shard_map.121 = (bf16[4,320,128]{2,1,0:T(8,128)(2,1)}, bf16[4,320,128]{2,1,0:T(8,128)(2,1)}, bf16[4,320,128]{2,1,0:T(8,128)(2,1)}, bf16[4,320,128]{2,1,0:T(8,128)(2,1)}, bf16[4,320,128]{2,1,0:T(8,128)(2,1)}) custom-call(s32[20]{0:T(128)} %min.12.listed_ref, bf16[320,2688]{1,0:T(8,128)(2,1)} %fusion.3.refs_0_.refs_1_.refs_2_.refs_3_.refs_4_, ...), custom_call_target="tpu_custom_call" | custom-call | tf_op jit(solution)/shard_map/pallas_call | solution.py:92
  47.9 3.9 %collective-permute-start.2 = (bf16[4,320,128]{2,1,0:T(8,128)(2,1)}, bf16[4,320,128]{2,1,0:T(8,128)(2,1)S(1)}, u32[]{:S(2)}, u32[]{:S(2)}) collective-permute-start(bf16[4,320,128]{2,1,0:T(8,128)(2,1)} %get-tuple-element.30), channel_id=1, source_target_pairs={{32,0},{48,16},{64,32},{80,48},{96,64},{112,80},{128,96},{144,112}... | collective-permute-start | bytes 983048 | tf_op jit(solution)/shard_map/ppermute | solution.py:35
  51.8 3.1 %collective-permute-start.3 = (bf16[4,320,128]{2,1,0:T(8,128)(2,1)}, bf16[4,320,128]{2,1,0:T(8,128)(2,1)S(1)}, u32[]{:S(2)}, u32[]{:S(2)}) collective-permute-start(bf16[4,320,128]{2,1,0:T(8,128)(2,1)} %get-tuple-element.31), channel_id=1, source_target_pairs={{16,0},{32,16},{48,32},{64,48},{80,64},{96,80},{112,96},{128,112},... | collective-permute-start | bytes 983048 | tf_op jit(solution)/shard_map/ppermute | solution.py:35
  54.8 2.2 %collective-permute-start.4 = (bf16[4,320,128]{2,1,0:T(8,128)(2,1)}, bf16[4,320,128]{2,1,0:T(8,128)(2,1)}, u32[]{:S(2)}, u32[]{:S(2)}) collective-permute-start(bf16[4,320,128]{2,1,0:T(8,128)(2,1)} %get-tuple-element.33), channel_id=1, source_target_pairs={{0,16},{16,32},{32,48},{48,64},{64,80},{80,96},{96,112},{112,128},... | collective-permute-start | bytes 983048 | tf_op jit(solution)/shard_map/ppermute | solution.py:35
  57.1 5.2 %collective-permute-start.5 = (bf16[4,320,128]{2,1,0:T(8,128)(2,1)}, bf16[4,320,128]{2,1,0:T(8,128)(2,1)}, u32[]{:S(2)}, u32[]{:S(2)}) collective-permute-start(bf16[4,320,128]{2,1,0:T(8,128)(2,1)} %get-tuple-element.34), channel_id=1, source_target_pairs={{0,32},{16,48},{32,64},{48,80},{64,96},{80,112},{96,128},{112,144}... | collective-permute-start | bytes 983048 | tf_op jit(solution)/shard_map/ppermute | solution.py:35
  62.6 1.7 %fusion.4 = bf16[2,8,21,128]{3,2,1,0:T(8,128)(2,1)S(1)} fusion(f32[2,8,1,21,640]{4,3,1,0,2:T(8,128)S(1)} %get-tuple-element.59, f32[2,8,1,21,640]{4,3,1,0,2:T(8,128)S(1)} %get-tuple-element.58, f32[640,128]{1,0:T(8,128)S(1)} %get-tuple-element.72, f32[640,128]{1,0:T(8,128)S(1)} %get-tuple-element.71), kind=kOutput, calls=%fused_computation.14 | convolution fusion | flops 661239808 | bytes 2461696 | tf_op jit(solution)/shard_map/wklom,mi->wkloi/dot_general | solution.py:57
  64.4 4.0 %add_convert_fusion.stencil_ref = bf16[21,4,128,128]{3,2,1,0:T(8,128)(2,1)} fusion(f32[21,4,128]{2,1,0:T(4,128)S(1)} %bitcast.54, s32[21,4,128]{2,1,0:T(4,128)S(1)} %get-tuple-element.67, f32[21,4,128]{2,1,0:T(4,128)S(1)} %bitcast.55, s32[21,4,128]{2,1,0:T(4,128)S(1)} %get-tuple-element.68, f32[21,4,128]{2,1,0:T(4,128)S(1)} %bitcast.56, ...), kind=kLoop, calls=%fused_computation | loop fusion | flops 16515072 | bytes 3096576 | tf_op jit(solution)/shard_map/convert_element_type | solution.py:194
  68.4 0.6 collective-permute-done.4.refs_3_
  69.1 9.9 %collective-permute-done.5.refs_4_ = bf16[4,320,128]{2,1,0:T(8,128)(2,1)} collective-permute-done((bf16[4,320,128]{2,1,0:T(8,128)(2,1)}, bf16[4,320,128]{2,1,0:T(8,128)(2,1)}, u32[]{:S(2)}, u32[]{:S(2)}) %collective-permute-start.5) | collective-permute-done | bytes 327712 | tf_op jit(solution)/shard_map/ppermute | solution.py:35
  79.0 7.0 %shard_map.122 = (bf16[320,2688]{1,0:T(8,128)(2,1)}, f32[8,2688]{1,0:T(8,128)}) custom-call(s32[84]{0:T(128)} %reshape.210.slot_ref, bf16[21,4,128,128]{3,2,1,0:T(8,128)(2,1)} %add_convert_fusion.stencil_ref, bf16[4,320,128]{2,1,0:T(8,128)(2,1)} %copy-done.6, bf16[4,320,128]{2,1,0:T(8,128)(2,1)} %copy-done.7, ...), custom_call_target="tpu_custom_call" | custom-call | tf_op jit(solution)/shard_map/pallas_call | solution.py:141
  86.1 1.5 %fusion.18 = bf16[2,8,1,2688]{3,1,2,0:T(8,128)(2,1)} fusion(bf16[2,8,1,2688]{3,1,0,2:T(8,128)(2,1)S(1)} %convert_element_type.94, f32[8,2688]{1,0:T(8,128)} %get-tuple-element.36), kind=kLoop, calls=%fused_computation.36 | loop fusion | flops 129024 | bytes 258048
  (51 shorter events, 2.1 us)
Async XLA Ops:
  0.6 1.2 %copy-start = (bf16[20,32,640]{2,1,0:T(8,128)(2,1)S(1)}, bf16[20,32,640]{2,1,0:T(8,128)(2,1)}, u32[]{:S(2)}) copy-start(bf16[20,32,640]{2,1,0:T(8,128)(2,1)} %param.11) | copy-start | bytes 2457604
  0.6 4.5 %copy-start.12 = (s32[640]{0:T(1024)S(1)}, s32[640]{0:T(1024)}, u32[]{:S(2)}) copy-start(s32[640]{0:T(1024)} %param.13) | copy-start | bytes 7684
  0.7 18.3 %copy-start.1 = (bf16[40,8,1,2688]{3,1,2,0:T(8,128)(2,1)S(1)}, bf16[40,8,1,2688]{3,1,2,0:T(8,128)(2,1)}, u32[]{:S(2)}) copy-start(bf16[40,8,1,2688]{3,1,2,0:T(8,128)(2,1)} %param.14) | copy-start | bytes 5160964
  3.3 26.6 %copy-start.11 = (bf16[3,8,1,2688]{3,1,2,0:T(8,128)(2,1)S(1)}, bf16[3,8,1,2688]{3,1,2,0:T(8,128)(2,1)}, u32[]{:S(2)}) copy-start(bf16[3,8,1,2688]{3,1,2,0:T(8,128)(2,1)} %param.15) | copy-start | bytes 387076
  5.1 26.5 %copy-start.14 = (s32[1,5,4]{1,2,0:T(4,128)S(1)}, s32[1,5,4]{1,2,0:T(4,128)}, u32[]{:S(2)}) copy-start(s32[1,5,4]{1,2,0:T(4,128)} %param.16) | copy-start | bytes 244
  5.2 27.2 %copy-start.13 = (s32[21,4]{0,1:T(4,128)S(1)}, s32[21,4]{0,1:T(4,128)}, u32[]{:S(2)}) copy-start(s32[21,4]{0,1:T(4,128)} %param.17) | copy-start | bytes 1012
  6.9 26.1 %all-to-all-start = ((bf16[32,2,320]{2,1,0:T(2,128)(2,1)}), bf16[32,2,320]{2,1,0:T(2,128)(2,1)}, u32[]{:S(2)}, u32[]{:S(2)}) async-start(bf16[32,2,320]{2,1,0:T(2,128)(2,1)} %reshape.219), calls=%async_computation | async-start | bytes 98304 | tf_op jit(solution)/shard_map/all_to_all | solution.py:178
  20.3 16.1 %collective-permute-start = (bf16[40,1,1,2688]{3,0,2,1:T(8,128)(2,1)}, bf16[40,1,1,2688]{3,0,2,1:T(8,128)(2,1)}, u32[]{:S(2)}, u32[]{:S(2)}) collective-permute-start(bf16[40,1,1,2688]{3,0,2,1:T(8,128)(2,1)} %copy.57), channel_id=1, source_target_pairs={{0,1},{1,2},{2,3},{3,4},{4,5},{5,6},{6,7},{7,8},{8,9},{9,10},{10,1... | collective-permute-start | bytes 645128 | tf_op jit(solution)/shard_map/ppermute | solution.py:23
  26.5 11.1 %collective-permute-start.1 = (bf16[40,1,1,2688]{3,0,2,1:T(8,128)(2,1)}, bf16[40,1,1,2688]{3,0,2,1:T(8,128)(2,1)}, u32[]{:S(2)}, u32[]{:S(2)}) collective-permute-start(bf16[40,1,1,2688]{3,0,2,1:T(8,128)(2,1)} %copy.58), channel_id=1, source_target_pairs={{1,0},{2,1},{3,2},{4,3},{5,4},{6,5},{7,6},{8,7},{9,8},{10,9},{11,1... | collective-permute-start | bytes 645128 | tf_op jit(solution)/shard_map/ppermute | solution.py:25
  37.6 3.2 %copy-start.4 = (f32[8,2688]{1,0:T(8,128)S(1)}, f32[8,2688]{1,0:T(8,128)}, u32[]{:S(2)}) copy-start(f32[8,2688]{1,0:T(8,128)} %get-tuple-element.56) | copy-start | bytes 258052
  37.6 3.2 %copy-start.5 = (f32[8,2688]{1,0:T(8,128)S(1)}, f32[8,2688]{1,0:T(8,128)}, u32[]{:S(2)}) copy-start(f32[8,2688]{1,0:T(8,128)} %get-tuple-element.57) | copy-start | bytes 258052
  43.3 4.4 %copy-start.2 = (bf16[21,4,4,128]{3,2,1,0:T(4,128)(2,1)S(1)}, bf16[21,4,4,128]{3,2,1,0:T(4,128)(2,1)}, u32[]{:S(2)}) copy-start(bf16[21,4,4,128]{3,2,1,0:T(4,128)(2,1)} %param.19) | copy-start | bytes 258052
  43.3 4.5 %copy-start.10 = (s32[21,4,128]{2,1,0:T(4,128)S(1)}, s32[21,4,128]{2,1,0:T(4,128)}, u32[]{:S(2)}) copy-start(s32[21,4,128]{2,1,0:T(4,128)} %param.18) | copy-start | bytes 129028
  43.3 19.0 %copy-start.8 = (f32[21,640]{1,0:T(8,128)S(1)}, f32[21,640]{1,0:T(8,128)}, u32[]{:S(2)}) copy-start(f32[21,640]{1,0:T(8,128)} %get-tuple-element.69) | copy-start | bytes 161284
  43.3 19.0 %copy-start.9 = (f32[21,640]{1,0:T(8,128)S(1)}, f32[21,640]{1,0:T(8,128)}, u32[]{:S(2)}) copy-start(f32[21,640]{1,0:T(8,128)} %get-tuple-element.70) | copy-start | bytes 161284
  47.9 20.5 %collective-permute-start.2 = (bf16[4,320,128]{2,1,0:T(8,128)(2,1)}, bf16[4,320,128]{2,1,0:T(8,128)(2,1)S(1)}, u32[]{:S(2)}, u32[]{:S(2)}) collective-permute-start(bf16[4,320,128]{2,1,0:T(8,128)(2,1)} %get-tuple-element.30), channel_id=1, source_target_pairs={{32,0},{48,16},{64,32},{80,48},{96,64},{112,80},{128,96},{144,112}... | collective-permute-start | bytes 983048 | tf_op jit(solution)/shard_map/ppermute | solution.py:35
  51.8 16.7 %collective-permute-start.3 = (bf16[4,320,128]{2,1,0:T(8,128)(2,1)}, bf16[4,320,128]{2,1,0:T(8,128)(2,1)S(1)}, u32[]{:S(2)}, u32[]{:S(2)}) collective-permute-start(bf16[4,320,128]{2,1,0:T(8,128)(2,1)} %get-tuple-element.31), channel_id=1, source_target_pairs={{16,0},{32,16},{48,32},{64,48},{80,64},{96,80},{112,96},{128,112},... | collective-permute-start | bytes 983048 | tf_op jit(solution)/shard_map/ppermute | solution.py:35
  54.8 14.2 %collective-permute-start.4 = (bf16[4,320,128]{2,1,0:T(8,128)(2,1)}, bf16[4,320,128]{2,1,0:T(8,128)(2,1)}, u32[]{:S(2)}, u32[]{:S(2)}) collective-permute-start(bf16[4,320,128]{2,1,0:T(8,128)(2,1)} %get-tuple-element.33), channel_id=1, source_target_pairs={{0,16},{16,32},{32,48},{48,64},{64,80},{80,96},{96,112},{112,128},... | collective-permute-start | bytes 983048 | tf_op jit(solution)/shard_map/ppermute | solution.py:35
  57.1 21.9 %collective-permute-start.5 = (bf16[4,320,128]{2,1,0:T(8,128)(2,1)}, bf16[4,320,128]{2,1,0:T(8,128)(2,1)}, u32[]{:S(2)}, u32[]{:S(2)}) collective-permute-start(bf16[4,320,128]{2,1,0:T(8,128)(2,1)} %get-tuple-element.34), channel_id=1, source_target_pairs={{0,32},{16,48},{32,64},{48,80},{64,96},{80,112},{96,128},{112,144}... | collective-permute-start | bytes 983048 | tf_op jit(solution)/shard_map/ppermute | solution.py:35
  64.4 21.7 %copy-start.3 = (bf16[2,8,1,2688]{3,1,0,2:T(8,128)(2,1)}, bf16[2,8,1,2688]{3,1,0,2:T(8,128)(2,1)S(1)}, u32[]{:S(2)}) copy-start(bf16[2,8,1,2688]{3,1,0,2:T(8,128)(2,1)S(1)} %convert_element_type.94) | copy-start | bytes 258052
  68.4 10.6 %copy-start.6 = (bf16[4,320,128]{2,1,0:T(8,128)(2,1)}, bf16[4,320,128]{2,1,0:T(8,128)(2,1)S(1)}, u32[]{:S(2)}) copy-start(bf16[4,320,128]{2,1,0:T(8,128)(2,1)S(1)} %collective-permute-done.2.refs_0_) | copy-start | bytes 983044
  68.4 10.6 %copy-start.7 = (bf16[4,320,128]{2,1,0:T(8,128)(2,1)}, bf16[4,320,128]{2,1,0:T(8,128)(2,1)S(1)}, u32[]{:S(2)}) copy-start(bf16[4,320,128]{2,1,0:T(8,128)(2,1)S(1)} %collective-permute-done.3.refs_1_) | copy-start | bytes 983044

commit v8 on v6

--- a/solution.py
+++ b/solution.py
@@ -97,7 +97,7 @@
     block_count, rows_per_block = stencil.shape[0], stencil.shape[1]
     count = len(pieces)
     cap, rows, _ = pieces[0].shape
-    group = 3 if block_count % 3 == 0 else 1
+    group = 7 if block_count % 7 == 0 else 1
 
     def body(slot_ref, stencil_ref, *refs):
         piece_refs = refs[:count]

time: 83 us -> 81.2 us (0.978)
  Pallas kernels: 13.3 us -> 11.5 us
    pallas_call x1, Pallas kernels: 8.8 us -> 7.07 us  [apply_stencil(): pl.pallas_call(body, grid_spec=grid_spec, out_shape=out_shape, compiler_p...]
  transfers between devices with their start and end apart: 7 -> 7, of which waited for: 2 -> 2; matrix products, arithmetic and copies ran while one was open for 20% -> 21% of each run, Pallas kernels for 0% -> 0%
where the time goes in v8:
time: 81.2 us; the launch traced here: 80.4 us
  starting transfers between devices  33.1 us (41%)
  other arithmetic  14 us (17%)
  local copies, waits for them, and re-layouts  11.8 us (15%)
  Pallas kernels  11.5 us (14%)
  waiting for transfers between devices  6.6 us (8%)
  matrix products  2.47 us (3%)
  between operations  0.98 us (1%)
    ppermute x4, starting transfers between devices, shifted(): lax.ppermute(value, axis, [(source, source + steps) for source in range(l...  13.3 us
    all_to_all x1, starting transfers between devices, shards(): lax.all_to_all(coefficients, 'band', split_axis=2, concat_axis=3, tiled=T...  13 us
    pallas_call x1, Pallas kernels, apply_stencil(): pl.pallas_call(body, grid_spec=grid_spec, out_shape=out_shape, compiler_p...  7.07 us
    convert_element_type x1, other arithmetic, shards(): stencil = stencil_matrix(depart_offset, depart_weight).astype(jnp.bfloat16)  5.09 us
    all_to_all x1, waiting for transfers between devices, shards(): lax.all_to_all(coefficients, 'band', split_axis=2, concat_axis=3, tiled=T...  5.03 us
    ppermute x1, starting transfers between devices, extended(): lax.ppermute(tail, axis, [(i, (i + 1) % count) for i in range(ends)])  4.96 us
    pallas_call x1, Pallas kernels, pack_blocks(): pl.pallas_call(body, grid_spec=grid_spec, out_shape=out_shape)  4.43 us
    unnamed x31, local copies, waits for them, and re-layouts  3.58 us
  transfers between devices with their start and end apart: 7, of which 2 were waited for; matrix products, arithmetic and copies ran while one was open for 21% of the time, Pallas kernels for 0%

profile of v8, /device:TPU:25, one launch (start us, length us, event | category | flops | bytes accessed | tf_op | source)
XLA Modules:
  0.0 80.4 jit_solution(1056755796366239932)
XLA Ops:
  0.7 2.8 %fusion.33 = (bf16[40,1,1,2688]{3,1,2,0:T(2,128)(2,1)S(1)}, bf16[40,1,1,2688]{3,1,2,0:T(2,128)(2,1)S(1)}) fusion(bf16[40,8,1,2688]{3,1,2,0:T(8,128)(2,1)} %param.14), kind=kLoop, calls=%fused_computation.77 | loop fusion | bytes 860160 | tf_op jit(solution)/shard_map/slice | solution.py:20
  3.5 0.7 copy.71
  4.2 5.0 %collective-permute-start = (bf16[40,1,1,2688]{3,0,2,1:T(8,128)(2,1)}, bf16[40,1,1,2688]{3,0,2,1:T(8,128)(2,1)}, u32[]{:S(2)}, u32[]{:S(2)}) collective-permute-start(bf16[40,1,1,2688]{3,0,2,1:T(8,128)(2,1)} %copy.71), channel_id=1, source_target_pairs={{0,1},{1,2},{2,3},{3,4},{4,5},{5,6},{6,7},{7,8},{8,9},{9,10},{10,1... | collective-permute-start | bytes 645128 | tf_op jit(solution)/shard_map/ppermute | solution.py:23
  9.2 0.7 copy.72
  9.9 1.9 %collective-permute-start.1 = (bf16[40,1,1,2688]{3,0,2,1:T(8,128)(2,1)}, bf16[40,1,1,2688]{3,0,2,1:T(8,128)(2,1)}, u32[]{:S(2)}, u32[]{:S(2)}) collective-permute-start(bf16[40,1,1,2688]{3,0,2,1:T(8,128)(2,1)} %copy.72), channel_id=1, source_target_pairs={{1,0},{2,1},{3,2},{4,3},{5,4},{6,5},{7,6},{8,7},{9,8},{10,9},{11,1... | collective-permute-start | bytes 645128 | tf_op jit(solution)/shard_map/ppermute | solution.py:25
  11.8 1.4 %fusion.16 = (f32[640,128]{1,0:T(8,128)S(1)}, f32[640,128]{1,0:T(8,128)S(1)}) fusion(s32[640]{0:T(1024)S(1)} %copy-done.10), kind=kLoop, calls=%fused_computation.32 | loop fusion | flops 737280 | bytes 657920 | tf_op jit(solution)/shard_map/cos | solution.py:56
  13.4 0.6 min.12.listed_ref
  14.1 0.6 reshape.224.slot_ref
  14.8 1.0 %cosine_multiply_fusion = (f32[21,640]{1,0:T(8,128)S(1)}, f32[21,640]{1,0:T(8,128)}) fusion(s32[21]{0:T(128)S(1)} %iota_multiply_fusion, s32[640]{0:T(1024)S(1)} %copy-done.10, f32[640]{0:T(1024)S(1)} %compare_select_fusion), kind=kLoop, calls=%fused_computation.58 | loop fusion | flops 147840 | bytes 112724 | tf_op jit(solution)/shard_map/mul | solution.py:48
  15.8 1.3 %copy.56 = bf16[40,1,1,2688]{3,1,2,0:T(2,128)(2,1)S(1)} copy(bf16[40,1,1,2688]{3,0,2,1:T(8,128)(2,1)} %collective-permute-done) | data formatting | bytes 430080 | tf_op jit(solution)/shard_map/ppermute | solution.py:23
  17.0 1.6 %collective-permute-done.1 = bf16[40,1,1,2688]{3,0,2,1:T(8,128)(2,1)} collective-permute-done((bf16[40,1,1,2688]{3,0,2,1:T(8,128)(2,1)}, bf16[40,1,1,2688]{3,0,2,1:T(8,128)(2,1)}, u32[]{:S(2)}, u32[]{:S(2)}) %collective-permute-start.1) | collective-permute-done | bytes 215072 | tf_op jit(solution)/shard_map/ppermute | solution.py:25
  18.6 1.3 %copy.58 = bf16[40,1,1,2688]{3,1,2,0:T(2,128)(2,1)S(1)} copy(bf16[40,1,1,2688]{3,0,2,1:T(8,128)(2,1)} %collective-permute-done.1) | data formatting | bytes 430080 | tf_op jit(solution)/shard_map/ppermute | solution.py:25
  19.9 3.0 %fusion.3.refs_0_.refs_1_.refs_2_.refs_3_.refs_4_ = bf16[320,2688]{1,0:T(8,128)(2,1)} fusion(bf16[40,8,1,2688]{3,1,2,0:T(8,128)(2,1)S(1)} %copy-done.1, bf16[40,1,1,2688]{3,1,2,0:T(2,128)(2,1)S(1)} %copy.58, bf16[40,1,1,2688]{3,1,2,0:T(2,128)(2,1)S(1)} %copy.56, f32[8,2688]{1,0:T(8,128)S(1)} %get-tuple-element.59, f32[8,2688]{1,0:T(8,128)S(1)} %get-tuple-element.60, ...), kind=kLoop, calls=%fused_computation.10 | loop fusion | flops 12902400 | bytes 4128768 | tf_op jit(solution)/shard_map/reshape | solution.py:166
  22.9 4.4 %shard_map.121 = (bf16[4,320,128]{2,1,0:T(8,128)(2,1)}, bf16[4,320,128]{2,1,0:T(8,128)(2,1)}, bf16[4,320,128]{2,1,0:T(8,128)(2,1)}, bf16[4,320,128]{2,1,0:T(8,128)(2,1)}, bf16[4,320,128]{2,1,0:T(8,128)(2,1)}) custom-call(s32[20]{0:T(128)} %min.12.listed_ref, bf16[320,2688]{1,0:T(8,128)(2,1)} %fusion.3.refs_0_.refs_1_.refs_2_.refs_3_.refs_4_, ...), custom_call_target="tpu_custom_call" | custom-call | tf_op jit(solution)/shard_map/pallas_call | solution.py:92
  27.3 0.8 slice_convert_fusion.3
  28.1 0.7 broadcast_add_fusion.2
  28.8 1.3 %collective-permute-start.2 = (bf16[4,320,128]{2,1,0:T(8,128)(2,1)}, bf16[4,320,128]{2,1,0:T(8,128)(2,1)S(1)}, u32[]{:S(2)}, u32[]{:S(2)}) collective-permute-start(bf16[4,320,128]{2,1,0:T(8,128)(2,1)} %get-tuple-element.30), channel_id=1, source_target_pairs={{32,0},{48,16},{64,32},{80,48},{96,64},{112,80},{128,96},{144,112}... | collective-permute-start | bytes 983048 | tf_op jit(solution)/shard_map/ppermute | solution.py:35
  30.1 1.3 %collective-permute-start.3 = (bf16[4,320,128]{2,1,0:T(8,128)(2,1)}, bf16[4,320,128]{2,1,0:T(8,128)(2,1)}, u32[]{:S(2)}, u32[]{:S(2)}) collective-permute-start(bf16[4,320,128]{2,1,0:T(8,128)(2,1)} %get-tuple-element.31), channel_id=1, source_target_pairs={{16,0},{32,16},{48,32},{64,48},{80,64},{96,80},{112,96},{128,112},... | collective-permute-start | bytes 983048 | tf_op jit(solution)/shard_map/ppermute | solution.py:35
  31.4 4.7 %collective-permute-start.4 = (bf16[4,320,128]{2,1,0:T(8,128)(2,1)}, bf16[4,320,128]{2,1,0:T(8,128)(2,1)}, u32[]{:S(2)}, u32[]{:S(2)}) collective-permute-start(bf16[4,320,128]{2,1,0:T(8,128)(2,1)} %get-tuple-element.33), channel_id=1, source_target_pairs={{0,16},{16,32},{32,48},{48,64},{64,80},{80,96},{96,112},{112,128},... | collective-permute-start | bytes 983048 | tf_op jit(solution)/shard_map/ppermute | solution.py:35
  36.1 6.0 %collective-permute-start.5 = (bf16[4,320,128]{2,1,0:T(8,128)(2,1)}, bf16[4,320,128]{2,1,0:T(8,128)(2,1)}, u32[]{:S(2)}, u32[]{:S(2)}) collective-permute-start(bf16[4,320,128]{2,1,0:T(8,128)(2,1)} %get-tuple-element.34), channel_id=1, source_target_pairs={{0,32},{16,48},{32,64},{48,80},{64,96},{80,112},{96,128},{112,144}... | collective-permute-start | bytes 983048 | tf_op jit(solution)/shard_map/ppermute | solution.py:35
  42.1 0.4 convolution_bitcast_fusion.1
  42.5 0.4 convolution_bitcast_fusion
  43.0 0.5 copy.61
  43.6 1.0 %reshape.234 = bf16[32,2,320]{2,1,0:T(2,128)(2,1)} reshape(bf16[32,4,8,20]{3,2,1,0:T(8,128)(2,1)S(1)} %bitcast.50) | data formatting | bytes 81920
  44.5 13.0 %all-to-all-start = ((bf16[32,2,320]{2,1,0:T(2,128)(2,1)}), bf16[32,2,320]{2,1,0:T(2,128)(2,1)S(1)}, u32[]{:S(2)}, u32[]{:S(2)}) async-start(bf16[32,2,320]{2,1,0:T(2,128)(2,1)} %reshape.234), calls=%async_computation | async-start | bytes 98304 | tf_op jit(solution)/shard_map/all_to_all | solution.py:203
  57.5 5.1 %add_convert_fusion.stencil_ref = bf16[21,4,128,128]{3,2,1,0:T(8,128)(2,1)} fusion(f32[21,4,128]{2,1,0:T(4,128)} %bitcast.54, s32[21,4,128]{2,1,0:T(4,128)} %get-tuple-element.70, f32[21,4,128]{2,1,0:T(4,128)} %bitcast.55, s32[21,4,128]{2,1,0:T(4,128)} %get-tuple-element.71, f32[21,4,128]{2,1,0:T(4,128)} %bitcast.56, s32[21,4,128]{2,1,0:T(4,128)} %get-tuple-element.69, ...), kind=kLoop, calls=%fused_computation | loop fusion | flops 16515072 | bytes 3096576 | tf_op jit(solution)/shard_map/convert_element_type | solution.py:176
  62.6 5.0 %all-to-all-done = bf16[32,2,320]{2,1,0:T(2,128)(2,1)S(1)} async-done(((bf16[32,2,320]{2,1,0:T(2,128)(2,1)}), bf16[32,2,320]{2,1,0:T(2,128)(2,1)S(1)}, u32[]{:S(2)}, u32[]{:S(2)}) %all-to-all-start) | async-done | bytes 40992 | tf_op jit(solution)/shard_map/all_to_all | solution.py:203
  68.0 0.4 copy.62
  69.2 1.7 %fusion.4 = bf16[2,8,21,128]{3,2,1,0:T(8,128)(2,1)S(1)} fusion(f32[2,8,1,21,640]{4,3,1,0,2:T(8,128)S(1)} %get-tuple-element.62, f32[2,8,1,21,640]{4,3,1,0,2:T(8,128)S(1)} %get-tuple-element.61, f32[640,128]{1,0:T(8,128)S(1)} %get-tuple-element.75, f32[640,128]{1,0:T(8,128)S(1)} %get-tuple-element.74), kind=kOutput, calls=%fused_computation.15 | convolution fusion | flops 661239808 | bytes 2461696 | tf_op jit(solution)/shard_map/wklom,mi->wkloi/dot_general | solution.py:57
  71.1 0.7 copy-done.6
  71.8 7.1 %shard_map.122 = (bf16[320,2688]{1,0:T(8,128)(2,1)}, f32[8,2688]{1,0:T(8,128)}) custom-call(s32[84]{0:T(128)} %reshape.224.slot_ref, bf16[21,4,128,128]{3,2,1,0:T(8,128)(2,1)} %add_convert_fusion.stencil_ref, bf16[4,320,128]{2,1,0:T(8,128)(2,1)} %copy-done.6, bf16[4,320,128]{2,1,0:T(8,128)(2,1)} %collective-permute-done.3.refs_1_, ...), custom_call_target="tpu_custom_call" | custom-call | tf_op jit(solution)/shard_map/pallas_call | solution.py:141
  78.9 1.5 %fusion.18 = bf16[2,8,1,2688]{3,1,2,0:T(8,128)(2,1)} fusion(bf16[2,8,1,2688]{3,1,0,2:T(8,128)(2,1)S(1)} %convert_element_type.106, f32[8,2688]{1,0:T(8,128)} %get-tuple-element.36), kind=kLoop, calls=%fused_computation.37 | loop fusion | flops 129024 | bytes 258048
  (46 shorter events, 1.8 us)
Async XLA Ops:
  0.6 41.4 %copy-start = (bf16[20,32,640]{2,1,0:T(8,128)(2,1)S(1)}, bf16[20,32,640]{2,1,0:T(8,128)(2,1)}, u32[]{:S(2)}) copy-start(bf16[20,32,640]{2,1,0:T(8,128)(2,1)} %param.12) | copy-start | bytes 2457604
  0.6 19.2 %copy-start.1 = (bf16[40,8,1,2688]{3,1,2,0:T(8,128)(2,1)S(1)}, bf16[40,8,1,2688]{3,1,2,0:T(8,128)(2,1)}, u32[]{:S(2)}) copy-start(bf16[40,8,1,2688]{3,1,2,0:T(8,128)(2,1)} %param.14) | copy-start | bytes 5160964
  0.7 11.2 %copy-start.10 = (s32[640]{0:T(1024)S(1)}, s32[640]{0:T(1024)}, u32[]{:S(2)}) copy-start(s32[640]{0:T(1024)} %param.13) | copy-start | bytes 7684
  0.7 12.6 %copy-start.9 = (bf16[3,8,1,2688]{3,1,2,0:T(8,128)(2,1)S(1)}, bf16[3,8,1,2688]{3,1,2,0:T(8,128)(2,1)}, u32[]{:S(2)}) copy-start(bf16[3,8,1,2688]{3,1,2,0:T(8,128)(2,1)} %param.15) | copy-start | bytes 387076
  0.7 12.7 %copy-start.12 = (s32[1,5,4]{1,2,0:T(4,128)S(1)}, s32[1,5,4]{1,2,0:T(4,128)}, u32[]{:S(2)}) copy-start(s32[1,5,4]{1,2,0:T(4,128)} %param.16) | copy-start | bytes 244
  0.7 13.4 %copy-start.11 = (s32[21,4]{0,1:T(4,128)S(1)}, s32[21,4]{0,1:T(4,128)}, u32[]{:S(2)}) copy-start(s32[21,4]{0,1:T(4,128)} %param.17) | copy-start | bytes 1012
  4.2 11.6 %collective-permute-start = (bf16[40,1,1,2688]{3,0,2,1:T(8,128)(2,1)}, bf16[40,1,1,2688]{3,0,2,1:T(8,128)(2,1)}, u32[]{:S(2)}, u32[]{:S(2)}) collective-permute-start(bf16[40,1,1,2688]{3,0,2,1:T(8,128)(2,1)} %copy.71), channel_id=1, source_target_pairs={{0,1},{1,2},{2,3},{3,4},{4,5},{5,6},{6,7},{7,8},{8,9},{9,10},{10,1... | collective-permute-start | bytes 645128 | tf_op jit(solution)/shard_map/ppermute | solution.py:23
  9.9 8.7 %collective-permute-start.1 = (bf16[40,1,1,2688]{3,0,2,1:T(8,128)(2,1)}, bf16[40,1,1,2688]{3,0,2,1:T(8,128)(2,1)}, u32[]{:S(2)}, u32[]{:S(2)}) collective-permute-start(bf16[40,1,1,2688]{3,0,2,1:T(8,128)(2,1)} %copy.72), channel_id=1, source_target_pairs={{1,0},{2,1},{3,2},{4,3},{5,4},{6,5},{7,6},{8,7},{9,8},{10,9},{11,1... | collective-permute-start | bytes 645128 | tf_op jit(solution)/shard_map/ppermute | solution.py:25
  22.9 4.4 %copy-start.4 = (bf16[21,4,4,128]{3,2,1,0:T(4,128)(2,1)S(1)}, bf16[21,4,4,128]{3,2,1,0:T(4,128)(2,1)}, u32[]{:S(2)}) copy-start(bf16[21,4,4,128]{3,2,1,0:T(4,128)(2,1)} %param.19) | copy-start | bytes 258052
  22.9 5.2 %copy-start.8 = (s32[21,4,128]{2,1,0:T(4,128)S(1)}, s32[21,4,128]{2,1,0:T(4,128)}, u32[]{:S(2)}) copy-start(s32[21,4,128]{2,1,0:T(4,128)} %param.18) | copy-start | bytes 129028
  22.9 19.2 %copy-start.2 = (bf16[4,8,20,640]{3,1,2,0:T(8,128)(2,1)S(1)}, bf16[4,8,20,640]{3,1,2,0:T(8,128)(2,1)}, u32[]{:S(2)}) copy-start(bf16[4,8,20,640]{3,1,2,0:T(8,128)(2,1)} %param.10) | copy-start | bytes 2457604
  22.9 19.6 %copy-start.3 = (bf16[20,32,640]{2,1,0:T(8,128)(2,1)S(1)}, bf16[20,32,640]{2,1,0:T(8,128)(2,1)}, u32[]{:S(2)}) copy-start(bf16[20,32,640]{2,1,0:T(8,128)(2,1)} %param.11) | copy-start | bytes 2457604
  28.8 42.3 %collective-permute-start.2 = (bf16[4,320,128]{2,1,0:T(8,128)(2,1)}, bf16[4,320,128]{2,1,0:T(8,128)(2,1)S(1)}, u32[]{:S(2)}, u32[]{:S(2)}) collective-permute-start(bf16[4,320,128]{2,1,0:T(8,128)(2,1)} %get-tuple-element.30), channel_id=1, source_target_pairs={{32,0},{48,16},{64,32},{80,48},{96,64},{112,80},{128,96},{144,112}... | collective-permute-start | bytes 983048 | tf_op jit(solution)/shard_map/ppermute | solution.py:35
  30.1 41.0 %collective-permute-start.3 = (bf16[4,320,128]{2,1,0:T(8,128)(2,1)}, bf16[4,320,128]{2,1,0:T(8,128)(2,1)}, u32[]{:S(2)}, u32[]{:S(2)}) collective-permute-start(bf16[4,320,128]{2,1,0:T(8,128)(2,1)} %get-tuple-element.31), channel_id=1, source_target_pairs={{16,0},{32,16},{48,32},{64,48},{80,64},{96,80},{112,96},{128,112},... | collective-permute-start | bytes 983048 | tf_op jit(solution)/shard_map/ppermute | solution.py:35
  31.4 39.7 %collective-permute-start.4 = (bf16[4,320,128]{2,1,0:T(8,128)(2,1)}, bf16[4,320,128]{2,1,0:T(8,128)(2,1)}, u32[]{:S(2)}, u32[]{:S(2)}) collective-permute-start(bf16[4,320,128]{2,1,0:T(8,128)(2,1)} %get-tuple-element.33), channel_id=1, source_target_pairs={{0,16},{16,32},{32,48},{48,64},{64,80},{80,96},{96,112},{112,128},... | collective-permute-start | bytes 983048 | tf_op jit(solution)/shard_map/ppermute | solution.py:35
  36.1 35.0 %collective-permute-start.5 = (bf16[4,320,128]{2,1,0:T(8,128)(2,1)}, bf16[4,320,128]{2,1,0:T(8,128)(2,1)}, u32[]{:S(2)}, u32[]{:S(2)}) collective-permute-start(bf16[4,320,128]{2,1,0:T(8,128)(2,1)} %get-tuple-element.34), channel_id=1, source_target_pairs={{0,32},{16,48},{32,64},{48,80},{64,96},{80,112},{96,128},{112,144}... | collective-permute-start | bytes 983048 | tf_op jit(solution)/shard_map/ppermute | solution.py:35
  44.5 24.5 %copy-start.7 = (f32[21,640]{1,0:T(8,128)S(1)}, f32[21,640]{1,0:T(8,128)}, u32[]{:S(2)}) copy-start(f32[21,640]{1,0:T(8,128)} %get-tuple-element.73) | copy-start | bytes 161284
  44.5 23.1 %all-to-all-start = ((bf16[32,2,320]{2,1,0:T(2,128)(2,1)}), bf16[32,2,320]{2,1,0:T(2,128)(2,1)S(1)}, u32[]{:S(2)}, u32[]{:S(2)}) async-start(bf16[32,2,320]{2,1,0:T(2,128)(2,1)} %reshape.234), calls=%async_computation | async-start | bytes 98304 | tf_op jit(solution)/shard_map/all_to_all | solution.py:203
  71.0 9.4 %copy-start.5 = (bf16[2,8,1,2688]{3,1,0,2:T(8,128)(2,1)}, bf16[2,8,1,2688]{3,1,0,2:T(8,128)(2,1)S(1)}, u32[]{:S(2)}) copy-start(bf16[2,8,1,2688]{3,1,0,2:T(8,128)(2,1)S(1)} %convert_element_type.106) | copy-start | bytes 258052
  71.1 0.7 copy-start.6

commit v9 on v8

--- a/solution.py
+++ b/solution.py
@@ -72,25 +72,23 @@
 
 
 def pack_blocks(listed, remapped, offsets, cap):
-    rows = remapped.shape[0]
-
-    def body(listed_ref, *refs):
+    rows, width = remapped.shape
+
+    def body(listed_ref, source_ref, *out_refs):
         for index in range(offsets):
-            refs[offsets + index][...] = refs[index][...][None]
-
-    def source_map(index):
-        return lambda entry, table: (0, table[index * cap + entry])
+            for entry in range(cap):
+                column = pl.multiple_of(listed_ref[index * cap + entry] * BLK, BLK)
+                out_refs[index][entry] = source_ref[:, pl.ds(column, BLK)]
 
     out_shape = [jax.ShapeDtypeStruct((cap, rows, BLK), remapped.dtype) for _ in range(offsets)]
     grid_spec = pltpu.PrefetchScalarGridSpec(
         num_scalar_prefetch=1,
-        grid=(cap,),
-        in_specs=[pl.BlockSpec((rows, BLK), source_map(index)) for index in range(offsets)],
-        out_specs=[pl.BlockSpec((1, rows, BLK), lambda entry, table: (entry, 0, 0))
+        grid=(1,),
+        in_specs=[pl.BlockSpec((rows, width), lambda step, table: (0, 0))],
+        out_specs=[pl.BlockSpec((cap, rows, BLK), lambda step, table: (0, 0, 0))
                    for _ in range(offsets)],
     )
-    return pl.pallas_call(body, grid_spec=grid_spec, out_shape=out_shape)(
-        listed, *([remapped] * offsets))
+    return pl.pallas_call(body, grid_spec=grid_spec, out_shape=out_shape)(listed, remapped)
 
 
 def apply_stencil(slots, stencil, pieces, bin_count, level_count):

time: 81.2 us -> 82.2 us (1.012)
  other arithmetic: 14 us -> 16.8 us
  local copies, waits for them, and re-layouts: 11.8 us -> 9.39 us
  waiting for transfers between devices: 6.6 us -> 7.82 us
    all_to_all x1, waiting for transfers between devices: 5.03 us -> 7.33 us  [shards(): lax.all_to_all(coefficients, 'band', split_axis=2, concat_axis=3, tiled=T...]
    unnamed x31 -> x37, local copies, waits for them, and re-layouts: 3.58 us -> 2.24 us
    ppermute x1, waiting for transfers between devices: 1.55 us -> 0.48 us  [extended(): lax.ppermute(head, axis, [((i + 1) % count, i) for i in range(ends)])]
    reshape x1, other arithmetic: 3.01 us -> 4.02 us  [shards(): vertical_sum.astype(jnp.bfloat16).reshape(rows, lat_count * lon_count)]
    ppermute x1, local copies, waits for them, and re-layouts: 1.27 us -> 0.33 us  [extended(): lax.ppermute(tail, axis, [(i, (i + 1) % count) for i in range(ends)])]
    ppermute x1, local copies, waits for them, and re-layouts: 1.27 us -> 0.33 us  [extended(): lax.ppermute(head, axis, [((i + 1) % count, i) for i in range(ends)])]
    cos x1, other arithmetic: 1.42 us -> 2.32 us  [synthesis(): rhs = jnp.concatenate([jnp.cos(near_angle), jnp.sin(near_angle)], axis=0)]
where the time goes in v9:
time: 82.2 us; the launch traced here: 81.5 us
  starting transfers between devices  33.2 us (40%)
  other arithmetic  16.8 us (20%)
  Pallas kernels  10.8 us (13%)
  local copies, waits for them, and re-layouts  9.39 us (11%)
  waiting for transfers between devices  7.82 us (10%)
  matrix products  2.5 us (3%)
  between operations  1 us (1%)
    ppermute x4, starting transfers between devices, shifted(): lax.ppermute(value, axis, [(source, source + steps) for source in range(l...  13.3 us
    all_to_all x1, starting transfers between devices, shards(): lax.all_to_all(coefficients, 'band', split_axis=2, concat_axis=3, tiled=T...  13 us
    all_to_all x1, waiting for transfers between devices, shards(): lax.all_to_all(coefficients, 'band', split_axis=2, concat_axis=3, tiled=T...  7.33 us
    pallas_call x1, Pallas kernels, apply_stencil(): pl.pallas_call(body, grid_spec=grid_spec, out_shape=out_shape, compiler_p...  7.05 us
    convert_element_type x1, other arithmetic, shards(): stencil = stencil_matrix(depart_offset, depart_weight).astype(jnp.bfloat16)  5.22 us
    ppermute x1, starting transfers between devices, extended(): lax.ppermute(tail, axis, [(i, (i + 1) % count) for i in range(ends)])  4.98 us
    reshape x1, other arithmetic, shards(): vertical_sum.astype(jnp.bfloat16).reshape(rows, lat_count * lon_count)  4.02 us
    pallas_call x1, Pallas kernels, pack_blocks(): pl.pallas_call(body, grid_spec=grid_spec, out_shape=out_shape)  3.74 us
  transfers between devices with their start and end apart: 7, of which 2 were waited for; matrix products, arithmetic and copies ran while one was open for 21% of the time, Pallas kernels for 0%

profile of v9, /device:TPU:25, one launch (start us, length us, event | category | flops | bytes accessed | tf_op | source)
XLA Modules:
  0.0 81.5 jit_solution(17777922548859075640)
XLA Ops:
  0.7 2.8 %fusion.33 = (bf16[40,1,1,2688]{3,1,2,0:T(2,128)(2,1)S(1)}, bf16[40,1,1,2688]{3,1,2,0:T(2,128)(2,1)S(1)}) fusion(bf16[40,8,1,2688]{3,1,2,0:T(8,128)(2,1)} %param.14), kind=kLoop, calls=%fused_computation.77 | loop fusion | bytes 860160 | tf_op jit(solution)/shard_map/slice | solution.py:20
  3.5 5.0 %collective-permute-start = (bf16[40,1,1,2688]{3,0,2,1:T(8,128)(2,1)S(1)}, bf16[40,1,1,2688]{3,0,2,1:T(8,128)(2,1)S(1)}, u32[]{:S(2)}, u32[]{:S(2)}) collective-permute-start(bf16[40,1,1,2688]{3,0,2,1:T(8,128)(2,1)S(1)} %copy.71), channel_id=1, source_target_pairs={{0,1},{1,2},{2,3},{3,4},{4,5},{5,6},{6,7},{7,8},{8,9},{9,10},{10,1... | collective-permute-start | bytes 645128 | tf_op jit(solution)/shard_map/ppermute | solution.py:23
  8.5 1.9 %collective-permute-start.1 = (bf16[40,1,1,2688]{3,0,2,1:T(8,128)(2,1)S(1)}, bf16[40,1,1,2688]{3,0,2,1:T(8,128)(2,1)S(1)}, u32[]{:S(2)}, u32[]{:S(2)}) collective-permute-start(bf16[40,1,1,2688]{3,0,2,1:T(8,128)(2,1)S(1)} %copy.72), channel_id=1, source_target_pairs={{1,0},{2,1},{3,2},{4,3},{5,4},{6,5},{7,6},{8,7},{9,8},{10,9},{11,1... | collective-permute-start | bytes 645128 | tf_op jit(solution)/shard_map/ppermute | solution.py:25
  10.5 2.3 %fusion.16 = (f32[640,128]{1,0:T(8,128)}, f32[640,128]{1,0:T(8,128)}) fusion(s32[640]{0:T(1024)S(1)} %copy-done.13), kind=kLoop, calls=%fused_computation.32 | loop fusion | flops 737280 | bytes 657920 | tf_op jit(solution)/shard_map/cos | solution.py:56
  12.9 0.7 slice_bitcast_fusion.2
  13.6 0.7 min.12.listed_ref
  14.4 0.6 reshape.224.slot_ref
  15.1 1.0 %cosine_multiply_fusion = (f32[21,640]{1,0:T(8,128)}, f32[21,640]{1,0:T(8,128)}) fusion(s32[21]{0:T(128)S(1)} %iota_multiply_fusion, s32[640]{0:T(1024)S(1)} %copy-done.13, f32[640]{0:T(1024)S(1)} %compare_select_fusion), kind=kLoop, calls=%fused_computation.58 | loop fusion | flops 147840 | bytes 112724 | tf_op jit(solution)/shard_map/mul | solution.py:48
  16.1 0.3 copy.56
  16.5 0.5 collective-permute-done.1
  16.9 0.3 copy.58
  17.3 4.0 %fusion.3.source_ref = bf16[320,2688]{1,0:T(8,128)(2,1)} fusion(bf16[40,8,1,2688]{3,1,2,0:T(8,128)(2,1)S(1)} %copy-done.1, bf16[40,1,1,2688]{3,1,2,0:T(2,128)(2,1)S(1)} %copy.58, bf16[40,1,1,2688]{3,1,2,0:T(2,128)(2,1)S(1)} %copy.56, f32[8,2688]{1,0:T(8,128)} %get-tuple-element.59, f32[8,2688]{1,0:T(8,128)} %get-tuple-element.60, ...), kind=kLoop, calls=%fused_computation.10 | loop fusion | flops 12902400 | bytes 4128768 | tf_op jit(solution)/shard_map/reshape | solution.py:164
  21.3 3.7 %shard_map.121 = (bf16[4,320,128]{2,1,0:T(8,128)(2,1)}, bf16[4,320,128]{2,1,0:T(8,128)(2,1)}, bf16[4,320,128]{2,1,0:T(8,128)(2,1)}, bf16[4,320,128]{2,1,0:T(8,128)(2,1)}, bf16[4,320,128]{2,1,0:T(8,128)(2,1)}) custom-call(s32[20]{0:T(128)} %min.12.listed_ref, bf16[320,2688]{1,0:T(8,128)(2,1)} %fusion.3.source_ref), custom_call_target="tpu_custom_call" | custom-call | tf_op jit(solution)/shard_map/pallas_call | solution.py:91
  25.1 0.8 slice_convert_fusion.3
  25.9 1.4 %broadcast_add_fusion.2 = (s32[21,4,128]{2,1,0:T(4,128)S(1)}, s32[21,4,128]{2,1,0:T(4,128)}, s32[21,4,128]{2,1,0:T(4,128)}) fusion(s32[21,4,128]{2,1,0:T(4,128)} %param.18), kind=kLoop, calls=%fused_computation.71 | loop fusion | flops 32256 | bytes 172032 | tf_op jit(solution)/shard_map/add | solution.py:67
  27.3 1.4 %collective-permute-start.2 = (bf16[4,320,128]{2,1,0:T(8,128)(2,1)}, bf16[4,320,128]{2,1,0:T(8,128)(2,1)S(1)}, u32[]{:S(2)}, u32[]{:S(2)}) collective-permute-start(bf16[4,320,128]{2,1,0:T(8,128)(2,1)} %get-tuple-element.30), channel_id=1, source_target_pairs={{32,0},{48,16},{64,32},{80,48},{96,64},{112,80},{128,96},{144,112}... | collective-permute-start | bytes 983048 | tf_op jit(solution)/shard_map/ppermute | solution.py:35
  28.7 1.3 %collective-permute-start.3 = (bf16[4,320,128]{2,1,0:T(8,128)(2,1)}, bf16[4,320,128]{2,1,0:T(8,128)(2,1)}, u32[]{:S(2)}, u32[]{:S(2)}) collective-permute-start(bf16[4,320,128]{2,1,0:T(8,128)(2,1)} %get-tuple-element.31), channel_id=1, source_target_pairs={{16,0},{32,16},{48,32},{64,48},{80,64},{96,80},{112,96},{128,112},... | collective-permute-start | bytes 983048 | tf_op jit(solution)/shard_map/ppermute | solution.py:35
  30.0 4.7 %collective-permute-start.4 = (bf16[4,320,128]{2,1,0:T(8,128)(2,1)}, bf16[4,320,128]{2,1,0:T(8,128)(2,1)}, u32[]{:S(2)}, u32[]{:S(2)}) collective-permute-start(bf16[4,320,128]{2,1,0:T(8,128)(2,1)} %get-tuple-element.33), channel_id=1, source_target_pairs={{0,16},{16,32},{32,48},{48,64},{64,80},{80,96},{96,112},{112,128},... | collective-permute-start | bytes 983048 | tf_op jit(solution)/shard_map/ppermute | solution.py:35
  34.8 5.9 %collective-permute-start.5 = (bf16[4,320,128]{2,1,0:T(8,128)(2,1)}, bf16[4,320,128]{2,1,0:T(8,128)(2,1)}, u32[]{:S(2)}, u32[]{:S(2)}) collective-permute-start(bf16[4,320,128]{2,1,0:T(8,128)(2,1)} %get-tuple-element.34), channel_id=1, source_target_pairs={{0,32},{16,48},{32,64},{48,80},{64,96},{80,112},{96,128},{112,144}... | collective-permute-start | bytes 983048 | tf_op jit(solution)/shard_map/ppermute | solution.py:35
  40.6 0.4 convolution_bitcast_fusion.1
  41.0 0.4 convolution_bitcast_fusion
  41.6 0.6 copy.61
  42.2 1.0 %reshape.234 = bf16[32,2,320]{2,1,0:T(2,128)(2,1)} reshape(bf16[32,4,8,20]{3,2,1,0:T(8,128)(2,1)S(1)} %bitcast.50) | data formatting | bytes 81920
  43.1 13.0 %all-to-all-start = ((bf16[32,2,320]{2,1,0:T(2,128)(2,1)}), bf16[32,2,320]{2,1,0:T(2,128)(2,1)S(1)}, u32[]{:S(2)}, u32[]{:S(2)}) async-start(bf16[32,2,320]{2,1,0:T(2,128)(2,1)} %reshape.234), calls=%async_computation | async-start | bytes 98304 | tf_op jit(solution)/shard_map/all_to_all | solution.py:201
  56.2 5.2 %add_convert_fusion.stencil_ref = bf16[21,4,128,128]{3,2,1,0:T(8,128)(2,1)} fusion(f32[21,4,128]{2,1,0:T(4,128)} %bitcast.54, s32[21,4,128]{2,1,0:T(4,128)} %get-tuple-element.70, f32[21,4,128]{2,1,0:T(4,128)} %bitcast.55, s32[21,4,128]{2,1,0:T(4,128)} %get-tuple-element.71, f32[21,4,128]{2,1,0:T(4,128)} %bitcast.56, s32[21,4,128]{2,1,0:T(4,128)S(1)} %get-tuple-element.69, ...), kind=kLoop, calls=%fused_computation | loop fusion | flops 16515072 | bytes 3096576 | tf_op jit(solution)/shard_map/convert_element_type | solution.py:174
  61.4 7.3 %all-to-all-done = bf16[32,2,320]{2,1,0:T(2,128)(2,1)S(1)} async-done(((bf16[32,2,320]{2,1,0:T(2,128)(2,1)}), bf16[32,2,320]{2,1,0:T(2,128)(2,1)S(1)}, u32[]{:S(2)}, u32[]{:S(2)}) %all-to-all-start) | async-done | bytes 40992 | tf_op jit(solution)/shard_map/all_to_all | solution.py:201
  68.7 0.4 reshape.235
  69.1 0.4 copy.62
  70.4 1.7 %fusion.4 = bf16[2,8,21,128]{3,2,1,0:T(8,128)(2,1)S(1)} fusion(f32[2,8,1,21,640]{4,3,1,0,2:T(8,128)S(1)} %get-tuple-element.62, f32[2,8,1,21,640]{4,3,1,0,2:T(8,128)S(1)} %get-tuple-element.61, f32[640,128]{1,0:T(8,128)S(1)} %copy-done.4, f32[640,128]{1,0:T(8,128)S(1)} %copy-done.3), kind=kOutput, calls=%fused_computation.15 | convolution fusion | flops 661239808 | bytes 2461696 | tf_op jit(solution)/shard_map/wklom,mi->wkloi/dot_general | solution.py:57
  72.2 0.7 copy-done.8
  72.9 7.0 %shard_map.122 = (bf16[320,2688]{1,0:T(8,128)(2,1)}, f32[8,2688]{1,0:T(8,128)}) custom-call(s32[84]{0:T(128)} %reshape.224.slot_ref, bf16[21,4,128,128]{3,2,1,0:T(8,128)(2,1)} %add_convert_fusion.stencil_ref, bf16[4,320,128]{2,1,0:T(8,128)(2,1)} %copy-done.8, bf16[4,320,128]{2,1,0:T(8,128)(2,1)} %collective-permute-done.3.refs_1_, ...), custom_call_target="tpu_custom_call" | custom-call | tf_op jit(solution)/shard_map/pallas_call | solution.py:139
  80.0 1.5 %fusion.18 = bf16[2,8,1,2688]{3,1,2,0:T(8,128)(2,1)} fusion(bf16[2,8,1,2688]{3,1,0,2:T(8,128)(2,1)S(1)} %convert_element_type.106, f32[8,2688]{1,0:T(8,128)} %get-tuple-element.36), kind=kLoop, calls=%fused_computation.37 | loop fusion | flops 129024 | bytes 258048
  (52 shorter events, 1.5 us)
Async XLA Ops:
  0.6 40.0 %copy-start = (bf16[20,32,640]{2,1,0:T(8,128)(2,1)S(1)}, bf16[20,32,640]{2,1,0:T(8,128)(2,1)}, u32[]{:S(2)}) copy-start(bf16[20,32,640]{2,1,0:T(8,128)(2,1)} %param.12) | copy-start | bytes 2457604
  0.6 16.6 %copy-start.1 = (bf16[40,8,1,2688]{3,1,2,0:T(8,128)(2,1)S(1)}, bf16[40,8,1,2688]{3,1,2,0:T(8,128)(2,1)}, u32[]{:S(2)}) copy-start(bf16[40,8,1,2688]{3,1,2,0:T(8,128)(2,1)} %param.14) | copy-start | bytes 5160964
  0.7 9.8 %copy-start.13 = (s32[640]{0:T(1024)S(1)}, s32[640]{0:T(1024)}, u32[]{:S(2)}) copy-start(s32[640]{0:T(1024)} %param.13) | copy-start | bytes 7684
  0.7 12.2 %copy-start.12 = (bf16[3,8,1,2688]{3,1,2,0:T(8,128)(2,1)S(1)}, bf16[3,8,1,2688]{3,1,2,0:T(8,128)(2,1)}, u32[]{:S(2)}) copy-start(bf16[3,8,1,2688]{3,1,2,0:T(8,128)(2,1)} %param.15) | copy-start | bytes 387076
  0.7 12.9 %copy-start.15 = (s32[1,5,4]{1,2,0:T(4,128)S(1)}, s32[1,5,4]{1,2,0:T(4,128)}, u32[]{:S(2)}) copy-start(s32[1,5,4]{1,2,0:T(4,128)} %param.16) | copy-start | bytes 244
  0.7 13.6 %copy-start.14 = (s32[21,4]{0,1:T(4,128)S(1)}, s32[21,4]{0,1:T(4,128)}, u32[]{:S(2)}) copy-start(s32[21,4]{0,1:T(4,128)} %param.17) | copy-start | bytes 1012
  3.5 12.6 %collective-permute-start = (bf16[40,1,1,2688]{3,0,2,1:T(8,128)(2,1)S(1)}, bf16[40,1,1,2688]{3,0,2,1:T(8,128)(2,1)S(1)}, u32[]{:S(2)}, u32[]{:S(2)}) collective-permute-start(bf16[40,1,1,2688]{3,0,2,1:T(8,128)(2,1)S(1)} %copy.71), channel_id=1, source_target_pairs={{0,1},{1,2},{2,3},{3,4},{4,5},{5,6},{6,7},{7,8},{8,9},{9,10},{10,1... | collective-permute-start | bytes 645128 | tf_op jit(solution)/shard_map/ppermute | solution.py:23
  8.5 8.4 %collective-permute-start.1 = (bf16[40,1,1,2688]{3,0,2,1:T(8,128)(2,1)S(1)}, bf16[40,1,1,2688]{3,0,2,1:T(8,128)(2,1)S(1)}, u32[]{:S(2)}, u32[]{:S(2)}) collective-permute-start(bf16[40,1,1,2688]{3,0,2,1:T(8,128)(2,1)S(1)} %copy.72), channel_id=1, source_target_pairs={{1,0},{2,1},{3,2},{4,3},{5,4},{6,5},{7,6},{8,7},{9,8},{10,9},{11,1... | collective-permute-start | bytes 645128 | tf_op jit(solution)/shard_map/ppermute | solution.py:25
  17.3 7.8 %copy-start.6 = (bf16[21,4,4,128]{3,2,1,0:T(4,128)(2,1)S(1)}, bf16[21,4,4,128]{3,2,1,0:T(4,128)(2,1)}, u32[]{:S(2)}) copy-start(bf16[21,4,4,128]{3,2,1,0:T(4,128)(2,1)} %param.19) | copy-start | bytes 258052
  17.3 23.3 %copy-start.2 = (bf16[4,8,20,640]{3,1,2,0:T(8,128)(2,1)S(1)}, bf16[4,8,20,640]{3,1,2,0:T(8,128)(2,1)}, u32[]{:S(2)}) copy-start(bf16[4,8,20,640]{3,1,2,0:T(8,128)(2,1)} %param.10) | copy-start | bytes 2457604
  21.3 19.7 %copy-start.5 = (bf16[20,32,640]{2,1,0:T(8,128)(2,1)S(1)}, bf16[20,32,640]{2,1,0:T(8,128)(2,1)}, u32[]{:S(2)}) copy-start(bf16[20,32,640]{2,1,0:T(8,128)(2,1)} %param.11) | copy-start | bytes 2457604
  27.3 28.8 %copy-start.11 = (s32[21,4,128]{2,1,0:T(4,128)S(1)}, s32[21,4,128]{2,1,0:T(4,128)}, u32[]{:S(2)}) copy-start(s32[21,4,128]{2,1,0:T(4,128)} %param.18) | copy-start | bytes 129028
  27.3 44.9 %collective-permute-start.2 = (bf16[4,320,128]{2,1,0:T(8,128)(2,1)}, bf16[4,320,128]{2,1,0:T(8,128)(2,1)S(1)}, u32[]{:S(2)}, u32[]{:S(2)}) collective-permute-start(bf16[4,320,128]{2,1,0:T(8,128)(2,1)} %get-tuple-element.30), channel_id=1, source_target_pairs={{32,0},{48,16},{64,32},{80,48},{96,64},{112,80},{128,96},{144,112}... | collective-permute-start | bytes 983048 | tf_op jit(solution)/shard_map/ppermute | solution.py:35
  28.7 43.5 %collective-permute-start.3 = (bf16[4,320,128]{2,1,0:T(8,128)(2,1)}, bf16[4,320,128]{2,1,0:T(8,128)(2,1)}, u32[]{:S(2)}, u32[]{:S(2)}) collective-permute-start(bf16[4,320,128]{2,1,0:T(8,128)(2,1)} %get-tuple-element.31), channel_id=1, source_target_pairs={{16,0},{32,16},{48,32},{64,48},{80,64},{96,80},{112,96},{128,112},... | collective-permute-start | bytes 983048 | tf_op jit(solution)/shard_map/ppermute | solution.py:35
  30.0 42.2 %collective-permute-start.4 = (bf16[4,320,128]{2,1,0:T(8,128)(2,1)}, bf16[4,320,128]{2,1,0:T(8,128)(2,1)}, u32[]{:S(2)}, u32[]{:S(2)}) collective-permute-start(bf16[4,320,128]{2,1,0:T(8,128)(2,1)} %get-tuple-element.33), channel_id=1, source_target_pairs={{0,16},{16,32},{32,48},{48,64},{64,80},{80,96},{96,112},{112,128},... | collective-permute-start | bytes 983048 | tf_op jit(solution)/shard_map/ppermute | solution.py:35
  34.8 37.5 %collective-permute-start.5 = (bf16[4,320,128]{2,1,0:T(8,128)(2,1)}, bf16[4,320,128]{2,1,0:T(8,128)(2,1)}, u32[]{:S(2)}, u32[]{:S(2)}) collective-permute-start(bf16[4,320,128]{2,1,0:T(8,128)(2,1)} %get-tuple-element.34), channel_id=1, source_target_pairs={{0,32},{16,48},{32,64},{48,80},{64,96},{80,112},{96,128},{112,144}... | collective-permute-start | bytes 983048 | tf_op jit(solution)/shard_map/ppermute | solution.py:35
  43.1 27.0 %copy-start.9 = (f32[21,640]{1,0:T(8,128)S(1)}, f32[21,640]{1,0:T(8,128)}, u32[]{:S(2)}) copy-start(f32[21,640]{1,0:T(8,128)} %get-tuple-element.72) | copy-start | bytes 161284
  43.1 27.0 %copy-start.10 = (f32[21,640]{1,0:T(8,128)S(1)}, f32[21,640]{1,0:T(8,128)}, u32[]{:S(2)}) copy-start(f32[21,640]{1,0:T(8,128)} %get-tuple-element.73) | copy-start | bytes 161284
  43.1 25.6 %all-to-all-start = ((bf16[32,2,320]{2,1,0:T(2,128)(2,1)}), bf16[32,2,320]{2,1,0:T(2,128)(2,1)S(1)}, u32[]{:S(2)}, u32[]{:S(2)}) async-start(bf16[32,2,320]{2,1,0:T(2,128)(2,1)} %reshape.234), calls=%async_computation | async-start | bytes 98304 | tf_op jit(solution)/shard_map/all_to_all | solution.py:201
  61.4 9.0 %copy-start.3 = (f32[640,128]{1,0:T(8,128)S(1)}, f32[640,128]{1,0:T(8,128)}, u32[]{:S(2)}) copy-start(f32[640,128]{1,0:T(8,128)} %get-tuple-element.74) | copy-start | bytes 983044
  61.4 9.0 %copy-start.4 = (f32[640,128]{1,0:T(8,128)S(1)}, f32[640,128]{1,0:T(8,128)}, u32[]{:S(2)}) copy-start(f32[640,128]{1,0:T(8,128)} %get-tuple-element.75) | copy-start | bytes 983044
  72.2 9.4 %copy-start.7 = (bf16[2,8,1,2688]{3,1,0,2:T(8,128)(2,1)}, bf16[2,8,1,2688]{3,1,0,2:T(8,128)(2,1)S(1)}, u32[]{:S(2)}) copy-start(bf16[2,8,1,2688]{3,1,0,2:T(8,128)(2,1)S(1)} %convert_element_type.106) | copy-start | bytes 258052
  72.2 0.7 copy-start.8

commit v10 on v9

--- a/solution.py
+++ b/solution.py
@@ -10,6 +10,8 @@
 WAVES = 640
 NLON = 2688
 BLK = 128
+BAND = ("band_major", "band_minor")
+BAND_MINOR = 4
 
 
 def extended(cells, sides, width):
@@ -30,7 +32,7 @@
 
 
 def shifted(value, axis, steps):
-    count = lax.axis_size(axis)
+    count = lax.axis_size(axis[0]) * lax.axis_size(axis[1])
     leading, last = (max(0, -steps), min(count, count - steps))
     return lax.ppermute(value, axis, [(source, source + steps) for source in range(leading, last)])
 
@@ -179,8 +181,8 @@
         if shift_by == 0:
             pieces.append(outgoing[offset_index])
         else:
-            pieces.append(shifted(outgoing[offset_index], "band", shift_by))
-    band_here = lax.axis_index("band")
+            pieces.append(shifted(outgoing[offset_index], BAND, shift_by))
+    band_here = lax.axis_index(BAND[0]) * lax.axis_size(BAND[1]) + lax.axis_index(BAND[1])
     wave_local = spectral.shape[2]
     own_waves = lax.dynamic_slice_in_dim(wave_numbers, band_here * wave_local, wave_local, 0)
     value_terms = jnp.einsum(
@@ -198,7 +200,12 @@
             slope_terms[3] + factor * value_terms[0],
         ]
     ).astype(jnp.bfloat16)
-    received = lax.all_to_all(coefficients, "band", split_axis=2, concat_axis=3, tiled=True)
+    minor = lax.axis_size(BAND[1])
+    parts, levels_here, lats, slots = coefficients.shape
+    staged = coefficients.reshape(parts, levels_here, lats // minor, minor, slots)
+    staged = lax.all_to_all(staged, BAND[1], split_axis=3, concat_axis=4, tiled=True)
+    staged = lax.all_to_all(staged, BAND[0], split_axis=2, concat_axis=4, tiled=True)
+    received = staged.reshape(parts, levels_here, 1, staged.shape[-1])
     wind_grid = synthesis(received, wave_numbers, NLON).astype(jnp.bfloat16)
     flat_new, average = apply_stencil(depart_slot.reshape(-1), stencil, pieces, bin_count, level_count)
     aerosol_new = flat_new.reshape(bin_count, level_count, lat_count, lon_count)
@@ -208,25 +215,30 @@
 
 
 def solution(mesh):
+    devices = mesh.devices
+    split = jax.sharding.Mesh(
+        devices.reshape(devices.shape[0] // BAND_MINOR, BAND_MINOR, devices.shape[1]),
+        (BAND[0], BAND[1], mesh.axis_names[1]),
+    )
     return jax.shard_map(
         shards,
-        mesh=mesh,
+        mesh=split,
         in_specs=(
-            P(None, "lev", "band", None),
-            P("band", None, None),
-            P("band", None, None),
+            P(None, "lev", BAND, None),
+            P(BAND, None, None),
+            P(BAND, None, None),
             P(),
-            P(None, "lev", "band", None),
-            P(None, "lev", "band", None),
-            P("band", None, None),
-            P("band", None),
-            P("band", None, None),
-            P("band", None, None, None),
+            P(None, "lev", BAND, None),
+            P(None, "lev", BAND, None),
+            P(BAND, None, None),
+            P(BAND, None),
+            P(BAND, None, None),
+            P(BAND, None, None, None),
         ),
         out_specs=(
-            P(None, "lev", "band", None),
-            P(None, "lev", "band", None),
-            P(None, "lev", "band", None),
+            P(None, "lev", BAND, None),
+            P(None, "lev", BAND, None),
+            P(None, "lev", BAND, None),
         ),
         check_vma=False,
     )

time: 82.2 us -> 85.2 us (1.036)
  the two profiles are of different devices: /device:TPU:25 before, /device:TPU:30 now
where the time goes in v10:
time: 85.2 us; the launch traced here: 84.6 us
  starting transfers between devices  34.7 us (41%)
  other arithmetic  14.2 us (17%)
  local copies, waits for them, and re-layouts  11 us (13%)
  Pallas kernels  10.8 us (13%)
  waiting for transfers between devices  10.3 us (12%)
  matrix products  2.5 us (3%)
  between operations  1.14 us (1%)
    ppermute x4, starting transfers between devices, shifted(): lax.ppermute(value, axis, [(source, source + steps) for source in range(l...  14.1 us
    all_to_all x1, starting transfers between devices, shards(): lax.all_to_all(staged, BAND[0], split_axis=2, concat_axis=4, tiled=True)  10.3 us
    all_to_all x1, waiting for transfers between devices, shards(): lax.all_to_all(staged, BAND[0], split_axis=2, concat_axis=4, tiled=True)  10.3 us
    pallas_call x1, Pallas kernels, apply_stencil(): pl.pallas_call(body, grid_spec=grid_spec, out_shape=out_shape, compiler_p...  7.05 us
    all_to_all x1, starting transfers between devices, shards(): lax.all_to_all(staged, BAND[1], split_axis=3, concat_axis=4, tiled=True)  4.77 us
    convert_element_type x1, other arithmetic, shards(): stencil = stencil_matrix(depart_offset, depart_weight).astype(jnp.bfloat16)  4.04 us
    reshape x1, other arithmetic, shards(): vertical_sum.astype(jnp.bfloat16).reshape(rows, lat_count * lon_count)  4.02 us
    pallas_call x1, Pallas kernels, pack_blocks(): pl.pallas_call(body, grid_spec=grid_spec, out_shape=out_shape)  3.72 us
  transfers between devices with their start and end apart: 8, of which 1 were waited for; matrix products, arithmetic and copies ran while one was open for 16% of the time, Pallas kernels for 0%

profile of v10, /device:TPU:30, one launch (start us, length us, event | category | flops | bytes accessed | tf_op | source)
XLA Modules:
  0.0 84.6 jit_solution(10394685257109874040)
XLA Ops:
  0.7 2.8 %fusion.33 = (bf16[40,1,1,2688]{3,1,2,0:T(2,128)(2,1)S(1)}, bf16[40,1,1,2688]{3,1,2,0:T(2,128)(2,1)S(1)}) fusion(bf16[40,8,1,2688]{3,1,2,0:T(8,128)(2,1)} %param.14), kind=kLoop, calls=%fused_computation.77 | loop fusion | bytes 860160 | tf_op jit(solution)/shard_map/slice | solution.py:22
  3.5 1.9 %collective-permute-start = (bf16[40,1,1,2688]{3,0,2,1:T(8,128)(2,1)S(1)}, bf16[40,1,1,2688]{3,0,2,1:T(8,128)(2,1)S(1)}, u32[]{:S(2)}, u32[]{:S(2)}) collective-permute-start(bf16[40,1,1,2688]{3,0,2,1:T(8,128)(2,1)S(1)} %copy.74), channel_id=1, source_target_pairs={{0,1},{1,2},{2,3},{3,4},{4,5},{5,6},{6,7},{7,8},{8,9},{9,10},{10,1... | collective-permute-start | bytes 645128 | tf_op jit(solution)/shard_map/ppermute | solution.py:25
  5.5 3.6 %collective-permute-start.1 = (bf16[40,1,1,2688]{3,0,2,1:T(8,128)(2,1)S(1)}, bf16[40,1,1,2688]{3,0,2,1:T(8,128)(2,1)S(1)}, u32[]{:S(2)}, u32[]{:S(2)}) collective-permute-start(bf16[40,1,1,2688]{3,0,2,1:T(8,128)(2,1)S(1)} %copy.75), channel_id=1, source_target_pairs={{1,0},{2,1},{3,2},{4,3},{5,4},{6,5},{7,6},{8,7},{9,8},{10,9},{11,1... | collective-permute-start | bytes 645128 | tf_op jit(solution)/shard_map/ppermute | solution.py:27
  9.2 2.3 %fusion.16 = (f32[640,128]{1,0:T(8,128)}, f32[640,128]{1,0:T(8,128)}) fusion(s32[640]{0:T(1024)S(1)} %copy-done.20), kind=kLoop, calls=%fused_computation.32 | loop fusion | flops 737280 | bytes 657920 | tf_op jit(solution)/shard_map/cos | solution.py:58
  11.5 0.7 slice_bitcast_fusion.2
  12.3 0.6 min.12.listed_ref
  13.0 0.7 reshape.238.slot_ref
  13.8 1.0 %cosine_multiply_fusion = (f32[21,640]{1,0:T(8,128)}, f32[21,640]{1,0:T(8,128)}) fusion(s32[21]{0:T(128)S(1)} %iota_multiply_fusion, s32[640]{0:T(1024)S(1)} %copy-done.20, f32[640]{0:T(1024)S(1)} %compare_select_fusion), kind=kLoop, calls=%fused_computation.58 | loop fusion | flops 147840 | bytes 112724 | tf_op jit(solution)/shard_map/mul | solution.py:50
  14.8 0.3 copy.52
  15.1 0.3 copy.54
  15.5 4.0 %fusion.3.source_ref = bf16[320,2688]{1,0:T(8,128)(2,1)} fusion(bf16[40,8,1,2688]{3,1,2,0:T(8,128)(2,1)S(1)} %copy-done.1, bf16[40,1,1,2688]{3,1,2,0:T(2,128)(2,1)S(1)} %copy.54, bf16[40,1,1,2688]{3,1,2,0:T(2,128)(2,1)S(1)} %copy.52, f32[8,2688]{1,0:T(8,128)} %get-tuple-element.56, f32[8,2688]{1,0:T(8,128)} %get-tuple-element.57, ...), kind=kLoop, calls=%fused_computation.10 | loop fusion | flops 12902400 | bytes 4128768 | tf_op jit(solution)/shard_map/reshape | solution.py:166
  19.5 3.7 %shard_map.121 = (bf16[4,320,128]{2,1,0:T(8,128)(2,1)}, bf16[4,320,128]{2,1,0:T(8,128)(2,1)}, bf16[4,320,128]{2,1,0:T(8,128)(2,1)}, bf16[4,320,128]{2,1,0:T(8,128)(2,1)}, bf16[4,320,128]{2,1,0:T(8,128)(2,1)}) custom-call(s32[20]{0:T(128)} %min.12.listed_ref, bf16[320,2688]{1,0:T(8,128)(2,1)} %fusion.3.source_ref), custom_call_target="tpu_custom_call" | custom-call | tf_op jit(solution)/shard_map/pallas_call | solution.py:93
  23.3 0.8 slice_convert_fusion.3
  24.0 0.4 convolution_bitcast_fusion.1
  24.5 0.4 convolution_bitcast_fusion
  25.7 1.1 %reshape.249 = bf16[4,2,2560]{2,1,0:T(2,128)(2,1)} reshape(bf16[4,4,8,8,20]{4,3,2,1,0:T(8,128)(2,1)S(1)} %copy_bitcast_fusion) | data formatting | bytes 81920
  26.8 4.8 %all-to-all-start = ((bf16[4,2,2560]{2,1,0:T(2,128)(2,1)}), bf16[4,2,2560]{2,1,0:T(2,128)(2,1)S(1)}, u32[]{:S(2)}, u32[]{:S(2)}) async-start(bf16[4,2,2560]{2,1,0:T(2,128)(2,1)} %reshape.249), calls=%async_computation | async-start | bytes 81920 | tf_op jit(solution)/shard_map/all_to_all | solution.py:206
  31.6 3.4 %collective-permute-start.2 = (bf16[4,320,128]{2,1,0:T(8,128)(2,1)}, bf16[4,320,128]{2,1,0:T(8,128)(2,1)S(1)}, u32[]{:S(2)}, u32[]{:S(2)}) collective-permute-start(bf16[4,320,128]{2,1,0:T(8,128)(2,1)} %get-tuple-element.30), channel_id=1, source_target_pairs={{32,0},{48,16},{64,32},{80,48},{96,64},{112,80},{128,96},{144,112}... | collective-permute-start | bytes 983048 | tf_op jit(solution)/shard_map/ppermute | solution.py:37
  35.0 1.9 %collective-permute-start.3 = (bf16[4,320,128]{2,1,0:T(8,128)(2,1)}, bf16[4,320,128]{2,1,0:T(8,128)(2,1)S(1)}, u32[]{:S(2)}, u32[]{:S(2)}) collective-permute-start(bf16[4,320,128]{2,1,0:T(8,128)(2,1)} %get-tuple-element.31), channel_id=1, source_target_pairs={{16,0},{32,16},{48,32},{64,48},{80,64},{96,80},{112,96},{128,112},... | collective-permute-start | bytes 983048 | tf_op jit(solution)/shard_map/ppermute | solution.py:37
  36.9 6.0 %collective-permute-start.4 = (bf16[4,320,128]{2,1,0:T(8,128)(2,1)}, bf16[4,320,128]{2,1,0:T(8,128)(2,1)S(1)}, u32[]{:S(2)}, u32[]{:S(2)}) collective-permute-start(bf16[4,320,128]{2,1,0:T(8,128)(2,1)} %get-tuple-element.33), channel_id=1, source_target_pairs={{0,16},{16,32},{32,48},{48,64},{64,80},{80,96},{96,112},{112,128},... | collective-permute-start | bytes 983048 | tf_op jit(solution)/shard_map/ppermute | solution.py:37
  43.0 2.8 %collective-permute-start.5 = (bf16[4,320,128]{2,1,0:T(8,128)(2,1)}, bf16[4,320,128]{2,1,0:T(8,128)(2,1)S(1)}, u32[]{:S(2)}, u32[]{:S(2)}) collective-permute-start(bf16[4,320,128]{2,1,0:T(8,128)(2,1)} %get-tuple-element.34), channel_id=1, source_target_pairs={{0,32},{16,48},{32,64},{48,80},{64,96},{80,112},{96,128},{112,144}... | collective-permute-start | bytes 983048 | tf_op jit(solution)/shard_map/ppermute | solution.py:37
  45.7 0.6 reshape.250
  46.6 0.8 reshape.248
  47.4 10.3 %all-to-all-start.1 = ((bf16[4,8,8,1,80]{4,1,0,3,2:T(8,128)(2,1)}), bf16[4,8,8,1,80]{4,1,0,3,2:T(8,128)(2,1)S(1)}, u32[]{:S(2)}, u32[]{:S(2)}) async-start(bf16[4,8,8,1,80]{4,1,0,3,2:T(8,128)(2,1)} %reshape.248), calls=%async_computation.1 | async-start | bytes 131072 | tf_op jit(solution)/shard_map/all_to_all | solution.py:207
  57.7 4.0 %add_convert_fusion.stencil_ref = bf16[21,4,128,128]{3,2,1,0:T(8,128)(2,1)} fusion(f32[21,4,128]{2,1,0:T(4,128)S(1)} %bitcast.66, s32[21,4,128]{2,1,0:T(4,128)S(1)} %get-tuple-element.67, f32[21,4,128]{2,1,0:T(4,128)S(1)} %bitcast.67, s32[21,4,128]{2,1,0:T(4,128)S(1)} %get-tuple-element.68, f32[21,4,128]{2,1,0:T(4,128)S(1)} %bitcast.68, ...), kind=kLoop, calls=%fused_computation | loop fusion | flops 16515072 | bytes 3096576 | tf_op jit(solution)/shard_map/convert_element_type | solution.py:176
  61.8 10.3 %all-to-all-done.1 = bf16[4,8,8,1,80]{4,1,0,3,2:T(8,128)(2,1)S(1)} async-done(((bf16[4,8,8,1,80]{4,1,0,3,2:T(8,128)(2,1)}), bf16[4,8,8,1,80]{4,1,0,3,2:T(8,128)(2,1)S(1)}, u32[]{:S(2)}, u32[]{:S(2)}) %all-to-all-start.1) | async-done | bytes 40992 | tf_op jit(solution)/shard_map/all_to_all | solution.py:207
  72.2 0.2 multiply_subtract_fusion
  72.5 1.7 %fusion.4 = bf16[2,8,21,128]{3,2,1,0:T(8,128)(2,1)S(1)} fusion(f32[2,8,1,21,640]{4,3,1,0,2:T(8,128)S(1)} %get-tuple-element.59, f32[2,8,1,21,640]{4,3,1,0,2:T(8,128)S(1)} %get-tuple-element.58, f32[640,128]{1,0:T(8,128)S(1)} %copy-done.4, f32[640,128]{1,0:T(8,128)S(1)} %copy-done.3), kind=kOutput, calls=%fused_computation.15 | convolution fusion | flops 661239808 | bytes 2461696 | tf_op jit(solution)/shard_map/wklom,mi->wkloi/dot_general | solution.py:59
  74.4 0.7 copy-done.8
  75.3 0.7 copy-done.11
  76.0 7.0 %shard_map.122 = (bf16[320,2688]{1,0:T(8,128)(2,1)}, f32[8,2688]{1,0:T(8,128)}) custom-call(s32[84]{0:T(128)} %reshape.238.slot_ref, bf16[21,4,128,128]{3,2,1,0:T(8,128)(2,1)} %add_convert_fusion.stencil_ref, bf16[4,320,128]{2,1,0:T(8,128)(2,1)} %copy-done.8, bf16[4,320,128]{2,1,0:T(8,128)(2,1)} %copy-done.9, ...), custom_call_target="tpu_custom_call" | custom-call | tf_op jit(solution)/shard_map/pallas_call | solution.py:141
  83.1 1.5 %fusion.18 = bf16[2,8,1,2688]{3,1,2,0:T(8,128)(2,1)} fusion(bf16[2,8,1,2688]{3,1,0,2:T(8,128)(2,1)S(1)} %convert_element_type.107, f32[8,2688]{1,0:T(8,128)} %get-tuple-element.36), kind=kLoop, calls=%fused_computation.37 | loop fusion | flops 129024 | bytes 258048
  (72 shorter events, 2.0 us)
Async XLA Ops:
  0.6 23.4 %copy-start = (bf16[20,32,640]{2,1,0:T(8,128)(2,1)S(1)}, bf16[20,32,640]{2,1,0:T(8,128)(2,1)}, u32[]{:S(2)}) copy-start(bf16[20,32,640]{2,1,0:T(8,128)(2,1)} %param.12) | copy-start | bytes 2457604
  0.6 14.8 %copy-start.1 = (bf16[40,8,1,2688]{3,1,2,0:T(8,128)(2,1)S(1)}, bf16[40,8,1,2688]{3,1,2,0:T(8,128)(2,1)}, u32[]{:S(2)}) copy-start(bf16[40,8,1,2688]{3,1,2,0:T(8,128)(2,1)} %param.14) | copy-start | bytes 5160964
  0.7 8.5 %copy-start.20 = (s32[640]{0:T(1024)S(1)}, s32[640]{0:T(1024)}, u32[]{:S(2)}) copy-start(s32[640]{0:T(1024)} %param.13) | copy-start | bytes 7684
  0.7 10.8 %copy-start.19 = (bf16[3,8,1,2688]{3,1,2,0:T(8,128)(2,1)S(1)}, bf16[3,8,1,2688]{3,1,2,0:T(8,128)(2,1)}, u32[]{:S(2)}) copy-start(bf16[3,8,1,2688]{3,1,2,0:T(8,128)(2,1)} %param.15) | copy-start | bytes 387076
  0.7 11.5 %copy-start.22 = (s32[1,5,4]{1,2,0:T(4,128)S(1)}, s32[1,5,4]{1,2,0:T(4,128)}, u32[]{:S(2)}) copy-start(s32[1,5,4]{1,2,0:T(4,128)} %param.16) | copy-start | bytes 244
  0.7 12.2 %copy-start.21 = (s32[21,4]{0,1:T(4,128)S(1)}, s32[21,4]{0,1:T(4,128)}, u32[]{:S(2)}) copy-start(s32[21,4]{0,1:T(4,128)} %param.17) | copy-start | bytes 1012
  3.5 11.3 %collective-permute-start = (bf16[40,1,1,2688]{3,0,2,1:T(8,128)(2,1)S(1)}, bf16[40,1,1,2688]{3,0,2,1:T(8,128)(2,1)S(1)}, u32[]{:S(2)}, u32[]{:S(2)}) collective-permute-start(bf16[40,1,1,2688]{3,0,2,1:T(8,128)(2,1)S(1)} %copy.74), channel_id=1, source_target_pairs={{0,1},{1,2},{2,3},{3,4},{4,5},{5,6},{6,7},{7,8},{8,9},{9,10},{10,1... | collective-permute-start | bytes 645128 | tf_op jit(solution)/shard_map/ppermute | solution.py:25
  5.5 9.6 %collective-permute-start.1 = (bf16[40,1,1,2688]{3,0,2,1:T(8,128)(2,1)S(1)}, bf16[40,1,1,2688]{3,0,2,1:T(8,128)(2,1)S(1)}, u32[]{:S(2)}, u32[]{:S(2)}) collective-permute-start(bf16[40,1,1,2688]{3,0,2,1:T(8,128)(2,1)S(1)} %copy.75), channel_id=1, source_target_pairs={{1,0},{2,1},{3,2},{4,3},{5,4},{6,5},{7,6},{8,7},{9,8},{10,9},{11,1... | collective-permute-start | bytes 645128 | tf_op jit(solution)/shard_map/ppermute | solution.py:27
  15.5 7.8 %copy-start.6 = (bf16[21,4,4,128]{3,2,1,0:T(4,128)(2,1)S(1)}, bf16[21,4,4,128]{3,2,1,0:T(4,128)(2,1)}, u32[]{:S(2)}) copy-start(bf16[21,4,4,128]{3,2,1,0:T(4,128)(2,1)} %param.19) | copy-start | bytes 258052
  15.5 8.5 %copy-start.2 = (bf16[4,8,20,640]{3,1,2,0:T(8,128)(2,1)S(1)}, bf16[4,8,20,640]{3,1,2,0:T(8,128)(2,1)}, u32[]{:S(2)}) copy-start(bf16[4,8,20,640]{3,1,2,0:T(8,128)(2,1)} %param.10) | copy-start | bytes 2457604
  19.5 4.9 %copy-start.5 = (bf16[20,32,640]{2,1,0:T(8,128)(2,1)S(1)}, bf16[20,32,640]{2,1,0:T(8,128)(2,1)}, u32[]{:S(2)}) copy-start(bf16[20,32,640]{2,1,0:T(8,128)(2,1)} %param.11) | copy-start | bytes 2457604
  24.0 7.5 %copy-start.14 = (s32[21,4,128]{2,1,0:T(4,128)S(1)}, s32[21,4,128]{2,1,0:T(4,128)}, u32[]{:S(2)}) copy-start(s32[21,4,128]{2,1,0:T(4,128)} %param.18) | copy-start | bytes 129028
  24.5 33.2 %copy-start.15 = (f32[21,4,1,128]{3,2,1,0:T(1,128)S(1)}, f32[21,4,1,128]{3,2,1,0:T(1,128)}, u32[]{:S(2)}) copy-start(f32[21,4,1,128]{3,2,1,0:T(1,128)} %get-tuple-element.60) | copy-start | bytes 129028
  24.9 32.8 %copy-start.16 = (f32[21,4,1,128]{3,2,1,0:T(1,128)S(1)}, f32[21,4,1,128]{3,2,1,0:T(1,128)}, u32[]{:S(2)}) copy-start(f32[21,4,1,128]{3,2,1,0:T(1,128)} %get-tuple-element.61) | copy-start | bytes 129028
  24.9 32.8 %copy-start.17 = (f32[21,4,1,128]{3,2,1,0:T(1,128)S(1)}, f32[21,4,1,128]{3,2,1,0:T(1,128)}, u32[]{:S(2)}) copy-start(f32[21,4,1,128]{3,2,1,0:T(1,128)} %get-tuple-element.62) | copy-start | bytes 129028
  24.9 32.8 %copy-start.18 = (f32[21,4,1,128]{3,2,1,0:T(1,128)S(1)}, f32[21,4,1,128]{3,2,1,0:T(1,128)}, u32[]{:S(2)}) copy-start(f32[21,4,1,128]{3,2,1,0:T(1,128)} %get-tuple-element.63) | copy-start | bytes 129028
  25.7 46.5 %copy-start.12 = (f32[21,640]{1,0:T(8,128)S(1)}, f32[21,640]{1,0:T(8,128)}, u32[]{:S(2)}) copy-start(f32[21,640]{1,0:T(8,128)} %get-tuple-element.69) | copy-start | bytes 161284
  25.7 46.5 %copy-start.13 = (f32[21,640]{1,0:T(8,128)S(1)}, f32[21,640]{1,0:T(8,128)}, u32[]{:S(2)}) copy-start(f32[21,640]{1,0:T(8,128)} %get-tuple-element.70) | copy-start | bytes 161284
  26.8 18.9 %all-to-all-start = ((bf16[4,2,2560]{2,1,0:T(2,128)(2,1)}), bf16[4,2,2560]{2,1,0:T(2,128)(2,1)S(1)}, u32[]{:S(2)}, u32[]{:S(2)}) async-start(bf16[4,2,2560]{2,1,0:T(2,128)(2,1)} %reshape.249), calls=%async_computation | async-start | bytes 81920 | tf_op jit(solution)/shard_map/all_to_all | solution.py:206
  31.6 42.7 %collective-permute-start.2 = (bf16[4,320,128]{2,1,0:T(8,128)(2,1)}, bf16[4,320,128]{2,1,0:T(8,128)(2,1)S(1)}, u32[]{:S(2)}, u32[]{:S(2)}) collective-permute-start(bf16[4,320,128]{2,1,0:T(8,128)(2,1)} %get-tuple-element.30), channel_id=1, source_target_pairs={{32,0},{48,16},{64,32},{80,48},{96,64},{112,80},{128,96},{144,112}... | collective-permute-start | bytes 983048 | tf_op jit(solution)/shard_map/ppermute | solution.py:37
  35.0 39.3 %collective-permute-start.3 = (bf16[4,320,128]{2,1,0:T(8,128)(2,1)}, bf16[4,320,128]{2,1,0:T(8,128)(2,1)S(1)}, u32[]{:S(2)}, u32[]{:S(2)}) collective-permute-start(bf16[4,320,128]{2,1,0:T(8,128)(2,1)} %get-tuple-element.31), channel_id=1, source_target_pairs={{16,0},{32,16},{48,32},{64,48},{80,64},{96,80},{112,96},{128,112},... | collective-permute-start | bytes 983048 | tf_op jit(solution)/shard_map/ppermute | solution.py:37
  36.9 37.4 %collective-permute-start.4 = (bf16[4,320,128]{2,1,0:T(8,128)(2,1)}, bf16[4,320,128]{2,1,0:T(8,128)(2,1)S(1)}, u32[]{:S(2)}, u32[]{:S(2)}) collective-permute-start(bf16[4,320,128]{2,1,0:T(8,128)(2,1)} %get-tuple-element.33), channel_id=1, source_target_pairs={{0,16},{16,32},{32,48},{48,64},{64,80},{80,96},{96,112},{112,128},... | collective-permute-start | bytes 983048 | tf_op jit(solution)/shard_map/ppermute | solution.py:37
  43.0 31.4 %collective-permute-start.5 = (bf16[4,320,128]{2,1,0:T(8,128)(2,1)}, bf16[4,320,128]{2,1,0:T(8,128)(2,1)S(1)}, u32[]{:S(2)}, u32[]{:S(2)}) collective-permute-start(bf16[4,320,128]{2,1,0:T(8,128)(2,1)} %get-tuple-element.34), channel_id=1, source_target_pairs={{0,32},{16,48},{32,64},{48,80},{64,96},{80,112},{96,128},{112,144}... | collective-permute-start | bytes 983048 | tf_op jit(solution)/shard_map/ppermute | solution.py:37
  47.4 24.7 %all-to-all-start.1 = ((bf16[4,8,8,1,80]{4,1,0,3,2:T(8,128)(2,1)}), bf16[4,8,8,1,80]{4,1,0,3,2:T(8,128)(2,1)S(1)}, u32[]{:S(2)}, u32[]{:S(2)}) async-start(bf16[4,8,8,1,80]{4,1,0,3,2:T(8,128)(2,1)} %reshape.248), calls=%async_computation.1 | async-start | bytes 131072 | tf_op jit(solution)/shard_map/all_to_all | solution.py:207
  57.7 14.7 %copy-start.3 = (f32[640,128]{1,0:T(8,128)S(1)}, f32[640,128]{1,0:T(8,128)}, u32[]{:S(2)}) copy-start(f32[640,128]{1,0:T(8,128)} %get-tuple-element.71) | copy-start | bytes 983044
  57.7 14.7 %copy-start.4 = (f32[640,128]{1,0:T(8,128)S(1)}, f32[640,128]{1,0:T(8,128)}, u32[]{:S(2)}) copy-start(f32[640,128]{1,0:T(8,128)} %get-tuple-element.72) | copy-start | bytes 983044
  74.3 10.3 %copy-start.7 = (bf16[2,8,1,2688]{3,1,0,2:T(8,128)(2,1)}, bf16[2,8,1,2688]{3,1,0,2:T(8,128)(2,1)S(1)}, u32[]{:S(2)}) copy-start(bf16[2,8,1,2688]{3,1,0,2:T(8,128)(2,1)S(1)} %convert_element_type.107) | copy-start | bytes 258052
  74.3 0.7 copy-start.8
  74.3 0.8 copy-start.9
  74.3 0.9 %copy-start.10 = (bf16[4,320,128]{2,1,0:T(8,128)(2,1)}, bf16[4,320,128]{2,1,0:T(8,128)(2,1)S(1)}, u32[]{:S(2)}) copy-start(bf16[4,320,128]{2,1,0:T(8,128)(2,1)S(1)} %collective-permute-done.4.refs_3_) | copy-start | bytes 983044
  75.3 0.7 copy-start.11

commit v11 on v9

--- a/solution.py
+++ b/solution.py
@@ -172,14 +172,6 @@
         )
     )
     stencil = stencil_matrix(depart_offset, depart_weight).astype(jnp.bfloat16)
-    reach_bands = offsets // 2
-    pieces = []
-    for offset_index in range(offsets):
-        shift_by = offset_index - reach_bands
-        if shift_by == 0:
-            pieces.append(outgoing[offset_index])
-        else:
-            pieces.append(shifted(outgoing[offset_index], "band", shift_by))
     band_here = lax.axis_index("band")
     wave_local = spectral.shape[2]
     own_waves = lax.dynamic_slice_in_dim(wave_numbers, band_here * wave_local, wave_local, 0)
@@ -199,6 +191,15 @@
         ]
     ).astype(jnp.bfloat16)
     received = lax.all_to_all(coefficients, "band", split_axis=2, concat_axis=3, tiled=True)
+    outgoing, received = lax.optimization_barrier((outgoing, received))
+    reach_bands = offsets // 2
+    pieces = []
+    for offset_index in range(offsets):
+        shift_by = offset_index - reach_bands
+        if shift_by == 0:
+            pieces.append(outgoing[offset_index])
+        else:
+            pieces.append(shifted(outgoing[offset_index], "band", shift_by))
     wind_grid = synthesis(received, wave_numbers, NLON).astype(jnp.bfloat16)
     flat_new, average = apply_stencil(depart_slot.reshape(-1), stencil, pieces, bin_count, level_count)
     aerosol_new = flat_new.reshape(bin_count, level_count, lat_count, lon_count)

time: 82.2 us -> 90.7 us (1.10)
  the two profiles are of different devices: /device:TPU:25 before, /device:TPU:90 now
where the time goes in v11:
time: 90.7 us; the launch traced here: 90.1 us
  starting transfers between devices  33.6 us (37%)
  waiting for transfers between devices  18.2 us (20%)
  other arithmetic  15 us (17%)
  Pallas kernels  10.8 us (12%)
  local copies, waits for them, and re-layouts  8.88 us (10%)
  matrix products  2.5 us (3%)
  between operations  1.11 us (1%)
    ppermute x4, starting transfers between devices, shifted(): lax.ppermute(value, axis, [(source, source + steps) for source in range(l...  15.5 us
    ppermute x4, waiting for transfers between devices, shifted(): lax.ppermute(value, axis, [(source, source + steps) for source in range(l...  14.4 us
    all_to_all x1, starting transfers between devices, shards(): lax.all_to_all(coefficients, 'band', split_axis=2, concat_axis=3, tiled=T...  12.6 us
    pallas_call x1, Pallas kernels, apply_stencil(): pl.pallas_call(body, grid_spec=grid_spec, out_shape=out_shape, compiler_p...  7.06 us
    convert_element_type x1, other arithmetic, shards(): stencil = stencil_matrix(depart_offset, depart_weight).astype(jnp.bfloat16)  4.08 us
    reshape x1, other arithmetic, shards(): vertical_sum.astype(jnp.bfloat16).reshape(rows, lat_count * lon_count)  4.02 us
    all_to_all x1, waiting for transfers between devices, shards(): lax.all_to_all(coefficients, 'band', split_axis=2, concat_axis=3, tiled=T...  3.85 us
    pallas_call x1, Pallas kernels, pack_blocks(): pl.pallas_call(body, grid_spec=grid_spec, out_shape=out_shape)  3.74 us
  transfers between devices with their start and end apart: 7, of which 4 were waited for; matrix products, arithmetic and copies ran while one was open for 13% of the time, Pallas kernels for 0%

profile of v11, /device:TPU:90, one launch (start us, length us, event | category | flops | bytes accessed | tf_op | source)
XLA Modules:
  0.0 90.1 jit_solution(13468607519114317855)
XLA Ops:
  0.7 2.8 %fusion.33 = (bf16[40,1,1,2688]{3,1,2,0:T(2,128)(2,1)S(1)}, bf16[40,1,1,2688]{3,1,2,0:T(2,128)(2,1)S(1)}) fusion(bf16[40,8,1,2688]{3,1,2,0:T(8,128)(2,1)} %param.14), kind=kLoop, calls=%fused_computation.77 | loop fusion | bytes 860160 | tf_op jit(solution)/shard_map/slice | solution.py:20
  3.5 1.9 %collective-permute-start = (bf16[40,1,1,2688]{3,0,2,1:T(8,128)(2,1)S(1)}, bf16[40,1,1,2688]{3,0,2,1:T(8,128)(2,1)S(1)}, u32[]{:S(2)}, u32[]{:S(2)}) collective-permute-start(bf16[40,1,1,2688]{3,0,2,1:T(8,128)(2,1)S(1)} %copy.57), channel_id=1, source_target_pairs={{0,1},{1,2},{2,3},{3,4},{4,5},{5,6},{6,7},{7,8},{8,9},{9,10},{10,1... | collective-permute-start | bytes 645128 | tf_op jit(solution)/shard_map/ppermute | solution.py:23
  5.5 3.6 %collective-permute-start.1 = (bf16[40,1,1,2688]{3,0,2,1:T(8,128)(2,1)S(1)}, bf16[40,1,1,2688]{3,0,2,1:T(8,128)(2,1)S(1)}, u32[]{:S(2)}, u32[]{:S(2)}) collective-permute-start(bf16[40,1,1,2688]{3,0,2,1:T(8,128)(2,1)S(1)} %copy.58), channel_id=1, source_target_pairs={{1,0},{2,1},{3,2},{4,3},{5,4},{6,5},{7,6},{8,7},{9,8},{10,9},{11,1... | collective-permute-start | bytes 645128 | tf_op jit(solution)/shard_map/ppermute | solution.py:25
  9.2 2.3 %fusion.16 = (f32[640,128]{1,0:T(8,128)}, f32[640,128]{1,0:T(8,128)}) fusion(s32[640]{0:T(1024)S(1)} %copy-done.17), kind=kLoop, calls=%fused_computation.32 | loop fusion | flops 737280 | bytes 657920 | tf_op jit(solution)/shard_map/cos | solution.py:56
  11.5 0.7 slice_bitcast_fusion.2
  12.3 0.6 min.12.listed_ref
  13.1 0.7 reshape.210.slot_ref
  13.7 1.0 %cosine_multiply_fusion = (f32[21,640]{1,0:T(8,128)}, f32[21,640]{1,0:T(8,128)}) fusion(s32[21]{0:T(128)S(1)} %iota_multiply_fusion, s32[640]{0:T(1024)S(1)} %copy-done.17, f32[640]{0:T(1024)S(1)} %compare_select_fusion), kind=kLoop, calls=%fused_computation.58 | loop fusion | flops 147840 | bytes 112724 | tf_op jit(solution)/shard_map/mul | solution.py:48
  15.1 0.3 copy.45
  15.5 4.0 %fusion.3.source_ref = bf16[320,2688]{1,0:T(8,128)(2,1)} fusion(bf16[40,8,1,2688]{3,1,2,0:T(8,128)(2,1)S(1)} %copy-done.1, bf16[40,1,1,2688]{3,1,2,0:T(2,128)(2,1)S(1)} %copy.45, bf16[40,1,1,2688]{3,1,2,0:T(2,128)(2,1)S(1)} %copy.43, f32[8,2688]{1,0:T(8,128)} %get-tuple-element.68, f32[8,2688]{1,0:T(8,128)} %get-tuple-element.69, ...), kind=kLoop, calls=%fused_computation.10 | loop fusion | flops 12902400 | bytes 4128768 | tf_op jit(solution)/shard_map/reshape | solution.py:164
  19.5 3.7 %shard_map.121 = (bf16[4,320,128]{2,1,0:T(8,128)(2,1)}, bf16[4,320,128]{2,1,0:T(8,128)(2,1)}, bf16[4,320,128]{2,1,0:T(8,128)(2,1)}, bf16[4,320,128]{2,1,0:T(8,128)(2,1)}, bf16[4,320,128]{2,1,0:T(8,128)(2,1)}) custom-call(s32[20]{0:T(128)} %min.12.listed_ref, bf16[320,2688]{1,0:T(8,128)(2,1)} %fusion.3.source_ref), custom_call_target="tpu_custom_call" | custom-call | tf_op jit(solution)/shard_map/pallas_call | solution.py:91
  23.2 0.7 slice_convert_fusion.3
  24.0 0.8 broadcast_add_fusion.2
  24.8 0.4 convolution_bitcast_fusion.1
  25.2 0.4 convolution_bitcast_fusion
  25.8 0.6 copy.48
  26.4 1.0 %reshape.219 = bf16[32,2,320]{2,1,0:T(2,128)(2,1)} reshape(bf16[32,4,8,20]{3,2,1,0:T(8,128)(2,1)S(1)} %bitcast.50) | data formatting | bytes 81920
  27.4 12.6 %all-to-all-start = ((bf16[32,2,320]{2,1,0:T(2,128)(2,1)}), bf16[32,2,320]{2,1,0:T(2,128)(2,1)S(1)}, u32[]{:S(2)}, u32[]{:S(2)}) async-start(bf16[32,2,320]{2,1,0:T(2,128)(2,1)} %reshape.219), calls=%async_computation | async-start | bytes 98304 | tf_op jit(solution)/shard_map/all_to_all | solution.py:193
  40.0 4.1 %add_convert_fusion.stencil_ref = bf16[21,4,128,128]{3,2,1,0:T(8,128)(2,1)} fusion(f32[21,4,128]{2,1,0:T(4,128)S(1)} %bitcast.54, s32[21,4,128]{2,1,0:T(4,128)S(1)} %get-tuple-element.79, f32[21,4,128]{2,1,0:T(4,128)S(1)} %bitcast.55, s32[21,4,128]{2,1,0:T(4,128)S(1)} %get-tuple-element.80, f32[21,4,128]{2,1,0:T(4,128)S(1)} %bitcast.56, ...), kind=kLoop, calls=%fused_computation | loop fusion | flops 16515072 | bytes 3096576 | tf_op jit(solution)/shard_map/convert_element_type | solution.py:174
  44.0 3.9 %all-to-all-done = bf16[32,2,320]{2,1,0:T(2,128)(2,1)S(1)} async-done(((bf16[32,2,320]{2,1,0:T(2,128)(2,1)}), bf16[32,2,320]{2,1,0:T(2,128)(2,1)S(1)}, u32[]{:S(2)}, u32[]{:S(2)}) %all-to-all-start) | async-done | bytes 40992 | tf_op jit(solution)/shard_map/all_to_all | solution.py:193
  47.9 0.4 reshape.220
  48.4 0.3 all_to_all.10
  48.7 4.3 %collective-permute-start.2 = (bf16[4,320,128]{2,1,0:T(8,128)(2,1)}, bf16[4,320,128]{2,1,0:T(8,128)(2,1)S(1)}, u32[]{:S(2)}, u32[]{:S(2)}) collective-permute-start(bf16[4,320,128]{2,1,0:T(8,128)(2,1)} %get-tuple-element.42), channel_id=1, source_target_pairs={{32,0},{48,16},{64,32},{80,48},{96,64},{112,80},{128,96},{144,112}... | collective-permute-start | bytes 983048 | tf_op jit(solution)/shard_map/ppermute | solution.py:35
  53.0 3.0 %collective-permute-start.3 = (bf16[4,320,128]{2,1,0:T(8,128)(2,1)}, bf16[4,320,128]{2,1,0:T(8,128)(2,1)S(1)}, u32[]{:S(2)}, u32[]{:S(2)}) collective-permute-start(bf16[4,320,128]{2,1,0:T(8,128)(2,1)} %get-tuple-element.43), channel_id=1, source_target_pairs={{16,0},{32,16},{48,32},{64,48},{80,64},{96,80},{112,96},{128,112},... | collective-permute-start | bytes 983048 | tf_op jit(solution)/shard_map/ppermute | solution.py:35
  56.0 2.8 %collective-permute-start.4 = (bf16[4,320,128]{2,1,0:T(8,128)(2,1)}, bf16[4,320,128]{2,1,0:T(8,128)(2,1)S(1)}, u32[]{:S(2)}, u32[]{:S(2)}) collective-permute-start(bf16[4,320,128]{2,1,0:T(8,128)(2,1)} %get-tuple-element.45), channel_id=1, source_target_pairs={{0,16},{16,32},{32,48},{48,64},{64,80},{80,96},{96,112},{112,128},... | collective-permute-start | bytes 983048 | tf_op jit(solution)/shard_map/ppermute | solution.py:35
  58.9 5.4 %collective-permute-start.5 = (bf16[4,320,128]{2,1,0:T(8,128)(2,1)S(1)}, bf16[4,320,128]{2,1,0:T(8,128)(2,1)S(1)}, u32[]{:S(2)}, u32[]{:S(2)}) collective-permute-start(bf16[4,320,128]{2,1,0:T(8,128)(2,1)S(1)} %copy-done.20), channel_id=1, source_target_pairs={{0,32},{16,48},{32,64},{48,80},{64,96},{80,112},{96,128},{112,144}... | collective-permute-start | bytes 983048 | tf_op jit(solution)/shard_map/ppermute | solution.py:35
  64.6 1.7 %fusion.4 = bf16[2,8,21,128]{3,2,1,0:T(8,128)(2,1)S(1)} fusion(f32[2,8,1,21,640]{4,3,1,0,2:T(8,128)S(1)} %get-tuple-element.71, f32[2,8,1,21,640]{4,3,1,0,2:T(8,128)S(1)} %get-tuple-element.70, f32[640,128]{1,0:T(8,128)S(1)} %copy-done.4, f32[640,128]{1,0:T(8,128)S(1)} %copy-done.3), kind=kOutput, calls=%fused_computation.15 | convolution fusion | flops 661239808 | bytes 2461696 | tf_op jit(solution)/shard_map/wklom,mi->wkloi/dot_general | solution.py:57
  66.4 2.9 %collective-permute-done.3.refs_1_ = bf16[4,320,128]{2,1,0:T(8,128)(2,1)S(1)} collective-permute-done((bf16[4,320,128]{2,1,0:T(8,128)(2,1)}, bf16[4,320,128]{2,1,0:T(8,128)(2,1)S(1)}, u32[]{:S(2)}, u32[]{:S(2)}) %collective-permute-start.3) | collective-permute-done | bytes 327712 | tf_op jit(solution)/shard_map/ppermute | solution.py:35
  69.5 11.3 %collective-permute-done.5.refs_4_ = bf16[4,320,128]{2,1,0:T(8,128)(2,1)S(1)} collective-permute-done((bf16[4,320,128]{2,1,0:T(8,128)(2,1)S(1)}, bf16[4,320,128]{2,1,0:T(8,128)(2,1)S(1)}, u32[]{:S(2)}, u32[]{:S(2)}) %collective-permute-start.5) | collective-permute-done | bytes 327712 | tf_op jit(solution)/shard_map/ppermute | solution.py:35
  80.8 0.7 copy-done.11
  81.5 7.1 %shard_map.122 = (bf16[320,2688]{1,0:T(8,128)(2,1)}, f32[8,2688]{1,0:T(8,128)}) custom-call(s32[84]{0:T(128)} %reshape.210.slot_ref, bf16[21,4,128,128]{3,2,1,0:T(8,128)(2,1)} %add_convert_fusion.stencil_ref, bf16[4,320,128]{2,1,0:T(8,128)(2,1)} %copy-done.8, bf16[4,320,128]{2,1,0:T(8,128)(2,1)} %copy-done.9, ...), custom_call_target="tpu_custom_call" | custom-call | tf_op jit(solution)/shard_map/pallas_call | solution.py:139
  88.6 1.5 %fusion.18 = bf16[2,8,1,2688]{3,1,2,0:T(8,128)(2,1)} fusion(bf16[2,8,1,2688]{3,1,0,2:T(8,128)(2,1)S(1)} %convert_element_type.94, f32[8,2688]{1,0:T(8,128)} %get-tuple-element.48), kind=kLoop, calls=%fused_computation.37 | loop fusion | flops 129024 | bytes 258048
  (62 shorter events, 1.5 us)
Async XLA Ops:
  0.6 24.1 %copy-start = (bf16[20,32,640]{2,1,0:T(8,128)(2,1)S(1)}, bf16[20,32,640]{2,1,0:T(8,128)(2,1)}, u32[]{:S(2)}) copy-start(bf16[20,32,640]{2,1,0:T(8,128)(2,1)} %param.12) | copy-start | bytes 2457604
  0.6 14.8 %copy-start.1 = (bf16[40,8,1,2688]{3,1,2,0:T(8,128)(2,1)S(1)}, bf16[40,8,1,2688]{3,1,2,0:T(8,128)(2,1)}, u32[]{:S(2)}) copy-start(bf16[40,8,1,2688]{3,1,2,0:T(8,128)(2,1)} %param.14) | copy-start | bytes 5160964
  0.7 8.5 %copy-start.17 = (s32[640]{0:T(1024)S(1)}, s32[640]{0:T(1024)}, u32[]{:S(2)}) copy-start(s32[640]{0:T(1024)} %param.13) | copy-start | bytes 7684
  0.7 10.8 %copy-start.16 = (bf16[3,8,1,2688]{3,1,2,0:T(8,128)(2,1)S(1)}, bf16[3,8,1,2688]{3,1,2,0:T(8,128)(2,1)}, u32[]{:S(2)}) copy-start(bf16[3,8,1,2688]{3,1,2,0:T(8,128)(2,1)} %param.15) | copy-start | bytes 387076
  0.7 11.5 %copy-start.19 = (s32[1,5,4]{1,2,0:T(4,128)S(1)}, s32[1,5,4]{1,2,0:T(4,128)}, u32[]{:S(2)}) copy-start(s32[1,5,4]{1,2,0:T(4,128)} %param.16) | copy-start | bytes 244
  0.7 12.3 %copy-start.18 = (s32[21,4]{0,1:T(4,128)S(1)}, s32[21,4]{0,1:T(4,128)}, u32[]{:S(2)}) copy-start(s32[21,4]{0,1:T(4,128)} %param.17) | copy-start | bytes 1012
  3.5 11.2 %collective-permute-start = (bf16[40,1,1,2688]{3,0,2,1:T(8,128)(2,1)S(1)}, bf16[40,1,1,2688]{3,0,2,1:T(8,128)(2,1)S(1)}, u32[]{:S(2)}, u32[]{:S(2)}) collective-permute-start(bf16[40,1,1,2688]{3,0,2,1:T(8,128)(2,1)S(1)} %copy.57), channel_id=1, source_target_pairs={{0,1},{1,2},{2,3},{3,4},{4,5},{5,6},{6,7},{7,8},{8,9},{9,10},{10,1... | collective-permute-start | bytes 645128 | tf_op jit(solution)/shard_map/ppermute | solution.py:23
  5.5 9.6 %collective-permute-start.1 = (bf16[40,1,1,2688]{3,0,2,1:T(8,128)(2,1)S(1)}, bf16[40,1,1,2688]{3,0,2,1:T(8,128)(2,1)S(1)}, u32[]{:S(2)}, u32[]{:S(2)}) collective-permute-start(bf16[40,1,1,2688]{3,0,2,1:T(8,128)(2,1)S(1)} %copy.58), channel_id=1, source_target_pairs={{1,0},{2,1},{3,2},{4,3},{5,4},{6,5},{7,6},{8,7},{9,8},{10,9},{11,1... | collective-permute-start | bytes 645128 | tf_op jit(solution)/shard_map/ppermute | solution.py:25
  15.4 7.8 %copy-start.6 = (bf16[21,4,4,128]{3,2,1,0:T(4,128)(2,1)S(1)}, bf16[21,4,4,128]{3,2,1,0:T(4,128)(2,1)}, u32[]{:S(2)}) copy-start(bf16[21,4,4,128]{3,2,1,0:T(4,128)(2,1)} %param.19) | copy-start | bytes 258052
  15.5 9.3 %copy-start.2 = (bf16[4,8,20,640]{3,1,2,0:T(8,128)(2,1)S(1)}, bf16[4,8,20,640]{3,1,2,0:T(8,128)(2,1)}, u32[]{:S(2)}) copy-start(bf16[4,8,20,640]{3,1,2,0:T(8,128)(2,1)} %param.10) | copy-start | bytes 2457604
  19.5 5.7 %copy-start.5 = (bf16[20,32,640]{2,1,0:T(8,128)(2,1)S(1)}, bf16[20,32,640]{2,1,0:T(8,128)(2,1)}, u32[]{:S(2)}) copy-start(bf16[20,32,640]{2,1,0:T(8,128)(2,1)} %param.11) | copy-start | bytes 2457604
  24.8 15.1 %copy-start.14 = (s32[21,4,128]{2,1,0:T(4,128)S(1)}, s32[21,4,128]{2,1,0:T(4,128)}, u32[]{:S(2)}) copy-start(s32[21,4,128]{2,1,0:T(4,128)} %param.18) | copy-start | bytes 129028
  24.8 15.1 %copy-start.15 = (f32[21,4,1,128]{3,2,1,0:T(1,128)S(1)}, f32[21,4,1,128]{3,2,1,0:T(1,128)}, u32[]{:S(2)}) copy-start(f32[21,4,1,128]{3,2,1,0:T(1,128)} %get-tuple-element.75) | copy-start | bytes 129028
  25.7 33.1 %copy-start.20 = (bf16[4,320,128]{2,1,0:T(8,128)(2,1)S(1)}, bf16[4,320,128]{2,1,0:T(8,128)(2,1)}, u32[]{:S(2)}) copy-start(bf16[4,320,128]{2,1,0:T(8,128)(2,1)} %get-tuple-element.46) | copy-start | bytes 983044
  25.8 38.5 %copy-start.12 = (f32[21,640]{1,0:T(8,128)S(1)}, f32[21,640]{1,0:T(8,128)}, u32[]{:S(2)}) copy-start(f32[21,640]{1,0:T(8,128)} %get-tuple-element.81) | copy-start | bytes 161284
  25.8 38.5 %copy-start.13 = (f32[21,640]{1,0:T(8,128)S(1)}, f32[21,640]{1,0:T(8,128)}, u32[]{:S(2)}) copy-start(f32[21,640]{1,0:T(8,128)} %get-tuple-element.82) | copy-start | bytes 161284
  27.4 20.5 %all-to-all-start = ((bf16[32,2,320]{2,1,0:T(2,128)(2,1)}), bf16[32,2,320]{2,1,0:T(2,128)(2,1)S(1)}, u32[]{:S(2)}, u32[]{:S(2)}) async-start(bf16[32,2,320]{2,1,0:T(2,128)(2,1)} %reshape.219), calls=%async_computation | async-start | bytes 98304 | tf_op jit(solution)/shard_map/all_to_all | solution.py:193
  39.9 24.6 %copy-start.3 = (f32[640,128]{1,0:T(8,128)S(1)}, f32[640,128]{1,0:T(8,128)}, u32[]{:S(2)}) copy-start(f32[640,128]{1,0:T(8,128)} %get-tuple-element.83) | copy-start | bytes 983044
  39.9 24.6 %copy-start.4 = (f32[640,128]{1,0:T(8,128)S(1)}, f32[640,128]{1,0:T(8,128)}, u32[]{:S(2)}) copy-start(f32[640,128]{1,0:T(8,128)} %get-tuple-element.84) | copy-start | bytes 983044
  48.7 17.6 %collective-permute-start.2 = (bf16[4,320,128]{2,1,0:T(8,128)(2,1)}, bf16[4,320,128]{2,1,0:T(8,128)(2,1)S(1)}, u32[]{:S(2)}, u32[]{:S(2)}) collective-permute-start(bf16[4,320,128]{2,1,0:T(8,128)(2,1)} %get-tuple-element.42), channel_id=1, source_target_pairs={{32,0},{48,16},{64,32},{80,48},{96,64},{112,80},{128,96},{144,112}... | collective-permute-start | bytes 983048 | tf_op jit(solution)/shard_map/ppermute | solution.py:35
  53.0 16.3 %collective-permute-start.3 = (bf16[4,320,128]{2,1,0:T(8,128)(2,1)}, bf16[4,320,128]{2,1,0:T(8,128)(2,1)S(1)}, u32[]{:S(2)}, u32[]{:S(2)}) collective-permute-start(bf16[4,320,128]{2,1,0:T(8,128)(2,1)} %get-tuple-element.43), channel_id=1, source_target_pairs={{16,0},{32,16},{48,32},{64,48},{80,64},{96,80},{112,96},{128,112},... | collective-permute-start | bytes 983048 | tf_op jit(solution)/shard_map/ppermute | solution.py:35
  56.0 13.5 %collective-permute-start.4 = (bf16[4,320,128]{2,1,0:T(8,128)(2,1)}, bf16[4,320,128]{2,1,0:T(8,128)(2,1)S(1)}, u32[]{:S(2)}, u32[]{:S(2)}) collective-permute-start(bf16[4,320,128]{2,1,0:T(8,128)(2,1)} %get-tuple-element.45), channel_id=1, source_target_pairs={{0,16},{16,32},{32,48},{48,64},{64,80},{80,96},{96,112},{112,128},... | collective-permute-start | bytes 983048 | tf_op jit(solution)/shard_map/ppermute | solution.py:35
  58.9 21.9 %collective-permute-start.5 = (bf16[4,320,128]{2,1,0:T(8,128)(2,1)S(1)}, bf16[4,320,128]{2,1,0:T(8,128)(2,1)S(1)}, u32[]{:S(2)}, u32[]{:S(2)}) collective-permute-start(bf16[4,320,128]{2,1,0:T(8,128)(2,1)S(1)} %copy-done.20), channel_id=1, source_target_pairs={{0,32},{16,48},{32,64},{48,80},{64,96},{80,112},{96,128},{112,144}... | collective-permute-start | bytes 983048 | tf_op jit(solution)/shard_map/ppermute | solution.py:35
  66.3 23.8 %copy-start.7 = (bf16[2,8,1,2688]{3,1,0,2:T(8,128)(2,1)}, bf16[2,8,1,2688]{3,1,0,2:T(8,128)(2,1)S(1)}, u32[]{:S(2)}) copy-start(bf16[2,8,1,2688]{3,1,0,2:T(8,128)(2,1)S(1)} %convert_element_type.94) | copy-start | bytes 258052
  66.4 14.4 %copy-start.8 = (bf16[4,320,128]{2,1,0:T(8,128)(2,1)}, bf16[4,320,128]{2,1,0:T(8,128)(2,1)S(1)}, u32[]{:S(2)}) copy-start(bf16[4,320,128]{2,1,0:T(8,128)(2,1)S(1)} %collective-permute-done.2.refs_0_) | copy-start | bytes 983044
  69.3 11.4 %copy-start.9 = (bf16[4,320,128]{2,1,0:T(8,128)(2,1)}, bf16[4,320,128]{2,1,0:T(8,128)(2,1)S(1)}, u32[]{:S(2)}) copy-start(bf16[4,320,128]{2,1,0:T(8,128)(2,1)S(1)} %collective-permute-done.3.refs_1_) | copy-start | bytes 983044
  69.5 11.3 %copy-start.10 = (bf16[4,320,128]{2,1,0:T(8,128)(2,1)}, bf16[4,320,128]{2,1,0:T(8,128)(2,1)S(1)}, u32[]{:S(2)}) copy-start(bf16[4,320,128]{2,1,0:T(8,128)(2,1)S(1)} %collective-permute-done.4.refs_3_) | copy-start | bytes 983044
  80.8 0.7 copy-start.11

commit v12 on v9

--- a/solution.py
+++ b/solution.py
@@ -166,9 +166,10 @@
     listed = jnp.clip(send_blocks[0], 0, block_total - 1)
     offsets, cap = listed.shape
     outgoing = pack_blocks(listed.reshape(-1), remapped, offsets, cap)
-    outgoing, spectral, legendre_value, legendre_slope, depart_offset, depart_weight = (
+    gate, spectral, legendre_value, legendre_slope, depart_offset, depart_weight, wave_numbers = (
         lax.optimization_barrier(
-            (outgoing, spectral, legendre_value, legendre_slope, depart_offset, depart_weight)
+            (outgoing, spectral, legendre_value, legendre_slope, depart_offset, depart_weight,
+             wave_numbers)
         )
     )
     stencil = stencil_matrix(depart_offset, depart_weight).astype(jnp.bfloat16)

time: 82.2 us -> 77.3 us (0.940)
  other arithmetic: 16.8 us -> 12.6 us
    ppermute x1, waiting for transfers between devices: 0.48 us -> 3.96 us  [extended(): lax.ppermute(head, axis, [((i + 1) % count, i) for i in range(ends)])]
    all_to_all x1, waiting for transfers between devices: 7.33 us -> 4.14 us  [shards(): lax.all_to_all(coefficients, 'band', split_axis=2, concat_axis=3, tiled=T...]
    add x1, other arithmetic: 1.44 us -> 0.02 us  [stencil_matrix(): depart_offset[:, :, None, :] + term_index]
    convert_element_type x1, other arithmetic: 5.22 us -> 4.06 us  [shards(): stencil = stencil_matrix(depart_offset, depart_weight).astype(jnp.bfloat16)]
    cos x1, other arithmetic: 2.32 us -> 1.42 us  [synthesis(): rhs = jnp.concatenate([jnp.cos(near_angle), jnp.sin(near_angle)], axis=0)]
    unnamed x37 -> x31, local copies, waits for them, and re-layouts: 2.24 us -> 1.54 us
  transfers between devices with their start and end apart: 7 -> 7, of which waited for: 2 -> 2; matrix products, arithmetic and copies ran while one was open for 21% -> 20% of each run, Pallas kernels for 0% -> 0%
where the time goes in v12:
time: 77.3 us; the launch traced here: 76.8 us
  starting transfers between devices  33.1 us (43%)
  other arithmetic  12.6 us (16%)
  Pallas kernels  10.8 us (14%)
  local copies, waits for them, and re-layouts  8.63 us (11%)
  waiting for transfers between devices  8.11 us (10%)
  matrix products  2.5 us (3%)
  between operations  1 us (1%)
    ppermute x4, starting transfers between devices, shifted(): lax.ppermute(value, axis, [(source, source + steps) for source in range(l...  13.3 us
    all_to_all x1, starting transfers between devices, shards(): lax.all_to_all(coefficients, 'band', split_axis=2, concat_axis=3, tiled=T...  12.9 us
    pallas_call x1, Pallas kernels, apply_stencil(): pl.pallas_call(body, grid_spec=grid_spec, out_shape=out_shape, compiler_p...  7.05 us
    ppermute x1, starting transfers between devices, extended(): lax.ppermute(tail, axis, [(i, (i + 1) % count) for i in range(ends)])  4.98 us
    all_to_all x1, waiting for transfers between devices, shards(): lax.all_to_all(coefficients, 'band', split_axis=2, concat_axis=3, tiled=T...  4.14 us
    convert_element_type x1, other arithmetic, shards(): stencil = stencil_matrix(depart_offset, depart_weight).astype(jnp.bfloat16)  4.06 us
    reshape x1, other arithmetic, shards(): vertical_sum.astype(jnp.bfloat16).reshape(rows, lat_count * lon_count)  4.02 us
    ppermute x1, waiting for transfers between devices, extended(): lax.ppermute(head, axis, [((i + 1) % count, i) for i in range(ends)])  3.96 us
  transfers between devices with their start and end apart: 7, of which 2 were waited for; matrix products, arithmetic and copies ran while one was open for 20% of the time, Pallas kernels for 0%

profile of v12, /device:TPU:25, one launch (start us, length us, event | category | flops | bytes accessed | tf_op | source)
XLA Modules:
  0.0 76.8 jit_solution(9546282903715323773)
XLA Ops:
  0.7 2.8 %fusion.33 = (bf16[40,1,1,2688]{3,1,2,0:T(2,128)(2,1)S(1)}, bf16[40,1,1,2688]{3,1,2,0:T(2,128)(2,1)S(1)}) fusion(bf16[40,8,1,2688]{3,1,2,0:T(8,128)(2,1)} %param.14), kind=kLoop, calls=%fused_computation.77 | loop fusion | bytes 860160 | tf_op jit(solution)/shard_map/slice | solution.py:20
  3.5 5.0 %collective-permute-start = (bf16[40,1,1,2688]{3,0,2,1:T(8,128)(2,1)S(1)}, bf16[40,1,1,2688]{3,0,2,1:T(8,128)(2,1)S(1)}, u32[]{:S(2)}, u32[]{:S(2)}) collective-permute-start(bf16[40,1,1,2688]{3,0,2,1:T(8,128)(2,1)S(1)} %copy.71), channel_id=1, source_target_pairs={{0,1},{1,2},{2,3},{3,4},{4,5},{5,6},{6,7},{7,8},{8,9},{9,10},{10,1... | collective-permute-start | bytes 645128 | tf_op jit(solution)/shard_map/ppermute | solution.py:23
  8.5 1.9 %collective-permute-start.1 = (bf16[40,1,1,2688]{3,0,2,1:T(8,128)(2,1)S(1)}, bf16[40,1,1,2688]{3,0,2,1:T(8,128)(2,1)S(1)}, u32[]{:S(2)}, u32[]{:S(2)}) collective-permute-start(bf16[40,1,1,2688]{3,0,2,1:T(8,128)(2,1)S(1)} %copy.72), channel_id=1, source_target_pairs={{1,0},{2,1},{3,2},{4,3},{5,4},{6,5},{7,6},{8,7},{9,8},{10,9},{11,1... | collective-permute-start | bytes 645128 | tf_op jit(solution)/shard_map/ppermute | solution.py:25
  10.5 0.7 slice_bitcast_fusion.2
  11.3 0.6 min.12.listed_ref
  12.0 0.6 reshape.224.slot_ref
  12.6 0.3 copy.56
  13.0 4.0 %collective-permute-done.1 = bf16[40,1,1,2688]{3,0,2,1:T(8,128)(2,1)S(1)} collective-permute-done((bf16[40,1,1,2688]{3,0,2,1:T(8,128)(2,1)S(1)}, bf16[40,1,1,2688]{3,0,2,1:T(8,128)(2,1)S(1)}, u32[]{:S(2)}, u32[]{:S(2)}) %collective-permute-start.1) | collective-permute-done | bytes 215072 | tf_op jit(solution)/shard_map/ppermute | solution.py:25
  16.9 0.3 copy.58
  17.3 4.0 %fusion.3.source_ref = bf16[320,2688]{1,0:T(8,128)(2,1)} fusion(bf16[40,8,1,2688]{3,1,2,0:T(8,128)(2,1)S(1)} %copy-done.1, bf16[40,1,1,2688]{3,1,2,0:T(2,128)(2,1)S(1)} %copy.58, bf16[40,1,1,2688]{3,1,2,0:T(2,128)(2,1)S(1)} %copy.56, f32[8,2688]{1,0:T(8,128)} %get-tuple-element.51, f32[8,2688]{1,0:T(8,128)} %get-tuple-element.52, ...), kind=kLoop, calls=%fused_computation.10 | loop fusion | flops 12902400 | bytes 4128768 | tf_op jit(solution)/shard_map/reshape | solution.py:164
  21.3 3.8 %shard_map.121 = (bf16[4,320,128]{2,1,0:T(8,128)(2,1)}, bf16[4,320,128]{2,1,0:T(8,128)(2,1)}, bf16[4,320,128]{2,1,0:T(8,128)(2,1)}, bf16[4,320,128]{2,1,0:T(8,128)(2,1)}, bf16[4,320,128]{2,1,0:T(8,128)(2,1)}) custom-call(s32[20]{0:T(128)} %min.12.listed_ref, bf16[320,2688]{1,0:T(8,128)(2,1)} %fusion.3.source_ref), custom_call_target="tpu_custom_call" | custom-call | tf_op jit(solution)/shard_map/pallas_call | solution.py:91
  25.1 1.4 %collective-permute-start.2 = (bf16[4,320,128]{2,1,0:T(8,128)(2,1)}, bf16[4,320,128]{2,1,0:T(8,128)(2,1)}, u32[]{:S(2)}, u32[]{:S(2)}) collective-permute-start(bf16[4,320,128]{2,1,0:T(8,128)(2,1)} %get-tuple-element.16), channel_id=1, source_target_pairs={{32,0},{48,16},{64,32},{80,48},{96,64},{112,80},{128,96},{144,112}... | collective-permute-start | bytes 983048 | tf_op jit(solution)/shard_map/ppermute | solution.py:35
  26.5 1.3 %collective-permute-start.3 = (bf16[4,320,128]{2,1,0:T(8,128)(2,1)}, bf16[4,320,128]{2,1,0:T(8,128)(2,1)}, u32[]{:S(2)}, u32[]{:S(2)}) collective-permute-start(bf16[4,320,128]{2,1,0:T(8,128)(2,1)} %get-tuple-element.17), channel_id=1, source_target_pairs={{16,0},{32,16},{48,32},{64,48},{80,64},{96,80},{112,96},{128,112},... | collective-permute-start | bytes 983048 | tf_op jit(solution)/shard_map/ppermute | solution.py:35
  27.8 4.7 %collective-permute-start.4 = (bf16[4,320,128]{2,1,0:T(8,128)(2,1)}, bf16[4,320,128]{2,1,0:T(8,128)(2,1)}, u32[]{:S(2)}, u32[]{:S(2)}) collective-permute-start(bf16[4,320,128]{2,1,0:T(8,128)(2,1)} %get-tuple-element.19), channel_id=1, source_target_pairs={{0,16},{16,32},{32,48},{48,64},{64,80},{80,96},{96,112},{112,128},... | collective-permute-start | bytes 983048 | tf_op jit(solution)/shard_map/ppermute | solution.py:35
  32.5 5.9 %collective-permute-start.5 = (bf16[4,320,128]{2,1,0:T(8,128)(2,1)}, bf16[4,320,128]{2,1,0:T(8,128)(2,1)}, u32[]{:S(2)}, u32[]{:S(2)}) collective-permute-start(bf16[4,320,128]{2,1,0:T(8,128)(2,1)} %get-tuple-element.20), channel_id=1, source_target_pairs={{0,32},{16,48},{32,64},{48,80},{64,96},{80,112},{96,128},{112,144}... | collective-permute-start | bytes 983048 | tf_op jit(solution)/shard_map/ppermute | solution.py:35
  38.4 1.4 %fusion.16 = (f32[640,128]{1,0:T(8,128)S(1)}, f32[640,128]{1,0:T(8,128)S(1)}) fusion(s32[640]{0:T(1024)S(1)} %copy-done.10), kind=kLoop, calls=%fused_computation.32 | loop fusion | flops 737280 | bytes 657920 | tf_op jit(solution)/shard_map/cos | solution.py:56
  39.9 0.7 slice_convert_fusion.3
  40.7 0.4 convolution_bitcast_fusion.1
  41.1 0.4 convolution_bitcast_fusion
  41.7 0.6 copy.61
  42.3 1.0 %reshape.234 = bf16[32,2,320]{2,1,0:T(2,128)(2,1)} reshape(bf16[32,4,8,20]{3,2,1,0:T(8,128)(2,1)S(1)} %bitcast.50) | data formatting | bytes 81920
  43.3 12.9 %all-to-all-start = ((bf16[32,2,320]{2,1,0:T(2,128)(2,1)}), bf16[32,2,320]{2,1,0:T(2,128)(2,1)S(1)}, u32[]{:S(2)}, u32[]{:S(2)}) async-start(bf16[32,2,320]{2,1,0:T(2,128)(2,1)} %reshape.234), calls=%async_computation | async-start | bytes 98304 | tf_op jit(solution)/shard_map/all_to_all | solution.py:202
  56.2 4.1 %add_convert_fusion.stencil_ref = bf16[21,4,128,128]{3,2,1,0:T(8,128)(2,1)} fusion(f32[21,4,128]{2,1,0:T(4,128)S(1)} %bitcast.54, s32[21,4,128]{2,1,0:T(4,128)S(1)} %get-tuple-element.62, f32[21,4,128]{2,1,0:T(4,128)S(1)} %bitcast.55, s32[21,4,128]{2,1,0:T(4,128)S(1)} %get-tuple-element.63, f32[21,4,128]{2,1,0:T(4,128)S(1)} %bitcast.56, ...), kind=kLoop, calls=%fused_computation | loop fusion | flops 16515072 | bytes 3096576 | tf_op jit(solution)/shard_map/convert_element_type | solution.py:175
  60.2 0.3 cosine_multiply_fusion
  60.6 4.1 %all-to-all-done = bf16[32,2,320]{2,1,0:T(2,128)(2,1)S(1)} async-done(((bf16[32,2,320]{2,1,0:T(2,128)(2,1)}), bf16[32,2,320]{2,1,0:T(2,128)(2,1)S(1)}, u32[]{:S(2)}, u32[]{:S(2)}) %all-to-all-start) | async-done | bytes 40992 | tf_op jit(solution)/shard_map/all_to_all | solution.py:202
  64.7 0.4 reshape.235
  65.1 0.4 copy.62
  65.5 0.3 copy.63
  65.8 0.3 reshape.226
  66.3 1.7 %fusion.4 = bf16[2,8,21,128]{3,2,1,0:T(8,128)(2,1)S(1)} fusion(f32[2,8,1,21,640]{4,3,1,0,2:T(8,128)S(1)} %get-tuple-element.54, f32[2,8,1,21,640]{4,3,1,0,2:T(8,128)S(1)} %get-tuple-element.53, f32[640,128]{1,0:T(8,128)S(1)} %get-tuple-element.67, f32[640,128]{1,0:T(8,128)S(1)} %get-tuple-element.66), kind=kOutput, calls=%fused_computation.15 | convolution fusion | flops 661239808 | bytes 2461696 | tf_op jit(solution)/shard_map/wklom,mi->wkloi/dot_general | solution.py:57
  68.2 7.1 %shard_map.122 = (bf16[320,2688]{1,0:T(8,128)(2,1)}, f32[8,2688]{1,0:T(8,128)}) custom-call(s32[84]{0:T(128)} %reshape.224.slot_ref, bf16[21,4,128,128]{3,2,1,0:T(8,128)(2,1)} %add_convert_fusion.stencil_ref, bf16[4,320,128]{2,1,0:T(8,128)(2,1)} %collective-permute-done.2.refs_0_, bf16[4,320,128]{2,1,0:T(8,128)(2,1)} %collective-permute-done.3.refs_1_, ...), custom_call_target="tpu_custom_call" | custom-call | tf_op jit(solution)/shard_map/pallas_call | solution.py:139
  75.2 1.5 %fusion.18 = bf16[2,8,1,2688]{3,1,2,0:T(8,128)(2,1)} fusion(bf16[2,8,1,2688]{3,1,0,2:T(8,128)(2,1)S(1)} %convert_element_type.106, f32[8,2688]{1,0:T(8,128)} %get-tuple-element.28), kind=kLoop, calls=%fused_computation.37 | loop fusion | flops 129024 | bytes 258048
  (46 shorter events, 0.9 us)
Async XLA Ops:
  0.6 40.0 %copy-start = (bf16[20,32,640]{2,1,0:T(8,128)(2,1)S(1)}, bf16[20,32,640]{2,1,0:T(8,128)(2,1)}, u32[]{:S(2)}) copy-start(bf16[20,32,640]{2,1,0:T(8,128)(2,1)} %param.12) | copy-start | bytes 2457604
  0.6 16.6 %copy-start.1 = (bf16[40,8,1,2688]{3,1,2,0:T(8,128)(2,1)S(1)}, bf16[40,8,1,2688]{3,1,2,0:T(8,128)(2,1)}, u32[]{:S(2)}) copy-start(bf16[40,8,1,2688]{3,1,2,0:T(8,128)(2,1)} %param.14) | copy-start | bytes 5160964
  0.7 9.8 %copy-start.9 = (bf16[3,8,1,2688]{3,1,2,0:T(8,128)(2,1)S(1)}, bf16[3,8,1,2688]{3,1,2,0:T(8,128)(2,1)}, u32[]{:S(2)}) copy-start(bf16[3,8,1,2688]{3,1,2,0:T(8,128)(2,1)} %param.15) | copy-start | bytes 387076
  0.7 10.5 %copy-start.12 = (s32[1,5,4]{1,2,0:T(4,128)S(1)}, s32[1,5,4]{1,2,0:T(4,128)}, u32[]{:S(2)}) copy-start(s32[1,5,4]{1,2,0:T(4,128)} %param.16) | copy-start | bytes 244
  0.7 11.2 %copy-start.11 = (s32[21,4]{0,1:T(4,128)S(1)}, s32[21,4]{0,1:T(4,128)}, u32[]{:S(2)}) copy-start(s32[21,4]{0,1:T(4,128)} %param.17) | copy-start | bytes 1012
  3.5 9.1 %collective-permute-start = (bf16[40,1,1,2688]{3,0,2,1:T(8,128)(2,1)S(1)}, bf16[40,1,1,2688]{3,0,2,1:T(8,128)(2,1)S(1)}, u32[]{:S(2)}, u32[]{:S(2)}) collective-permute-start(bf16[40,1,1,2688]{3,0,2,1:T(8,128)(2,1)S(1)} %copy.71), channel_id=1, source_target_pairs={{0,1},{1,2},{2,3},{3,4},{4,5},{5,6},{6,7},{7,8},{8,9},{9,10},{10,1... | collective-permute-start | bytes 645128 | tf_op jit(solution)/shard_map/ppermute | solution.py:23
  8.5 8.4 %collective-permute-start.1 = (bf16[40,1,1,2688]{3,0,2,1:T(8,128)(2,1)S(1)}, bf16[40,1,1,2688]{3,0,2,1:T(8,128)(2,1)S(1)}, u32[]{:S(2)}, u32[]{:S(2)}) collective-permute-start(bf16[40,1,1,2688]{3,0,2,1:T(8,128)(2,1)S(1)} %copy.72), channel_id=1, source_target_pairs={{1,0},{2,1},{3,2},{4,3},{5,4},{6,5},{7,6},{8,7},{9,8},{10,9},{11,1... | collective-permute-start | bytes 645128 | tf_op jit(solution)/shard_map/ppermute | solution.py:25
  17.3 21.1 %copy-start.10 = (s32[640]{0:T(1024)S(1)}, s32[640]{0:T(1024)}, u32[]{:S(2)}) copy-start(s32[640]{0:T(1024)} %param.13) | copy-start | bytes 7684
  17.3 22.6 %copy-start.4 = (bf16[21,4,4,128]{3,2,1,0:T(4,128)(2,1)S(1)}, bf16[21,4,4,128]{3,2,1,0:T(4,128)(2,1)}, u32[]{:S(2)}) copy-start(bf16[21,4,4,128]{3,2,1,0:T(4,128)(2,1)} %param.19) | copy-start | bytes 258052
  17.3 23.3 %copy-start.2 = (bf16[4,8,20,640]{3,1,2,0:T(8,128)(2,1)S(1)}, bf16[4,8,20,640]{3,1,2,0:T(8,128)(2,1)}, u32[]{:S(2)}) copy-start(bf16[4,8,20,640]{3,1,2,0:T(8,128)(2,1)} %param.10) | copy-start | bytes 2457604
  21.3 19.3 %copy-start.6 = (s32[21,4,128]{2,1,0:T(4,128)S(1)}, s32[21,4,128]{2,1,0:T(4,128)}, u32[]{:S(2)}) copy-start(s32[21,4,128]{2,1,0:T(4,128)} %param.18) | copy-start | bytes 129028
  25.1 16.0 %copy-start.3 = (bf16[20,32,640]{2,1,0:T(8,128)(2,1)S(1)}, bf16[20,32,640]{2,1,0:T(8,128)(2,1)}, u32[]{:S(2)}) copy-start(bf16[20,32,640]{2,1,0:T(8,128)(2,1)} %param.11) | copy-start | bytes 2457604
  25.1 43.0 %collective-permute-start.2 = (bf16[4,320,128]{2,1,0:T(8,128)(2,1)}, bf16[4,320,128]{2,1,0:T(8,128)(2,1)}, u32[]{:S(2)}, u32[]{:S(2)}) collective-permute-start(bf16[4,320,128]{2,1,0:T(8,128)(2,1)} %get-tuple-element.16), channel_id=1, source_target_pairs={{32,0},{48,16},{64,32},{80,48},{96,64},{112,80},{128,96},{144,112}... | collective-permute-start | bytes 983048 | tf_op jit(solution)/shard_map/ppermute | solution.py:35
  26.5 41.6 %collective-permute-start.3 = (bf16[4,320,128]{2,1,0:T(8,128)(2,1)}, bf16[4,320,128]{2,1,0:T(8,128)(2,1)}, u32[]{:S(2)}, u32[]{:S(2)}) collective-permute-start(bf16[4,320,128]{2,1,0:T(8,128)(2,1)} %get-tuple-element.17), channel_id=1, source_target_pairs={{16,0},{32,16},{48,32},{64,48},{80,64},{96,80},{112,96},{128,112},... | collective-permute-start | bytes 983048 | tf_op jit(solution)/shard_map/ppermute | solution.py:35
  27.8 40.3 %collective-permute-start.4 = (bf16[4,320,128]{2,1,0:T(8,128)(2,1)}, bf16[4,320,128]{2,1,0:T(8,128)(2,1)}, u32[]{:S(2)}, u32[]{:S(2)}) collective-permute-start(bf16[4,320,128]{2,1,0:T(8,128)(2,1)} %get-tuple-element.19), channel_id=1, source_target_pairs={{0,16},{16,32},{32,48},{48,64},{64,80},{80,96},{96,112},{112,128},... | collective-permute-start | bytes 983048 | tf_op jit(solution)/shard_map/ppermute | solution.py:35
  32.5 35.6 %collective-permute-start.5 = (bf16[4,320,128]{2,1,0:T(8,128)(2,1)}, bf16[4,320,128]{2,1,0:T(8,128)(2,1)}, u32[]{:S(2)}, u32[]{:S(2)}) collective-permute-start(bf16[4,320,128]{2,1,0:T(8,128)(2,1)} %get-tuple-element.20), channel_id=1, source_target_pairs={{0,32},{16,48},{32,64},{48,80},{64,96},{80,112},{96,128},{112,144}... | collective-permute-start | bytes 983048 | tf_op jit(solution)/shard_map/ppermute | solution.py:35
  40.6 15.5 %copy-start.7 = (s32[21,4,128]{2,1,0:T(4,128)S(1)}, s32[21,4,128]{2,1,0:T(4,128)}, u32[]{:S(2)}) copy-start(s32[21,4,128]{2,1,0:T(4,128)} %param.18) | copy-start | bytes 129028
  40.7 15.5 %copy-start.8 = (f32[21,4,1,128]{3,2,1,0:T(1,128)S(1)}, f32[21,4,1,128]{3,2,1,0:T(1,128)}, u32[]{:S(2)}) copy-start(f32[21,4,1,128]{3,2,1,0:T(1,128)} %get-tuple-element.58) | copy-start | bytes 129028
  43.3 21.4 %all-to-all-start = ((bf16[32,2,320]{2,1,0:T(2,128)(2,1)}), bf16[32,2,320]{2,1,0:T(2,128)(2,1)S(1)}, u32[]{:S(2)}, u32[]{:S(2)}) async-start(bf16[32,2,320]{2,1,0:T(2,128)(2,1)} %reshape.234), calls=%async_computation | async-start | bytes 98304 | tf_op jit(solution)/shard_map/all_to_all | solution.py:202
  68.1 8.7 %copy-start.5 = (bf16[2,8,1,2688]{3,1,0,2:T(8,128)(2,1)}, bf16[2,8,1,2688]{3,1,0,2:T(8,128)(2,1)S(1)}, u32[]{:S(2)}) copy-start(bf16[2,8,1,2688]{3,1,0,2:T(8,128)(2,1)S(1)} %convert_element_type.106) | copy-start | bytes 258052

commit v13 on v7

--- a/solution.py
+++ b/solution.py
@@ -72,25 +72,23 @@
 
 
 def pack_blocks(listed, remapped, offsets, cap):
-    rows = remapped.shape[0]
-
-    def body(listed_ref, *refs):
+    rows, width = remapped.shape
+
+    def body(listed_ref, source_ref, *out_refs):
         for index in range(offsets):
-            refs[offsets + index][...] = refs[index][...][None]
-
-    def source_map(index):
-        return lambda entry, table: (0, table[index * cap + entry])
+            for entry in range(cap):
+                column = pl.multiple_of(listed_ref[index * cap + entry] * BLK, BLK)
+                out_refs[index][entry] = source_ref[:, pl.ds(column, BLK)]
 
     out_shape = [jax.ShapeDtypeStruct((cap, rows, BLK), remapped.dtype) for _ in range(offsets)]
     grid_spec = pltpu.PrefetchScalarGridSpec(
         num_scalar_prefetch=1,
-        grid=(cap,),
-        in_specs=[pl.BlockSpec((rows, BLK), source_map(index)) for index in range(offsets)],
-        out_specs=[pl.BlockSpec((1, rows, BLK), lambda entry, table: (entry, 0, 0))
+        grid=(1,),
+        in_specs=[pl.BlockSpec((rows, width), lambda step, table: (0, 0))],
+        out_specs=[pl.BlockSpec((cap, rows, BLK), lambda step, table: (0, 0, 0))
                    for _ in range(offsets)],
     )
-    return pl.pallas_call(body, grid_spec=grid_spec, out_shape=out_shape)(
-        listed, *([remapped] * offsets))
+    return pl.pallas_call(body, grid_spec=grid_spec, out_shape=out_shape)(listed, remapped)
 
 
 def apply_stencil(slots, stencil, pieces, bin_count, level_count):
@@ -156,7 +154,6 @@
     depart_offset,
     depart_weight,
 ):
-    padded = extended(aerosol_old, (("lev", 1),), 1)
     band_here = lax.axis_index("band")
     wave_local = spectral.shape[2]
     own_waves = lax.dynamic_slice_in_dim(wave_numbers, band_here * wave_local, wave_local, 0)
@@ -175,8 +172,7 @@
             slope_terms[3] + factor * value_terms[0],
         ]
     ).astype(jnp.bfloat16)
-    received = lax.all_to_all(coefficients, "band", split_axis=2, concat_axis=3, tiled=True)
-    received, padded = lax.optimization_barrier((received, padded))
+    padded = extended(aerosol_old, (("lev", 1),), 1)
     weights = vertical_weight.astype(jnp.float32)
     vertical_sum = (
         weights[0] * padded[:, :-2] + weights[1] * padded[:, 1:-1] + weights[2] * padded[:, 2:]
@@ -188,8 +184,8 @@
     listed = jnp.clip(send_blocks[0], 0, block_total - 1)
     offsets, cap = listed.shape
     outgoing = pack_blocks(listed.reshape(-1), remapped, offsets, cap)
-    outgoing, received, depart_offset, depart_weight = lax.optimization_barrier(
-        (outgoing, received, depart_offset, depart_weight)
+    gate, coefficients, depart_offset, depart_weight, wave_numbers = lax.optimization_barrier(
+        (outgoing, coefficients, depart_offset, depart_weight, wave_numbers)
     )
     stencil = stencil_matrix(depart_offset, depart_weight).astype(jnp.bfloat16)
     reach_bands = offsets // 2
@@ -200,6 +196,7 @@
             pieces.append(outgoing[offset_index])
         else:
             pieces.append(shifted(outgoing[offset_index], "band", shift_by))
+    received = lax.all_to_all(coefficients, "band", split_axis=2, concat_axis=3, tiled=True)
     wind_grid = synthesis(received, wave_numbers, NLON).astype(jnp.bfloat16)
     flat_new, average = apply_stencil(depart_slot.reshape(-1), stencil, pieces, bin_count, level_count)
     aerosol_new = flat_new.reshape(bin_count, level_count, lat_count, lon_count)

time: 88.4 us -> 83.1 us (0.940)
  the two profiles are of different devices: /device:TPU:91 before, /device:TPU:16 now
where the time goes in v13:
time: 83.1 us; the launch traced here: 82.4 us
  starting transfers between devices  31.7 us (38%)
  other arithmetic  14.6 us (18%)
  local copies, waits for them, and re-layouts  13.5 us (16%)
  Pallas kernels  10.8 us (13%)
  waiting for transfers between devices  6.91 us (8%)
  matrix products  3.93 us (5%)
  between operations  0.99 us (1%)
    all_to_all x1, starting transfers between devices, shards(): lax.all_to_all(coefficients, 'band', split_axis=2, concat_axis=3, tiled=T...  14.1 us
    ppermute x4, starting transfers between devices, shifted(): lax.ppermute(value, axis, [(source, source + steps) for source in range(l...  13.3 us
    pallas_call x1, Pallas kernels, apply_stencil(): pl.pallas_call(body, grid_spec=grid_spec, out_shape=out_shape, compiler_p...  7.05 us
    all_to_all x1, waiting for transfers between devices, shards(): lax.all_to_all(coefficients, 'band', split_axis=2, concat_axis=3, tiled=T...  6.89 us
    unnamed x35, local copies, waits for them, and re-layouts  4.53 us
    convert_element_type x1, other arithmetic, shards(): stencil = stencil_matrix(depart_offset, depart_weight).astype(jnp.bfloat16)  4.16 us
    reshape x1, other arithmetic, shards(): vertical_sum.astype(jnp.bfloat16).reshape(rows, lat_count * lon_count)  3.9 us
    pallas_call x1, Pallas kernels, pack_blocks(): pl.pallas_call(body, grid_spec=grid_spec, out_shape=out_shape)  3.71 us
  transfers between devices with their start and end apart: 7, of which 1 were waited for; matrix products, arithmetic and copies ran while one was open for 24% of the time, Pallas kernels for 0%

profile of v13, /device:TPU:16, one launch (start us, length us, event | category | flops | bytes accessed | tf_op | source)
XLA Modules:
  0.0 82.4 jit_solution(4540049290379066012)
XLA Ops:
  0.7 2.8 %fusion.33 = (bf16[40,1,1,2688]{3,1,2,0:T(2,128)(2,1)S(1)}, bf16[40,1,1,2688]{3,1,2,0:T(2,128)(2,1)S(1)}) fusion(bf16[40,8,1,2688]{3,1,2,0:T(8,128)(2,1)} %param.14), kind=kLoop, calls=%fused_computation.77 | loop fusion | bytes 860160 | tf_op jit(solution)/shard_map/slice | solution.py:20
  3.5 0.7 copy.72
  4.2 1.9 %collective-permute-start.1 = (bf16[40,1,1,2688]{3,0,2,1:T(8,128)(2,1)}, bf16[40,1,1,2688]{3,0,2,1:T(8,128)(2,1)}, u32[]{:S(2)}, u32[]{:S(2)}) collective-permute-start(bf16[40,1,1,2688]{3,0,2,1:T(8,128)(2,1)} %copy.72), channel_id=1, source_target_pairs={{1,0},{2,1},{3,2},{4,3},{5,4},{6,5},{7,6},{8,7},{9,8},{10,9},{11,1... | collective-permute-start | bytes 645128 | tf_op jit(solution)/shard_map/ppermute | solution.py:25
  6.1 0.7 copy.71
  6.8 2.4 %collective-permute-start = (bf16[40,1,1,2688]{3,0,2,1:T(8,128)(2,1)}, bf16[40,1,1,2688]{3,0,2,1:T(8,128)(2,1)}, u32[]{:S(2)}, u32[]{:S(2)}) collective-permute-start(bf16[40,1,1,2688]{3,0,2,1:T(8,128)(2,1)} %copy.71), channel_id=1, source_target_pairs={{0,1},{1,2},{2,3},{3,4},{4,5},{5,6},{6,7},{7,8},{8,9},{9,10},{10,1... | collective-permute-start | bytes 645128 | tf_op jit(solution)/shard_map/ppermute | solution.py:23
  9.3 0.6 min.12.listed_ref
  10.0 0.7 reshape.224.slot_ref
  10.8 0.7 slice_bitcast_fusion.2
  11.4 1.1 %convolution_bitcast_fusion = f32[4,8,32,20]{2,1,0,3:T(8,128)} fusion(bf16[20,32,640]{2,1,0:T(8,128)(2,1)S(1)} %copy-done, bf16[4,8,20,640]{3,1,2,0:T(8,128)(2,1)S(1)} %copy-done.2), kind=kOutput, calls=%fused_computation.13 | convolution fusion | flops 26214400 | bytes 1720320 | tf_op jit(solution)/shard_map/slj,xksj->xkls/dot_general | solution.py:160
  12.5 1.1 %convolution_bitcast_fusion.1 = f32[4,8,32,20]{2,1,0,3:T(8,128)} fusion(bf16[20,32,640]{2,1,0:T(8,128)(2,1)S(1)} %copy-done.3, bf16[4,8,20,640]{3,1,2,0:T(8,128)(2,1)S(1)} %copy-done.2), kind=kOutput, calls=%fused_computation.14 | convolution fusion | flops 26214400 | bytes 1720320 | tf_op jit(solution)/shard_map/slj,xksj->xkls/dot_general | solution.py:163
  13.7 1.3 %fusion.26 = (bf16[1,8,32,20]{2,1,0,3:T(8,128)(2,1)S(1)}, bf16[1,8,32,20]{2,1,0,3:T(8,128)(2,1)S(1)}, bf16[1,8,32,20]{2,1,0,3:T(8,128)(2,1)S(1)}, bf16[1,8,32,20]{2,1,0,3:T(8,128)(2,1)S(1)}) fusion(f32[4,8,32,20]{2,1,0,3:T(8,128)} %convolution_bitcast_fusion, f32[4,8,32,20]{2,1,0,3:T(8,128)} %convolution_bitcast_fusion.1, f32[20]{0:T(128)S(1)} %convert_multiply_fusion), kind=kLoop, calls=%fused_computation.53 | loop fusion | flops 71680 | bytes 204880 | tf_op jit(solution)/shard_map/convert.5
  15.1 1.3 %copy.58 = bf16[40,1,1,2688]{3,1,2,0:T(2,128)(2,1)S(1)} copy(bf16[40,1,1,2688]{3,0,2,1:T(8,128)(2,1)} %collective-permute-done.1) | data formatting | bytes 430080 | tf_op jit(solution)/shard_map/ppermute | solution.py:25
  16.4 1.3 %copy.56 = bf16[40,1,1,2688]{3,1,2,0:T(2,128)(2,1)S(1)} copy(bf16[40,1,1,2688]{3,0,2,1:T(8,128)(2,1)} %collective-permute-done) | data formatting | bytes 430080 | tf_op jit(solution)/shard_map/ppermute | solution.py:23
  17.6 3.9 %fusion.3.source_ref = bf16[320,2688]{1,0:T(8,128)(2,1)} fusion(bf16[40,8,1,2688]{3,1,2,0:T(8,128)(2,1)S(1)} %copy-done.1, bf16[40,1,1,2688]{3,1,2,0:T(2,128)(2,1)S(1)} %copy.58, bf16[40,1,1,2688]{3,1,2,0:T(2,128)(2,1)S(1)} %copy.56, f32[8,2688]{1,0:T(8,128)S(1)} %get-tuple-element.47, f32[8,2688]{1,0:T(8,128)} %get-tuple-element.48, ...), kind=kLoop, calls=%fused_computation.10 | loop fusion | flops 12902400 | bytes 4128768 | tf_op jit(solution)/shard_map/reshape | solution.py:182
  21.6 3.7 %shard_map.121 = (bf16[4,320,128]{2,1,0:T(8,128)(2,1)}, bf16[4,320,128]{2,1,0:T(8,128)(2,1)}, bf16[4,320,128]{2,1,0:T(8,128)(2,1)}, bf16[4,320,128]{2,1,0:T(8,128)(2,1)}, bf16[4,320,128]{2,1,0:T(8,128)(2,1)}) custom-call(s32[20]{0:T(128)} %min.12.listed_ref, bf16[320,2688]{1,0:T(8,128)(2,1)} %fusion.3.source_ref), custom_call_target="tpu_custom_call" | custom-call | tf_op jit(solution)/shard_map/pallas_call | solution.py:91
  25.3 1.3 %collective-permute-start.2 = (bf16[4,320,128]{2,1,0:T(8,128)(2,1)}, bf16[4,320,128]{2,1,0:T(8,128)(2,1)S(1)}, u32[]{:S(2)}, u32[]{:S(2)}) collective-permute-start(bf16[4,320,128]{2,1,0:T(8,128)(2,1)} %get-tuple-element.14), channel_id=1, source_target_pairs={{32,0},{48,16},{64,32},{80,48},{96,64},{112,80},{128,96},{144,112}... | collective-permute-start | bytes 983048 | tf_op jit(solution)/shard_map/ppermute | solution.py:35
  26.6 1.3 %collective-permute-start.3 = (bf16[4,320,128]{2,1,0:T(8,128)(2,1)}, bf16[4,320,128]{2,1,0:T(8,128)(2,1)S(1)}, u32[]{:S(2)}, u32[]{:S(2)}) collective-permute-start(bf16[4,320,128]{2,1,0:T(8,128)(2,1)} %get-tuple-element.15), channel_id=1, source_target_pairs={{16,0},{32,16},{48,32},{64,48},{80,64},{96,80},{112,96},{128,112},... | collective-permute-start | bytes 983048 | tf_op jit(solution)/shard_map/ppermute | solution.py:35
  27.9 4.6 %collective-permute-start.4 = (bf16[4,320,128]{2,1,0:T(8,128)(2,1)}, bf16[4,320,128]{2,1,0:T(8,128)(2,1)S(1)}, u32[]{:S(2)}, u32[]{:S(2)}) collective-permute-start(bf16[4,320,128]{2,1,0:T(8,128)(2,1)} %get-tuple-element.17), channel_id=1, source_target_pairs={{0,16},{16,32},{32,48},{48,64},{64,80},{80,96},{96,112},{112,128},... | collective-permute-start | bytes 983048 | tf_op jit(solution)/shard_map/ppermute | solution.py:35
  32.4 6.1 %collective-permute-start.5 = (bf16[4,320,128]{2,1,0:T(8,128)(2,1)}, bf16[4,320,128]{2,1,0:T(8,128)(2,1)S(1)}, u32[]{:S(2)}, u32[]{:S(2)}) collective-permute-start(bf16[4,320,128]{2,1,0:T(8,128)(2,1)} %get-tuple-element.18), channel_id=1, source_target_pairs={{0,32},{16,48},{32,64},{48,80},{64,96},{80,112},{96,128},{112,144}... | collective-permute-start | bytes 983048 | tf_op jit(solution)/shard_map/ppermute | solution.py:35
  38.6 1.4 %fusion.16 = (f32[640,128]{1,0:T(8,128)S(1)}, f32[640,128]{1,0:T(8,128)S(1)}) fusion(s32[640]{0:T(1024)S(1)} %copy-done.12), kind=kLoop, calls=%fused_computation.32 | loop fusion | flops 737280 | bytes 657920 | tf_op jit(solution)/shard_map/cos | solution.py:56
  40.0 0.5 copy.61
  40.6 1.0 %reshape.234 = bf16[32,2,320]{2,1,0:T(2,128)(2,1)} reshape(bf16[32,4,8,20]{3,2,1,0:T(8,128)(2,1)S(1)} %bitcast.50) | data formatting | bytes 81920
  41.5 14.1 %all-to-all-start = ((bf16[32,2,320]{2,1,0:T(2,128)(2,1)}), bf16[32,2,320]{2,1,0:T(2,128)(2,1)S(1)}, u32[]{:S(2)}, u32[]{:S(2)}) async-start(bf16[32,2,320]{2,1,0:T(2,128)(2,1)} %reshape.234), calls=%async_computation | async-start | bytes 98304 | tf_op jit(solution)/shard_map/all_to_all | solution.py:199
  55.9 4.2 %add_convert_fusion.stencil_ref = bf16[21,4,128,128]{3,2,1,0:T(8,128)(2,1)} fusion(f32[21,4,128]{2,1,0:T(4,128)S(1)} %bitcast.54, s32[21,4,128]{2,1,0:T(4,128)S(1)} %get-tuple-element.58, f32[21,4,128]{2,1,0:T(4,128)S(1)} %bitcast.55, s32[21,4,128]{2,1,0:T(4,128)S(1)} %get-tuple-element.59, f32[21,4,128]{2,1,0:T(4,128)S(1)} %bitcast.56, ...), kind=kLoop, calls=%fused_computation | loop fusion | flops 16515072 | bytes 3096576 | tf_op jit(solution)/shard_map/convert_element_type | solution.py:190
  60.0 1.0 %cosine_multiply_fusion = (f32[21,640]{1,0:T(8,128)S(1)}, f32[21,640]{1,0:T(8,128)}) fusion(s32[21]{0:T(128)S(1)} %iota_multiply_fusion, s32[640]{0:T(1024)S(1)} %copy-done.12, f32[640]{0:T(1024)S(1)} %compare_select_fusion), kind=kLoop, calls=%fused_computation.58 | loop fusion | flops 147840 | bytes 112724 | tf_op jit(solution)/shard_map/mul | solution.py:48
  61.0 6.9 %all-to-all-done = bf16[32,2,320]{2,1,0:T(2,128)(2,1)S(1)} async-done(((bf16[32,2,320]{2,1,0:T(2,128)(2,1)}), bf16[32,2,320]{2,1,0:T(2,128)(2,1)S(1)}, u32[]{:S(2)}, u32[]{:S(2)}) %all-to-all-start) | async-done | bytes 40992 | tf_op jit(solution)/shard_map/all_to_all | solution.py:199
  69.2 1.1 %multiply_subtract_fusion = (f32[2,8,1,21,640]{4,3,1,0,2:T(8,128)S(1)}, f32[2,8,1,21,640]{4,3,1,0,2:T(8,128)S(1)}) fusion(f32[21,640]{1,0:T(8,128)} %get-tuple-element.61, f32[2,8,640]{2,1,0:T(8,128)S(1)} %get-tuple-element.56, f32[21,640]{1,0:T(8,128)S(1)} %get-tuple-element.60, f32[2,8,640]{2,1,0:T(8,128)S(1)} %get-tuple-element.55), kind=kLoop, calls=%fused_computation.17 | loop fusion | flops 1505280 | bytes 1909760 | tf_op jit(solution)/shard_map/sub | solution.py:53
  70.3 1.7 %fusion.4 = bf16[2,8,21,128]{3,2,1,0:T(8,128)(2,1)S(1)} fusion(f32[2,8,1,21,640]{4,3,1,0,2:T(8,128)S(1)} %get-tuple-element.50, f32[2,8,1,21,640]{4,3,1,0,2:T(8,128)S(1)} %get-tuple-element.49, f32[640,128]{1,0:T(8,128)S(1)} %get-tuple-element.63, f32[640,128]{1,0:T(8,128)S(1)} %get-tuple-element.62), kind=kOutput, calls=%fused_computation.15 | convolution fusion | flops 661239808 | bytes 2461696 | tf_op jit(solution)/shard_map/wklom,mi->wkloi/dot_general | solution.py:57
  72.2 0.7 copy-done.6
  73.1 0.7 copy-done.9
  73.8 7.0 %shard_map.122 = (bf16[320,2688]{1,0:T(8,128)(2,1)}, f32[8,2688]{1,0:T(8,128)}) custom-call(s32[84]{0:T(128)} %reshape.224.slot_ref, bf16[21,4,128,128]{3,2,1,0:T(8,128)(2,1)} %add_convert_fusion.stencil_ref, bf16[4,320,128]{2,1,0:T(8,128)(2,1)} %copy-done.6, bf16[4,320,128]{2,1,0:T(8,128)(2,1)} %copy-done.7, ...), custom_call_target="tpu_custom_call" | custom-call | tf_op jit(solution)/shard_map/pallas_call | solution.py:139
  80.9 1.5 %fusion.18 = bf16[2,8,1,2688]{3,1,2,0:T(8,128)(2,1)} fusion(bf16[2,8,1,2688]{3,1,0,2:T(8,128)(2,1)S(1)} %convert_element_type.106, f32[8,2688]{1,0:T(8,128)} %get-tuple-element.24), kind=kLoop, calls=%fused_computation.37 | loop fusion | flops 129024 | bytes 258048
  (50 shorter events, 2.2 us)
Async XLA Ops:
  0.6 10.8 %copy-start = (bf16[20,32,640]{2,1,0:T(8,128)(2,1)S(1)}, bf16[20,32,640]{2,1,0:T(8,128)(2,1)}, u32[]{:S(2)}) copy-start(bf16[20,32,640]{2,1,0:T(8,128)(2,1)} %param.11) | copy-start | bytes 2457604
  0.6 8.6 %copy-start.14 = (s32[1,5,4]{1,2,0:T(4,128)S(1)}, s32[1,5,4]{1,2,0:T(4,128)}, u32[]{:S(2)}) copy-start(s32[1,5,4]{1,2,0:T(4,128)} %param.16) | copy-start | bytes 244
  0.7 9.3 %copy-start.13 = (s32[21,4]{0,1:T(4,128)S(1)}, s32[21,4]{0,1:T(4,128)}, u32[]{:S(2)}) copy-start(s32[21,4]{0,1:T(4,128)} %param.17) | copy-start | bytes 1012
  0.7 10.1 %copy-start.11 = (bf16[3,8,1,2688]{3,1,2,0:T(8,128)(2,1)S(1)}, bf16[3,8,1,2688]{3,1,2,0:T(8,128)(2,1)}, u32[]{:S(2)}) copy-start(bf16[3,8,1,2688]{3,1,2,0:T(8,128)(2,1)} %param.15) | copy-start | bytes 387076
  0.7 10.7 %copy-start.2 = (bf16[4,8,20,640]{3,1,2,0:T(8,128)(2,1)S(1)}, bf16[4,8,20,640]{3,1,2,0:T(8,128)(2,1)}, u32[]{:S(2)}) copy-start(bf16[4,8,20,640]{3,1,2,0:T(8,128)(2,1)} %param.10) | copy-start | bytes 2457604
  4.2 10.9 %collective-permute-start.1 = (bf16[40,1,1,2688]{3,0,2,1:T(8,128)(2,1)}, bf16[40,1,1,2688]{3,0,2,1:T(8,128)(2,1)}, u32[]{:S(2)}, u32[]{:S(2)}) collective-permute-start(bf16[40,1,1,2688]{3,0,2,1:T(8,128)(2,1)} %copy.72), channel_id=1, source_target_pairs={{1,0},{2,1},{3,2},{4,3},{5,4},{6,5},{7,6},{8,7},{9,8},{10,9},{11,1... | collective-permute-start | bytes 645128 | tf_op jit(solution)/shard_map/ppermute | solution.py:25
  6.1 7.6 %copy-start.12 = (s32[640]{0:T(1024)S(1)}, s32[640]{0:T(1024)}, u32[]{:S(2)}) copy-start(s32[640]{0:T(1024)} %param.13) | copy-start | bytes 7684
  6.8 9.5 %collective-permute-start = (bf16[40,1,1,2688]{3,0,2,1:T(8,128)(2,1)}, bf16[40,1,1,2688]{3,0,2,1:T(8,128)(2,1)}, u32[]{:S(2)}, u32[]{:S(2)}) collective-permute-start(bf16[40,1,1,2688]{3,0,2,1:T(8,128)(2,1)} %copy.71), channel_id=1, source_target_pairs={{0,1},{1,2},{2,3},{3,4},{4,5},{5,6},{6,7},{7,8},{8,9},{9,10},{10,1... | collective-permute-start | bytes 645128 | tf_op jit(solution)/shard_map/ppermute | solution.py:23
  10.7 1.8 %copy-start.3 = (bf16[20,32,640]{2,1,0:T(8,128)(2,1)S(1)}, bf16[20,32,640]{2,1,0:T(8,128)(2,1)}, u32[]{:S(2)}) copy-start(bf16[20,32,640]{2,1,0:T(8,128)(2,1)} %param.12) | copy-start | bytes 2457604
  11.4 6.2 %copy-start.1 = (bf16[40,8,1,2688]{3,1,2,0:T(8,128)(2,1)S(1)}, bf16[40,8,1,2688]{3,1,2,0:T(8,128)(2,1)}, u32[]{:S(2)}) copy-start(bf16[40,8,1,2688]{3,1,2,0:T(8,128)(2,1)} %param.14) | copy-start | bytes 5160964
  21.5 34.1 %copy-start.10 = (s32[21,4,128]{2,1,0:T(4,128)S(1)}, s32[21,4,128]{2,1,0:T(4,128)}, u32[]{:S(2)}) copy-start(s32[21,4,128]{2,1,0:T(4,128)} %param.18) | copy-start | bytes 129028
  21.6 34.2 %copy-start.4 = (bf16[21,4,4,128]{3,2,1,0:T(4,128)(2,1)S(1)}, bf16[21,4,4,128]{3,2,1,0:T(4,128)(2,1)}, u32[]{:S(2)}) copy-start(bf16[21,4,4,128]{3,2,1,0:T(4,128)(2,1)} %param.19) | copy-start | bytes 258052
  25.3 46.9 %collective-permute-start.2 = (bf16[4,320,128]{2,1,0:T(8,128)(2,1)}, bf16[4,320,128]{2,1,0:T(8,128)(2,1)S(1)}, u32[]{:S(2)}, u32[]{:S(2)}) collective-permute-start(bf16[4,320,128]{2,1,0:T(8,128)(2,1)} %get-tuple-element.14), channel_id=1, source_target_pairs={{32,0},{48,16},{64,32},{80,48},{96,64},{112,80},{128,96},{144,112}... | collective-permute-start | bytes 983048 | tf_op jit(solution)/shard_map/ppermute | solution.py:35
  26.6 45.6 %collective-permute-start.3 = (bf16[4,320,128]{2,1,0:T(8,128)(2,1)}, bf16[4,320,128]{2,1,0:T(8,128)(2,1)S(1)}, u32[]{:S(2)}, u32[]{:S(2)}) collective-permute-start(bf16[4,320,128]{2,1,0:T(8,128)(2,1)} %get-tuple-element.15), channel_id=1, source_target_pairs={{16,0},{32,16},{48,32},{64,48},{80,64},{96,80},{112,96},{128,112},... | collective-permute-start | bytes 983048 | tf_op jit(solution)/shard_map/ppermute | solution.py:35
  27.9 44.3 %collective-permute-start.4 = (bf16[4,320,128]{2,1,0:T(8,128)(2,1)}, bf16[4,320,128]{2,1,0:T(8,128)(2,1)S(1)}, u32[]{:S(2)}, u32[]{:S(2)}) collective-permute-start(bf16[4,320,128]{2,1,0:T(8,128)(2,1)} %get-tuple-element.17), channel_id=1, source_target_pairs={{0,16},{16,32},{32,48},{48,64},{64,80},{80,96},{96,112},{112,128},... | collective-permute-start | bytes 983048 | tf_op jit(solution)/shard_map/ppermute | solution.py:35
  32.4 39.8 %collective-permute-start.5 = (bf16[4,320,128]{2,1,0:T(8,128)(2,1)}, bf16[4,320,128]{2,1,0:T(8,128)(2,1)S(1)}, u32[]{:S(2)}, u32[]{:S(2)}) collective-permute-start(bf16[4,320,128]{2,1,0:T(8,128)(2,1)} %get-tuple-element.18), channel_id=1, source_target_pairs={{0,32},{16,48},{32,64},{48,80},{64,96},{80,112},{96,128},{112,144}... | collective-permute-start | bytes 983048 | tf_op jit(solution)/shard_map/ppermute | solution.py:35
  41.5 26.3 %all-to-all-start = ((bf16[32,2,320]{2,1,0:T(2,128)(2,1)}), bf16[32,2,320]{2,1,0:T(2,128)(2,1)S(1)}, u32[]{:S(2)}, u32[]{:S(2)}) async-start(bf16[32,2,320]{2,1,0:T(2,128)(2,1)} %reshape.234), calls=%async_computation | async-start | bytes 98304 | tf_op jit(solution)/shard_map/all_to_all | solution.py:199
  72.1 10.3 %copy-start.5 = (bf16[2,8,1,2688]{3,1,0,2:T(8,128)(2,1)}, bf16[2,8,1,2688]{3,1,0,2:T(8,128)(2,1)S(1)}, u32[]{:S(2)}) copy-start(bf16[2,8,1,2688]{3,1,0,2:T(8,128)(2,1)S(1)} %convert_element_type.106) | copy-start | bytes 258052
  72.1 0.7 copy-start.6
  72.1 0.8 %copy-start.7 = (bf16[4,320,128]{2,1,0:T(8,128)(2,1)}, bf16[4,320,128]{2,1,0:T(8,128)(2,1)S(1)}, u32[]{:S(2)}) copy-start(bf16[4,320,128]{2,1,0:T(8,128)(2,1)S(1)} %collective-permute-done.3.refs_1_) | copy-start | bytes 983044
  72.2 0.9 %copy-start.8 = (bf16[4,320,128]{2,1,0:T(8,128)(2,1)}, bf16[4,320,128]{2,1,0:T(8,128)(2,1)S(1)}, u32[]{:S(2)}) copy-start(bf16[4,320,128]{2,1,0:T(8,128)(2,1)S(1)} %collective-permute-done.4.refs_3_) | copy-start | bytes 983044
  73.1 0.7 copy-start.9

commit v14 on v12

--- a/solution.py
+++ b/solution.py
@@ -174,13 +174,13 @@
     )
     stencil = stencil_matrix(depart_offset, depart_weight).astype(jnp.bfloat16)
     reach_bands = offsets // 2
-    pieces = []
+    pieces = [None] * offsets
     for offset_index in range(offsets):
         shift_by = offset_index - reach_bands
         if shift_by == 0:
-            pieces.append(outgoing[offset_index])
-        else:
-            pieces.append(shifted(outgoing[offset_index], "band", shift_by))
+            pieces[offset_index] = outgoing[offset_index]
+        elif abs(shift_by) == 1:
+            pieces[offset_index] = shifted(outgoing[offset_index], "band", shift_by)
     band_here = lax.axis_index("band")
     wave_local = spectral.shape[2]
     own_waves = lax.dynamic_slice_in_dim(wave_numbers, band_here * wave_local, wave_local, 0)
@@ -200,6 +200,10 @@
         ]
     ).astype(jnp.bfloat16)
     received = lax.all_to_all(coefficients, "band", split_axis=2, concat_axis=3, tiled=True)
+    far = [index for index in range(offsets) if abs(index - reach_bands) > 1]
+    late, received = lax.optimization_barrier(([outgoing[index] for index in far], received))
+    for index, value in zip(far, late):
+        pieces[index] = shifted(value, "band", index - reach_bands)
     wind_grid = synthesis(received, wave_numbers, NLON).astype(jnp.bfloat16)
     flat_new, average = apply_stencil(depart_slot.reshape(-1), stencil, pieces, bin_count, level_count)
     aerosol_new = flat_new.reshape(bin_count, level_count, lat_count, lon_count)

time: 77.3 us -> 87.8 us (1.14)
  the two profiles are of different devices: /device:TPU:25 before, /device:TPU:31 now
where the time goes in v14:
time: 87.8 us; the launch traced here: 87.2 us
  starting transfers between devices  34.8 us (40%)
  waiting for transfers between devices  16.6 us (19%)
  other arithmetic  12.6 us (14%)
  Pallas kernels  10.8 us (12%)
  local copies, waits for them, and re-layouts  8.88 us (10%)
  matrix products  2.5 us (3%)
  between operations  1.05 us (1%)
    ppermute x4, starting transfers between devices, shifted(): lax.ppermute(value, axis, [(source, source + steps) for source in range(l...  15.4 us
    all_to_all x1, starting transfers between devices, shards(): lax.all_to_all(coefficients, 'band', split_axis=2, concat_axis=3, tiled=T...  12.6 us
    ppermute x4, waiting for transfers between devices, shifted(): lax.ppermute(value, axis, [(source, source + steps) for source in range(l...  9.64 us
    pallas_call x1, Pallas kernels, apply_stencil(): pl.pallas_call(body, grid_spec=grid_spec, out_shape=out_shape, compiler_p...  7.05 us
    ppermute x1, starting transfers between devices, extended(): lax.ppermute(tail, axis, [(i, (i + 1) % count) for i in range(ends)])  4.98 us
    convert_element_type x1, other arithmetic, shards(): stencil = stencil_matrix(depart_offset, depart_weight).astype(jnp.bfloat16)  4.03 us
    reshape x1, other arithmetic, shards(): vertical_sum.astype(jnp.bfloat16).reshape(rows, lat_count * lon_count)  4.02 us
    ppermute x1, waiting for transfers between devices, extended(): lax.ppermute(head, axis, [((i + 1) % count, i) for i in range(ends)])  3.92 us
  transfers between devices with their start and end apart: 7, of which 4 were waited for; matrix products, arithmetic and copies ran while one was open for 16% of the time, Pallas kernels for 0%

profile of v14, /device:TPU:31, one launch (start us, length us, event | category | flops | bytes accessed | tf_op | source)
XLA Modules:
  0.0 87.2 jit_solution(8309841460362844579)
XLA Ops:
  0.7 2.8 %fusion.33 = (bf16[40,1,1,2688]{3,1,2,0:T(2,128)(2,1)S(1)}, bf16[40,1,1,2688]{3,1,2,0:T(2,128)(2,1)S(1)}) fusion(bf16[40,8,1,2688]{3,1,2,0:T(8,128)(2,1)} %param.14), kind=kLoop, calls=%fused_computation.77 | loop fusion | bytes 860160 | tf_op jit(solution)/shard_map/slice | solution.py:20
  3.5 5.0 %collective-permute-start = (bf16[40,1,1,2688]{3,0,2,1:T(8,128)(2,1)S(1)}, bf16[40,1,1,2688]{3,0,2,1:T(8,128)(2,1)S(1)}, u32[]{:S(2)}, u32[]{:S(2)}) collective-permute-start(bf16[40,1,1,2688]{3,0,2,1:T(8,128)(2,1)S(1)} %copy.57), channel_id=1, source_target_pairs={{0,1},{1,2},{2,3},{3,4},{4,5},{5,6},{6,7},{7,8},{8,9},{9,10},{10,1... | collective-permute-start | bytes 645128 | tf_op jit(solution)/shard_map/ppermute | solution.py:23
  8.5 1.9 %collective-permute-start.1 = (bf16[40,1,1,2688]{3,0,2,1:T(8,128)(2,1)S(1)}, bf16[40,1,1,2688]{3,0,2,1:T(8,128)(2,1)S(1)}, u32[]{:S(2)}, u32[]{:S(2)}) collective-permute-start(bf16[40,1,1,2688]{3,0,2,1:T(8,128)(2,1)S(1)} %copy.58), channel_id=1, source_target_pairs={{1,0},{2,1},{3,2},{4,3},{5,4},{6,5},{7,6},{8,7},{9,8},{10,9},{11,1... | collective-permute-start | bytes 645128 | tf_op jit(solution)/shard_map/ppermute | solution.py:25
  10.5 0.7 slice_bitcast_fusion.2
  11.3 0.6 min.12.listed_ref
  12.0 0.7 reshape.210.slot_ref
  12.7 0.3 copy.43
  13.0 3.9 %collective-permute-done.1 = bf16[40,1,1,2688]{3,0,2,1:T(8,128)(2,1)S(1)} collective-permute-done((bf16[40,1,1,2688]{3,0,2,1:T(8,128)(2,1)S(1)}, bf16[40,1,1,2688]{3,0,2,1:T(8,128)(2,1)S(1)}, u32[]{:S(2)}, u32[]{:S(2)}) %collective-permute-start.1) | collective-permute-done | bytes 215072 | tf_op jit(solution)/shard_map/ppermute | solution.py:25
  17.3 4.0 %fusion.3.source_ref = bf16[320,2688]{1,0:T(8,128)(2,1)} fusion(bf16[40,8,1,2688]{3,1,2,0:T(8,128)(2,1)S(1)} %copy-done.1, bf16[40,1,1,2688]{3,1,2,0:T(2,128)(2,1)S(1)} %copy.45, bf16[40,1,1,2688]{3,1,2,0:T(2,128)(2,1)S(1)} %copy.43, f32[8,2688]{1,0:T(8,128)} %get-tuple-element.54, f32[8,2688]{1,0:T(8,128)} %get-tuple-element.55, ...), kind=kLoop, calls=%fused_computation.10 | loop fusion | flops 12902400 | bytes 4128768 | tf_op jit(solution)/shard_map/reshape | solution.py:164
  21.3 3.7 %shard_map.121 = (bf16[4,320,128]{2,1,0:T(8,128)(2,1)}, bf16[4,320,128]{2,1,0:T(8,128)(2,1)}, bf16[4,320,128]{2,1,0:T(8,128)(2,1)}, bf16[4,320,128]{2,1,0:T(8,128)(2,1)}, bf16[4,320,128]{2,1,0:T(8,128)(2,1)}) custom-call(s32[20]{0:T(128)} %min.12.listed_ref, bf16[320,2688]{1,0:T(8,128)(2,1)} %fusion.3.source_ref), custom_call_target="tpu_custom_call" | custom-call | tf_op jit(solution)/shard_map/pallas_call | solution.py:91
  25.1 2.6 %collective-permute-start.3 = (bf16[4,320,128]{2,1,0:T(8,128)(2,1)}, bf16[4,320,128]{2,1,0:T(8,128)(2,1)}, u32[]{:S(2)}, u32[]{:S(2)}) collective-permute-start(bf16[4,320,128]{2,1,0:T(8,128)(2,1)} %get-tuple-element.21), channel_id=1, source_target_pairs={{16,0},{32,16},{48,32},{64,48},{80,64},{96,80},{112,96},{128,112},... | collective-permute-start | bytes 983048 | tf_op jit(solution)/shard_map/ppermute | solution.py:35
  27.7 4.9 %collective-permute-start.4 = (bf16[4,320,128]{2,1,0:T(8,128)(2,1)}, bf16[4,320,128]{2,1,0:T(8,128)(2,1)}, u32[]{:S(2)}, u32[]{:S(2)}) collective-permute-start(bf16[4,320,128]{2,1,0:T(8,128)(2,1)} %get-tuple-element.23), channel_id=1, source_target_pairs={{0,16},{16,32},{32,48},{48,64},{64,80},{80,96},{96,112},{112,128},... | collective-permute-start | bytes 983048 | tf_op jit(solution)/shard_map/ppermute | solution.py:35
  32.6 1.4 %fusion.16 = (f32[640,128]{1,0:T(8,128)S(1)}, f32[640,128]{1,0:T(8,128)S(1)}) fusion(s32[640]{0:T(1024)S(1)} %copy-done.12), kind=kLoop, calls=%fused_computation.32 | loop fusion | flops 737280 | bytes 657920 | tf_op jit(solution)/shard_map/cos | solution.py:56
  34.1 0.7 slice_convert_fusion.3
  34.9 0.4 convolution_bitcast_fusion.1
  35.3 0.4 convolution_bitcast_fusion
  36.0 0.6 copy.48
  36.5 1.0 %reshape.219 = bf16[32,2,320]{2,1,0:T(2,128)(2,1)} reshape(bf16[32,4,8,20]{3,2,1,0:T(8,128)(2,1)S(1)} %bitcast.50) | data formatting | bytes 81920
  37.5 12.6 %all-to-all-start = ((bf16[32,2,320]{2,1,0:T(2,128)(2,1)}), bf16[32,2,320]{2,1,0:T(2,128)(2,1)S(1)}, u32[]{:S(2)}, u32[]{:S(2)}) async-start(bf16[32,2,320]{2,1,0:T(2,128)(2,1)} %reshape.219), calls=%async_computation | async-start | bytes 98304 | tf_op jit(solution)/shard_map/all_to_all | solution.py:202
  50.1 4.0 %add_convert_fusion.stencil_ref = bf16[21,4,128,128]{3,2,1,0:T(8,128)(2,1)} fusion(f32[21,4,128]{2,1,0:T(4,128)S(1)} %bitcast.54, s32[21,4,128]{2,1,0:T(4,128)S(1)} %get-tuple-element.65, f32[21,4,128]{2,1,0:T(4,128)S(1)} %bitcast.55, s32[21,4,128]{2,1,0:T(4,128)S(1)} %get-tuple-element.66, f32[21,4,128]{2,1,0:T(4,128)S(1)} %bitcast.56, ...), kind=kLoop, calls=%fused_computation | loop fusion | flops 16515072 | bytes 3096576 | tf_op jit(solution)/shard_map/convert_element_type | solution.py:175
  54.1 0.3 cosine_multiply_fusion
  54.4 3.0 %all-to-all-done = bf16[32,2,320]{2,1,0:T(2,128)(2,1)S(1)} async-done(((bf16[32,2,320]{2,1,0:T(2,128)(2,1)}), bf16[32,2,320]{2,1,0:T(2,128)(2,1)S(1)}, u32[]{:S(2)}, u32[]{:S(2)}) %all-to-all-start) | async-done | bytes 40992 | tf_op jit(solution)/shard_map/all_to_all | solution.py:202
  57.5 0.4 reshape.220
  57.9 0.3 all_to_all.10
  58.3 3.5 %collective-permute-start.2 = (bf16[4,320,128]{2,1,0:T(8,128)(2,1)S(1)}, bf16[4,320,128]{2,1,0:T(8,128)(2,1)S(1)}, u32[]{:S(2)}, u32[]{:S(2)}) collective-permute-start(bf16[4,320,128]{2,1,0:T(8,128)(2,1)S(1)} %copy-done.16), channel_id=1, source_target_pairs={{32,0},{48,16},{64,32},{80,48},{96,64},{112,80},{128,96},{144,112}... | collective-permute-start | bytes 983048 | tf_op jit(solution)/shard_map/ppermute | solution.py:35
  61.8 4.4 %collective-permute-start.5 = (bf16[4,320,128]{2,1,0:T(8,128)(2,1)S(1)}, bf16[4,320,128]{2,1,0:T(8,128)(2,1)S(1)}, u32[]{:S(2)}, u32[]{:S(2)}) collective-permute-start(bf16[4,320,128]{2,1,0:T(8,128)(2,1)S(1)} %copy-done.15), channel_id=1, source_target_pairs={{0,32},{16,48},{32,64},{48,80},{64,96},{80,112},{96,128},{112,144}... | collective-permute-start | bytes 983048 | tf_op jit(solution)/shard_map/ppermute | solution.py:35
  66.4 1.7 %fusion.4 = bf16[2,8,21,128]{3,2,1,0:T(8,128)(2,1)S(1)} fusion(f32[2,8,1,21,640]{4,3,1,0,2:T(8,128)S(1)} %get-tuple-element.57, f32[2,8,1,21,640]{4,3,1,0,2:T(8,128)S(1)} %get-tuple-element.56, f32[640,128]{1,0:T(8,128)S(1)} %get-tuple-element.70, f32[640,128]{1,0:T(8,128)S(1)} %get-tuple-element.69), kind=kOutput, calls=%fused_computation.15 | convolution fusion | flops 661239808 | bytes 2461696 | tf_op jit(solution)/shard_map/wklom,mi->wkloi/dot_general | solution.py:57
  68.3 2.5 %collective-permute-done.2.refs_0_ = bf16[4,320,128]{2,1,0:T(8,128)(2,1)S(1)} collective-permute-done((bf16[4,320,128]{2,1,0:T(8,128)(2,1)S(1)}, bf16[4,320,128]{2,1,0:T(8,128)(2,1)S(1)}, u32[]{:S(2)}, u32[]{:S(2)}) %collective-permute-start.2) | collective-permute-done | bytes 327712 | tf_op jit(solution)/shard_map/ppermute | solution.py:35
  70.8 7.1 %collective-permute-done.5.refs_4_ = bf16[4,320,128]{2,1,0:T(8,128)(2,1)S(1)} collective-permute-done((bf16[4,320,128]{2,1,0:T(8,128)(2,1)S(1)}, bf16[4,320,128]{2,1,0:T(8,128)(2,1)S(1)}, u32[]{:S(2)}, u32[]{:S(2)}) %collective-permute-start.5) | collective-permute-done | bytes 327712 | tf_op jit(solution)/shard_map/ppermute | solution.py:35
  77.9 0.7 copy-done.7
  78.6 7.0 %shard_map.122 = (bf16[320,2688]{1,0:T(8,128)(2,1)}, f32[8,2688]{1,0:T(8,128)}) custom-call(s32[84]{0:T(128)} %reshape.210.slot_ref, bf16[21,4,128,128]{3,2,1,0:T(8,128)(2,1)} %add_convert_fusion.stencil_ref, bf16[4,320,128]{2,1,0:T(8,128)(2,1)} %copy-done.6, bf16[4,320,128]{2,1,0:T(8,128)(2,1)} %collective-permute-done.3.refs_1_, ...), custom_call_target="tpu_custom_call" | custom-call | tf_op jit(solution)/shard_map/pallas_call | solution.py:139
  85.7 1.5 %fusion.18 = bf16[2,8,1,2688]{3,1,2,0:T(8,128)(2,1)} fusion(bf16[2,8,1,2688]{3,1,0,2:T(8,128)(2,1)S(1)} %convert_element_type.94, f32[8,2688]{1,0:T(8,128)} %get-tuple-element.34), kind=kLoop, calls=%fused_computation.37 | loop fusion | flops 129024 | bytes 258048
  (54 shorter events, 1.4 us)
Async XLA Ops:
  0.6 34.2 %copy-start = (bf16[20,32,640]{2,1,0:T(8,128)(2,1)S(1)}, bf16[20,32,640]{2,1,0:T(8,128)(2,1)}, u32[]{:S(2)}) copy-start(bf16[20,32,640]{2,1,0:T(8,128)(2,1)} %param.12) | copy-start | bytes 2457604
  0.6 16.6 %copy-start.1 = (bf16[40,8,1,2688]{3,1,2,0:T(8,128)(2,1)S(1)}, bf16[40,8,1,2688]{3,1,2,0:T(8,128)(2,1)}, u32[]{:S(2)}) copy-start(bf16[40,8,1,2688]{3,1,2,0:T(8,128)(2,1)} %param.14) | copy-start | bytes 5160964
  0.7 9.8 %copy-start.11 = (bf16[3,8,1,2688]{3,1,2,0:T(8,128)(2,1)S(1)}, bf16[3,8,1,2688]{3,1,2,0:T(8,128)(2,1)}, u32[]{:S(2)}) copy-start(bf16[3,8,1,2688]{3,1,2,0:T(8,128)(2,1)} %param.15) | copy-start | bytes 387076
  0.7 10.5 %copy-start.14 = (s32[1,5,4]{1,2,0:T(4,128)S(1)}, s32[1,5,4]{1,2,0:T(4,128)}, u32[]{:S(2)}) copy-start(s32[1,5,4]{1,2,0:T(4,128)} %param.16) | copy-start | bytes 244
  0.7 11.2 %copy-start.13 = (s32[21,4]{0,1:T(4,128)S(1)}, s32[21,4]{0,1:T(4,128)}, u32[]{:S(2)}) copy-start(s32[21,4]{0,1:T(4,128)} %param.17) | copy-start | bytes 1012
  3.5 9.2 %collective-permute-start = (bf16[40,1,1,2688]{3,0,2,1:T(8,128)(2,1)S(1)}, bf16[40,1,1,2688]{3,0,2,1:T(8,128)(2,1)S(1)}, u32[]{:S(2)}, u32[]{:S(2)}) collective-permute-start(bf16[40,1,1,2688]{3,0,2,1:T(8,128)(2,1)S(1)} %copy.57), channel_id=1, source_target_pairs={{0,1},{1,2},{2,3},{3,4},{4,5},{5,6},{6,7},{7,8},{8,9},{9,10},{10,1... | collective-permute-start | bytes 645128 | tf_op jit(solution)/shard_map/ppermute | solution.py:23
  8.5 8.4 %collective-permute-start.1 = (bf16[40,1,1,2688]{3,0,2,1:T(8,128)(2,1)S(1)}, bf16[40,1,1,2688]{3,0,2,1:T(8,128)(2,1)S(1)}, u32[]{:S(2)}, u32[]{:S(2)}) collective-permute-start(bf16[40,1,1,2688]{3,0,2,1:T(8,128)(2,1)S(1)} %copy.58), channel_id=1, source_target_pairs={{1,0},{2,1},{3,2},{4,3},{5,4},{6,5},{7,6},{8,7},{9,8},{10,9},{11,1... | collective-permute-start | bytes 645128 | tf_op jit(solution)/shard_map/ppermute | solution.py:25
  17.3 15.3 %copy-start.12 = (s32[640]{0:T(1024)S(1)}, s32[640]{0:T(1024)}, u32[]{:S(2)}) copy-start(s32[640]{0:T(1024)} %param.13) | copy-start | bytes 7684
  17.3 16.8 %copy-start.4 = (bf16[21,4,4,128]{3,2,1,0:T(4,128)(2,1)S(1)}, bf16[21,4,4,128]{3,2,1,0:T(4,128)(2,1)}, u32[]{:S(2)}) copy-start(bf16[21,4,4,128]{3,2,1,0:T(4,128)(2,1)} %param.19) | copy-start | bytes 258052
  17.3 17.5 %copy-start.2 = (bf16[4,8,20,640]{3,1,2,0:T(8,128)(2,1)S(1)}, bf16[4,8,20,640]{3,1,2,0:T(8,128)(2,1)}, u32[]{:S(2)}) copy-start(bf16[4,8,20,640]{3,1,2,0:T(8,128)(2,1)} %param.10) | copy-start | bytes 2457604
  21.3 13.5 %copy-start.8 = (s32[21,4,128]{2,1,0:T(4,128)S(1)}, s32[21,4,128]{2,1,0:T(4,128)}, u32[]{:S(2)}) copy-start(s32[21,4,128]{2,1,0:T(4,128)} %param.18) | copy-start | bytes 129028
  25.1 10.2 %copy-start.3 = (bf16[20,32,640]{2,1,0:T(8,128)(2,1)S(1)}, bf16[20,32,640]{2,1,0:T(8,128)(2,1)}, u32[]{:S(2)}) copy-start(bf16[20,32,640]{2,1,0:T(8,128)(2,1)} %param.11) | copy-start | bytes 2457604
  25.1 43.2 %collective-permute-start.3 = (bf16[4,320,128]{2,1,0:T(8,128)(2,1)}, bf16[4,320,128]{2,1,0:T(8,128)(2,1)}, u32[]{:S(2)}, u32[]{:S(2)}) collective-permute-start(bf16[4,320,128]{2,1,0:T(8,128)(2,1)} %get-tuple-element.21), channel_id=1, source_target_pairs={{16,0},{32,16},{48,32},{64,48},{80,64},{96,80},{112,96},{128,112},... | collective-permute-start | bytes 983048 | tf_op jit(solution)/shard_map/ppermute | solution.py:35
  27.7 40.6 %collective-permute-start.4 = (bf16[4,320,128]{2,1,0:T(8,128)(2,1)}, bf16[4,320,128]{2,1,0:T(8,128)(2,1)}, u32[]{:S(2)}, u32[]{:S(2)}) collective-permute-start(bf16[4,320,128]{2,1,0:T(8,128)(2,1)} %get-tuple-element.23), channel_id=1, source_target_pairs={{0,16},{16,32},{32,48},{48,64},{64,80},{80,96},{96,112},{112,128},... | collective-permute-start | bytes 983048 | tf_op jit(solution)/shard_map/ppermute | solution.py:35
  34.8 15.2 %copy-start.9 = (s32[21,4,128]{2,1,0:T(4,128)S(1)}, s32[21,4,128]{2,1,0:T(4,128)}, u32[]{:S(2)}) copy-start(s32[21,4,128]{2,1,0:T(4,128)} %param.18) | copy-start | bytes 129028
  34.9 15.2 %copy-start.10 = (f32[21,4,1,128]{3,2,1,0:T(1,128)S(1)}, f32[21,4,1,128]{3,2,1,0:T(1,128)}, u32[]{:S(2)}) copy-start(f32[21,4,1,128]{3,2,1,0:T(1,128)} %get-tuple-element.61) | copy-start | bytes 129028
  35.9 22.4 %copy-start.16 = (bf16[4,320,128]{2,1,0:T(8,128)(2,1)S(1)}, bf16[4,320,128]{2,1,0:T(8,128)(2,1)}, u32[]{:S(2)}) copy-start(bf16[4,320,128]{2,1,0:T(8,128)(2,1)} %get-tuple-element.31) | copy-start | bytes 983044
  35.9 25.9 %copy-start.15 = (bf16[4,320,128]{2,1,0:T(8,128)(2,1)S(1)}, bf16[4,320,128]{2,1,0:T(8,128)(2,1)}, u32[]{:S(2)}) copy-start(bf16[4,320,128]{2,1,0:T(8,128)(2,1)} %get-tuple-element.32) | copy-start | bytes 983044
  37.5 20.0 %all-to-all-start = ((bf16[32,2,320]{2,1,0:T(2,128)(2,1)}), bf16[32,2,320]{2,1,0:T(2,128)(2,1)S(1)}, u32[]{:S(2)}, u32[]{:S(2)}) async-start(bf16[32,2,320]{2,1,0:T(2,128)(2,1)} %reshape.219), calls=%async_computation | async-start | bytes 98304 | tf_op jit(solution)/shard_map/all_to_all | solution.py:202
  58.3 12.5 %collective-permute-start.2 = (bf16[4,320,128]{2,1,0:T(8,128)(2,1)S(1)}, bf16[4,320,128]{2,1,0:T(8,128)(2,1)S(1)}, u32[]{:S(2)}, u32[]{:S(2)}) collective-permute-start(bf16[4,320,128]{2,1,0:T(8,128)(2,1)S(1)} %copy-done.16), channel_id=1, source_target_pairs={{32,0},{48,16},{64,32},{80,48},{96,64},{112,80},{128,96},{144,112}... | collective-permute-start | bytes 983048 | tf_op jit(solution)/shard_map/ppermute | solution.py:35
  61.8 16.1 %collective-permute-start.5 = (bf16[4,320,128]{2,1,0:T(8,128)(2,1)S(1)}, bf16[4,320,128]{2,1,0:T(8,128)(2,1)S(1)}, u32[]{:S(2)}, u32[]{:S(2)}) collective-permute-start(bf16[4,320,128]{2,1,0:T(8,128)(2,1)S(1)} %copy-done.15), channel_id=1, source_target_pairs={{0,32},{16,48},{32,64},{48,80},{64,96},{80,112},{96,128},{112,144}... | collective-permute-start | bytes 983048 | tf_op jit(solution)/shard_map/ppermute | solution.py:35
  68.2 19.0 %copy-start.5 = (bf16[2,8,1,2688]{3,1,0,2:T(8,128)(2,1)}, bf16[2,8,1,2688]{3,1,0,2:T(8,128)(2,1)S(1)}, u32[]{:S(2)}) copy-start(bf16[2,8,1,2688]{3,1,0,2:T(8,128)(2,1)S(1)} %convert_element_type.94) | copy-start | bytes 258052
  70.8 7.1 %copy-start.6 = (bf16[4,320,128]{2,1,0:T(8,128)(2,1)}, bf16[4,320,128]{2,1,0:T(8,128)(2,1)S(1)}, u32[]{:S(2)}) copy-start(bf16[4,320,128]{2,1,0:T(8,128)(2,1)S(1)} %collective-permute-done.2.refs_0_) | copy-start | bytes 983044
  77.9 0.7 copy-start.7

commit v15 on v12

--- a/solution.py
+++ b/solution.py
@@ -91,15 +91,15 @@
     return pl.pallas_call(body, grid_spec=grid_spec, out_shape=out_shape)(listed, remapped)
 
 
-def apply_stencil(slots, stencil, pieces, bin_count, level_count):
+def apply_stencil(slots, stencil, pieces, wind, bin_count, level_count):
     block_count, rows_per_block = stencil.shape[0], stencil.shape[1]
     count = len(pieces)
     cap, rows, _ = pieces[0].shape
     group = 7 if block_count % 7 == 0 else 1
 
-    def body(slot_ref, stencil_ref, *refs):
+    def body(slot_ref, stencil_ref, wind_ref, *refs):
         piece_refs = refs[:count]
-        out_ref, mean_ref, pool_ref, sems = refs[count:]
+        out_ref, flux_ref, pool_ref, sems = refs[count:]
         block = pl.program_id(0)
 
         @pl.when(block == 0)
@@ -122,24 +122,30 @@
             result = total.astype(out_ref.dtype)
             out_ref[:, member * BLK:(member + 1) * BLK] = result
             summed = result.astype(jnp.float32).reshape(bin_count, level_count, BLK).sum(axis=0)
-            mean_ref[:, member * BLK:(member + 1) * BLK] = summed / bin_count
+            average = summed / bin_count
+            for part in range(wind_ref.shape[0]):
+                wide = wind_ref[part, :, member * BLK:(member + 1) * BLK].astype(jnp.float32)
+                flux_ref[part, :, member * BLK:(member + 1) * BLK] = (wide * average).astype(
+                    flux_ref.dtype)
 
     grid_spec = pltpu.PrefetchScalarGridSpec(
         num_scalar_prefetch=1,
         grid=(block_count // group,),
-        in_specs=[pl.BlockSpec((group, rows_per_block, BLK, BLK), lambda b, table: (b, 0, 0, 0))]
+        in_specs=[pl.BlockSpec((group, rows_per_block, BLK, BLK), lambda b, table: (b, 0, 0, 0)),
+                  pl.BlockSpec((wind.shape[0], level_count, group * BLK), lambda b, table: (0, 0, b))]
         + [pl.BlockSpec(memory_space=pl.ANY) for _ in range(count)],
         out_specs=[pl.BlockSpec((rows, group * BLK), lambda b, table: (0, b)),
-                   pl.BlockSpec((level_count, group * BLK), lambda b, table: (0, b))],
+                   pl.BlockSpec((wind.shape[0], level_count, group * BLK),
+                                lambda b, table: (0, 0, b))],
         scratch_shapes=[pltpu.VMEM((count * cap, rows, BLK), pieces[0].dtype),
                         pltpu.SemaphoreType.DMA((count,))],
     )
     out_shape = [jax.ShapeDtypeStruct((rows, block_count * BLK), pieces[0].dtype),
-                 jax.ShapeDtypeStruct((level_count, block_count * BLK), jnp.float32)]
+                 jax.ShapeDtypeStruct(wind.shape, wind.dtype)]
     return pl.pallas_call(
         body, grid_spec=grid_spec, out_shape=out_shape,
         compiler_params=pltpu.CompilerParams(dimension_semantics=("arbitrary",)),
-    )(slots, stencil, *pieces)
+    )(slots, stencil, wind, *pieces)
 
 
 def shards(
@@ -201,10 +207,11 @@
     ).astype(jnp.bfloat16)
     received = lax.all_to_all(coefficients, "band", split_axis=2, concat_axis=3, tiled=True)
     wind_grid = synthesis(received, wave_numbers, NLON).astype(jnp.bfloat16)
-    flat_new, average = apply_stencil(depart_slot.reshape(-1), stencil, pieces, bin_count, level_count)
+    wind_rows = wind_grid.reshape(wind_grid.shape[0], level_count, lat_count * lon_count)
+    flat_new, flux_rows = apply_stencil(depart_slot.reshape(-1), stencil, pieces, wind_rows,
+                                        bin_count, level_count)
     aerosol_new = flat_new.reshape(bin_count, level_count, lat_count, lon_count)
-    average = average.reshape(level_count, lat_count, lon_count)
-    aerosol_flux = (wind_grid.astype(jnp.float32) * average[None]).astype(jnp.bfloat16)
+    aerosol_flux = flux_rows.reshape(wind_grid.shape)
     return (wind_grid, aerosol_new, aerosol_flux)
 
 

time: 77.3 us -> 77.9 us (level)
  the two profiles are of different devices: /device:TPU:25 before, /device:TPU:32 now
where the time goes in v15:
time: 77.9 us; the launch traced here: 77.4 us
  starting transfers between devices  31.9 us (41%)
  other arithmetic  12.5 us (16%)
  Pallas kernels  10.6 us (14%)
  local copies, waits for them, and re-layouts  10 us (13%)
  waiting for transfers between devices  8.68 us (11%)
  matrix products  2.5 us (3%)
  between operations  1.1 us (1%)
    ppermute x4, starting transfers between devices, shifted(): lax.ppermute(value, axis, [(source, source + steps) for source in range(l...  14.1 us
    all_to_all x1, starting transfers between devices, shards(): lax.all_to_all(coefficients, 'band', split_axis=2, concat_axis=3, tiled=T...  13.4 us
    pallas_call x1, Pallas kernels, apply_stencil(): pl.pallas_call(body, grid_spec=grid_spec, out_shape=out_shape, compiler_p...  7.07 us
    all_to_all x1, waiting for transfers between devices, shards(): lax.all_to_all(coefficients, 'band', split_axis=2, concat_axis=3, tiled=T...  5.24 us
    convert_element_type x1, other arithmetic, shards(): stencil = stencil_matrix(depart_offset, depart_weight).astype(jnp.bfloat16)  4.1 us
    reshape x1, other arithmetic, shards(): vertical_sum.astype(jnp.bfloat16).reshape(rows, lat_count * lon_count)  4.03 us
    pallas_call x1, Pallas kernels, pack_blocks(): pl.pallas_call(body, grid_spec=grid_spec, out_shape=out_shape)  3.58 us
    ppermute x1, waiting for transfers between devices, extended(): lax.ppermute(tail, axis, [(i, (i + 1) % count) for i in range(ends)])  3.43 us
  transfers between devices with their start and end apart: 7, of which 2 were waited for; matrix products, arithmetic and copies ran while one was open for 23% of the time, Pallas kernels for 0%

profile of v15, /device:TPU:32, one launch (start us, length us, event | category | flops | bytes accessed | tf_op | source)
XLA Modules:
  0.0 77.4 jit_solution(11866126485235411712)
XLA Ops:
  0.7 2.8 %fusion.32 = (bf16[40,1,1,2688]{3,1,2,0:T(2,128)(2,1)S(1)}, bf16[40,1,1,2688]{3,1,2,0:T(2,128)(2,1)S(1)}) fusion(bf16[40,8,1,2688]{3,1,2,0:T(8,128)(2,1)} %param.14), kind=kLoop, calls=%fused_computation.75 | loop fusion | bytes 860160 | tf_op jit(solution)/shard_map/slice | solution.py:20
  3.5 1.9 %collective-permute-start.1 = (bf16[40,1,1,2688]{3,0,2,1:T(8,128)(2,1)S(1)}, bf16[40,1,1,2688]{3,0,2,1:T(8,128)(2,1)S(1)}, u32[]{:S(2)}, u32[]{:S(2)}) collective-permute-start(bf16[40,1,1,2688]{3,0,2,1:T(8,128)(2,1)S(1)} %copy.72), channel_id=1, source_target_pairs={{1,0},{2,1},{3,2},{4,3},{5,4},{6,5},{7,6},{8,7},{9,8},{10,9},{11,1... | collective-permute-start | bytes 645128 | tf_op jit(solution)/shard_map/ppermute | solution.py:25
  5.5 2.4 %collective-permute-start = (bf16[40,1,1,2688]{3,0,2,1:T(8,128)(2,1)S(1)}, bf16[40,1,1,2688]{3,0,2,1:T(8,128)(2,1)S(1)}, u32[]{:S(2)}, u32[]{:S(2)}) collective-permute-start(bf16[40,1,1,2688]{3,0,2,1:T(8,128)(2,1)S(1)} %copy.71), channel_id=1, source_target_pairs={{0,1},{1,2},{2,3},{3,4},{4,5},{5,6},{6,7},{7,8},{8,9},{9,10},{10,1... | collective-permute-start | bytes 645128 | tf_op jit(solution)/shard_map/ppermute | solution.py:23
  7.9 0.7 slice_bitcast_fusion.2
  8.7 0.7 min.12.listed_ref
  9.5 0.6 reshape.211.slot_ref
  10.1 0.3 copy.58
  10.5 3.4 %collective-permute-done = bf16[40,1,1,2688]{3,0,2,1:T(8,128)(2,1)S(1)} collective-permute-done((bf16[40,1,1,2688]{3,0,2,1:T(8,128)(2,1)S(1)}, bf16[40,1,1,2688]{3,0,2,1:T(8,128)(2,1)S(1)}, u32[]{:S(2)}, u32[]{:S(2)}) %collective-permute-start) | collective-permute-done | bytes 215072 | tf_op jit(solution)/shard_map/ppermute | solution.py:23
  13.9 0.3 copy.56
  14.3 4.0 %fusion.3.source_ref = bf16[320,2688]{1,0:T(8,128)(2,1)} fusion(bf16[40,8,1,2688]{3,1,2,0:T(8,128)(2,1)S(1)} %copy-done.1, bf16[40,1,1,2688]{3,1,2,0:T(2,128)(2,1)S(1)} %copy.58, bf16[40,1,1,2688]{3,1,2,0:T(2,128)(2,1)S(1)} %copy.56, f32[8,2688]{1,0:T(8,128)} %get-tuple-element.51, f32[8,2688]{1,0:T(8,128)} %get-tuple-element.52, ...), kind=kLoop, calls=%fused_computation.10 | loop fusion | flops 12902400 | bytes 4128768 | tf_op jit(solution)/shard_map/reshape | solution.py:170
  18.3 3.6 %shard_map.121 = (bf16[4,320,128]{2,1,0:T(8,128)(2,1)}, bf16[4,320,128]{2,1,0:T(8,128)(2,1)}, bf16[4,320,128]{2,1,0:T(8,128)(2,1)}, bf16[4,320,128]{2,1,0:T(8,128)(2,1)}, bf16[4,320,128]{2,1,0:T(8,128)(2,1)}) custom-call(s32[20]{0:T(128)} %min.12.listed_ref, bf16[320,2688]{1,0:T(8,128)(2,1)} %fusion.3.source_ref), custom_call_target="tpu_custom_call" | custom-call | tf_op jit(solution)/shard_map/pallas_call | solution.py:91
  21.9 1.4 %collective-permute-start.2 = (bf16[4,320,128]{2,1,0:T(8,128)(2,1)}, bf16[4,320,128]{2,1,0:T(8,128)(2,1)}, u32[]{:S(2)}, u32[]{:S(2)}) collective-permute-start(bf16[4,320,128]{2,1,0:T(8,128)(2,1)} %get-tuple-element.16), channel_id=1, source_target_pairs={{32,0},{48,16},{64,32},{80,48},{96,64},{112,80},{128,96},{144,112}... | collective-permute-start | bytes 983048 | tf_op jit(solution)/shard_map/ppermute | solution.py:35
  23.3 1.3 %collective-permute-start.3 = (bf16[4,320,128]{2,1,0:T(8,128)(2,1)}, bf16[4,320,128]{2,1,0:T(8,128)(2,1)}, u32[]{:S(2)}, u32[]{:S(2)}) collective-permute-start(bf16[4,320,128]{2,1,0:T(8,128)(2,1)} %get-tuple-element.17), channel_id=1, source_target_pairs={{16,0},{32,16},{48,32},{64,48},{80,64},{96,80},{112,96},{128,112},... | collective-permute-start | bytes 983048 | tf_op jit(solution)/shard_map/ppermute | solution.py:35
  24.6 5.3 %collective-permute-start.4 = (bf16[4,320,128]{2,1,0:T(8,128)(2,1)}, bf16[4,320,128]{2,1,0:T(8,128)(2,1)}, u32[]{:S(2)}, u32[]{:S(2)}) collective-permute-start(bf16[4,320,128]{2,1,0:T(8,128)(2,1)} %get-tuple-element.19), channel_id=1, source_target_pairs={{0,16},{16,32},{32,48},{48,64},{64,80},{80,96},{96,112},{112,128},... | collective-permute-start | bytes 983048 | tf_op jit(solution)/shard_map/ppermute | solution.py:35
  29.9 6.1 %collective-permute-start.5 = (bf16[4,320,128]{2,1,0:T(8,128)(2,1)}, bf16[4,320,128]{2,1,0:T(8,128)(2,1)}, u32[]{:S(2)}, u32[]{:S(2)}) collective-permute-start(bf16[4,320,128]{2,1,0:T(8,128)(2,1)} %get-tuple-element.20), channel_id=1, source_target_pairs={{0,32},{16,48},{32,64},{48,80},{64,96},{80,112},{96,128},{112,144}... | collective-permute-start | bytes 983048 | tf_op jit(solution)/shard_map/ppermute | solution.py:35
  36.0 1.4 %fusion.16 = (f32[640,128]{1,0:T(8,128)S(1)}, f32[640,128]{1,0:T(8,128)S(1)}) fusion(s32[640]{0:T(1024)S(1)} %copy-done.9), kind=kLoop, calls=%fused_computation.32 | loop fusion | flops 737280 | bytes 657920 | tf_op jit(solution)/shard_map/cos | solution.py:56
  37.5 1.4 %broadcast_add_fusion.2 = (s32[21,4,128]{2,1,0:T(4,128)}, s32[21,4,128]{2,1,0:T(4,128)S(1)}, s32[21,4,128]{2,1,0:T(4,128)S(1)}) fusion(s32[21,4,128]{2,1,0:T(4,128)} %param.18), kind=kLoop, calls=%fused_computation.69 | loop fusion | flops 32256 | bytes 172032 | tf_op jit(solution)/shard_map/add | solution.py:67
  39.0 0.7 slice_convert_fusion.3
  39.7 0.4 convolution_bitcast_fusion.1
  40.1 0.4 convolution_bitcast_fusion
  40.7 0.6 copy.61
  41.3 1.0 %reshape.222 = bf16[32,2,320]{2,1,0:T(2,128)(2,1)} reshape(bf16[32,4,8,20]{3,2,1,0:T(8,128)(2,1)S(1)} %bitcast.51) | data formatting | bytes 81920
  42.2 13.4 %all-to-all-start = ((bf16[32,2,320]{2,1,0:T(2,128)(2,1)}), bf16[32,2,320]{2,1,0:T(2,128)(2,1)S(1)}, u32[]{:S(2)}, u32[]{:S(2)}) async-start(bf16[32,2,320]{2,1,0:T(2,128)(2,1)} %reshape.222), calls=%async_computation | async-start | bytes 98304 | tf_op jit(solution)/shard_map/all_to_all | solution.py:208
  55.7 4.1 %add_convert_fusion.stencil_ref = bf16[21,4,128,128]{3,2,1,0:T(8,128)(2,1)} fusion(f32[21,4,128]{2,1,0:T(4,128)S(1)} %bitcast.54, s32[21,4,128]{2,1,0:T(4,128)S(1)} %get-tuple-element.62, f32[21,4,128]{2,1,0:T(4,128)S(1)} %bitcast.55, s32[21,4,128]{2,1,0:T(4,128)S(1)} %get-tuple-element.63, f32[21,4,128]{2,1,0:T(4,128)S(1)} %bitcast.56, ...), kind=kLoop, calls=%fused_computation | loop fusion | flops 16515072 | bytes 3096576 | tf_op jit(solution)/shard_map/convert_element_type | solution.py:181
  59.8 0.3 cosine_multiply_fusion
  60.1 5.2 %all-to-all-done = bf16[32,2,320]{2,1,0:T(2,128)(2,1)S(1)} async-done(((bf16[32,2,320]{2,1,0:T(2,128)(2,1)}), bf16[32,2,320]{2,1,0:T(2,128)(2,1)S(1)}, u32[]{:S(2)}, u32[]{:S(2)}) %all-to-all-start) | async-done | bytes 40992 | tf_op jit(solution)/shard_map/all_to_all | solution.py:208
  65.4 0.4 reshape.223
  65.8 0.4 copy.62
  67.0 1.7 %fusion.4 = bf16[2,8,21,128]{3,2,1,0:T(8,128)(2,1)S(1)} fusion(f32[2,8,1,21,640]{4,3,1,0,2:T(8,128)S(1)} %get-tuple-element.54, f32[2,8,1,21,640]{4,3,1,0,2:T(8,128)S(1)} %get-tuple-element.53, f32[640,128]{1,0:T(8,128)S(1)} %get-tuple-element.67, f32[640,128]{1,0:T(8,128)S(1)} %get-tuple-element.66), kind=kOutput, calls=%fused_computation.15 | convolution fusion | flops 661239808 | bytes 2461696 | tf_op jit(solution)/shard_map/wklom,mi->wkloi/dot_general | solution.py:57
  68.7 0.7 convert_element_type.86.wind_ref
  69.4 0.7 convert_element_type.84
  70.1 7.1 %shard_map.122 = (bf16[320,2688]{1,0:T(8,128)(2,1)}, bf16[2,8,2688]{2,1,0:T(8,128)(2,1)}) custom-call(s32[84]{0:T(128)} %reshape.211.slot_ref, bf16[21,4,128,128]{3,2,1,0:T(8,128)(2,1)} %add_convert_fusion.stencil_ref, bf16[2,8,2688]{2,1,0:T(8,128)(2,1)} %convert_element_type.86.wind_ref, bf16[4,320,128]{2,1,0:T(8,128)(2,1)} %collective-permute-done.2.refs_0_, ...), custom_call_target="tpu_custom_call" | custom-call | tf_op jit(solution)/shard_map/pallas_call | solution.py:145
  (44 shorter events, 1.4 us)
Async XLA Ops:
  0.6 39.1 %copy-start = (bf16[20,32,640]{2,1,0:T(8,128)(2,1)S(1)}, bf16[20,32,640]{2,1,0:T(8,128)(2,1)}, u32[]{:S(2)}) copy-start(bf16[20,32,640]{2,1,0:T(8,128)(2,1)} %param.12) | copy-start | bytes 2457604
  0.6 13.6 %copy-start.1 = (bf16[40,8,1,2688]{3,1,2,0:T(8,128)(2,1)S(1)}, bf16[40,8,1,2688]{3,1,2,0:T(8,128)(2,1)}, u32[]{:S(2)}) copy-start(bf16[40,8,1,2688]{3,1,2,0:T(8,128)(2,1)} %param.14) | copy-start | bytes 5160964
  0.7 7.2 %copy-start.8 = (bf16[3,8,1,2688]{3,1,2,0:T(8,128)(2,1)S(1)}, bf16[3,8,1,2688]{3,1,2,0:T(8,128)(2,1)}, u32[]{:S(2)}) copy-start(bf16[3,8,1,2688]{3,1,2,0:T(8,128)(2,1)} %param.15) | copy-start | bytes 387076
  0.7 8.0 %copy-start.11 = (s32[1,5,4]{1,2,0:T(4,128)S(1)}, s32[1,5,4]{1,2,0:T(4,128)}, u32[]{:S(2)}) copy-start(s32[1,5,4]{1,2,0:T(4,128)} %param.16) | copy-start | bytes 244
  0.7 8.7 %copy-start.10 = (s32[21,4]{0,1:T(4,128)S(1)}, s32[21,4]{0,1:T(4,128)}, u32[]{:S(2)}) copy-start(s32[21,4]{0,1:T(4,128)} %param.17) | copy-start | bytes 1012
  3.5 6.6 %collective-permute-start.1 = (bf16[40,1,1,2688]{3,0,2,1:T(8,128)(2,1)S(1)}, bf16[40,1,1,2688]{3,0,2,1:T(8,128)(2,1)S(1)}, u32[]{:S(2)}, u32[]{:S(2)}) collective-permute-start(bf16[40,1,1,2688]{3,0,2,1:T(8,128)(2,1)S(1)} %copy.72), channel_id=1, source_target_pairs={{1,0},{2,1},{3,2},{4,3},{5,4},{6,5},{7,6},{8,7},{9,8},{10,9},{11,1... | collective-permute-start | bytes 645128 | tf_op jit(solution)/shard_map/ppermute | solution.py:25
  5.5 8.4 %collective-permute-start = (bf16[40,1,1,2688]{3,0,2,1:T(8,128)(2,1)S(1)}, bf16[40,1,1,2688]{3,0,2,1:T(8,128)(2,1)S(1)}, u32[]{:S(2)}, u32[]{:S(2)}) collective-permute-start(bf16[40,1,1,2688]{3,0,2,1:T(8,128)(2,1)S(1)} %copy.71), channel_id=1, source_target_pairs={{0,1},{1,2},{2,3},{3,4},{4,5},{5,6},{6,7},{7,8},{8,9},{9,10},{10,1... | collective-permute-start | bytes 645128 | tf_op jit(solution)/shard_map/ppermute | solution.py:23
  14.2 21.8 %copy-start.9 = (s32[640]{0:T(1024)S(1)}, s32[640]{0:T(1024)}, u32[]{:S(2)}) copy-start(s32[640]{0:T(1024)} %param.13) | copy-start | bytes 7684
  14.2 24.7 %copy-start.4 = (bf16[21,4,4,128]{3,2,1,0:T(4,128)(2,1)S(1)}, bf16[21,4,4,128]{3,2,1,0:T(4,128)(2,1)}, u32[]{:S(2)}) copy-start(bf16[21,4,4,128]{3,2,1,0:T(4,128)(2,1)} %param.19) | copy-start | bytes 258052
  14.3 25.5 %copy-start.2 = (bf16[4,8,20,640]{3,1,2,0:T(8,128)(2,1)S(1)}, bf16[4,8,20,640]{3,1,2,0:T(8,128)(2,1)}, u32[]{:S(2)}) copy-start(bf16[4,8,20,640]{3,1,2,0:T(8,128)(2,1)} %param.10) | copy-start | bytes 2457604
  21.9 18.3 %copy-start.3 = (bf16[20,32,640]{2,1,0:T(8,128)(2,1)S(1)}, bf16[20,32,640]{2,1,0:T(8,128)(2,1)}, u32[]{:S(2)}) copy-start(bf16[20,32,640]{2,1,0:T(8,128)(2,1)} %param.11) | copy-start | bytes 2457604
  21.9 48.3 %collective-permute-start.2 = (bf16[4,320,128]{2,1,0:T(8,128)(2,1)}, bf16[4,320,128]{2,1,0:T(8,128)(2,1)}, u32[]{:S(2)}, u32[]{:S(2)}) collective-permute-start(bf16[4,320,128]{2,1,0:T(8,128)(2,1)} %get-tuple-element.16), channel_id=1, source_target_pairs={{32,0},{48,16},{64,32},{80,48},{96,64},{112,80},{128,96},{144,112}... | collective-permute-start | bytes 983048 | tf_op jit(solution)/shard_map/ppermute | solution.py:35
  23.3 46.8 %collective-permute-start.3 = (bf16[4,320,128]{2,1,0:T(8,128)(2,1)}, bf16[4,320,128]{2,1,0:T(8,128)(2,1)}, u32[]{:S(2)}, u32[]{:S(2)}) collective-permute-start(bf16[4,320,128]{2,1,0:T(8,128)(2,1)} %get-tuple-element.17), channel_id=1, source_target_pairs={{16,0},{32,16},{48,32},{64,48},{80,64},{96,80},{112,96},{128,112},... | collective-permute-start | bytes 983048 | tf_op jit(solution)/shard_map/ppermute | solution.py:35
  24.6 45.5 %collective-permute-start.4 = (bf16[4,320,128]{2,1,0:T(8,128)(2,1)}, bf16[4,320,128]{2,1,0:T(8,128)(2,1)}, u32[]{:S(2)}, u32[]{:S(2)}) collective-permute-start(bf16[4,320,128]{2,1,0:T(8,128)(2,1)} %get-tuple-element.19), channel_id=1, source_target_pairs={{0,16},{16,32},{32,48},{48,64},{64,80},{80,96},{96,112},{112,128},... | collective-permute-start | bytes 983048 | tf_op jit(solution)/shard_map/ppermute | solution.py:35
  29.9 40.2 %collective-permute-start.5 = (bf16[4,320,128]{2,1,0:T(8,128)(2,1)}, bf16[4,320,128]{2,1,0:T(8,128)(2,1)}, u32[]{:S(2)}, u32[]{:S(2)}) collective-permute-start(bf16[4,320,128]{2,1,0:T(8,128)(2,1)} %get-tuple-element.20), channel_id=1, source_target_pairs={{0,32},{16,48},{32,64},{48,80},{64,96},{80,112},{96,128},{112,144}... | collective-permute-start | bytes 983048 | tf_op jit(solution)/shard_map/ppermute | solution.py:35
  39.7 16.0 %copy-start.5 = (s32[21,4,128]{2,1,0:T(4,128)S(1)}, s32[21,4,128]{2,1,0:T(4,128)}, u32[]{:S(2)}) copy-start(s32[21,4,128]{2,1,0:T(4,128)} %param.18) | copy-start | bytes 129028
  39.7 16.0 %copy-start.6 = (s32[21,4,128]{2,1,0:T(4,128)S(1)}, s32[21,4,128]{2,1,0:T(4,128)}, u32[]{:S(2)}) copy-start(s32[21,4,128]{2,1,0:T(4,128)} %get-tuple-element.61) | copy-start | bytes 129028
  39.7 16.0 %copy-start.7 = (f32[21,4,1,128]{3,2,1,0:T(1,128)S(1)}, f32[21,4,1,128]{3,2,1,0:T(1,128)}, u32[]{:S(2)}) copy-start(f32[21,4,1,128]{3,2,1,0:T(1,128)} %get-tuple-element.58) | copy-start | bytes 129028
  42.2 23.2 %all-to-all-start = ((bf16[32,2,320]{2,1,0:T(2,128)(2,1)}), bf16[32,2,320]{2,1,0:T(2,128)(2,1)S(1)}, u32[]{:S(2)}, u32[]{:S(2)}) async-start(bf16[32,2,320]{2,1,0:T(2,128)(2,1)} %reshape.222), calls=%async_computation | async-start | bytes 98304 | tf_op jit(solution)/shard_map/all_to_all | solution.py:208

commit v16 on v12

--- a/solution.py
+++ b/solution.py
@@ -95,7 +95,7 @@
     block_count, rows_per_block = stencil.shape[0], stencil.shape[1]
     count = len(pieces)
     cap, rows, _ = pieces[0].shape
-    group = 7 if block_count % 7 == 0 else 1
+    group = block_count
 
     def body(slot_ref, stencil_ref, *refs):
         piece_refs = refs[:count]

time: 77.3 us -> 77.2 us (level)
  no operation moved by 1% of the time
where the time goes in v16:
time: 77.2 us; the launch traced here: 76.7 us
  starting transfers between devices  33.1 us (43%)
  other arithmetic  12.6 us (16%)
  Pallas kernels  10.7 us (14%)
  local copies, waits for them, and re-layouts  8.63 us (11%)
  waiting for transfers between devices  8.11 us (11%)
  matrix products  2.5 us (3%)
  between operations  1 us (1%)
    ppermute x4, starting transfers between devices, shifted(): lax.ppermute(value, axis, [(source, source + steps) for source in range(l...  13.3 us
    all_to_all x1, starting transfers between devices, shards(): lax.all_to_all(coefficients, 'band', split_axis=2, concat_axis=3, tiled=T...  12.9 us
    pallas_call x1, Pallas kernels, apply_stencil(): pl.pallas_call(body, grid_spec=grid_spec, out_shape=out_shape, compiler_p...  6.99 us
    ppermute x1, starting transfers between devices, extended(): lax.ppermute(tail, axis, [(i, (i + 1) % count) for i in range(ends)])  4.98 us
    all_to_all x1, waiting for transfers between devices, shards(): lax.all_to_all(coefficients, 'band', split_axis=2, concat_axis=3, tiled=T...  4.14 us
    convert_element_type x1, other arithmetic, shards(): stencil = stencil_matrix(depart_offset, depart_weight).astype(jnp.bfloat16)  4.06 us
    reshape x1, other arithmetic, shards(): vertical_sum.astype(jnp.bfloat16).reshape(rows, lat_count * lon_count)  4.02 us
    ppermute x1, waiting for transfers between devices, extended(): lax.ppermute(head, axis, [((i + 1) % count, i) for i in range(ends)])  3.96 us
  transfers between devices with their start and end apart: 7, of which 2 were waited for; matrix products, arithmetic and copies ran while one was open for 20% of the time, Pallas kernels for 0%

profile of v16, /device:TPU:25, one launch (start us, length us, event | category | flops | bytes accessed | tf_op | source)
XLA Modules:
  0.0 76.7 jit_solution(1492466803636725042)
XLA Ops:
  0.7 2.8 %fusion.33 = (bf16[40,1,1,2688]{3,1,2,0:T(2,128)(2,1)S(1)}, bf16[40,1,1,2688]{3,1,2,0:T(2,128)(2,1)S(1)}) fusion(bf16[40,8,1,2688]{3,1,2,0:T(8,128)(2,1)} %param.14), kind=kLoop, calls=%fused_computation.77 | loop fusion | bytes 860160 | tf_op jit(solution)/shard_map/slice | solution.py:20
  3.5 5.0 %collective-permute-start = (bf16[40,1,1,2688]{3,0,2,1:T(8,128)(2,1)S(1)}, bf16[40,1,1,2688]{3,0,2,1:T(8,128)(2,1)S(1)}, u32[]{:S(2)}, u32[]{:S(2)}) collective-permute-start(bf16[40,1,1,2688]{3,0,2,1:T(8,128)(2,1)S(1)} %copy.71), channel_id=1, source_target_pairs={{0,1},{1,2},{2,3},{3,4},{4,5},{5,6},{6,7},{7,8},{8,9},{9,10},{10,1... | collective-permute-start | bytes 645128 | tf_op jit(solution)/shard_map/ppermute | solution.py:23
  8.5 1.9 %collective-permute-start.1 = (bf16[40,1,1,2688]{3,0,2,1:T(8,128)(2,1)S(1)}, bf16[40,1,1,2688]{3,0,2,1:T(8,128)(2,1)S(1)}, u32[]{:S(2)}, u32[]{:S(2)}) collective-permute-start(bf16[40,1,1,2688]{3,0,2,1:T(8,128)(2,1)S(1)} %copy.72), channel_id=1, source_target_pairs={{1,0},{2,1},{3,2},{4,3},{5,4},{6,5},{7,6},{8,7},{9,8},{10,9},{11,1... | collective-permute-start | bytes 645128 | tf_op jit(solution)/shard_map/ppermute | solution.py:25
  10.5 0.7 slice_bitcast_fusion.2
  11.3 0.6 min.12.listed_ref
  12.0 0.6 reshape.224.slot_ref
  12.6 0.3 copy.56
  13.0 4.0 %collective-permute-done.1 = bf16[40,1,1,2688]{3,0,2,1:T(8,128)(2,1)S(1)} collective-permute-done((bf16[40,1,1,2688]{3,0,2,1:T(8,128)(2,1)S(1)}, bf16[40,1,1,2688]{3,0,2,1:T(8,128)(2,1)S(1)}, u32[]{:S(2)}, u32[]{:S(2)}) %collective-permute-start.1) | collective-permute-done | bytes 215072 | tf_op jit(solution)/shard_map/ppermute | solution.py:25
  16.9 0.3 copy.58
  17.3 4.0 %fusion.3.source_ref = bf16[320,2688]{1,0:T(8,128)(2,1)} fusion(bf16[40,8,1,2688]{3,1,2,0:T(8,128)(2,1)S(1)} %copy-done.1, bf16[40,1,1,2688]{3,1,2,0:T(2,128)(2,1)S(1)} %copy.58, bf16[40,1,1,2688]{3,1,2,0:T(2,128)(2,1)S(1)} %copy.56, f32[8,2688]{1,0:T(8,128)} %get-tuple-element.51, f32[8,2688]{1,0:T(8,128)} %get-tuple-element.52, ...), kind=kLoop, calls=%fused_computation.10 | loop fusion | flops 12902400 | bytes 4128768 | tf_op jit(solution)/shard_map/reshape | solution.py:164
  21.3 3.8 %shard_map.121 = (bf16[4,320,128]{2,1,0:T(8,128)(2,1)}, bf16[4,320,128]{2,1,0:T(8,128)(2,1)}, bf16[4,320,128]{2,1,0:T(8,128)(2,1)}, bf16[4,320,128]{2,1,0:T(8,128)(2,1)}, bf16[4,320,128]{2,1,0:T(8,128)(2,1)}) custom-call(s32[20]{0:T(128)} %min.12.listed_ref, bf16[320,2688]{1,0:T(8,128)(2,1)} %fusion.3.source_ref), custom_call_target="tpu_custom_call" | custom-call | tf_op jit(solution)/shard_map/pallas_call | solution.py:91
  25.1 1.4 %collective-permute-start.2 = (bf16[4,320,128]{2,1,0:T(8,128)(2,1)}, bf16[4,320,128]{2,1,0:T(8,128)(2,1)}, u32[]{:S(2)}, u32[]{:S(2)}) collective-permute-start(bf16[4,320,128]{2,1,0:T(8,128)(2,1)} %get-tuple-element.16), channel_id=1, source_target_pairs={{32,0},{48,16},{64,32},{80,48},{96,64},{112,80},{128,96},{144,112}... | collective-permute-start | bytes 983048 | tf_op jit(solution)/shard_map/ppermute | solution.py:35
  26.5 1.3 %collective-permute-start.3 = (bf16[4,320,128]{2,1,0:T(8,128)(2,1)}, bf16[4,320,128]{2,1,0:T(8,128)(2,1)}, u32[]{:S(2)}, u32[]{:S(2)}) collective-permute-start(bf16[4,320,128]{2,1,0:T(8,128)(2,1)} %get-tuple-element.17), channel_id=1, source_target_pairs={{16,0},{32,16},{48,32},{64,48},{80,64},{96,80},{112,96},{128,112},... | collective-permute-start | bytes 983048 | tf_op jit(solution)/shard_map/ppermute | solution.py:35
  27.8 4.7 %collective-permute-start.4 = (bf16[4,320,128]{2,1,0:T(8,128)(2,1)}, bf16[4,320,128]{2,1,0:T(8,128)(2,1)}, u32[]{:S(2)}, u32[]{:S(2)}) collective-permute-start(bf16[4,320,128]{2,1,0:T(8,128)(2,1)} %get-tuple-element.19), channel_id=1, source_target_pairs={{0,16},{16,32},{32,48},{48,64},{64,80},{80,96},{96,112},{112,128},... | collective-permute-start | bytes 983048 | tf_op jit(solution)/shard_map/ppermute | solution.py:35
  32.5 5.9 %collective-permute-start.5 = (bf16[4,320,128]{2,1,0:T(8,128)(2,1)}, bf16[4,320,128]{2,1,0:T(8,128)(2,1)}, u32[]{:S(2)}, u32[]{:S(2)}) collective-permute-start(bf16[4,320,128]{2,1,0:T(8,128)(2,1)} %get-tuple-element.20), channel_id=1, source_target_pairs={{0,32},{16,48},{32,64},{48,80},{64,96},{80,112},{96,128},{112,144}... | collective-permute-start | bytes 983048 | tf_op jit(solution)/shard_map/ppermute | solution.py:35
  38.4 1.4 %fusion.16 = (f32[640,128]{1,0:T(8,128)S(1)}, f32[640,128]{1,0:T(8,128)S(1)}) fusion(s32[640]{0:T(1024)S(1)} %copy-done.10), kind=kLoop, calls=%fused_computation.32 | loop fusion | flops 737280 | bytes 657920 | tf_op jit(solution)/shard_map/cos | solution.py:56
  39.9 0.7 slice_convert_fusion.3
  40.7 0.4 convolution_bitcast_fusion.1
  41.1 0.4 convolution_bitcast_fusion
  41.7 0.6 copy.61
  42.3 1.0 %reshape.234 = bf16[32,2,320]{2,1,0:T(2,128)(2,1)} reshape(bf16[32,4,8,20]{3,2,1,0:T(8,128)(2,1)S(1)} %bitcast.50) | data formatting | bytes 81920
  43.3 12.9 %all-to-all-start = ((bf16[32,2,320]{2,1,0:T(2,128)(2,1)}), bf16[32,2,320]{2,1,0:T(2,128)(2,1)S(1)}, u32[]{:S(2)}, u32[]{:S(2)}) async-start(bf16[32,2,320]{2,1,0:T(2,128)(2,1)} %reshape.234), calls=%async_computation | async-start | bytes 98304 | tf_op jit(solution)/shard_map/all_to_all | solution.py:202
  56.2 4.1 %add_convert_fusion.stencil_ref = bf16[21,4,128,128]{3,2,1,0:T(8,128)(2,1)} fusion(f32[21,4,128]{2,1,0:T(4,128)S(1)} %bitcast.54, s32[21,4,128]{2,1,0:T(4,128)S(1)} %get-tuple-element.62, f32[21,4,128]{2,1,0:T(4,128)S(1)} %bitcast.55, s32[21,4,128]{2,1,0:T(4,128)S(1)} %get-tuple-element.63, f32[21,4,128]{2,1,0:T(4,128)S(1)} %bitcast.56, ...), kind=kLoop, calls=%fused_computation | loop fusion | flops 16515072 | bytes 3096576 | tf_op jit(solution)/shard_map/convert_element_type | solution.py:175
  60.2 0.3 cosine_multiply_fusion
  60.6 4.1 %all-to-all-done = bf16[32,2,320]{2,1,0:T(2,128)(2,1)S(1)} async-done(((bf16[32,2,320]{2,1,0:T(2,128)(2,1)}), bf16[32,2,320]{2,1,0:T(2,128)(2,1)S(1)}, u32[]{:S(2)}, u32[]{:S(2)}) %all-to-all-start) | async-done | bytes 40992 | tf_op jit(solution)/shard_map/all_to_all | solution.py:202
  64.7 0.4 reshape.235
  65.1 0.4 copy.62
  65.5 0.3 copy.63
  65.8 0.3 reshape.226
  66.3 1.7 %fusion.4 = bf16[2,8,21,128]{3,2,1,0:T(8,128)(2,1)S(1)} fusion(f32[2,8,1,21,640]{4,3,1,0,2:T(8,128)S(1)} %get-tuple-element.54, f32[2,8,1,21,640]{4,3,1,0,2:T(8,128)S(1)} %get-tuple-element.53, f32[640,128]{1,0:T(8,128)S(1)} %get-tuple-element.67, f32[640,128]{1,0:T(8,128)S(1)} %get-tuple-element.66), kind=kOutput, calls=%fused_computation.15 | convolution fusion | flops 661239808 | bytes 2461696 | tf_op jit(solution)/shard_map/wklom,mi->wkloi/dot_general | solution.py:57
  68.2 7.0 %shard_map.122 = (bf16[320,2688]{1,0:T(8,128)(2,1)}, f32[8,2688]{1,0:T(8,128)}) custom-call(s32[84]{0:T(128)} %reshape.224.slot_ref, bf16[21,4,128,128]{3,2,1,0:T(8,128)(2,1)} %add_convert_fusion.stencil_ref, bf16[4,320,128]{2,1,0:T(8,128)(2,1)} %collective-permute-done.2.refs_0_, bf16[4,320,128]{2,1,0:T(8,128)(2,1)} %collective-permute-done.3.refs_1_, ...), custom_call_target="tpu_custom_call" | custom-call | tf_op jit(solution)/shard_map/pallas_call | solution.py:139
  75.2 1.5 %fusion.18 = bf16[2,8,1,2688]{3,1,2,0:T(8,128)(2,1)} fusion(bf16[2,8,1,2688]{3,1,0,2:T(8,128)(2,1)S(1)} %convert_element_type.106, f32[8,2688]{1,0:T(8,128)} %get-tuple-element.28), kind=kLoop, calls=%fused_computation.37 | loop fusion | flops 129024 | bytes 258048
  (46 shorter events, 0.9 us)
Async XLA Ops:
  0.6 40.0 %copy-start = (bf16[20,32,640]{2,1,0:T(8,128)(2,1)S(1)}, bf16[20,32,640]{2,1,0:T(8,128)(2,1)}, u32[]{:S(2)}) copy-start(bf16[20,32,640]{2,1,0:T(8,128)(2,1)} %param.12) | copy-start | bytes 2457604
  0.6 16.6 %copy-start.1 = (bf16[40,8,1,2688]{3,1,2,0:T(8,128)(2,1)S(1)}, bf16[40,8,1,2688]{3,1,2,0:T(8,128)(2,1)}, u32[]{:S(2)}) copy-start(bf16[40,8,1,2688]{3,1,2,0:T(8,128)(2,1)} %param.14) | copy-start | bytes 5160964
  0.7 9.8 %copy-start.9 = (bf16[3,8,1,2688]{3,1,2,0:T(8,128)(2,1)S(1)}, bf16[3,8,1,2688]{3,1,2,0:T(8,128)(2,1)}, u32[]{:S(2)}) copy-start(bf16[3,8,1,2688]{3,1,2,0:T(8,128)(2,1)} %param.15) | copy-start | bytes 387076
  0.7 10.5 %copy-start.12 = (s32[1,5,4]{1,2,0:T(4,128)S(1)}, s32[1,5,4]{1,2,0:T(4,128)}, u32[]{:S(2)}) copy-start(s32[1,5,4]{1,2,0:T(4,128)} %param.16) | copy-start | bytes 244
  0.7 11.2 %copy-start.11 = (s32[21,4]{0,1:T(4,128)S(1)}, s32[21,4]{0,1:T(4,128)}, u32[]{:S(2)}) copy-start(s32[21,4]{0,1:T(4,128)} %param.17) | copy-start | bytes 1012
  3.5 9.1 %collective-permute-start = (bf16[40,1,1,2688]{3,0,2,1:T(8,128)(2,1)S(1)}, bf16[40,1,1,2688]{3,0,2,1:T(8,128)(2,1)S(1)}, u32[]{:S(2)}, u32[]{:S(2)}) collective-permute-start(bf16[40,1,1,2688]{3,0,2,1:T(8,128)(2,1)S(1)} %copy.71), channel_id=1, source_target_pairs={{0,1},{1,2},{2,3},{3,4},{4,5},{5,6},{6,7},{7,8},{8,9},{9,10},{10,1... | collective-permute-start | bytes 645128 | tf_op jit(solution)/shard_map/ppermute | solution.py:23
  8.5 8.4 %collective-permute-start.1 = (bf16[40,1,1,2688]{3,0,2,1:T(8,128)(2,1)S(1)}, bf16[40,1,1,2688]{3,0,2,1:T(8,128)(2,1)S(1)}, u32[]{:S(2)}, u32[]{:S(2)}) collective-permute-start(bf16[40,1,1,2688]{3,0,2,1:T(8,128)(2,1)S(1)} %copy.72), channel_id=1, source_target_pairs={{1,0},{2,1},{3,2},{4,3},{5,4},{6,5},{7,6},{8,7},{9,8},{10,9},{11,1... | collective-permute-start | bytes 645128 | tf_op jit(solution)/shard_map/ppermute | solution.py:25
  17.3 21.1 %copy-start.10 = (s32[640]{0:T(1024)S(1)}, s32[640]{0:T(1024)}, u32[]{:S(2)}) copy-start(s32[640]{0:T(1024)} %param.13) | copy-start | bytes 7684
  17.3 22.6 %copy-start.4 = (bf16[21,4,4,128]{3,2,1,0:T(4,128)(2,1)S(1)}, bf16[21,4,4,128]{3,2,1,0:T(4,128)(2,1)}, u32[]{:S(2)}) copy-start(bf16[21,4,4,128]{3,2,1,0:T(4,128)(2,1)} %param.19) | copy-start | bytes 258052
  17.3 23.3 %copy-start.2 = (bf16[4,8,20,640]{3,1,2,0:T(8,128)(2,1)S(1)}, bf16[4,8,20,640]{3,1,2,0:T(8,128)(2,1)}, u32[]{:S(2)}) copy-start(bf16[4,8,20,640]{3,1,2,0:T(8,128)(2,1)} %param.10) | copy-start | bytes 2457604
  21.3 19.3 %copy-start.6 = (s32[21,4,128]{2,1,0:T(4,128)S(1)}, s32[21,4,128]{2,1,0:T(4,128)}, u32[]{:S(2)}) copy-start(s32[21,4,128]{2,1,0:T(4,128)} %param.18) | copy-start | bytes 129028
  25.1 16.0 %copy-start.3 = (bf16[20,32,640]{2,1,0:T(8,128)(2,1)S(1)}, bf16[20,32,640]{2,1,0:T(8,128)(2,1)}, u32[]{:S(2)}) copy-start(bf16[20,32,640]{2,1,0:T(8,128)(2,1)} %param.11) | copy-start | bytes 2457604
  25.1 43.0 %collective-permute-start.2 = (bf16[4,320,128]{2,1,0:T(8,128)(2,1)}, bf16[4,320,128]{2,1,0:T(8,128)(2,1)}, u32[]{:S(2)}, u32[]{:S(2)}) collective-permute-start(bf16[4,320,128]{2,1,0:T(8,128)(2,1)} %get-tuple-element.16), channel_id=1, source_target_pairs={{32,0},{48,16},{64,32},{80,48},{96,64},{112,80},{128,96},{144,112}... | collective-permute-start | bytes 983048 | tf_op jit(solution)/shard_map/ppermute | solution.py:35
  26.5 41.6 %collective-permute-start.3 = (bf16[4,320,128]{2,1,0:T(8,128)(2,1)}, bf16[4,320,128]{2,1,0:T(8,128)(2,1)}, u32[]{:S(2)}, u32[]{:S(2)}) collective-permute-start(bf16[4,320,128]{2,1,0:T(8,128)(2,1)} %get-tuple-element.17), channel_id=1, source_target_pairs={{16,0},{32,16},{48,32},{64,48},{80,64},{96,80},{112,96},{128,112},... | collective-permute-start | bytes 983048 | tf_op jit(solution)/shard_map/ppermute | solution.py:35
  27.8 40.3 %collective-permute-start.4 = (bf16[4,320,128]{2,1,0:T(8,128)(2,1)}, bf16[4,320,128]{2,1,0:T(8,128)(2,1)}, u32[]{:S(2)}, u32[]{:S(2)}) collective-permute-start(bf16[4,320,128]{2,1,0:T(8,128)(2,1)} %get-tuple-element.19), channel_id=1, source_target_pairs={{0,16},{16,32},{32,48},{48,64},{64,80},{80,96},{96,112},{112,128},... | collective-permute-start | bytes 983048 | tf_op jit(solution)/shard_map/ppermute | solution.py:35
  32.5 35.6 %collective-permute-start.5 = (bf16[4,320,128]{2,1,0:T(8,128)(2,1)}, bf16[4,320,128]{2,1,0:T(8,128)(2,1)}, u32[]{:S(2)}, u32[]{:S(2)}) collective-permute-start(bf16[4,320,128]{2,1,0:T(8,128)(2,1)} %get-tuple-element.20), channel_id=1, source_target_pairs={{0,32},{16,48},{32,64},{48,80},{64,96},{80,112},{96,128},{112,144}... | collective-permute-start | bytes 983048 | tf_op jit(solution)/shard_map/ppermute | solution.py:35
  40.6 15.5 %copy-start.7 = (s32[21,4,128]{2,1,0:T(4,128)S(1)}, s32[21,4,128]{2,1,0:T(4,128)}, u32[]{:S(2)}) copy-start(s32[21,4,128]{2,1,0:T(4,128)} %param.18) | copy-start | bytes 129028
  40.7 15.5 %copy-start.8 = (f32[21,4,1,128]{3,2,1,0:T(1,128)S(1)}, f32[21,4,1,128]{3,2,1,0:T(1,128)}, u32[]{:S(2)}) copy-start(f32[21,4,1,128]{3,2,1,0:T(1,128)} %get-tuple-element.58) | copy-start | bytes 129028
  43.3 21.4 %all-to-all-start = ((bf16[32,2,320]{2,1,0:T(2,128)(2,1)}), bf16[32,2,320]{2,1,0:T(2,128)(2,1)S(1)}, u32[]{:S(2)}, u32[]{:S(2)}) async-start(bf16[32,2,320]{2,1,0:T(2,128)(2,1)} %reshape.234), calls=%async_computation | async-start | bytes 98304 | tf_op jit(solution)/shard_map/all_to_all | solution.py:202
  68.1 8.6 %copy-start.5 = (bf16[2,8,1,2688]{3,1,0,2:T(8,128)(2,1)}, bf16[2,8,1,2688]{3,1,0,2:T(8,128)(2,1)S(1)}, u32[]{:S(2)}) copy-start(bf16[2,8,1,2688]{3,1,0,2:T(8,128)(2,1)S(1)} %convert_element_type.106) | copy-start | bytes 258052

commit v17 on v15

--- a/solution.py
+++ b/solution.py
@@ -95,7 +95,7 @@
     block_count, rows_per_block = stencil.shape[0], stencil.shape[1]
     count = len(pieces)
     cap, rows, _ = pieces[0].shape
-    group = 7 if block_count % 7 == 0 else 1
+    group = block_count
 
     def body(slot_ref, stencil_ref, wind_ref, *refs):
         piece_refs = refs[:count]

time: 77.9 us -> 77.8 us (level)
  no operation moved by 1% of the time
where the time goes in v17:
time: 77.8 us; the launch traced here: 77.3 us
  starting transfers between devices  31.9 us (41%)
  other arithmetic  12.5 us (16%)
  Pallas kernels  10.6 us (14%)
  local copies, waits for them, and re-layouts  10 us (13%)
  waiting for transfers between devices  8.68 us (11%)
  matrix products  2.5 us (3%)
  between operations  1.1 us (1%)
    ppermute x4, starting transfers between devices, shifted(): lax.ppermute(value, axis, [(source, source + steps) for source in range(l...  14.1 us
    all_to_all x1, starting transfers between devices, shards(): lax.all_to_all(coefficients, 'band', split_axis=2, concat_axis=3, tiled=T...  13.4 us
    pallas_call x1, Pallas kernels, apply_stencil(): pl.pallas_call(body, grid_spec=grid_spec, out_shape=out_shape, compiler_p...  7 us
    all_to_all x1, waiting for transfers between devices, shards(): lax.all_to_all(coefficients, 'band', split_axis=2, concat_axis=3, tiled=T...  5.24 us
    convert_element_type x1, other arithmetic, shards(): stencil = stencil_matrix(depart_offset, depart_weight).astype(jnp.bfloat16)  4.1 us
    reshape x1, other arithmetic, shards(): vertical_sum.astype(jnp.bfloat16).reshape(rows, lat_count * lon_count)  4.03 us
    pallas_call x1, Pallas kernels, pack_blocks(): pl.pallas_call(body, grid_spec=grid_spec, out_shape=out_shape)  3.58 us
    ppermute x1, waiting for transfers between devices, extended(): lax.ppermute(tail, axis, [(i, (i + 1) % count) for i in range(ends)])  3.43 us
  transfers between devices with their start and end apart: 7, of which 2 were waited for; matrix products, arithmetic and copies ran while one was open for 23% of the time, Pallas kernels for 0%

profile of v17, /device:TPU:32, one launch (start us, length us, event | category | flops | bytes accessed | tf_op | source)
XLA Modules:
  0.0 77.3 jit_solution(14063495120422709850)
XLA Ops:
  0.7 2.8 %fusion.32 = (bf16[40,1,1,2688]{3,1,2,0:T(2,128)(2,1)S(1)}, bf16[40,1,1,2688]{3,1,2,0:T(2,128)(2,1)S(1)}) fusion(bf16[40,8,1,2688]{3,1,2,0:T(8,128)(2,1)} %param.14), kind=kLoop, calls=%fused_computation.75 | loop fusion | bytes 860160 | tf_op jit(solution)/shard_map/slice | solution.py:20
  3.5 1.9 %collective-permute-start.1 = (bf16[40,1,1,2688]{3,0,2,1:T(8,128)(2,1)S(1)}, bf16[40,1,1,2688]{3,0,2,1:T(8,128)(2,1)S(1)}, u32[]{:S(2)}, u32[]{:S(2)}) collective-permute-start(bf16[40,1,1,2688]{3,0,2,1:T(8,128)(2,1)S(1)} %copy.72), channel_id=1, source_target_pairs={{1,0},{2,1},{3,2},{4,3},{5,4},{6,5},{7,6},{8,7},{9,8},{10,9},{11,1... | collective-permute-start | bytes 645128 | tf_op jit(solution)/shard_map/ppermute | solution.py:25
  5.5 2.4 %collective-permute-start = (bf16[40,1,1,2688]{3,0,2,1:T(8,128)(2,1)S(1)}, bf16[40,1,1,2688]{3,0,2,1:T(8,128)(2,1)S(1)}, u32[]{:S(2)}, u32[]{:S(2)}) collective-permute-start(bf16[40,1,1,2688]{3,0,2,1:T(8,128)(2,1)S(1)} %copy.71), channel_id=1, source_target_pairs={{0,1},{1,2},{2,3},{3,4},{4,5},{5,6},{6,7},{7,8},{8,9},{9,10},{10,1... | collective-permute-start | bytes 645128 | tf_op jit(solution)/shard_map/ppermute | solution.py:23
  7.9 0.7 slice_bitcast_fusion.2
  8.7 0.7 min.12.listed_ref
  9.5 0.6 reshape.211.slot_ref
  10.1 0.3 copy.58
  10.5 3.4 %collective-permute-done = bf16[40,1,1,2688]{3,0,2,1:T(8,128)(2,1)S(1)} collective-permute-done((bf16[40,1,1,2688]{3,0,2,1:T(8,128)(2,1)S(1)}, bf16[40,1,1,2688]{3,0,2,1:T(8,128)(2,1)S(1)}, u32[]{:S(2)}, u32[]{:S(2)}) %collective-permute-start) | collective-permute-done | bytes 215072 | tf_op jit(solution)/shard_map/ppermute | solution.py:23
  13.9 0.3 copy.56
  14.3 4.0 %fusion.3.source_ref = bf16[320,2688]{1,0:T(8,128)(2,1)} fusion(bf16[40,8,1,2688]{3,1,2,0:T(8,128)(2,1)S(1)} %copy-done.1, bf16[40,1,1,2688]{3,1,2,0:T(2,128)(2,1)S(1)} %copy.58, bf16[40,1,1,2688]{3,1,2,0:T(2,128)(2,1)S(1)} %copy.56, f32[8,2688]{1,0:T(8,128)} %get-tuple-element.51, f32[8,2688]{1,0:T(8,128)} %get-tuple-element.52, ...), kind=kLoop, calls=%fused_computation.10 | loop fusion | flops 12902400 | bytes 4128768 | tf_op jit(solution)/shard_map/reshape | solution.py:170
  18.3 3.6 %shard_map.121 = (bf16[4,320,128]{2,1,0:T(8,128)(2,1)}, bf16[4,320,128]{2,1,0:T(8,128)(2,1)}, bf16[4,320,128]{2,1,0:T(8,128)(2,1)}, bf16[4,320,128]{2,1,0:T(8,128)(2,1)}, bf16[4,320,128]{2,1,0:T(8,128)(2,1)}) custom-call(s32[20]{0:T(128)} %min.12.listed_ref, bf16[320,2688]{1,0:T(8,128)(2,1)} %fusion.3.source_ref), custom_call_target="tpu_custom_call" | custom-call | tf_op jit(solution)/shard_map/pallas_call | solution.py:91
  21.9 1.4 %collective-permute-start.2 = (bf16[4,320,128]{2,1,0:T(8,128)(2,1)}, bf16[4,320,128]{2,1,0:T(8,128)(2,1)}, u32[]{:S(2)}, u32[]{:S(2)}) collective-permute-start(bf16[4,320,128]{2,1,0:T(8,128)(2,1)} %get-tuple-element.16), channel_id=1, source_target_pairs={{32,0},{48,16},{64,32},{80,48},{96,64},{112,80},{128,96},{144,112}... | collective-permute-start | bytes 983048 | tf_op jit(solution)/shard_map/ppermute | solution.py:35
  23.3 1.3 %collective-permute-start.3 = (bf16[4,320,128]{2,1,0:T(8,128)(2,1)}, bf16[4,320,128]{2,1,0:T(8,128)(2,1)}, u32[]{:S(2)}, u32[]{:S(2)}) collective-permute-start(bf16[4,320,128]{2,1,0:T(8,128)(2,1)} %get-tuple-element.17), channel_id=1, source_target_pairs={{16,0},{32,16},{48,32},{64,48},{80,64},{96,80},{112,96},{128,112},... | collective-permute-start | bytes 983048 | tf_op jit(solution)/shard_map/ppermute | solution.py:35
  24.6 5.3 %collective-permute-start.4 = (bf16[4,320,128]{2,1,0:T(8,128)(2,1)}, bf16[4,320,128]{2,1,0:T(8,128)(2,1)}, u32[]{:S(2)}, u32[]{:S(2)}) collective-permute-start(bf16[4,320,128]{2,1,0:T(8,128)(2,1)} %get-tuple-element.19), channel_id=1, source_target_pairs={{0,16},{16,32},{32,48},{48,64},{64,80},{80,96},{96,112},{112,128},... | collective-permute-start | bytes 983048 | tf_op jit(solution)/shard_map/ppermute | solution.py:35
  29.9 6.1 %collective-permute-start.5 = (bf16[4,320,128]{2,1,0:T(8,128)(2,1)}, bf16[4,320,128]{2,1,0:T(8,128)(2,1)}, u32[]{:S(2)}, u32[]{:S(2)}) collective-permute-start(bf16[4,320,128]{2,1,0:T(8,128)(2,1)} %get-tuple-element.20), channel_id=1, source_target_pairs={{0,32},{16,48},{32,64},{48,80},{64,96},{80,112},{96,128},{112,144}... | collective-permute-start | bytes 983048 | tf_op jit(solution)/shard_map/ppermute | solution.py:35
  36.0 1.4 %fusion.16 = (f32[640,128]{1,0:T(8,128)S(1)}, f32[640,128]{1,0:T(8,128)S(1)}) fusion(s32[640]{0:T(1024)S(1)} %copy-done.9), kind=kLoop, calls=%fused_computation.32 | loop fusion | flops 737280 | bytes 657920 | tf_op jit(solution)/shard_map/cos | solution.py:56
  37.5 1.4 %broadcast_add_fusion.2 = (s32[21,4,128]{2,1,0:T(4,128)}, s32[21,4,128]{2,1,0:T(4,128)S(1)}, s32[21,4,128]{2,1,0:T(4,128)S(1)}) fusion(s32[21,4,128]{2,1,0:T(4,128)} %param.18), kind=kLoop, calls=%fused_computation.69 | loop fusion | flops 32256 | bytes 172032 | tf_op jit(solution)/shard_map/add | solution.py:67
  39.0 0.7 slice_convert_fusion.3
  39.7 0.4 convolution_bitcast_fusion.1
  40.1 0.4 convolution_bitcast_fusion
  40.7 0.6 copy.61
  41.3 1.0 %reshape.222 = bf16[32,2,320]{2,1,0:T(2,128)(2,1)} reshape(bf16[32,4,8,20]{3,2,1,0:T(8,128)(2,1)S(1)} %bitcast.51) | data formatting | bytes 81920
  42.2 13.4 %all-to-all-start = ((bf16[32,2,320]{2,1,0:T(2,128)(2,1)}), bf16[32,2,320]{2,1,0:T(2,128)(2,1)S(1)}, u32[]{:S(2)}, u32[]{:S(2)}) async-start(bf16[32,2,320]{2,1,0:T(2,128)(2,1)} %reshape.222), calls=%async_computation | async-start | bytes 98304 | tf_op jit(solution)/shard_map/all_to_all | solution.py:208
  55.7 4.1 %add_convert_fusion.stencil_ref = bf16[21,4,128,128]{3,2,1,0:T(8,128)(2,1)} fusion(f32[21,4,128]{2,1,0:T(4,128)S(1)} %bitcast.54, s32[21,4,128]{2,1,0:T(4,128)S(1)} %get-tuple-element.62, f32[21,4,128]{2,1,0:T(4,128)S(1)} %bitcast.55, s32[21,4,128]{2,1,0:T(4,128)S(1)} %get-tuple-element.63, f32[21,4,128]{2,1,0:T(4,128)S(1)} %bitcast.56, ...), kind=kLoop, calls=%fused_computation | loop fusion | flops 16515072 | bytes 3096576 | tf_op jit(solution)/shard_map/convert_element_type | solution.py:181
  59.8 0.3 cosine_multiply_fusion
  60.1 5.2 %all-to-all-done = bf16[32,2,320]{2,1,0:T(2,128)(2,1)S(1)} async-done(((bf16[32,2,320]{2,1,0:T(2,128)(2,1)}), bf16[32,2,320]{2,1,0:T(2,128)(2,1)S(1)}, u32[]{:S(2)}, u32[]{:S(2)}) %all-to-all-start) | async-done | bytes 40992 | tf_op jit(solution)/shard_map/all_to_all | solution.py:208
  65.4 0.4 reshape.223
  65.8 0.4 copy.62
  67.0 1.7 %fusion.4 = bf16[2,8,21,128]{3,2,1,0:T(8,128)(2,1)S(1)} fusion(f32[2,8,1,21,640]{4,3,1,0,2:T(8,128)S(1)} %get-tuple-element.54, f32[2,8,1,21,640]{4,3,1,0,2:T(8,128)S(1)} %get-tuple-element.53, f32[640,128]{1,0:T(8,128)S(1)} %get-tuple-element.67, f32[640,128]{1,0:T(8,128)S(1)} %get-tuple-element.66), kind=kOutput, calls=%fused_computation.15 | convolution fusion | flops 661239808 | bytes 2461696 | tf_op jit(solution)/shard_map/wklom,mi->wkloi/dot_general | solution.py:57
  68.7 0.7 convert_element_type.86.wind_ref
  69.4 0.7 convert_element_type.84
  70.1 7.0 %shard_map.122 = (bf16[320,2688]{1,0:T(8,128)(2,1)}, bf16[2,8,2688]{2,1,0:T(8,128)(2,1)}) custom-call(s32[84]{0:T(128)} %reshape.211.slot_ref, bf16[21,4,128,128]{3,2,1,0:T(8,128)(2,1)} %add_convert_fusion.stencil_ref, bf16[2,8,2688]{2,1,0:T(8,128)(2,1)} %convert_element_type.86.wind_ref, bf16[4,320,128]{2,1,0:T(8,128)(2,1)} %collective-permute-done.2.refs_0_, ...), custom_call_target="tpu_custom_call" | custom-call | tf_op jit(solution)/shard_map/pallas_call | solution.py:145
  (44 shorter events, 1.4 us)
Async XLA Ops:
  0.6 39.1 %copy-start = (bf16[20,32,640]{2,1,0:T(8,128)(2,1)S(1)}, bf16[20,32,640]{2,1,0:T(8,128)(2,1)}, u32[]{:S(2)}) copy-start(bf16[20,32,640]{2,1,0:T(8,128)(2,1)} %param.12) | copy-start | bytes 2457604
  0.6 13.6 %copy-start.1 = (bf16[40,8,1,2688]{3,1,2,0:T(8,128)(2,1)S(1)}, bf16[40,8,1,2688]{3,1,2,0:T(8,128)(2,1)}, u32[]{:S(2)}) copy-start(bf16[40,8,1,2688]{3,1,2,0:T(8,128)(2,1)} %param.14) | copy-start | bytes 5160964
  0.7 7.2 %copy-start.8 = (bf16[3,8,1,2688]{3,1,2,0:T(8,128)(2,1)S(1)}, bf16[3,8,1,2688]{3,1,2,0:T(8,128)(2,1)}, u32[]{:S(2)}) copy-start(bf16[3,8,1,2688]{3,1,2,0:T(8,128)(2,1)} %param.15) | copy-start | bytes 387076
  0.7 8.0 %copy-start.11 = (s32[1,5,4]{1,2,0:T(4,128)S(1)}, s32[1,5,4]{1,2,0:T(4,128)}, u32[]{:S(2)}) copy-start(s32[1,5,4]{1,2,0:T(4,128)} %param.16) | copy-start | bytes 244
  0.7 8.7 %copy-start.10 = (s32[21,4]{0,1:T(4,128)S(1)}, s32[21,4]{0,1:T(4,128)}, u32[]{:S(2)}) copy-start(s32[21,4]{0,1:T(4,128)} %param.17) | copy-start | bytes 1012
  3.5 6.6 %collective-permute-start.1 = (bf16[40,1,1,2688]{3,0,2,1:T(8,128)(2,1)S(1)}, bf16[40,1,1,2688]{3,0,2,1:T(8,128)(2,1)S(1)}, u32[]{:S(2)}, u32[]{:S(2)}) collective-permute-start(bf16[40,1,1,2688]{3,0,2,1:T(8,128)(2,1)S(1)} %copy.72), channel_id=1, source_target_pairs={{1,0},{2,1},{3,2},{4,3},{5,4},{6,5},{7,6},{8,7},{9,8},{10,9},{11,1... | collective-permute-start | bytes 645128 | tf_op jit(solution)/shard_map/ppermute | solution.py:25
  5.5 8.4 %collective-permute-start = (bf16[40,1,1,2688]{3,0,2,1:T(8,128)(2,1)S(1)}, bf16[40,1,1,2688]{3,0,2,1:T(8,128)(2,1)S(1)}, u32[]{:S(2)}, u32[]{:S(2)}) collective-permute-start(bf16[40,1,1,2688]{3,0,2,1:T(8,128)(2,1)S(1)} %copy.71), channel_id=1, source_target_pairs={{0,1},{1,2},{2,3},{3,4},{4,5},{5,6},{6,7},{7,8},{8,9},{9,10},{10,1... | collective-permute-start | bytes 645128 | tf_op jit(solution)/shard_map/ppermute | solution.py:23
  14.2 21.8 %copy-start.9 = (s32[640]{0:T(1024)S(1)}, s32[640]{0:T(1024)}, u32[]{:S(2)}) copy-start(s32[640]{0:T(1024)} %param.13) | copy-start | bytes 7684
  14.2 24.7 %copy-start.4 = (bf16[21,4,4,128]{3,2,1,0:T(4,128)(2,1)S(1)}, bf16[21,4,4,128]{3,2,1,0:T(4,128)(2,1)}, u32[]{:S(2)}) copy-start(bf16[21,4,4,128]{3,2,1,0:T(4,128)(2,1)} %param.19) | copy-start | bytes 258052
  14.3 25.5 %copy-start.2 = (bf16[4,8,20,640]{3,1,2,0:T(8,128)(2,1)S(1)}, bf16[4,8,20,640]{3,1,2,0:T(8,128)(2,1)}, u32[]{:S(2)}) copy-start(bf16[4,8,20,640]{3,1,2,0:T(8,128)(2,1)} %param.10) | copy-start | bytes 2457604
  21.9 18.3 %copy-start.3 = (bf16[20,32,640]{2,1,0:T(8,128)(2,1)S(1)}, bf16[20,32,640]{2,1,0:T(8,128)(2,1)}, u32[]{:S(2)}) copy-start(bf16[20,32,640]{2,1,0:T(8,128)(2,1)} %param.11) | copy-start | bytes 2457604
  21.9 48.3 %collective-permute-start.2 = (bf16[4,320,128]{2,1,0:T(8,128)(2,1)}, bf16[4,320,128]{2,1,0:T(8,128)(2,1)}, u32[]{:S(2)}, u32[]{:S(2)}) collective-permute-start(bf16[4,320,128]{2,1,0:T(8,128)(2,1)} %get-tuple-element.16), channel_id=1, source_target_pairs={{32,0},{48,16},{64,32},{80,48},{96,64},{112,80},{128,96},{144,112}... | collective-permute-start | bytes 983048 | tf_op jit(solution)/shard_map/ppermute | solution.py:35
  23.3 46.8 %collective-permute-start.3 = (bf16[4,320,128]{2,1,0:T(8,128)(2,1)}, bf16[4,320,128]{2,1,0:T(8,128)(2,1)}, u32[]{:S(2)}, u32[]{:S(2)}) collective-permute-start(bf16[4,320,128]{2,1,0:T(8,128)(2,1)} %get-tuple-element.17), channel_id=1, source_target_pairs={{16,0},{32,16},{48,32},{64,48},{80,64},{96,80},{112,96},{128,112},... | collective-permute-start | bytes 983048 | tf_op jit(solution)/shard_map/ppermute | solution.py:35
  24.6 45.5 %collective-permute-start.4 = (bf16[4,320,128]{2,1,0:T(8,128)(2,1)}, bf16[4,320,128]{2,1,0:T(8,128)(2,1)}, u32[]{:S(2)}, u32[]{:S(2)}) collective-permute-start(bf16[4,320,128]{2,1,0:T(8,128)(2,1)} %get-tuple-element.19), channel_id=1, source_target_pairs={{0,16},{16,32},{32,48},{48,64},{64,80},{80,96},{96,112},{112,128},... | collective-permute-start | bytes 983048 | tf_op jit(solution)/shard_map/ppermute | solution.py:35
  29.9 40.2 %collective-permute-start.5 = (bf16[4,320,128]{2,1,0:T(8,128)(2,1)}, bf16[4,320,128]{2,1,0:T(8,128)(2,1)}, u32[]{:S(2)}, u32[]{:S(2)}) collective-permute-start(bf16[4,320,128]{2,1,0:T(8,128)(2,1)} %get-tuple-element.20), channel_id=1, source_target_pairs={{0,32},{16,48},{32,64},{48,80},{64,96},{80,112},{96,128},{112,144}... | collective-permute-start | bytes 983048 | tf_op jit(solution)/shard_map/ppermute | solution.py:35
  39.7 16.0 %copy-start.5 = (s32[21,4,128]{2,1,0:T(4,128)S(1)}, s32[21,4,128]{2,1,0:T(4,128)}, u32[]{:S(2)}) copy-start(s32[21,4,128]{2,1,0:T(4,128)} %param.18) | copy-start | bytes 129028
  39.7 16.0 %copy-start.6 = (s32[21,4,128]{2,1,0:T(4,128)S(1)}, s32[21,4,128]{2,1,0:T(4,128)}, u32[]{:S(2)}) copy-start(s32[21,4,128]{2,1,0:T(4,128)} %get-tuple-element.61) | copy-start | bytes 129028
  39.7 16.0 %copy-start.7 = (f32[21,4,1,128]{3,2,1,0:T(1,128)S(1)}, f32[21,4,1,128]{3,2,1,0:T(1,128)}, u32[]{:S(2)}) copy-start(f32[21,4,1,128]{3,2,1,0:T(1,128)} %get-tuple-element.58) | copy-start | bytes 129028
  42.2 23.2 %all-to-all-start = ((bf16[32,2,320]{2,1,0:T(2,128)(2,1)}), bf16[32,2,320]{2,1,0:T(2,128)(2,1)S(1)}, u32[]{:S(2)}, u32[]{:S(2)}) async-start(bf16[32,2,320]{2,1,0:T(2,128)(2,1)} %reshape.222), calls=%async_computation | async-start | bytes 98304 | tf_op jit(solution)/shard_map/all_to_all | solution.py:208
